TPU v7x, 32 devices: a whole 2x2x4 slice. The times are simulated.
32 devices in a mesh: fsdp: 8 (over y, x, core), dp: 4 (over z).
Axes of the slice: x: 2, y: 2, z: 4, core: 2. Of those that a mesh axis runs over, the one named last changes fastest.
Arguments:
- tokens: bfloat16 [12288, 8192], P(('fsdp', 'dp')), may hold values from -6 to 6
- output_gradient: bfloat16 [12288, 1024], P(('fsdp', 'dp')), may hold values from -6 to 6
- frozen_value_weight: bfloat16 [8192, 1024], P('fsdp'), may hold values from -0.0625 to 0.0625
- adapter_down_maps: bfloat16 [32, 16, 8192], P(('fsdp', 'dp')), may hold values from -0.0625 to 0.0625
- adapter_up_maps: bfloat16 [32, 16, 1024], P(('fsdp', 'dp')), may hold values from -1.5 to 1.5
- block_tenant_ids: int32 [96], P(('fsdp', 'dp')), may hold values from 0 to 31, as said below
- block_live_rows: int32 [96], P(('fsdp', 'dp')), may hold values from 33 to 128, as said below
- tenant_owner_slot: int32 [32], replicated, may hold values from 0 to 31, as said below
Outputs:
- output: bfloat16 [12288, 1024], P(('fsdp', 'dp'))
- token_gradient: bfloat16 [12288, 8192], P(('fsdp', 'dp'))
- grad_down: bfloat16 [32, 16, 8192], P(('fsdp', 'dp'))
- grad_up: bfloat16 [32, 16, 1024], P(('fsdp', 'dp'))
Inputs may be any that keep to these rules, and one draw needn't show every extreme that they name: `block_tenant_ids`: A block held by a device whose index along dp is d names a tenant t with tenant_owner_slot[t] mod (size of dp) = d; tenant_owner_slot is a permutation. `block_live_rows`: the first block of every device is full. `tenant_owner_slot`: each slot is named once.
All inputs are finite; a program needn't handle non-finite values.
Results may differ from a plain program's by a relative error of at most 0.01.
Values may be sent and summed in bfloat16 or wider, within the bound.
No kernel may reach another device: no remote copies, remote signals or barrier semaphores. Data moves between devices by JAX's collectives and lax.ppermute only.
A program may use at most 192 MiB of HBM per device.

v0:
```python
import jax
import jax.numpy as jnp
from jax import lax
from jax.sharding import PartitionSpec as P

ADAPTER_SCALE = 2.0


def on_device(
    tokens,
    output_gradient,
    frozen_value_weight,
    adapter_down_maps,
    adapter_up_maps,
    block_tenant_ids,
    block_live_rows,
    tenant_owner_slot,
):
    tok_rows = tokens.shape[0]
    model_width_size = tokens.shape[1]
    value_width_size = output_gradient.shape[1]
    adapter_rank_size = adapter_down_maps.shape[1]
    number_of_blocks = block_tenant_ids.shape[0]
    block_length = tok_rows // number_of_blocks
    groups = lax.axis_size("dp")
    members = lax.axis_size("fsdp")
    tenant_ids = jnp.arange(tenant_owner_slot.shape[0], dtype=jnp.int32)
    slot_ids = jnp.sum(
        jnp.where(block_tenant_ids[:, None] == tenant_ids[None, :], tenant_owner_slot[None, :], 0),
        axis=1,
    )
    member_ids = slot_ids // groups
    live_rows = (jnp.arange(block_length)[None, :] < block_live_rows[:, None]).astype(jnp.float32)
    live_column = live_rows[:, :, None]
    down_all, up_all = (
        lax.all_gather(adapter_down_maps, "fsdp", axis=0, tiled=True),
        lax.all_gather(adapter_up_maps, "fsdp", axis=0, tiled=True),
    )
    onehot = (member_ids[:, None] == jnp.arange(members)[None, :]).astype(jnp.bfloat16)
    down_block = jnp.dot(onehot, down_all.reshape(members, -1), preferred_element_type=jnp.float32)
    down_block = down_block.astype(jnp.bfloat16).reshape(
        number_of_blocks, adapter_rank_size, model_width_size
    )
    up_block = jnp.dot(onehot, up_all.reshape(members, -1), preferred_element_type=jnp.float32)
    up_block = up_block.astype(jnp.bfloat16).reshape(
        number_of_blocks, adapter_rank_size, value_width_size
    )
    token_blocks = tokens.reshape(number_of_blocks, block_length, model_width_size)
    cot_blocks = output_gradient.reshape(number_of_blocks, block_length, value_width_size)
    low_rank_state = (
        jnp.einsum("cvj,coj->cvo", token_blocks, down_block, preferred_element_type=jnp.float32)
        * live_column
    ).astype(jnp.bfloat16)
    low_rank_gradient = (
        ADAPTER_SCALE
        * jnp.einsum("btv,bkv->btk", cot_blocks, up_block, preferred_element_type=jnp.float32)
        * live_column
    ).astype(jnp.bfloat16)
    adapter_output = jnp.einsum(
        "znr,zrm->znm", low_rank_state, up_block, preferred_element_type=jnp.float32
    )
    adapter_backward = jnp.einsum(
        "uio,uof->uif", low_rank_gradient, down_block, preferred_element_type=jnp.float32
    )
    weight_piece = lax.all_gather(frozen_value_weight, "fsdp", axis=0, tiled=True)
    output_total = jnp.dot(tokens, weight_piece, preferred_element_type=jnp.float32)
    backward_piece = lax.dot_general(
        output_gradient, weight_piece, (((1,), (1,)), ((), ())), preferred_element_type=jnp.float32
    )
    output = live_column * (
        output_total.reshape(number_of_blocks, block_length, value_width_size)
        + ADAPTER_SCALE * adapter_output
    )
    output = output.astype(jnp.bfloat16).reshape(tok_rows, value_width_size)
    token_gradient = live_column * (
        backward_piece.reshape(number_of_blocks, block_length, model_width_size) + adapter_backward
    )
    token_gradient = token_gradient.astype(jnp.bfloat16).reshape(tok_rows, model_width_size)
    partial_down = jnp.einsum(
        "vio,vih->voh", low_rank_gradient, token_blocks, preferred_element_type=jnp.float32
    )
    partial_up = ADAPTER_SCALE * jnp.einsum(
        "btk,btv->bkv", low_rank_state, cot_blocks, preferred_element_type=jnp.float32
    )
    member_range = jnp.arange(members, dtype=jnp.int32)
    table_down = jnp.zeros((members, adapter_rank_size, model_width_size), jnp.float32)
    table_up = jnp.zeros((members, adapter_rank_size, value_width_size), jnp.float32)
    for block_num in range(number_of_blocks):
        picked = (member_range == member_ids[block_num]).astype(jnp.float32)[:, None, None]
        table_down = table_down + picked * partial_down[block_num][None]
        table_up = table_up + picked * partial_up[block_num][None]
    term_down = table_down.astype(jnp.bfloat16)
    term_up = table_up.astype(jnp.bfloat16)
    sum_down, sum_up = (
        lax.psum_scatter(
            term_down.astype(jnp.float32).astype(jnp.bfloat16),
            "fsdp",
            scatter_dimension=0,
            tiled=True,
        ).astype(jnp.float32),
        lax.psum_scatter(
            term_up.astype(jnp.float32).astype(jnp.bfloat16),
            "fsdp",
            scatter_dimension=0,
            tiled=True,
        ).astype(jnp.float32),
    )
    return (output, token_gradient, sum_down.astype(jnp.bfloat16), sum_up.astype(jnp.bfloat16))


def solution(mesh):
    placed = (
        P(("fsdp", "dp"), None),
        P(("fsdp", "dp"), None),
        P("fsdp", None),
        P(("fsdp", "dp"), None, None),
        P(("fsdp", "dp"), None, None),
        P(("fsdp", "dp")),
        P(("fsdp", "dp")),
        P(),
    )
    return jax.shard_map(
        on_device,
        mesh=mesh,
        in_specs=placed,
        out_specs=(
            P(("fsdp", "dp"), None),
            P(("fsdp", "dp"), None),
            P(("fsdp", "dp"), None, None),
            P(("fsdp", "dp"), None, None),
        ),
        check_vma=False,
    )
```

profile of v0, /device:TPU:0, one launch (start us, length us, event | category | flops | bytes accessed | tf_op | source)
XLA Modules:
  0.0 221.4 jit_solution(15387211955821967845)
XLA Ops:
  7.2 0.0 copy-start
  7.2 0.0 all-gather.5.cloned.1.call-start
  7.2 0.7 all-gather.5.cloned.1.call-update
  7.9 0.0 all-gather.3.cloned.1.call-start
  8.0 0.7 all-gather.3.cloned.1.call-update
  8.7 0.0 reduce-scatter.3.cloned.1.call-start
  8.7 11.0 %all_gather.11 = bf16[8,16,1024]{2,1,0:T(8,128)(2,1)S(1)} all-gather(bf16[1,16,1024]{2,1,0:T(8,128)(2,1)} %param.12), channel_id=1, replica_groups=mesh['fsdp'=8,'dp'=4] {'fsdp'}, dimensions={0}, use_global_device_ids=true | all-gather | bytes 294912 | tf_op jit(solution)/shard_map/all_gather | solution.py:37
  19.7 0.1 copy.14
  19.8 0.9 select_reduce_fusion
  20.7 0.6 fusion.14
  21.3 0.6 compare_convert_fusion.2
  22.0 1.3 compare_convert_fusion
  23.3 0.7 fusion.10
  24.0 0.3 convolution_convert_fusion.1
  24.3 0.0 copy-done
  24.3 0.3 fusion.1
  24.6 3.7 %fusion.17 = f32[3,16,8192]{2,1,0:T(8,128)S(1)} fusion(bf16[3,16,128]{2,1,0:T(8,128)(2,1)S(1)} %fusion.1, bf16[3,128,8192]{2,1,0:T(8,128)(2,1)} %bitcast.53), kind=kOutput, calls=%fused_computation.43 | convolution fusion | flops 100663296 | bytes 7876608 | tf_op jit(solution)/shard_map/vio,vih->voh/dot_general | solution.py:79
  28.3 0.0 copy-start.1
  28.3 0.1 slice_bitcast_fusion.2
  28.4 2.2 add_convert_fusion
  30.6 0.0 reduce-scatter.3.cloned.1.call-update
  30.6 0.2 reduce-scatter.5.cloned.1.call-start
  30.8 0.0 copy-done.1
  30.8 0.1 fusion.11
  30.9 9.6 %all-gather.5.cloned.1.call-done = bf16[8,16,8192]{2,1,0:T(8,128)(2,1)} async-done(((bf16[1,16,8192]{2,1,0:T(8,128)(2,1)}), bf16[8,16,8192]{2,1,0:T(8,128)(2,1)}) %all-gather.5.cloned.1.call-update) | async-done | bytes 2097168 | tf_op jit(solution)/shard_map/all_gather | solution.py:36
  40.5 2.7 %copy.12 = bf16[1,8,16,8192]{3,1,2,0:T(8,128)(2,1)S(1)} copy(bf16[1,8,16,8192]{3,2,1,0:T(8,128)(2,1)} %bitcast.60) | data formatting | bytes 4194304
  43.3 0.8 convolution_convert_fusion
  44.0 4.5 %fusion = bf16[3,16,128]{2,1,0:T(8,128)(2,1)S(1)} fusion(bf16[3,128,8192]{2,1,0:T(8,128)(2,1)} %bitcast.54, bf16[1,3,16,8192]{3,1,2,0:T(4,128)(2,1)S(1)} %bitcast.57, f32[3,128]{1,0:T(4,128)S(1)} %fusion.11), kind=kOutput, calls=%fused_computation.8 | convolution fusion | flops 100675584 | bytes 7091712 | tf_op jit(solution)/shard_map/cvj,coj->cvo/dot_general | solution.py:51
  48.6 0.2 convolution_multiply_fusion
  48.8 0.9 add_convert_fusion.1
  49.7 0.0 reduce-scatter.5.cloned.1.call-update
  49.7 82.6 %all-gather.3.cloned.1.call-done = bf16[8192,1024]{1,0:T(8,128)(2,1)} async-done(((bf16[1024,1024]{1,0:T(8,128)(2,1)}), bf16[8192,1024]{1,0:T(8,128)(2,1)}) %all-gather.3.cloned.1.call-update) | async-done | bytes 16777232 | tf_op jit(solution)/shard_map/all_gather | solution.py:65
  132.3 12.1 %fusion.15 = f32[384,1024]{1,0:T(8,128)S(1)} fusion(bf16[384,8192]{1,0:T(8,128)(2,1)} %param.8, bf16[8192,1024]{1,0:T(8,128)(2,1)} %all-gather.3.cloned.1.call-done), kind=kOutput, calls=%fused_computation.41 | convolution fusion | flops 6442450944 | bytes 24641536 | tf_op jit(solution)/shard_map/dot_general | solution.py:66
  144.4 13.4 %fusion.16 = f32[384,8192]{1,0:T(8,128)} fusion(bf16[384,1024]{1,0:T(8,128)(2,1)S(1)} %copy-done, bf16[8192,1024]{1,0:T(8,128)(2,1)} %all-gather.3.cloned.1.call-done), kind=kOutput, calls=%fused_computation.42 | convolution fusion | flops 6442450944 | bytes 30146560 | tf_op jit(solution)/shard_map/dot_general | solution.py:67
  157.8 9.2 %multiply_convert_fusion = bf16[3,128,8192]{2,1,0:T(8,128)(2,1)} fusion(f32[3,128,8192]{2,1,0:T(8,128)} %bitcast.55, bf16[3,16,128]{2,1,0:T(8,128)(2,1)S(1)} %fusion.1, f32[3,128]{1,0:T(4,128)S(1)} %fusion.11, bf16[1,3,16,8192]{3,1,2,0:T(4,128)(2,1)S(1)} %bitcast.58), kind=kOutput, calls=%fused_computation.2 | convolution fusion | flops 110100480 | bytes 19674624 | tf_op jit(solution)/shard_map/uio,uof->uif/dot_general | solution.py:62
  167.0 1.3 multiply_convert_fusion.1
  168.3 9.2 %reduce-scatter.3.cloned.1.call-done = bf16[1,16,8192]{2,1,0:T(8,128)(2,1)} async-done(((bf16[8,16,8192]{2,1,0:T(8,128)(2,1)}), bf16[1,16,8192]{2,1,0:T(8,128)(2,1)}) %reduce-scatter.3.cloned.1.call-update) | async-done | bytes 262160 | tf_op jit(solution)/shard_map/reduce_scatter | solution.py:95
  177.4 37.4 %reduce-scatter.5.cloned.1.call-done = bf16[1,16,1024]{2,1,0:T(8,128)(2,1)} async-done(((bf16[8,16,1024]{2,1,0:T(8,128)(2,1)}), bf16[1,16,1024]{2,1,0:T(8,128)(2,1)}) %reduce-scatter.5.cloned.1.call-update) | async-done | bytes 32784 | tf_op jit(solution)/shard_map/reduce_scatter | solution.py:101
  (2 shorter events, 0.0 us)
Async XLA Ops:
  7.2 17.1 %copy-start = (bf16[384,1024]{1,0:T(8,128)(2,1)S(1)}, bf16[384,1024]{1,0:T(8,128)(2,1)}, u32[]{:S(2)}) copy-start(bf16[384,1024]{1,0:T(8,128)(2,1)} %param.9) | copy-start | bytes 2359300
  7.2 33.4 %all-gather.5.cloned.1.call-start = ((), (), s32[]{:S(2)}) async-start(), calls=%async_computation.3 | async-start | bytes 2359296 | tf_op jit(solution)/shard_map/all_gather | solution.py:36
  7.9 124.4 %all-gather.3.cloned.1.call-start = ((), (), s32[]{:S(2)}) async-start(), calls=%async_computation.2 | async-start | bytes 18874368 | tf_op jit(solution)/shard_map/all_gather | solution.py:65
  8.7 168.8 %reduce-scatter.3.cloned.1.call-start = ((), (), s32[]{:S(2)}) async-start(), calls=%async_computation.4 | async-start | bytes 2359296 | tf_op jit(solution)/shard_map/reduce_scatter | solution.py:95
  28.3 2.5 %copy-start.1 = (s32[3]{0:T(128)S(1)}, s32[3]{0:T(128)}, u32[]{:S(2)}) copy-start(s32[3]{0:T(128)} %param.14) | copy-start | bytes 40
  30.6 184.2 %reduce-scatter.5.cloned.1.call-start = ((), (), s32[]{:S(2)}) async-start(), calls=%async_computation.5 | async-start | bytes 294912 | tf_op jit(solution)/shard_map/reduce_scatter | solution.py:101
Sparse Core Ops, SparseCore 0:
  9.9 30.5 all-gather.4
  42.4 89.8 all-gather.2
  136.2 41.2 reduce-scatter.2
  181.2 33.5 reduce-scatter.4
where the time goes:
time: 222 us; the launch traced here: 221 us
  waiting for transfers between devices  140 us (63%)
  matrix products  45.8 us (21%)
  between operations  13.8 us (6%)
  blocking collectives  11 us (5%)
  other arithmetic  6.64 us (3%)
  local copies, waits for them, and re-layouts  3.62 us (2%)
    all_gather x1, waiting for transfers between devices, on_device(): lax.all_gather(frozen_value_weight, 'fsdp', axis=0, tiled=True)  82.6 us
    reduce_scatter x1, waiting for transfers between devices, on_device(): lax.psum_scatter(term_up.astype(jnp.float32).astype(jnp.bfloat16), 'fsdp'...  37.4 us
    dot_general x1, matrix products, on_device(): lax.dot_general(output_gradient, weight_piece, (((1,), (1,)), ((), ())),...  13.4 us
    dot_general x1, matrix products, on_device(): jnp.dot(tokens, weight_piece, preferred_element_type=jnp.float32)  12.1 us
    all_gather x1, blocking collectives, on_device(): lax.all_gather(adapter_up_maps, 'fsdp', axis=0, tiled=True)  11 us
    all_gather x1, waiting for transfers between devices, on_device(): lax.all_gather(adapter_down_maps, 'fsdp', axis=0, tiled=True)  9.62 us
    dot_general x1, matrix products, on_device(): jnp.einsum('uio,uof->uif', low_rank_gradient, down_block, preferred_eleme...  9.17 us
    reduce_scatter x1, waiting for transfers between devices, on_device(): lax.psum_scatter(term_down.astype(jnp.float32).astype(jnp.bfloat16), 'fsd...  9.16 us
  transfers between devices with their start and end apart: 4, of which 4 were waited for; matrix products, arithmetic and copies ran while one was open for 25% of the time, Pallas kernels for 0%

commit v1 on v0

v1 whole, which is shorter than its diff:
```python
import jax
import jax.numpy as jnp
from jax import lax
from jax.sharding import PartitionSpec as P

ADAPTER_SCALE = 2.0


def xor_pairs(count, step):
    return [(src, src ^ step) for src in range(count)]


def on_device(
    tokens,
    output_gradient,
    frozen_value_weight,
    adapter_down_maps,
    adapter_up_maps,
    block_tenant_ids,
    block_live_rows,
    tenant_owner_slot,
):
    tok_rows, model_width = tokens.shape
    value_width = output_gradient.shape[1]
    rank = adapter_down_maps.shape[1]
    blocks = block_tenant_ids.shape[0]
    block_length = tok_rows // blocks
    groups = lax.axis_size("dp")
    members = lax.axis_size("fsdp")
    shard_rows = frozen_value_weight.shape[0]
    me = lax.axis_index("fsdp")

    own_adapter = jnp.concatenate([adapter_down_maps[0], adapter_up_maps[0]], axis=1)
    gathered = [own_adapter]
    for step in range(1, members):
        gathered.append(lax.ppermute(own_adapter, "fsdp", xor_pairs(members, step)))
    adapter_stack = jnp.stack(gathered)

    slot_ids = jnp.take(tenant_owner_slot, block_tenant_ids)
    member_ids = slot_ids // groups
    picked = jnp.stack([lax.dynamic_index_in_dim(adapter_stack, me ^ member_ids[b], 0, keepdims=False)
                        for b in range(blocks)])
    down_block = picked[:, :, :model_width]
    up_block = picked[:, :, model_width:]

    live_rows = (jnp.arange(block_length)[None, :] < block_live_rows[:, None]).astype(jnp.float32)
    live_column = live_rows[:, :, None]
    token_blocks = tokens.reshape(blocks, block_length, model_width)
    cot_blocks = output_gradient.reshape(blocks, block_length, value_width)

    low_rank_state = (
        jnp.einsum("cvj,coj->cvo", token_blocks, down_block, preferred_element_type=jnp.float32)
        * live_column
    ).astype(jnp.bfloat16)
    low_rank_gradient = (
        ADAPTER_SCALE
        * jnp.einsum("btv,bkv->btk", cot_blocks, up_block, preferred_element_type=jnp.float32)
        * live_column
    ).astype(jnp.bfloat16)

    partial_down = jnp.einsum(
        "vio,vih->voh", low_rank_gradient, token_blocks, preferred_element_type=jnp.float32
    )
    partial_up = ADAPTER_SCALE * jnp.einsum(
        "btk,btv->bkv", low_rank_state, cot_blocks, preferred_element_type=jnp.float32
    )
    partial = jnp.concatenate([partial_down, partial_up], axis=2)

    def table_row(member):
        row = jnp.zeros(partial.shape[1:], jnp.float32)
        for b in range(blocks):
            row = row + jnp.where(member_ids[b] == member, partial[b], 0.0)
        return row.astype(jnp.bfloat16)

    grad_sum = table_row(me).astype(jnp.float32)
    for step in range(1, members):
        sent = table_row(me ^ step)
        grad_sum = grad_sum + lax.ppermute(sent, "fsdp", xor_pairs(members, step)).astype(jnp.float32)
    grad_sum = grad_sum.astype(jnp.bfloat16)
    grad_down = grad_sum[None, :, :model_width]
    grad_up = grad_sum[None, :, model_width:]

    weight_parts = {0: frozen_value_weight}
    for step in range(2, members, 2):
        weight_parts[step] = lax.ppermute(frozen_value_weight, "fsdp", xor_pairs(members, step))
    for step in range(0, members, 2):
        weight_parts[step + 1] = lax.ppermute(weight_parts[step], "fsdp", xor_pairs(members, 1))

    adapter_output = jnp.einsum(
        "znr,zrm->znm", low_rank_state, up_block, preferred_element_type=jnp.float32
    ).reshape(tok_rows, value_width)
    live_flat = live_rows.reshape(tok_rows, 1)
    masked_cot = (output_gradient * live_flat).astype(jnp.bfloat16)

    output_total = ADAPTER_SCALE * adapter_output
    token_gradient = jnp.zeros((tok_rows, model_width), jnp.bfloat16)
    for step in range(members):
        weight_piece = weight_parts[step]
        column = (me ^ step) * shard_rows
        token_piece = lax.dynamic_slice_in_dim(tokens, column, shard_rows, axis=1)
        output_total = output_total + jnp.dot(
            token_piece, weight_piece, preferred_element_type=jnp.float32
        )
        down_piece = lax.dynamic_slice_in_dim(down_block, column, shard_rows, axis=2)
        backward_piece = lax.dot_general(
            masked_cot, weight_piece, (((1,), (1,)), ((), ())), preferred_element_type=jnp.float32
        ) + jnp.einsum(
            "uio,uof->uif", low_rank_gradient, down_piece, preferred_element_type=jnp.float32
        ).reshape(tok_rows, shard_rows)
        token_gradient = lax.dynamic_update_slice_in_dim(
            token_gradient, backward_piece.astype(jnp.bfloat16), column, axis=1
        )
    output = (live_flat * output_total).astype(jnp.bfloat16)
    return (output, token_gradient, grad_down, grad_up)


def solution(mesh):
    placed = (
        P(("fsdp", "dp"), None),
        P(("fsdp", "dp"), None),
        P("fsdp", None),
        P(("fsdp", "dp"), None, None),
        P(("fsdp", "dp"), None, None),
        P(("fsdp", "dp")),
        P(("fsdp", "dp")),
        P(),
    )
    return jax.shard_map(
        on_device,
        mesh=mesh,
        in_specs=placed,
        out_specs=(
            P(("fsdp", "dp"), None),
            P(("fsdp", "dp"), None),
            P(("fsdp", "dp"), None, None),
            P(("fsdp", "dp"), None, None),
        ),
        check_vma=False,
    )
```

time: 222 us -> 208 us (0.937)
  waiting for transfers between devices: 140 us -> 117 us
  starting transfers between devices: 0.34 us -> 19 us
  blocking collectives: 11 us -> 0 us
  matrix products: 45.8 us -> 38.2 us
  local copies, waits for them, and re-layouts: 3.62 us -> 8.64 us
  between operations: 13.8 us -> 18.7 us
    ppermute x0 -> x21, waiting for transfers between devices: none -> 117 us  [the longest x3 89.6 us: on_device(): lax.ppermute(frozen_value_weight, 'fsdp', xor_pairs(members, step))]
    all_gather x2 -> x0, waiting for transfers between devices: 92.2 us -> none  [the longest x1 82.6 us: on_device(): lax.all_gather(frozen_value_weight, 'fsdp', axis=0, tiled=True)]
    reduce_scatter x2 -> x0, waiting for transfers between devices: 46.5 us -> none  [the longest x1 37.4 us: on_device(): lax.psum_scatter(term_up.astype(jnp.float32).astype(jnp.bfloat16), 'fsdp'...]
    ppermute x0 -> x21, starting transfers between devices: none -> 19 us  [the longest x7 7.73 us: on_device(): gathered.append(lax.ppermute(own_adapter, 'fsdp', xor_pairs(members, step)))]
    all_gather x1 -> x0, blocking collectives: 11 us -> none  [on_device(): lax.all_gather(adapter_up_maps, 'fsdp', axis=0, tiled=True)]
    convert_element_type x4, other arithmetic: 4.98 us -> 1.23 us  [the longest x3 0.85 us: table_row(): return row.astype(jnp.bfloat16)]
    dot_general x1, matrix products: 4.53 us -> 1.73 us  [on_device(): jnp.einsum('cvj,coj->cvo', token_blocks, down_block, preferred_element_ty...]
    dot_general x1, matrix products: 3.72 us -> 0.93 us  [on_device(): jnp.einsum('vio,vih->voh', low_rank_gradient, token_blocks, preferred_ele...]
  transfers between devices with their start and end apart: 4 -> 21, of which waited for: 4 -> 5; matrix products, arithmetic and copies ran while one was open for 25% -> 20% of each run, Pallas kernels for 0% -> 0%
where the time goes in v1:
time: 208 us; the launch traced here: 207 us
  waiting for transfers between devices  117 us (56%)
  matrix products  38.2 us (18%)
  starting transfers between devices  19 us (9%)
  between operations  18.7 us (9%)
  local copies, waits for them, and re-layouts  8.64 us (4%)
  other arithmetic  6.11 us (3%)
    ppermute x3, waiting for transfers between devices, on_device(): lax.ppermute(frozen_value_weight, 'fsdp', xor_pairs(members, step))  89.6 us
    dot_general x8, matrix products, on_device(): jnp.dot(token_piece, weight_piece, preferred_element_type=jnp.float32)  16.7 us
    ppermute x7, waiting for transfers between devices, on_device(): lax.ppermute(sent, 'fsdp', xor_pairs(members, step)).astype(jnp.float32)  15.9 us
    dot_general x8, matrix products, on_device(): lax.dot_general(masked_cot, weight_piece, (((1,), (1,)), ((), ())), prefe...  14.6 us
    ppermute x7, waiting for transfers between devices, on_device(): gathered.append(lax.ppermute(own_adapter, 'fsdp', xor_pairs(members, step)))  11.2 us
    ppermute x7, starting transfers between devices, on_device(): gathered.append(lax.ppermute(own_adapter, 'fsdp', xor_pairs(members, step)))  7.73 us
    ppermute x7, starting transfers between devices, on_device(): lax.ppermute(sent, 'fsdp', xor_pairs(members, step)).astype(jnp.float32)  7.17 us
    unnamed x22, local copies, waits for them, and re-layouts  5.2 us
  transfers between devices with their start and end apart: 21, of which 5 were waited for; matrix products, arithmetic and copies ran while one was open for 20% of the time, Pallas kernels for 0%

profile of v1, /device:TPU:0, one launch (start us, length us, event | category | flops | bytes accessed | tf_op | source)
XLA Modules:
  0.0 207.4 jit_solution(5817819878519196637)
XLA Ops:
  0.6 1.0 pad_maximum_fusion.2
  2.2 2.6 %collective-permute-start.1 = (bf16[16,9216]{1,0:T(8,128)(2,1)S(1)}, bf16[16,9216]{1,0:T(8,128)(2,1)}, u32[]{:S(2)}, u32[]{:S(2)}) collective-permute-start(bf16[16,9216]{1,0:T(8,128)(2,1)S(1)} %pad_maximum_fusion.2), channel_id=1, source_target_pairs={{0,8},{4,12},{8,0},{12,4},{16,24},{20,28},{24,16},{28,20},{1,9},{5... | collective-permute-start | bytes 884744 | tf_op jit(solution)/shard_map/ppermute | solution.py:36
  4.8 1.8 collective-permute-start.3
  6.6 0.7 compare_select_fusion
  7.2 0.6 gather_fusion
  7.9 0.7 and_select_fusion
  8.6 0.6 fusion.97
  11.1 1.0 bitcast_dynamic-update-slice_fusion.7
  12.1 0.7 fusion.91
  12.8 0.7 fusion.93
  29.2 3.0 %fusion.40 = f32[384,1024]{1,0:T(8,128)S(1)} fusion(bf16[1024,1024]{1,0:T(8,128)(2,1)} %param.10, bf16[384,8192]{1,0:T(8,128)(2,1)} %param.8, s32[]{:T(128)S(6)} %select_n.239), kind=kOutput, calls=%fused_computation.60 | convolution fusion | flops 805306368 | bytes 4456452 | tf_op jit(solution)/shard_map/dot_general | solution.py:101
  32.2 2.7 %collective-permute-start.5 = (bf16[16,9216]{1,0:T(8,128)(2,1)S(1)}, bf16[16,9216]{1,0:T(8,128)(2,1)S(1)}, u32[]{:S(2)}, u32[]{:S(2)}) collective-permute-start(bf16[16,9216]{1,0:T(8,128)(2,1)S(1)} %pad_maximum_fusion.2), channel_id=1, source_target_pairs={{0,24},{4,28},{8,16},{12,20},{16,8},{20,12},{24,0},{28,4},{1,25},{... | collective-permute-start | bytes 884744 | tf_op jit(solution)/shard_map/ppermute | solution.py:36
  34.8 1.0 bitcast_dynamic-update-slice_fusion.6
  36.0 1.0 bitcast_dynamic-update-slice_fusion.5
  37.1 5.9 %collective-permute-done.5 = bf16[16,9216]{1,0:T(8,128)(2,1)S(1)} collective-permute-done((bf16[16,9216]{1,0:T(8,128)(2,1)S(1)}, bf16[16,9216]{1,0:T(8,128)(2,1)S(1)}, u32[]{:S(2)}, u32[]{:S(2)}) %collective-permute-start.5) | collective-permute-done | bytes 294944 | tf_op jit(solution)/shard_map/ppermute | solution.py:36
  43.0 5.3 %collective-permute-done.6 = bf16[16,9216]{1,0:T(8,128)(2,1)S(1)} collective-permute-done((bf16[16,9216]{1,0:T(8,128)(2,1)S(1)}, bf16[16,9216]{1,0:T(8,128)(2,1)S(1)}, u32[]{:S(2)}, u32[]{:S(2)}) %collective-permute-start.6) | collective-permute-done | bytes 294944 | tf_op jit(solution)/shard_map/ppermute | solution.py:36
  48.6 0.9 copy-done.3
  49.8 0.9 fusion.98
  50.8 1.7 fusion.25
  53.5 1.8 collective-permute-start.15
  55.3 1.7 collective-permute-start.17
  57.1 2.6 %collective-permute-start.19 = (bf16[16,9216]{1,0:T(8,128)(2,1)S(1)}, bf16[16,9216]{1,0:T(8,128)(2,1)S(1)}, u32[]{:S(2)}, u32[]{:S(2)}) collective-permute-start(bf16[16,9216]{1,0:T(8,128)(2,1)S(1)} %get-tuple-element.15), channel_id=1, source_target_pairs={{0,24},{4,28},{8,16},{12,20},{16,8},{20,12},{24,0},{28,4},{1,25},{... | collective-permute-start | bytes 884744 | tf_op jit(solution)/shard_map/ppermute | solution.py:78
  61.9 0.7 broadcast_in_dim.44
  62.7 0.8 copy-done.4
  63.5 1.0 fusion.17
  65.5 3.5 %collective-permute-done.16 = bf16[16,9216]{1,0:T(8,128)(2,1)S(1)} collective-permute-done((bf16[16,9216]{1,0:T(8,128)(2,1)S(1)}, bf16[16,9216]{1,0:T(8,128)(2,1)S(1)}, u32[]{:S(2)}, u32[]{:S(2)}) %collective-permute-start.16) | collective-permute-done | bytes 294944 | tf_op jit(solution)/shard_map/ppermute | solution.py:78
  69.0 0.8 collective-permute-start.14
  70.7 12.4 %collective-permute-done.18 = bf16[16,9216]{1,0:T(8,128)(2,1)S(1)} collective-permute-done((bf16[16,9216]{1,0:T(8,128)(2,1)S(1)}, bf16[16,9216]{1,0:T(8,128)(2,1)S(1)}, u32[]{:S(2)}, u32[]{:S(2)}) %collective-permute-start.18) | collective-permute-done | bytes 294944 | tf_op jit(solution)/shard_map/ppermute | solution.py:78
  83.1 1.8 collective-permute-start.8
  84.9 1.5 collective-permute-start.10
  87.0 0.7 slice_bitcast_fusion
  87.7 89.6 %collective-permute-done.10 = bf16[1024,1024]{1,0:T(8,128)(2,1)S(1)} collective-permute-done((bf16[1024,1024]{1,0:T(8,128)(2,1)S(1)}, bf16[1024,1024]{1,0:T(8,128)(2,1)S(1)}, u32[]{:S(2)}, u32[]{:S(2)}) %collective-permute-start.10) | collective-permute-done | bytes 2097184 | tf_op jit(solution)/shard_map/ppermute | solution.py:85
  177.3 0.6 slice_bitcast_fusion.1
  178.5 1.0 fusion.32
  179.5 2.8 %fusion.36 = f32[384,1024]{1,0:T(8,128)S(1)} fusion(bf16[1024,1024]{1,0:T(8,128)(2,1)} %collective-permute-done.8, bf16[384,8192]{1,0:T(8,128)(2,1)S(1)} %bitcast.150, s32[]{:T(128)S(6)} %select_n.241), kind=kOutput, calls=%fused_computation.56 | convolution fusion | flops 805306368 | bytes 4456452 | tf_op jit(solution)/shard_map/dot_general | solution.py:101
  182.3 1.0 fusion.28
  183.3 1.3 copy-done.5
  184.6 1.0 fusion.38
  185.6 2.6 %fusion.18 = bf16[384,8192]{1,0:T(8,128)(2,1)S(1)} fusion(bf16[384,8192]{1,0:T(8,128)(2,1)S(1)} %fusion.17, s32[]{:T(128)S(6)} %select_n.240, f32[3,128,1024]{2,1,0:T(8,128)S(1)} %fusion.71, bf16[1024,1024]{1,0:T(8,128)(2,1)} %copy-done.5, bf16[384,1024]{1,0:T(8,128)(2,1)S(1)} %copy-done.3, f32[384]{0:T(512)S(1)} %get-tuple-element.16), kind=kOutput, calls=%fused_computation.34 | convolution fusion | flops 807272448 | bytes 5244932 | tf_op jit(solution)/shard_map/dot_general | solution.py:105
  188.3 2.6 %fusion.19 = bf16[384,8192]{1,0:T(8,128)(2,1)S(1)} fusion(bf16[384,8192]{1,0:T(8,128)(2,1)S(1)} %fusion.18, s32[]{:T(128)S(6)} %select_n.241, f32[3,128,1024]{2,1,0:T(8,128)S(1)} %fusion.69, bf16[1024,1024]{1,0:T(8,128)(2,1)} %collective-permute-done.8, bf16[384,1024]{1,0:T(8,128)(2,1)S(1)} %copy-done.3, f32[384]{0:T(512)S(1)} %get-tuple-element.16), kind=kOutput, calls=%fused_computation.35 | convolution fusion | flops 807272448 | bytes 5244932 | tf_op jit(solution)/shard_map/dot_general | solution.py:105
  190.9 2.6 %fusion.30 = f32[384,1024]{1,0:T(8,128)S(1)} fusion(bf16[1024,1024]{1,0:T(8,128)(2,1)} %collective-permute-done.11, bf16[384,8192]{1,0:T(8,128)(2,1)S(1)} %bitcast.150, s32[]{:T(128)S(6)} %select_n.244), kind=kOutput, calls=%fused_computation.50 | convolution fusion | flops 805306368 | bytes 4456452 | tf_op jit(solution)/shard_map/dot_general | solution.py:101
  193.5 2.6 %fusion.34 = f32[384,1024]{1,0:T(8,128)S(1)} fusion(bf16[1024,1024]{1,0:T(8,128)(2,1)} %collective-permute-done.9, bf16[384,8192]{1,0:T(8,128)(2,1)S(1)} %bitcast.150, s32[]{:T(128)S(6)} %select_n.242), kind=kOutput, calls=%fused_computation.54 | convolution fusion | flops 805306368 | bytes 4456452 | tf_op jit(solution)/shard_map/dot_general | solution.py:101
  196.1 2.6 %fusion.20 = bf16[384,8192]{1,0:T(8,128)(2,1)S(1)} fusion(bf16[384,8192]{1,0:T(8,128)(2,1)S(1)} %fusion.19, s32[]{:T(128)S(6)} %select_n.242, f32[3,128,1024]{2,1,0:T(8,128)S(1)} %fusion.67, bf16[1024,1024]{1,0:T(8,128)(2,1)} %collective-permute-done.9, bf16[384,1024]{1,0:T(8,128)(2,1)S(1)} %copy-done.3, f32[384]{0:T(512)S(1)} %get-tuple-element.16), kind=kOutput, calls=%fused_computation.36 | convolution fusion | flops 807272448 | bytes 5244932 | tf_op jit(solution)/shard_map/dot_general | solution.py:105
  198.7 1.0 fusion.21
  199.7 2.6 %fusion.22 = bf16[384,8192]{1,0:T(8,128)(2,1)S(1)} fusion(bf16[384,8192]{1,0:T(8,128)(2,1)S(1)} %fusion.21, s32[]{:T(128)S(6)} %select_n.244, f32[3,128,1024]{2,1,0:T(8,128)S(1)} %fusion.63, bf16[1024,1024]{1,0:T(8,128)(2,1)} %collective-permute-done.11, bf16[384,1024]{1,0:T(8,128)(2,1)S(1)} %copy-done.3, f32[384]{0:T(512)S(1)} %get-tuple-element.16), kind=kOutput, calls=%fused_computation.38 | convolution fusion | flops 807272448 | bytes 5244932 | tf_op jit(solution)/shard_map/dot_general | solution.py:105
  202.4 1.0 fusion.23
  203.4 1.1 fusion.24
  204.5 2.9 %fusion.16 = bf16[384,1024]{1,0:T(8,128)(2,1)} fusion(f32[384,1024]{1,0:T(8,128)S(1)} %fusion.28, f32[384,1024]{1,0:T(8,128)S(1)} %fusion.30, f32[384,1024]{1,0:T(8,128)S(1)} %fusion.32, f32[384,1024]{1,0:T(8,128)S(1)} %fusion.34, f32[384,1024]{1,0:T(8,128)S(1)} %fusion.36, f32[384,1024]{1,0:T(8,128)S(1)} %fusion.38, f32[384,1024]{1,0:T(8,128)S(1)} %fusion.40, ...), kind=kOutput, calls=%fused_computation.30 | convolution fusion | flops 809238528 | bytes 16254980 | tf_op jit(solution)/shard_map/dot_general | solution.py:101
  (67 shorter events, 7.6 us)
Async XLA Ops:
  0.6 6.6 %copy-start = (s32[32]{0:T(128)S(1)}, s32[32]{0:T(128)}, u32[]{:S(2)}) copy-start(s32[32]{0:T(128)} %param.15) | copy-start | bytes 388
  1.6 30.5 %collective-permute-start = (bf16[16,9216]{1,0:T(8,128)(2,1)S(1)}, bf16[16,9216]{1,0:T(8,128)(2,1)}, u32[]{:S(2)}, u32[]{:S(2)}) collective-permute-start(bf16[16,9216]{1,0:T(8,128)(2,1)S(1)} %pad_maximum_fusion.2), channel_id=1, source_target_pairs={{0,4},{4,0},{8,12},{12,8},{16,20},{20,16},{24,28},{28,24},{1,5},{5... | collective-permute-start | bytes 884744 | tf_op jit(solution)/shard_map/ppermute | solution.py:36
  2.2 33.7 %collective-permute-start.1 = (bf16[16,9216]{1,0:T(8,128)(2,1)S(1)}, bf16[16,9216]{1,0:T(8,128)(2,1)}, u32[]{:S(2)}, u32[]{:S(2)}) collective-permute-start(bf16[16,9216]{1,0:T(8,128)(2,1)S(1)} %pad_maximum_fusion.2), channel_id=1, source_target_pairs={{0,8},{4,12},{8,0},{12,4},{16,24},{20,28},{24,16},{28,20},{1,9},{5... | collective-permute-start | bytes 884744 | tf_op jit(solution)/shard_map/ppermute | solution.py:36
  4.7 32.2 %collective-permute-start.2 = (bf16[16,9216]{1,0:T(8,128)(2,1)S(1)}, bf16[16,9216]{1,0:T(8,128)(2,1)S(1)}, u32[]{:S(2)}, u32[]{:S(2)}) collective-permute-start(bf16[16,9216]{1,0:T(8,128)(2,1)S(1)} %pad_maximum_fusion.2), channel_id=1, source_target_pairs={{0,12},{4,8},{8,4},{12,0},{16,28},{20,24},{24,20},{28,16},{1,13},{... | collective-permute-start | bytes 884744 | tf_op jit(solution)/shard_map/ppermute | solution.py:36
  4.8 32.2 %collective-permute-start.3 = (bf16[16,9216]{1,0:T(8,128)(2,1)S(1)}, bf16[16,9216]{1,0:T(8,128)(2,1)S(1)}, u32[]{:S(2)}, u32[]{:S(2)}) collective-permute-start(bf16[16,9216]{1,0:T(8,128)(2,1)S(1)} %pad_maximum_fusion.2), channel_id=1, source_target_pairs={{0,16},{4,20},{8,24},{12,28},{16,0},{20,4},{24,8},{28,12},{1,17},{... | collective-permute-start | bytes 884744 | tf_op jit(solution)/shard_map/ppermute | solution.py:36
  6.6 30.5 %collective-permute-start.4 = (bf16[16,9216]{1,0:T(8,128)(2,1)S(1)}, bf16[16,9216]{1,0:T(8,128)(2,1)S(1)}, u32[]{:S(2)}, u32[]{:S(2)}) collective-permute-start(bf16[16,9216]{1,0:T(8,128)(2,1)S(1)} %pad_maximum_fusion.2), channel_id=1, source_target_pairs={{0,20},{4,16},{8,28},{12,24},{16,4},{20,0},{24,12},{28,8},{1,21},{... | collective-permute-start | bytes 884744 | tf_op jit(solution)/shard_map/ppermute | solution.py:36
  29.2 20.6 %slice-start = ((s8[6291456]{0:T(1024)(128)(4,1)}), s8[4194304]{0:T(1024)(128)(4,1)S(1)}, s32[]{:S(2)}) async-start(s8[6291456]{0:T(1024)(128)(4,1)} %bitcast.149), calls=%async_computation | async-start | bytes 8388608
  32.2 10.8 %collective-permute-start.5 = (bf16[16,9216]{1,0:T(8,128)(2,1)S(1)}, bf16[16,9216]{1,0:T(8,128)(2,1)S(1)}, u32[]{:S(2)}, u32[]{:S(2)}) collective-permute-start(bf16[16,9216]{1,0:T(8,128)(2,1)S(1)} %pad_maximum_fusion.2), channel_id=1, source_target_pairs={{0,24},{4,28},{8,16},{12,20},{16,8},{20,12},{24,0},{28,4},{1,25},{... | collective-permute-start | bytes 884744 | tf_op jit(solution)/shard_map/ppermute | solution.py:36
  35.8 12.4 %collective-permute-start.6 = (bf16[16,9216]{1,0:T(8,128)(2,1)S(1)}, bf16[16,9216]{1,0:T(8,128)(2,1)S(1)}, u32[]{:S(2)}, u32[]{:S(2)}) collective-permute-start(bf16[16,9216]{1,0:T(8,128)(2,1)S(1)} %pad_maximum_fusion.2), channel_id=1, source_target_pairs={{0,28},{4,24},{8,20},{12,16},{16,12},{20,8},{24,4},{28,0},{1,29},{... | collective-permute-start | bytes 884744 | tf_op jit(solution)/shard_map/ppermute | solution.py:36
  37.1 12.8 %slice-start.1 = ((s8[6291456]{0:T(1024)(128)(4,1)}), s8[2097152]{0:T(1024)(128)(4,1)S(1)}, s32[]{:S(2)}) async-start(s8[6291456]{0:T(1024)(128)(4,1)} %bitcast.149), calls=%async_computation.1 | async-start | bytes 4194304
  48.4 1.1 copy-start.3
  53.5 11.9 %collective-permute-start.15 = (bf16[16,9216]{1,0:T(8,128)(2,1)S(1)}, bf16[16,9216]{1,0:T(8,128)(2,1)S(1)}, u32[]{:S(2)}, u32[]{:S(2)}) collective-permute-start(bf16[16,9216]{1,0:T(8,128)(2,1)S(1)} %get-tuple-element.11), channel_id=1, source_target_pairs={{0,8},{4,12},{8,0},{12,4},{16,24},{20,28},{24,16},{28,20},{1,9},{5... | collective-permute-start | bytes 884744 | tf_op jit(solution)/shard_map/ppermute | solution.py:78
  55.3 13.7 %collective-permute-start.16 = (bf16[16,9216]{1,0:T(8,128)(2,1)S(1)}, bf16[16,9216]{1,0:T(8,128)(2,1)S(1)}, u32[]{:S(2)}, u32[]{:S(2)}) collective-permute-start(bf16[16,9216]{1,0:T(8,128)(2,1)S(1)} %get-tuple-element.14), channel_id=1, source_target_pairs={{0,12},{4,8},{8,4},{12,0},{16,28},{20,24},{24,20},{28,16},{1,13},{... | collective-permute-start | bytes 884744 | tf_op jit(solution)/shard_map/ppermute | solution.py:78
  55.3 15.3 %collective-permute-start.17 = (bf16[16,9216]{1,0:T(8,128)(2,1)S(1)}, bf16[16,9216]{1,0:T(8,128)(2,1)S(1)}, u32[]{:S(2)}, u32[]{:S(2)}) collective-permute-start(bf16[16,9216]{1,0:T(8,128)(2,1)S(1)} %get-tuple-element.13), channel_id=1, source_target_pairs={{0,16},{4,20},{8,24},{12,28},{16,0},{20,4},{24,8},{28,12},{1,17},{... | collective-permute-start | bytes 884744 | tf_op jit(solution)/shard_map/ppermute | solution.py:78
  57.0 26.2 %collective-permute-start.18 = (bf16[16,9216]{1,0:T(8,128)(2,1)S(1)}, bf16[16,9216]{1,0:T(8,128)(2,1)S(1)}, u32[]{:S(2)}, u32[]{:S(2)}) collective-permute-start(bf16[16,9216]{1,0:T(8,128)(2,1)S(1)} %get-tuple-element.12), channel_id=1, source_target_pairs={{0,20},{4,16},{8,28},{12,24},{16,4},{20,0},{24,12},{28,8},{1,21},{... | collective-permute-start | bytes 884744 | tf_op jit(solution)/shard_map/ppermute | solution.py:78
  57.1 27.8 %collective-permute-start.19 = (bf16[16,9216]{1,0:T(8,128)(2,1)S(1)}, bf16[16,9216]{1,0:T(8,128)(2,1)S(1)}, u32[]{:S(2)}, u32[]{:S(2)}) collective-permute-start(bf16[16,9216]{1,0:T(8,128)(2,1)S(1)} %get-tuple-element.15), channel_id=1, source_target_pairs={{0,24},{4,28},{8,16},{12,20},{16,8},{20,12},{24,0},{28,4},{1,25},{... | collective-permute-start | bytes 884744 | tf_op jit(solution)/shard_map/ppermute | solution.py:78
  61.9 1.6 copy-start.4
  65.4 21.1 %collective-permute-start.20 = (bf16[16,9216]{1,0:T(8,128)(2,1)S(1)}, bf16[16,9216]{1,0:T(8,128)(2,1)S(1)}, u32[]{:S(2)}, u32[]{:S(2)}) collective-permute-start(bf16[16,9216]{1,0:T(8,128)(2,1)S(1)} %fusion.58), channel_id=1, source_target_pairs={{0,28},{4,24},{8,20},{12,16},{16,12},{20,8},{24,4},{28,0},{1,29},{... | collective-permute-start | bytes 884744 | tf_op jit(solution)/shard_map/ppermute | solution.py:78
  69.0 17.7 %collective-permute-start.14 = (bf16[16,9216]{1,0:T(8,128)(2,1)S(1)}, bf16[16,9216]{1,0:T(8,128)(2,1)S(1)}, u32[]{:S(2)}, u32[]{:S(2)}) collective-permute-start(bf16[16,9216]{1,0:T(8,128)(2,1)S(1)} %get-tuple-element.4), channel_id=1, source_target_pairs={{0,4},{4,0},{8,12},{12,8},{16,20},{20,16},{24,28},{28,24},{1,5},{5... | collective-permute-start | bytes 884744 | tf_op jit(solution)/shard_map/ppermute | solution.py:78
  70.6 112.6 %collective-permute-start.7 = (bf16[1024,1024]{1,0:T(8,128)(2,1)S(1)}, bf16[1024,1024]{1,0:T(8,128)(2,1)S(1)}, u32[]{:S(2)}, u32[]{:S(2)}) collective-permute-start(bf16[1024,1024]{1,0:T(8,128)(2,1)S(1)} %copy-done.4), channel_id=1, source_target_pairs={{0,4},{4,0},{8,12},{12,8},{16,20},{20,16},{24,28},{28,24},{1,5},{5... | collective-permute-start | bytes 6291464 | tf_op jit(solution)/shard_map/ppermute | solution.py:87
  83.1 94.8 %collective-permute-start.8 = (bf16[1024,1024]{1,0:T(8,128)(2,1)S(1)}, bf16[1024,1024]{1,0:T(8,128)(2,1)}, u32[]{:S(2)}, u32[]{:S(2)}) collective-permute-start(bf16[1024,1024]{1,0:T(8,128)(2,1)S(1)} %copy-done.4), channel_id=1, source_target_pairs={{0,8},{4,12},{8,0},{12,4},{16,24},{20,28},{24,16},{28,20},{1,9},{5... | collective-permute-start | bytes 6291464 | tf_op jit(solution)/shard_map/ppermute | solution.py:85
  84.9 92.4 %collective-permute-start.10 = (bf16[1024,1024]{1,0:T(8,128)(2,1)S(1)}, bf16[1024,1024]{1,0:T(8,128)(2,1)S(1)}, u32[]{:S(2)}, u32[]{:S(2)}) collective-permute-start(bf16[1024,1024]{1,0:T(8,128)(2,1)S(1)} %copy-done.4), channel_id=1, source_target_pairs={{0,16},{4,20},{8,24},{12,28},{16,0},{20,4},{24,8},{28,12},{1,17},{... | collective-permute-start | bytes 6291464 | tf_op jit(solution)/shard_map/ppermute | solution.py:85
  86.5 93.0 %collective-permute-start.12 = (bf16[1024,1024]{1,0:T(8,128)(2,1)S(1)}, bf16[1024,1024]{1,0:T(8,128)(2,1)S(1)}, u32[]{:S(2)}, u32[]{:S(2)}) collective-permute-start(bf16[1024,1024]{1,0:T(8,128)(2,1)S(1)} %copy-done.4), channel_id=1, source_target_pairs={{0,24},{4,28},{8,16},{12,20},{16,8},{20,12},{24,0},{28,4},{1,25},{... | collective-permute-start | bytes 6291464 | tf_op jit(solution)/shard_map/ppermute | solution.py:85
  177.3 13.6 %collective-permute-start.11 = (bf16[1024,1024]{1,0:T(8,128)(2,1)S(1)}, bf16[1024,1024]{1,0:T(8,128)(2,1)}, u32[]{:S(2)}, u32[]{:S(2)}) collective-permute-start(bf16[1024,1024]{1,0:T(8,128)(2,1)S(1)} %collective-permute-done.10), channel_id=1, source_target_pairs={{0,4},{4,0},{8,12},{12,8},{16,20},{20,16},{24,28},{28,24},{1,5},{5... | collective-permute-start | bytes 6291464 | tf_op jit(solution)/shard_map/ppermute | solution.py:87
  178.0 15.5 %collective-permute-start.9 = (bf16[1024,1024]{1,0:T(8,128)(2,1)}, bf16[1024,1024]{1,0:T(8,128)(2,1)}, u32[]{:S(2)}, u32[]{:S(2)}) collective-permute-start(bf16[1024,1024]{1,0:T(8,128)(2,1)} %collective-permute-done.8), channel_id=1, source_target_pairs={{0,4},{4,0},{8,12},{12,8},{16,20},{20,16},{24,28},{28,24},{1,5},{5... | collective-permute-start | bytes 6291464 | tf_op jit(solution)/shard_map/ppermute | solution.py:87
  179.5 24.0 %collective-permute-start.13 = (bf16[1024,1024]{1,0:T(8,128)(2,1)S(1)}, bf16[1024,1024]{1,0:T(8,128)(2,1)S(1)}, u32[]{:S(2)}, u32[]{:S(2)}) collective-permute-start(bf16[1024,1024]{1,0:T(8,128)(2,1)S(1)} %collective-permute-done.12), channel_id=1, source_target_pairs={{0,4},{4,0},{8,12},{12,8},{16,20},{20,16},{24,28},{28,24},{1,5},{5... | collective-permute-start | bytes 6291464 | tf_op jit(solution)/shard_map/ppermute | solution.py:87
  183.3 1.3 copy-start.5
  204.5 3.0 %copy-start.2 = (bf16[384,8192]{1,0:T(8,128)(2,1)}, bf16[384,8192]{1,0:T(8,128)(2,1)S(1)}, u32[]{:S(2)}) copy-start(bf16[384,8192]{1,0:T(8,128)(2,1)S(1)} %fusion.24) | copy-start | bytes 18874372
  204.5 2.9 %copy-start.1 = (s32[32]{0:T(128)S(1)}, s32[32]{0:T(128)}, u32[]{:S(2)}) copy-start(s32[32]{0:T(128)} %param.15) | copy-start | bytes 388

commit v2 on v0

--- a/solution.py
+++ b/solution.py
@@ -62,7 +62,11 @@
     adapter_backward = jnp.einsum(
         "uio,uof->uif", low_rank_gradient, down_block, preferred_element_type=jnp.float32
     )
-    weight_piece = lax.all_gather(frozen_value_weight, "fsdp", axis=0, tiled=True)
+    quarter_rows = frozen_value_weight.shape[0] // groups
+    weight_quarter = lax.dynamic_slice_in_dim(
+        frozen_value_weight, lax.axis_index("dp") * quarter_rows, quarter_rows, axis=0
+    )
+    weight_piece = lax.all_gather(weight_quarter, ("fsdp", "dp"), axis=0, tiled=True)
     output_total = jnp.dot(tokens, weight_piece, preferred_element_type=jnp.float32)
     backward_piece = lax.dot_general(
         output_gradient, weight_piece, (((1,), (1,)), ((), ())), preferred_element_type=jnp.float32

time: 222 us -> 247 us (1.11)
  waiting for transfers between devices: 140 us -> 169 us
  matrix products: 45.8 us -> 40.1 us
    all_gather x1, waiting for transfers between devices: 82.6 us -> 109 us  [on_device(): lax.all_gather(weight_quarter, ('fsdp', 'dp'), axis=0, tiled=True)]
    reduce_scatter x1, waiting for transfers between devices: 9.16 us -> 14.2 us  [on_device(): lax.psum_scatter(term_down.astype(jnp.float32).astype(jnp.bfloat16), 'fsd...]
    dot_general x1, matrix products: 9.17 us -> 4.9 us  [on_device(): jnp.einsum('uio,uof->uif', low_rank_gradient, down_block, preferred_eleme...]
    dot_general x1, matrix products: 13.4 us -> 10.6 us  [on_device(): lax.dot_general(output_gradient, weight_piece, (((1,), (1,)), ((), ())),...]
  transfers between devices with their start and end apart: 4 -> 4, of which waited for: 4 -> 4; matrix products, arithmetic and copies ran while one was open for 25% -> 21% of each run, Pallas kernels for 0% -> 0%
where the time goes in v2:
time: 247 us; the launch traced here: 246 us
  waiting for transfers between devices  169 us (68%)
  matrix products  40.1 us (16%)
  between operations  13.9 us (6%)
  blocking collectives  11 us (4%)
  other arithmetic  6.62 us (3%)
  local copies, waits for them, and re-layouts  5.25 us (2%)
    all_gather x1, waiting for transfers between devices, on_device(): lax.all_gather(weight_quarter, ('fsdp', 'dp'), axis=0, tiled=True)  109 us
    reduce_scatter x1, waiting for transfers between devices, on_device(): lax.psum_scatter(term_up.astype(jnp.float32).astype(jnp.bfloat16), 'fsdp'...  37.4 us
    reduce_scatter x1, waiting for transfers between devices, on_device(): lax.psum_scatter(term_down.astype(jnp.float32).astype(jnp.bfloat16), 'fsd...  14.2 us
    dot_general x1, matrix products, on_device(): jnp.dot(tokens, weight_piece, preferred_element_type=jnp.float32)  12.3 us
    all_gather x1, blocking collectives, on_device(): lax.all_gather(adapter_up_maps, 'fsdp', axis=0, tiled=True)  11 us
    dot_general x1, matrix products, on_device(): lax.dot_general(output_gradient, weight_piece, (((1,), (1,)), ((), ())),...  10.6 us
    all_gather x1, waiting for transfers between devices, on_device(): lax.all_gather(adapter_down_maps, 'fsdp', axis=0, tiled=True)  7.55 us
  transfers between devices with their start and end apart: 4, of which 4 were waited for; matrix products, arithmetic and copies ran while one was open for 21% of the time, Pallas kernels for 0%

profile of v2, /device:TPU:0, one launch (start us, length us, event | category | flops | bytes accessed | tf_op | source)
XLA Modules:
  0.0 246.2 jit_solution(16766610053296585307)
XLA Ops:
  7.2 0.0 copy-start
  7.2 0.0 all-gather.5.cloned.1.call-start
  7.2 0.7 all-gather.5.cloned.1.call-update
  7.9 0.0 all-gather.3.cloned.1.call-start
  8.0 0.8 copy-done
  8.8 0.8 constant_dynamic-slice_fusion
  9.6 0.0 all-gather.3.cloned.1.call-update
  9.6 0.0 reduce-scatter.3.cloned.1.call-start
  9.7 11.0 %all_gather.11 = bf16[8,16,1024]{2,1,0:T(8,128)(2,1)S(1)} all-gather(bf16[1,16,1024]{2,1,0:T(8,128)(2,1)} %param.12), channel_id=1, replica_groups=mesh['fsdp'=8,'dp'=4] {'fsdp'}, dimensions={0}, use_global_device_ids=true | all-gather | bytes 294912 | tf_op jit(solution)/shard_map/all_gather | solution.py:37
  20.6 0.1 copy.14
  20.8 0.9 select_reduce_fusion
  21.7 0.6 fusion.14
  22.3 0.6 compare_convert_fusion.2
  22.9 1.3 compare_convert_fusion
  24.2 0.7 fusion.10
  24.9 0.3 convolution_convert_fusion.1
  25.2 1.5 fusion.1
  26.7 3.7 %fusion.16 = f32[3,16,8192]{2,1,0:T(8,128)S(1)} fusion(bf16[3,16,128]{2,1,0:T(8,128)(2,1)S(1)} %fusion.1, bf16[3,128,8192]{2,1,0:T(8,128)(2,1)} %bitcast.55), kind=kOutput, calls=%fused_computation.43 | convolution fusion | flops 100663296 | bytes 7876608 | tf_op jit(solution)/shard_map/vio,vih->voh/dot_general | solution.py:83
  30.4 0.0 copy-start.3
  30.4 0.1 slice_bitcast_fusion.2
  30.5 2.1 add_convert_fusion
  32.7 0.0 reduce-scatter.3.cloned.1.call-update
  32.7 0.2 reduce-scatter.5.cloned.1.call-start
  32.9 0.0 copy-done.3
  32.9 0.1 fusion.11
  33.0 7.5 %all-gather.5.cloned.1.call-done = bf16[8,16,8192]{2,1,0:T(8,128)(2,1)} async-done(((bf16[1,16,8192]{2,1,0:T(8,128)(2,1)}), bf16[8,16,8192]{2,1,0:T(8,128)(2,1)}) %all-gather.5.cloned.1.call-update) | async-done | bytes 2097168 | tf_op jit(solution)/shard_map/all_gather | solution.py:36
  40.5 2.7 %copy.12 = bf16[1,8,16,8192]{3,1,2,0:T(8,128)(2,1)S(1)} copy(bf16[1,8,16,8192]{3,2,1,0:T(8,128)(2,1)} %bitcast.64) | data formatting | bytes 4194304
  43.3 0.8 convolution_convert_fusion
  44.0 0.0 copy-start.1
  44.1 4.6 %fusion = bf16[3,16,128]{2,1,0:T(8,128)(2,1)S(1)} fusion(bf16[3,128,8192]{2,1,0:T(8,128)(2,1)} %bitcast.56, bf16[1,3,16,8192]{3,1,2,0:T(4,128)(2,1)S(1)} %bitcast.59, f32[3,128]{1,0:T(4,128)S(1)} %fusion.11), kind=kOutput, calls=%fused_computation.8 | convolution fusion | flops 100675584 | bytes 7091712 | tf_op jit(solution)/shard_map/cvj,coj->cvo/dot_general | solution.py:51
  48.7 0.0 copy-done.1
  48.7 0.2 convolution_multiply_fusion
  48.9 0.9 add_convert_fusion.1
  49.8 0.0 reduce-scatter.5.cloned.1.call-update
  49.8 109.2 %all-gather.3.cloned.1.call-done = bf16[8192,1024]{1,0:T(8,128)(2,1)} async-done(((bf16[256,1024]{1,0:T(8,128)(2,1)}), bf16[8192,1024]{1,0:T(8,128)(2,1)}) %all-gather.3.cloned.1.call-update) | async-done | bytes 16777232 | tf_op jit(solution)/shard_map/all_gather | solution.py:69
  159.0 0.0 copy-start.2
  159.0 12.3 %fusion.17 = f32[1024,384]{0,1:T(8,128)S(1)} fusion(bf16[384,8192]{1,0:T(8,128)(2,1)} %param.8, bf16[8192,1024]{1,0:T(8,128)(2,1)} %all-gather.3.cloned.1.call-done), kind=kOutput, calls=%fused_computation.44 | convolution fusion | flops 6442450944 | bytes 24641536 | tf_op jit(solution)/shard_map/dot_general | solution.py:70
  171.3 0.0 copy-done.2
  171.3 10.6 %fusion.15 = f32[8192,384]{0,1:T(8,128)S(1)} fusion(bf16[8192,1024]{1,0:T(8,128)(2,1)} %all-gather.3.cloned.1.call-done, bf16[384,1024]{1,0:T(8,128)(2,1)S(1)} %copy-done.2), kind=kOutput, calls=%fused_computation.42 | convolution fusion | flops 6442450944 | bytes 30146560 | tf_op jit(solution)/shard_map/dot_general | solution.py:71
  181.9 4.9 %multiply_convert_fusion = bf16[3,128,8192]{2,1,0:T(8,128)(2,1)} fusion(f32[3,128,8192]{2,1,0:T(8,128)S(1)} %bitcast.57, bf16[3,16,128]{2,1,0:T(8,128)(2,1)S(1)} %fusion.1, f32[3,128]{1,0:T(4,128)S(1)} %fusion.11, bf16[1,3,16,8192]{3,1,2,0:T(4,128)(2,1)S(1)} %bitcast.60), kind=kOutput, calls=%fused_computation.2 | convolution fusion | flops 110100480 | bytes 19674624 | tf_op jit(solution)/shard_map/uio,uof->uif/dot_general | solution.py:62
  186.8 1.3 multiply_convert_fusion.1
  188.1 14.2 %reduce-scatter.3.cloned.1.call-done = bf16[1,16,8192]{2,1,0:T(8,128)(2,1)} async-done(((bf16[8,16,8192]{2,1,0:T(8,128)(2,1)}), bf16[1,16,8192]{2,1,0:T(8,128)(2,1)}) %reduce-scatter.3.cloned.1.call-update) | async-done | bytes 262160 | tf_op jit(solution)/shard_map/reduce_scatter | solution.py:99
  202.3 37.4 %reduce-scatter.5.cloned.1.call-done = bf16[1,16,1024]{2,1,0:T(8,128)(2,1)} async-done(((bf16[8,16,1024]{2,1,0:T(8,128)(2,1)}), bf16[1,16,1024]{2,1,0:T(8,128)(2,1)}) %reduce-scatter.5.cloned.1.call-update) | async-done | bytes 32784 | tf_op jit(solution)/shard_map/reduce_scatter | solution.py:105
  (2 shorter events, 0.0 us)
Async XLA Ops:
  7.2 1.6 copy-start
  7.2 33.4 %all-gather.5.cloned.1.call-start = ((), (), s32[]{:S(2)}) async-start(), calls=%async_computation.3 | async-start | bytes 2359296 | tf_op jit(solution)/shard_map/all_gather | solution.py:36
  7.9 151.1 %all-gather.3.cloned.1.call-start = ((), (), s32[]{:S(2)}) async-start(), calls=%async_computation.2 | async-start | bytes 17301504 | tf_op jit(solution)/shard_map/all_gather | solution.py:69
  9.6 192.7 %reduce-scatter.3.cloned.1.call-start = ((), (), s32[]{:S(2)}) async-start(), calls=%async_computation.4 | async-start | bytes 2359296 | tf_op jit(solution)/shard_map/reduce_scatter | solution.py:99
  30.4 2.5 %copy-start.3 = (s32[3]{0:T(128)S(1)}, s32[3]{0:T(128)}, u32[]{:S(2)}) copy-start(s32[3]{0:T(128)} %param.14) | copy-start | bytes 40
  32.7 207.0 %reduce-scatter.5.cloned.1.call-start = ((), (), s32[]{:S(2)}) async-start(), calls=%async_computation.5 | async-start | bytes 294912 | tf_op jit(solution)/shard_map/reduce_scatter | solution.py:105
  44.0 4.6 %copy-start.1 = (bf16[384,1024]{1,0:T(8,128)(2,1)S(1)}, bf16[384,1024]{1,0:T(8,128)(2,1)}, u32[]{:S(2)}) copy-start(bf16[384,1024]{1,0:T(8,128)(2,1)} %param.9) | copy-start | bytes 2359300
  159.0 12.3 %copy-start.2 = (bf16[384,1024]{1,0:T(8,128)(2,1)S(1)}, bf16[384,1024]{1,0:T(8,128)(2,1)}, u32[]{:S(2)}) copy-start(bf16[384,1024]{1,0:T(8,128)(2,1)} %param.9) | copy-start | bytes 2359300
Sparse Core Ops, SparseCore 0:
  9.9 30.5 all-gather.4
  44.1 114.8 all-gather.2
  162.9 39.3 reduce-scatter.2
  206.0 33.5 reduce-scatter.4

commit v3 on v1

--- a/solution.py
+++ b/solution.py
@@ -4,10 +4,60 @@
 from jax.sharding import PartitionSpec as P
 
 ADAPTER_SCALE = 2.0
+WEIGHT_CHUNKS = 2
 
 
 def xor_pairs(count, step):
     return [(src, src ^ step) for src in range(count)]
+
+
+def relay_gather(shard, members, groups, me, dp_index):
+    flat = members * groups
+    parity = me % 2
+    if members != 8 or groups % 2 != 0:
+        parts = {0: shard}
+        for step in range(2, members, 2):
+            parts[step] = lax.ppermute(shard, "fsdp", xor_pairs(members, step))
+        for step in range(0, members, 2):
+            parts[step + 1] = lax.ppermute(parts[step], "fsdp", xor_pairs(members, 1))
+        return [(me ^ step, parts[step]) for step in range(members)]
+
+    def flat_pairs(target):
+        pairs = []
+        for i in range(members):
+            for d in range(groups):
+                role = (i % 2) ^ (d % 2)
+                ti, td = target(i, d, role)
+                pairs.append((i * groups + d, ti * groups + td))
+        return pairs
+
+    first_pairs = flat_pairs(lambda i, d, role: (i ^ (2 + 2 * role), d))
+    relay_pairs = flat_pairs(lambda i, d, role: (i ^ (4 - 2 * role), d))
+    partner_pairs = flat_pairs(lambda i, d, role: (i, d ^ 1))
+    role = parity ^ (dp_index % 2)
+    rows = shard.shape[0] // WEIGHT_CHUNKS
+    chunks = []
+    for k in range(WEIGHT_CHUNKS):
+        piece = shard[k * rows:(k + 1) * rows]
+        first = lax.ppermute(piece, ("fsdp", "dp"), first_pairs)
+        relayed = lax.ppermute(first, ("fsdp", "dp"), relay_pairs)
+        partner = lax.ppermute(first, ("fsdp", "dp"), partner_pairs)
+        own_four = jnp.stack([piece, first, relayed, partner])
+        sibling_four = lax.ppermute(own_four, "fsdp", xor_pairs(members, 1))
+        chunks.append((piece, first, relayed, partner, sibling_four))
+    sources = [me, me ^ (2 + 2 * role), me ^ 6, me ^ (4 - 2 * role)]
+    sibling = me ^ 1
+    sibling_role = 1 - role
+    sibling_sources = [sibling, sibling ^ (2 + 2 * sibling_role), sibling ^ 6,
+                       sibling ^ (4 - 2 * sibling_role)]
+    result = []
+    for k in range(WEIGHT_CHUNKS):
+        piece, first, relayed, partner, sibling_four = chunks[k]
+        for source, value in zip(sources, (piece, first, relayed, partner)):
+            result.append((source, k, value))
+        for index, source in enumerate(sibling_sources):
+            result.append((source, k, sibling_four[index]))
+    return result
 
 
 def on_device(
@@ -22,19 +72,24 @@
 ):
     tok_rows, model_width = tokens.shape
     value_width = output_gradient.shape[1]
-    rank = adapter_down_maps.shape[1]
     blocks = block_tenant_ids.shape[0]
     block_length = tok_rows // blocks
     groups = lax.axis_size("dp")
     members = lax.axis_size("fsdp")
     shard_rows = frozen_value_weight.shape[0]
     me = lax.axis_index("fsdp")
+    dp_index = lax.axis_index("dp")
+    even_steps = list(range(2, members, 2))
 
     own_adapter = jnp.concatenate([adapter_down_maps[0], adapter_up_maps[0]], axis=1)
-    gathered = [own_adapter]
-    for step in range(1, members):
-        gathered.append(lax.ppermute(own_adapter, "fsdp", xor_pairs(members, step)))
-    adapter_stack = jnp.stack(gathered)
+    by_step = {0: own_adapter}
+    for step in even_steps:
+        by_step[step] = lax.ppermute(own_adapter, "fsdp", xor_pairs(members, step))
+    same_parity = jnp.stack([by_step[step] for step in range(0, members, 2)])
+    other_parity = lax.ppermute(same_parity, "fsdp", xor_pairs(members, 1))
+    for index, step in enumerate(range(0, members, 2)):
+        by_step[step ^ 1] = other_parity[index]
+    adapter_stack = jnp.stack([by_step[step] for step in range(members)])
 
     slot_ids = jnp.take(tenant_owner_slot, block_tenant_ids)
     member_ids = slot_ids // groups
@@ -72,20 +127,24 @@
             row = row + jnp.where(member_ids[b] == member, partial[b], 0.0)
         return row.astype(jnp.bfloat16)
 
-    grad_sum = table_row(me).astype(jnp.float32)
-    for step in range(1, members):
-        sent = table_row(me ^ step)
+    sibling = me ^ 1
+    for_sibling = jnp.stack([table_row(sibling ^ step) for step in range(0, members, 2)])
+    from_sibling = lax.ppermute(for_sibling, "fsdp", xor_pairs(members, 1))
+    pair_sums = [
+        table_row(me ^ step).astype(jnp.float32) + from_sibling[index].astype(jnp.float32)
+        for index, step in enumerate(range(0, members, 2))
+    ]
+    grad_sum = pair_sums[0]
+    for index, step in enumerate(even_steps):
+        sent = pair_sums[index + 1].astype(jnp.bfloat16)
         grad_sum = grad_sum + lax.ppermute(sent, "fsdp", xor_pairs(members, step)).astype(jnp.float32)
     grad_sum = grad_sum.astype(jnp.bfloat16)
     grad_down = grad_sum[None, :, :model_width]
     grad_up = grad_sum[None, :, model_width:]
 
-    weight_parts = {0: frozen_value_weight}
-    for step in range(2, members, 2):
-        weight_parts[step] = lax.ppermute(frozen_value_weight, "fsdp", xor_pairs(members, step))
-    for step in range(0, members, 2):
-        weight_parts[step + 1] = lax.ppermute(weight_parts[step], "fsdp", xor_pairs(members, 1))
-
+    weight_pieces = relay_gather(frozen_value_weight, members, groups, me, dp_index)
+    if weight_pieces and len(weight_pieces[0]) == 2:
+        weight_pieces = [(source, 0, value) for source, value in weight_pieces]
     adapter_output = jnp.einsum(
         "znr,zrm->znm", low_rank_state, up_block, preferred_element_type=jnp.float32
     ).reshape(tok_rows, value_width)
@@ -94,19 +153,19 @@
 
     output_total = ADAPTER_SCALE * adapter_output
     token_gradient = jnp.zeros((tok_rows, model_width), jnp.bfloat16)
-    for step in range(members):
-        weight_piece = weight_parts[step]
-        column = (me ^ step) * shard_rows
-        token_piece = lax.dynamic_slice_in_dim(tokens, column, shard_rows, axis=1)
+    for source, chunk, weight_piece in weight_pieces:
+        piece_rows = weight_piece.shape[0]
+        column = source * shard_rows + chunk * piece_rows
+        token_piece = lax.dynamic_slice_in_dim(tokens, column, piece_rows, axis=1)
         output_total = output_total + jnp.dot(
             token_piece, weight_piece, preferred_element_type=jnp.float32
         )
-        down_piece = lax.dynamic_slice_in_dim(down_block, column, shard_rows, axis=2)
+        down_piece = lax.dynamic_slice_in_dim(down_block, column, piece_rows, axis=2)
         backward_piece = lax.dot_general(
             masked_cot, weight_piece, (((1,), (1,)), ((), ())), preferred_element_type=jnp.float32
         ) + jnp.einsum(
             "uio,uof->uif", low_rank_gradient, down_piece, preferred_element_type=jnp.float32
-        ).reshape(tok_rows, shard_rows)
+        ).reshape(tok_rows, piece_rows)
         token_gradient = lax.dynamic_update_slice_in_dim(
             token_gradient, backward_piece.astype(jnp.bfloat16), column, axis=1
         )

time: 208 us -> 159 us (0.76)
  waiting for transfers between devices: 117 us -> 20.5 us
  matrix products: 38.2 us -> 70.4 us
  local copies, waits for them, and re-layouts: 8.64 us -> 19.2 us
  other arithmetic: 6.11 us -> 14.5 us
  starting transfers between devices: 19 us -> 14.5 us
    ppermute x14 -> x13, waiting for transfers between devices: 101 us -> 7.78 us  [the longest x3 7.44 us: on_device(): by_step[step] = lax.ppermute(own_adapter, 'fsdp', xor_pairs(members, step))]
    dot_general x8 -> x16, matrix products: 3.23 us -> 19.4 us  [on_device(): jnp.einsum('uio,uof->uif', low_rank_gradient, down_piece, preferred_eleme...]
    dot_general x8 -> x16, matrix products: 16.7 us -> 32.9 us  [on_device(): jnp.dot(token_piece, weight_piece, preferred_element_type=jnp.float32)]
    another operation x0 -> x5, other arithmetic: none -> 9.33 us  [the longest x2 4.13 us: relay_gather(): own_four = jnp.stack([piece, first, relayed, partner])]
    unnamed x22 -> x70, local copies, waits for them, and re-layouts: 5.2 us -> 11 us
    another operation x1 -> x2, local copies, waits for them, and re-layouts: 0.02 us -> 4.78 us  [the longest x1 3.79 us: relay_gather(): own_four = jnp.stack([piece, first, relayed, partner])]
    ppermute x7 -> x3, starting transfers between devices: 7.17 us -> 3.49 us  [on_device(): lax.ppermute(sent, 'fsdp', xor_pairs(members, step)).astype(jnp.float32)]
    ppermute x7 -> x3, waiting for transfers between devices: 15.9 us -> 12.7 us  [on_device(): lax.ppermute(sent, 'fsdp', xor_pairs(members, step)).astype(jnp.float32)]
  transfers between devices with their start and end apart: 21 -> 16, of which waited for: 5 -> 4; matrix products, arithmetic and copies ran while one was open for 20% -> 46% of each run, Pallas kernels for 0% -> 0%
where the time goes in v3:
time: 159 us; the launch traced here: 158 us
  matrix products  70.4 us (44%)
  waiting for transfers between devices  20.5 us (13%)
  local copies, waits for them, and re-layouts  19.2 us (12%)
  between operations  18.9 us (12%)
  other arithmetic  14.5 us (9%)
  starting transfers between devices  14.5 us (9%)
    dot_general x16, matrix products, on_device(): jnp.dot(token_piece, weight_piece, preferred_element_type=jnp.float32)  32.9 us
    dot_general x16, matrix products, on_device(): jnp.einsum('uio,uof->uif', low_rank_gradient, down_piece, preferred_eleme...  19.4 us
    dot_general x16, matrix products, on_device(): lax.dot_general(masked_cot, weight_piece, (((1,), (1,)), ((), ())), prefe...  14.6 us
    ppermute x3, waiting for transfers between devices, on_device(): lax.ppermute(sent, 'fsdp', xor_pairs(members, step)).astype(jnp.float32)  12.7 us
    unnamed x70, local copies, waits for them, and re-layouts  11 us
    ppermute x3, waiting for transfers between devices, on_device(): by_step[step] = lax.ppermute(own_adapter, 'fsdp', xor_pairs(members, step))  7.44 us
    ppermute x3, starting transfers between devices, on_device(): by_step[step] = lax.ppermute(own_adapter, 'fsdp', xor_pairs(members, step))  4.55 us
    another operation x2, other arithmetic, relay_gather(): own_four = jnp.stack([piece, first, relayed, partner])  4.13 us
  transfers between devices with their start and end apart: 16, of which 4 were waited for; matrix products, arithmetic and copies ran while one was open for 46% of the time, Pallas kernels for 0%

profile of v3, /device:TPU:0, one launch (start us, length us, event | category | flops | bytes accessed | tf_op | source)
XLA Modules:
  0.0 158.0 jit_solution(17941178485737102676)
XLA Ops:
  0.6 1.7 %fusion.161 = (bf16[1,16,9216]{2,1,0:T(8,128)(2,1)S(1)}, bf16[16,9216]{1,0:T(8,128)(2,1)}) fusion(bf16[16,1024]{1,0:T(8,128)(2,1)} %bitcast.196, bf16[16,8192]{1,0:T(8,128)(2,1)} %bitcast.178), kind=kLoop, calls=%fused_computation.235 | loop fusion | flops 589824 | bytes 884736 | tf_op jit(solution)/shard_map/stack | solution.py:92
  2.4 3.0 %collective-permute-start = (bf16[16,9216]{1,0:T(8,128)(2,1)}, bf16[16,9216]{1,0:T(8,128)(2,1)}, u32[]{:S(2)}, u32[]{:S(2)}) collective-permute-start(bf16[16,9216]{1,0:T(8,128)(2,1)} %get-tuple-element.22), channel_id=1, source_target_pairs={{0,8},{4,12},{8,0},{12,4},{16,24},{20,28},{24,16},{28,20},{1,9},{5... | collective-permute-start | bytes 884744 | tf_op jit(solution)/shard_map/ppermute | solution.py:87
  5.4 1.5 collective-permute-start.1
  6.9 3.8 %slice_bitcast_fusion.27 = (bf16[1,512,1024]{2,1,0:T(8,128)(2,1)}, bf16[1,512,1024]{2,1,0:T(8,128)(2,1)}, bf16[512,1024]{1,0:T(8,128)(2,1)}, bf16[512,1024]{1,0:T(8,128)(2,1)}) fusion(bf16[1024,1024]{1,0:T(8,128)(2,1)} %param.10), kind=kLoop, calls=%fused_computation.240 | loop fusion | bytes 6291456 | tf_op jit(solution)/shard_map/stack | solution.py:45
  10.7 1.9 %collective-permute-start.4 = (bf16[512,1024]{1,0:T(8,128)(2,1)}, bf16[512,1024]{1,0:T(8,128)(2,1)}, u32[]{:S(2)}, u32[]{:S(2)}) collective-permute-start(bf16[512,1024]{1,0:T(8,128)(2,1)} %get-tuple-element.17), channel_id=1, source_target_pairs={{0,8},{1,17},{2,10},{3,19},{4,20},{5,13},{6,22},{7,15},{8,0},{9,25... | collective-permute-start | bytes 3145736 | tf_op jit(solution)/shard_map/ppermute | solution.py:42
  14.3 7.4 %collective-permute-done.1 = bf16[16,9216]{1,0:T(8,128)(2,1)} collective-permute-done((bf16[16,9216]{1,0:T(8,128)(2,1)}, bf16[16,9216]{1,0:T(8,128)(2,1)}, u32[]{:S(2)}, u32[]{:S(2)}) %collective-permute-start.1) | collective-permute-done | bytes 294944 | tf_op jit(solution)/shard_map/ppermute | solution.py:87
  21.8 2.3 %pad_maximum_fusion.2 = bf16[4,16,9216]{2,1,0:T(8,128)(2,1)} fusion(bf16[1,16,9216]{2,1,0:T(8,128)(2,1)} %bitcast.6, bf16[1,16,9216]{2,1,0:T(8,128)(2,1)} %bitcast.5, bf16[1,16,9216]{2,1,0:T(8,128)(2,1)} %bitcast.4, bf16[1,16,9216]{2,1,0:T(8,128)(2,1)S(1)} %get-tuple-element.21), kind=kLoop, calls=%fused_computation.75 | loop fusion | flops 1769472 | bytes 2359296 | tf_op jit(solution)/shard_map/stack | solution.py:88
  42.3 2.1 %fusion.76 = f32[384,1024]{1,0:T(8,128)S(1)} fusion(bf16[384,8192]{1,0:T(8,128)(2,1)} %param.8, s32[]{:T(128)S(6)} %select_n.300, bf16[1024,1024]{1,0:T(8,128)(2,1)} %param.10), kind=kOutput, calls=%fused_computation.127 | convolution fusion | flops 402653184 | bytes 3014660 | tf_op jit(solution)/shard_map/dot_general | solution.py:160
  44.4 1.9 %fusion.88 = f32[384,1024]{1,0:T(8,128)S(1)} fusion(bf16[384,8192]{1,0:T(8,128)(2,1)} %param.8, s32[]{:T(128)S(6)} %select_n.290, bf16[1024,1024]{1,0:T(8,128)(2,1)} %param.10), kind=kOutput, calls=%fused_computation.139 | convolution fusion | flops 402653184 | bytes 3014660 | tf_op jit(solution)/shard_map/dot_general | solution.py:160
  46.3 1.8 %collective-permute-start.5 = (bf16[512,1024]{1,0:T(8,128)(2,1)}, bf16[512,1024]{1,0:T(8,128)(2,1)S(1)}, u32[]{:S(2)}, u32[]{:S(2)}) collective-permute-start(bf16[512,1024]{1,0:T(8,128)(2,1)} %collective-permute-done.4), channel_id=1, source_target_pairs={{0,16},{1,9},{2,18},{3,11},{4,12},{5,21},{6,14},{7,23},{8,24},{9,1... | collective-permute-start | bytes 3145736 | tf_op jit(solution)/shard_map/ppermute | solution.py:43
  50.2 1.6 %fusion.74 = f32[384,1024]{1,0:T(8,128)S(1)} fusion(bf16[512,1024]{1,0:T(8,128)(2,1)S(1)} %collective-permute-done.8, bf16[384,8192]{1,0:T(8,128)(2,1)} %param.8, s32[]{:T(128)S(6)} %select_n.301), kind=kOutput, calls=%fused_computation.125 | convolution fusion | flops 402653184 | bytes 3014660 | tf_op jit(solution)/shard_map/dot_general | solution.py:160
  51.8 1.8 %fusion.86 = f32[384,1024]{1,0:T(8,128)S(1)} fusion(bf16[512,1024]{1,0:T(8,128)(2,1)} %collective-permute-done.4, bf16[384,8192]{1,0:T(8,128)(2,1)S(1)} %bitcast.168, s32[]{:T(128)S(6)} %select_n.293), kind=kOutput, calls=%fused_computation.137 | convolution fusion | flops 402653184 | bytes 3014660 | tf_op jit(solution)/shard_map/dot_general | solution.py:160
  62.0 1.2 fusion.105
  63.3 1.2 fusion.107
  64.5 1.2 fusion.121
  67.8 1.7 %fusion.49 = bf16[3,16,128]{2,1,0:T(8,128)(2,1)S(1)} fusion(bf16[3,128,8192]{2,1,0:T(8,128)(2,1)S(1)} %bitcast.170, f32[3,128]{1,0:T(4,128)S(1)} %get-tuple-element.24, bf16[3,16,9216]{2,1,0:T(8,128)(2,1)S(1)} %pad_maximum_fusion.4), kind=kOutput, calls=%fused_computation.80 | convolution fusion | flops 100675584 | bytes 7092224 | tf_op jit(solution)/shard_map/cvj,coj->cvo/dot_general | solution.py:107
  71.9 1.2 fusion.109
  73.1 1.3 fusion.111
  74.4 1.3 fusion.113
  76.8 1.2 fusion.117
  78.0 1.2 fusion.119
  79.2 1.2 fusion.103
  80.4 1.2 fusion.101
  81.6 1.2 fusion.99
  82.8 1.2 fusion.97
  84.0 1.2 fusion.95
  85.2 1.2 fusion.93
  88.0 1.8 %fusion.18 = bf16[384,8192]{1,0:T(8,128)(2,1)S(1)} fusion(bf16[384,8192]{1,0:T(8,128)(2,1)S(1)} %broadcast_in_dim.44, s32[]{:T(128)S(6)} %select_n.290, f32[384,512]{1,0:T(8,128)} %bitcast.193, bf16[1024,1024]{1,0:T(8,128)(2,1)S(1)} %copy-done.2, bf16[384,1024]{1,0:T(8,128)(2,1)S(1)} %copy-done.11, f32[384]{0:T(512)S(1)} %get-tuple-element.23), kind=kOutput, calls=%fused_computation.44 | convolution fusion | flops 404226048 | bytes 3016708 | tf_op jit(solution)/shard_map/dot_general | solution.py:164
  89.9 1.9 %fusion.20 = bf16[384,8192]{1,0:T(8,128)(2,1)S(1)} fusion(bf16[384,8192]{1,0:T(8,128)(2,1)S(1)} %fusion.18, s32[]{:T(128)S(6)} %select_n.293, f32[384,512]{1,0:T(8,128)S(1)} %bitcast.192, bf16[512,1024]{1,0:T(8,128)(2,1)} %collective-permute-done.4, bf16[384,1024]{1,0:T(8,128)(2,1)S(1)} %copy-done.11, f32[384]{0:T(512)S(1)} %get-tuple-element.23), kind=kOutput, calls=%fused_computation.46 | convolution fusion | flops 404226048 | bytes 3016708 | tf_op jit(solution)/shard_map/dot_general | solution.py:164
  91.9 2.0 %pad_maximum_fusion = bf16[4,512,1024]{2,1,0:T(8,128)(2,1)S(1)} fusion(bf16[1,512,1024]{2,1,0:T(8,128)(2,1)S(1)} %bitcast.175, bf16[1,512,1024]{2,1,0:T(8,128)(2,1)S(1)} %bitcast.174, bf16[1,512,1024]{2,1,0:T(8,128)(2,1)} %bitcast.13, bf16[1,512,1024]{2,1,0:T(8,128)(2,1)S(1)} %copy-done.10), kind=kLoop, calls=%fused_computation.1 | loop fusion | flops 6291456 | bytes 8388608 | tf_op jit(solution)/shard_map/stack | solution.py:45
  94.7 2.2 %pad_maximum_fusion.1 = bf16[4,512,1024]{2,1,0:T(8,128)(2,1)S(1)} fusion(bf16[1,512,1024]{2,1,0:T(8,128)(2,1)S(1)} %bitcast.172, bf16[1,512,1024]{2,1,0:T(8,128)(2,1)S(1)} %bitcast.173, bf16[1,512,1024]{2,1,0:T(8,128)(2,1)S(1)} %bitcast.171, bf16[1,512,1024]{2,1,0:T(8,128)(2,1)} %get-tuple-element.15), kind=kLoop, calls=%fused_computation.2 | loop fusion | flops 6291456 | bytes 8388608 | tf_op jit(solution)/shard_map/stack | solution.py:45
  97.6 1.8 %fusion.22 = bf16[384,8192]{1,0:T(8,128)(2,1)S(1)} fusion(bf16[384,8192]{1,0:T(8,128)(2,1)S(1)} %fusion.20, s32[]{:T(128)S(6)} %select_n.294, f32[384,512]{1,0:T(8,128)} %bitcast.195, bf16[512,1024]{1,0:T(8,128)(2,1)S(1)} %collective-permute-done.5, bf16[384,1024]{1,0:T(8,128)(2,1)S(1)} %copy-done.11, f32[384]{0:T(512)S(1)} %get-tuple-element.23), kind=kOutput, calls=%fused_computation.48 | convolution fusion | flops 404226048 | bytes 3016708 | tf_op jit(solution)/shard_map/dot_general | solution.py:164
  99.3 1.8 %fusion.24 = bf16[384,8192]{1,0:T(8,128)(2,1)S(1)} fusion(bf16[384,8192]{1,0:T(8,128)(2,1)S(1)} %fusion.22, s32[]{:T(128)S(6)} %select_n.295, f32[384,512]{1,0:T(8,128)} %bitcast.194, bf16[512,1024]{1,0:T(8,128)(2,1)S(1)} %collective-permute-done.6, bf16[384,1024]{1,0:T(8,128)(2,1)S(1)} %copy-done.11, f32[384]{0:T(512)S(1)} %get-tuple-element.23), kind=kOutput, calls=%fused_computation.50 | convolution fusion | flops 404226048 | bytes 3016708 | tf_op jit(solution)/shard_map/dot_general | solution.py:164
  101.1 2.3 %fusion.90 = (bf16[16,9216]{1,0:T(8,128)(2,1)}, bf16[16,9216]{1,0:T(8,128)(2,1)S(1)}, bf16[16,9216]{1,0:T(8,128)(2,1)S(1)}) fusion(f32[1,16,9216]{2,1,0:T(8,128)S(1)} %get-tuple-element.7, f32[1,16,9216]{2,1,0:T(8,128)S(1)} %get-tuple-element.6, f32[1,16,9216]{2,1,0:T(8,128)S(1)} %get-tuple-element.5, bf16[4,16,9216]{2,1,0:T(8,128)(2,1)} %collective-permute-done.12, ...), kind=kLoop, calls=%fused_computation.141 | loop fusion | flops 4423680 | bytes 3538953 | tf_op jit(solution)/shard_map/convert_element_type | solution.py:139
  103.4 2.0 %collective-permute-start.13 = (bf16[16,9216]{1,0:T(8,128)(2,1)}, bf16[16,9216]{1,0:T(8,128)(2,1)S(1)}, u32[]{:S(2)}, u32[]{:S(2)}) collective-permute-start(bf16[16,9216]{1,0:T(8,128)(2,1)} %get-tuple-element.8), channel_id=1, source_target_pairs={{0,8},{4,12},{8,0},{12,4},{16,24},{20,28},{24,16},{28,20},{1,9},{5... | collective-permute-start | bytes 884744 | tf_op jit(solution)/shard_map/ppermute | solution.py:140
  105.7 1.2 collective-permute-start.15
  108.1 5.4 %collective-permute-done.13 = bf16[16,9216]{1,0:T(8,128)(2,1)S(1)} collective-permute-done((bf16[16,9216]{1,0:T(8,128)(2,1)}, bf16[16,9216]{1,0:T(8,128)(2,1)S(1)}, u32[]{:S(2)}, u32[]{:S(2)}) %collective-permute-start.13) | collective-permute-done | bytes 294944 | tf_op jit(solution)/shard_map/ppermute | solution.py:140
  113.5 7.3 %collective-permute-done.14 = bf16[16,9216]{1,0:T(8,128)(2,1)S(1)} collective-permute-done((bf16[16,9216]{1,0:T(8,128)(2,1)S(1)}, bf16[16,9216]{1,0:T(8,128)(2,1)S(1)}, u32[]{:S(2)}, u32[]{:S(2)}) %collective-permute-start.14) | collective-permute-done | bytes 294944 | tf_op jit(solution)/shard_map/ppermute | solution.py:140
  120.8 1.4 fusion.63
  123.5 1.7 %fusion.52 = f32[384,1024]{1,0:T(8,128)} fusion(bf16[4,512,1024]{2,1,0:T(8,128)(2,1)S(1)} %collective-permute-done.7, bf16[384,8192]{1,0:T(8,128)(2,1)S(1)} %bitcast.168, s32[]{:T(128)S(6)} %select_n.297), kind=kOutput, calls=%fused_computation.91 | convolution fusion | flops 402653184 | bytes 3014660 | tf_op jit(solution)/shard_map/dot_general | solution.py:160
  125.3 1.8 %fusion.54 = f32[384,1024]{1,0:T(8,128)} fusion(bf16[4,512,1024]{2,1,0:T(8,128)(2,1)S(1)} %collective-permute-done.7, bf16[384,8192]{1,0:T(8,128)(2,1)S(1)} %bitcast.168, s32[]{:T(128)S(6)} %select_n.299), kind=kOutput, calls=%fused_computation.93 | convolution fusion | flops 402653184 | bytes 3014660 | tf_op jit(solution)/shard_map/dot_general | solution.py:160
  131.3 1.8 %fusion.56 = f32[384,1024]{1,0:T(8,128)} fusion(bf16[4,512,1024]{2,1,0:T(8,128)(2,1)S(1)} %collective-permute-done.11, bf16[384,8192]{1,0:T(8,128)(2,1)S(1)} %bitcast.168, s32[]{:T(128)S(6)} %select_n.305), kind=kOutput, calls=%fused_computation.95 | convolution fusion | flops 402653184 | bytes 3014660 | tf_op jit(solution)/shard_map/dot_general | solution.py:160
  133.1 1.8 %fusion.58 = f32[384,1024]{1,0:T(8,128)} fusion(bf16[4,512,1024]{2,1,0:T(8,128)(2,1)S(1)} %collective-permute-done.11, bf16[384,8192]{1,0:T(8,128)(2,1)S(1)} %bitcast.168, s32[]{:T(128)S(6)} %select_n.307), kind=kOutput, calls=%fused_computation.97 | convolution fusion | flops 402653184 | bytes 3014660 | tf_op jit(solution)/shard_map/dot_general | solution.py:160
  134.8 1.7 %fusion.57 = f32[384,1024]{1,0:T(8,128)} fusion(bf16[4,512,1024]{2,1,0:T(8,128)(2,1)S(1)} %collective-permute-done.11, bf16[384,8192]{1,0:T(8,128)(2,1)S(1)} %bitcast.168, s32[]{:T(128)S(6)} %select_n.306), kind=kOutput, calls=%fused_computation.96 | convolution fusion | flops 402653184 | bytes 3014660 | tf_op jit(solution)/shard_map/dot_general | solution.py:160
  136.6 1.7 %fusion.53 = f32[384,1024]{1,0:T(8,128)} fusion(bf16[4,512,1024]{2,1,0:T(8,128)(2,1)S(1)} %collective-permute-done.7, bf16[384,8192]{1,0:T(8,128)(2,1)S(1)} %bitcast.168, s32[]{:T(128)S(6)} %select_n.298), kind=kOutput, calls=%fused_computation.92 | convolution fusion | flops 402653184 | bytes 3014660 | tf_op jit(solution)/shard_map/dot_general | solution.py:160
  138.3 1.8 %fusion.55 = f32[384,1024]{1,0:T(8,128)} fusion(bf16[4,512,1024]{2,1,0:T(8,128)(2,1)S(1)} %collective-permute-done.11, bf16[384,8192]{1,0:T(8,128)(2,1)S(1)} %bitcast.168, s32[]{:T(128)S(6)} %select_n.304), kind=kOutput, calls=%fused_computation.94 | convolution fusion | flops 402653184 | bytes 3014660 | tf_op jit(solution)/shard_map/dot_general | solution.py:160
  140.1 1.8 %fusion.51 = f32[384,1024]{1,0:T(8,128)} fusion(bf16[4,512,1024]{2,1,0:T(8,128)(2,1)S(1)} %collective-permute-done.7, bf16[384,8192]{1,0:T(8,128)(2,1)S(1)} %bitcast.168, s32[]{:T(128)S(6)} %select_n.296), kind=kOutput, calls=%fused_computation.90 | convolution fusion | flops 402653184 | bytes 3014660 | tf_op jit(solution)/shard_map/dot_general | solution.py:160
  148.4 9.6 %fusion.16 = bf16[384,1024]{1,0:T(8,128)(2,1)} fusion(f32[384,1024]{1,0:T(8,128)} %fusion.58, f32[384,1024]{1,0:T(8,128)} %fusion.57, f32[384,1024]{1,0:T(8,128)} %fusion.56, f32[384,1024]{1,0:T(8,128)} %fusion.55, f32[384,1024]{1,0:T(8,128)S(1)} %fusion.72, f32[384,1024]{1,0:T(8,128)S(1)} %fusion.74, f32[384,1024]{1,0:T(8,128)S(1)} %fusion.76, ...), kind=kOutput, calls=%fused_computation.25 | convolution fusion | flops 409731072 | bytes 27396100 | tf_op jit(solution)/shard_map/dot_general | solution.py:160
  (134 shorter events, 34.8 us)
Async XLA Ops:
  0.6 13.0 %copy-start = (s32[32]{0:T(128)S(1)}, s32[32]{0:T(128)}, u32[]{:S(2)}) copy-start(s32[32]{0:T(128)} %param.15) | copy-start | bytes 388
  2.4 10.4 %copy-start.12 = (bf16[1,16,8192]{2,1,0:T(8,128)(2,1)S(1)}, bf16[1,16,8192]{2,1,0:T(8,128)(2,1)}, u32[]{:S(2)}) copy-start(bf16[1,16,8192]{2,1,0:T(8,128)(2,1)} %param.11) | copy-start | bytes 786436
  2.4 10.4 %copy-start.27 = (bf16[1,16,1024]{2,1,0:T(8,128)(2,1)S(1)}, bf16[1,16,1024]{2,1,0:T(8,128)(2,1)}, u32[]{:S(2)}) copy-start(bf16[1,16,1024]{2,1,0:T(8,128)(2,1)} %param.12) | copy-start | bytes 98308
  2.4 11.1 %copy-start.29 = (s32[3]{0:T(128)S(1)}, s32[3]{0:T(128)}, u32[]{:S(2)}) copy-start(s32[3]{0:T(128)} %param.13) | copy-start | bytes 40
  2.4 11.1 %copy-start.28 = (s32[3]{0:T(128)S(1)}, s32[3]{0:T(128)}, u32[]{:S(2)}) copy-start(s32[3]{0:T(128)} %param.14) | copy-start | bytes 40
  2.4 11.9 %collective-permute-start = (bf16[16,9216]{1,0:T(8,128)(2,1)}, bf16[16,9216]{1,0:T(8,128)(2,1)}, u32[]{:S(2)}, u32[]{:S(2)}) collective-permute-start(bf16[16,9216]{1,0:T(8,128)(2,1)} %get-tuple-element.22), channel_id=1, source_target_pairs={{0,8},{4,12},{8,0},{12,4},{16,24},{20,28},{24,16},{28,20},{1,9},{5... | collective-permute-start | bytes 884744 | tf_op jit(solution)/shard_map/ppermute | solution.py:87
  5.4 16.4 %collective-permute-start.1 = (bf16[16,9216]{1,0:T(8,128)(2,1)}, bf16[16,9216]{1,0:T(8,128)(2,1)}, u32[]{:S(2)}, u32[]{:S(2)}) collective-permute-start(bf16[16,9216]{1,0:T(8,128)(2,1)} %get-tuple-element.22), channel_id=1, source_target_pairs={{0,16},{4,20},{8,24},{12,28},{16,0},{20,4},{24,8},{28,12},{1,17},{... | collective-permute-start | bytes 884744 | tf_op jit(solution)/shard_map/ppermute | solution.py:87
  6.9 14.9 %collective-permute-start.2 = (bf16[16,9216]{1,0:T(8,128)(2,1)}, bf16[16,9216]{1,0:T(8,128)(2,1)}, u32[]{:S(2)}, u32[]{:S(2)}) collective-permute-start(bf16[16,9216]{1,0:T(8,128)(2,1)} %get-tuple-element.22), channel_id=1, source_target_pairs={{0,24},{4,28},{8,16},{12,20},{16,8},{20,12},{24,0},{28,4},{1,25},{... | collective-permute-start | bytes 884744 | tf_op jit(solution)/shard_map/ppermute | solution.py:87
  10.7 35.6 %collective-permute-start.4 = (bf16[512,1024]{1,0:T(8,128)(2,1)}, bf16[512,1024]{1,0:T(8,128)(2,1)}, u32[]{:S(2)}, u32[]{:S(2)}) collective-permute-start(bf16[512,1024]{1,0:T(8,128)(2,1)} %get-tuple-element.17), channel_id=1, source_target_pairs={{0,8},{1,17},{2,10},{3,19},{4,20},{5,13},{6,22},{7,15},{8,0},{9,25... | collective-permute-start | bytes 3145736 | tf_op jit(solution)/shard_map/ppermute | solution.py:42
  12.7 36.5 %collective-permute-start.8 = (bf16[512,1024]{1,0:T(8,128)(2,1)}, bf16[512,1024]{1,0:T(8,128)(2,1)S(1)}, u32[]{:S(2)}, u32[]{:S(2)}) collective-permute-start(bf16[512,1024]{1,0:T(8,128)(2,1)} %get-tuple-element.16), channel_id=1, source_target_pairs={{0,8},{1,17},{2,10},{3,19},{4,20},{5,13},{6,22},{7,15},{8,0},{9,25... | collective-permute-start | bytes 3145736 | tf_op jit(solution)/shard_map/ppermute | solution.py:42
  13.6 38.2 %slice-start = ((s8[6291456]{0:T(1024)(128)(4,1)}), s8[2097152]{0:T(1024)(128)(4,1)S(1)}, s32[]{:S(2)}) async-start(s8[6291456]{0:T(1024)(128)(4,1)} %bitcast.167), calls=%async_computation | async-start | bytes 4194304
  24.1 29.5 %collective-permute-start.3 = (bf16[4,16,9216]{2,1,0:T(8,128)(2,1)}, bf16[4,16,9216]{2,1,0:T(8,128)(2,1)}, u32[]{:S(2)}, u32[]{:S(2)}) collective-permute-start(bf16[4,16,9216]{2,1,0:T(8,128)(2,1)} %pad_maximum_fusion.2), channel_id=1, source_target_pairs={{0,4},{4,0},{8,12},{12,8},{16,20},{20,16},{24,28},{28,24},{1,5},{5... | collective-permute-start | bytes 3538952 | tf_op jit(solution)/shard_map/ppermute | solution.py:89
  42.3 9.5 %slice-start.1 = ((s8[6291456]{0:T(1024)(128)(4,1)}), s8[4194304]{0:T(1024)(128)(4,1)S(1)}, s32[]{:S(2)}) async-start(s8[6291456]{0:T(1024)(128)(4,1)} %bitcast.167), calls=%async_computation.1 | async-start | bytes 8388608
  46.3 7.3 %copy-start.26 = (bf16[8,16,9216]{2,1,0:T(8,128)(2,1)S(1)}, bf16[8,16,9216]{2,1,0:T(8,128)(2,1)}, u32[]{:S(2)}) copy-start(bf16[8,16,9216]{2,1,0:T(8,128)(2,1)} %constant_dynamic-update-slice_fusion.3) | copy-start | bytes 7077892
  46.3 45.5 %collective-permute-start.5 = (bf16[512,1024]{1,0:T(8,128)(2,1)}, bf16[512,1024]{1,0:T(8,128)(2,1)S(1)}, u32[]{:S(2)}, u32[]{:S(2)}) collective-permute-start(bf16[512,1024]{1,0:T(8,128)(2,1)} %collective-permute-done.4), channel_id=1, source_target_pairs={{0,16},{1,9},{2,18},{3,11},{4,12},{5,21},{6,14},{7,23},{8,24},{9,1... | collective-permute-start | bytes 3145736 | tf_op jit(solution)/shard_map/ppermute | solution.py:43
  48.1 43.7 %collective-permute-start.6 = (bf16[512,1024]{1,0:T(8,128)(2,1)}, bf16[512,1024]{1,0:T(8,128)(2,1)S(1)}, u32[]{:S(2)}, u32[]{:S(2)}) collective-permute-start(bf16[512,1024]{1,0:T(8,128)(2,1)} %collective-permute-done.4), channel_id=1, source_target_pairs={{0,1},{1,0},{2,3},{3,2},{4,5},{5,4},{6,7},{7,6},{8,9},{9,8},{10,11... | collective-permute-start | bytes 3145736 | tf_op jit(solution)/shard_map/ppermute | solution.py:44
  49.1 45.3 %collective-permute-start.9 = (bf16[512,1024]{1,0:T(8,128)(2,1)S(1)}, bf16[512,1024]{1,0:T(8,128)(2,1)S(1)}, u32[]{:S(2)}, u32[]{:S(2)}) collective-permute-start(bf16[512,1024]{1,0:T(8,128)(2,1)S(1)} %collective-permute-done.8), channel_id=1, source_target_pairs={{0,16},{1,9},{2,18},{3,11},{4,12},{5,21},{6,14},{7,23},{8,24},{9,1... | collective-permute-start | bytes 3145736 | tf_op jit(solution)/shard_map/ppermute | solution.py:43
  49.7 45.1 %collective-permute-start.10 = (bf16[512,1024]{1,0:T(8,128)(2,1)S(1)}, bf16[512,1024]{1,0:T(8,128)(2,1)S(1)}, u32[]{:S(2)}, u32[]{:S(2)}) collective-permute-start(bf16[512,1024]{1,0:T(8,128)(2,1)S(1)} %collective-permute-done.8), channel_id=1, source_target_pairs={{0,1},{1,0},{2,3},{3,2},{4,5},{5,4},{6,7},{7,6},{8,9},{9,8},{10,11... | collective-permute-start | bytes 3145736 | tf_op jit(solution)/shard_map/ppermute | solution.py:44
  60.6 1.1 copy-start.11
  71.9 29.2 %collective-permute-start.12 = (bf16[4,16,9216]{2,1,0:T(8,128)(2,1)}, bf16[4,16,9216]{2,1,0:T(8,128)(2,1)}, u32[]{:S(2)}, u32[]{:S(2)}) collective-permute-start(bf16[4,16,9216]{2,1,0:T(8,128)(2,1)} %pad_maximum_fusion.3), channel_id=1, source_target_pairs={{0,4},{4,0},{8,12},{12,8},{16,20},{20,16},{24,28},{28,24},{1,5},{5... | collective-permute-start | bytes 3538952 | tf_op jit(solution)/shard_map/ppermute | solution.py:132
  86.4 1.6 %copy-start.2 = (bf16[1024,1024]{1,0:T(8,128)(2,1)S(1)}, bf16[1024,1024]{1,0:T(8,128)(2,1)}, u32[]{:S(2)}) copy-start(bf16[1024,1024]{1,0:T(8,128)(2,1)} %param.10) | copy-start | bytes 6291460
  88.0 1.8 %copy-start.25 = (f32[3,128,512]{2,1,0:T(8,128)S(1)}, f32[3,128,512]{2,1,0:T(8,128)}, u32[]{:S(2)}) copy-start(f32[3,128,512]{2,1,0:T(8,128)} %fusion.121) | copy-start | bytes 2359300
  89.9 2.0 %copy-start.10 = (bf16[1,512,1024]{2,1,0:T(8,128)(2,1)S(1)}, bf16[1,512,1024]{2,1,0:T(8,128)(2,1)}, u32[]{:S(2)}) copy-start(bf16[1,512,1024]{2,1,0:T(8,128)(2,1)} %get-tuple-element.14) | copy-start | bytes 3145732
  91.8 5.7 %copy-start.8 = (bf16[512,1024]{1,0:T(8,128)(2,1)}, bf16[512,1024]{1,0:T(8,128)(2,1)S(1)}, u32[]{:S(2)}) copy-start(bf16[512,1024]{1,0:T(8,128)(2,1)S(1)} %collective-permute-done.5) | copy-start | bytes 3145732
  93.8 29.7 %collective-permute-start.7 = (bf16[4,512,1024]{2,1,0:T(8,128)(2,1)S(1)}, bf16[4,512,1024]{2,1,0:T(8,128)(2,1)S(1)}, u32[]{:S(2)}, u32[]{:S(2)}) collective-permute-start(bf16[4,512,1024]{2,1,0:T(8,128)(2,1)S(1)} %pad_maximum_fusion), channel_id=1, source_target_pairs={{0,4},{4,0},{8,12},{12,8},{16,20},{20,16},{24,28},{28,24},{1,5},{5... | collective-permute-start | bytes 12582920 | tf_op jit(solution)/shard_map/ppermute | solution.py:46
  94.4 12.5 %copy-start.6 = (bf16[512,1024]{1,0:T(8,128)(2,1)}, bf16[512,1024]{1,0:T(8,128)(2,1)S(1)}, u32[]{:S(2)}) copy-start(bf16[512,1024]{1,0:T(8,128)(2,1)S(1)} %collective-permute-done.9) | copy-start | bytes 3145732
  94.7 2.2 %copy-start.4 = (bf16[512,1024]{1,0:T(8,128)(2,1)}, bf16[512,1024]{1,0:T(8,128)(2,1)S(1)}, u32[]{:S(2)}) copy-start(bf16[512,1024]{1,0:T(8,128)(2,1)S(1)} %collective-permute-done.10) | copy-start | bytes 3145732
  96.9 34.3 %collective-permute-start.11 = (bf16[4,512,1024]{2,1,0:T(8,128)(2,1)S(1)}, bf16[4,512,1024]{2,1,0:T(8,128)(2,1)S(1)}, u32[]{:S(2)}, u32[]{:S(2)}) collective-permute-start(bf16[4,512,1024]{2,1,0:T(8,128)(2,1)S(1)} %pad_maximum_fusion.1), channel_id=1, source_target_pairs={{0,4},{4,0},{8,12},{12,8},{16,20},{20,16},{24,28},{28,24},{1,5},{5... | collective-permute-start | bytes 12582920 | tf_op jit(solution)/shard_map/ppermute | solution.py:46
  103.4 4.1 %copy-start.9 = (bf16[512,1024]{1,0:T(8,128)(2,1)S(1)}, bf16[512,1024]{1,0:T(8,128)(2,1)}, u32[]{:S(2)}) copy-start(bf16[512,1024]{1,0:T(8,128)(2,1)} %copy-done.8) | copy-start | bytes 3145732
  103.4 10.1 %collective-permute-start.13 = (bf16[16,9216]{1,0:T(8,128)(2,1)}, bf16[16,9216]{1,0:T(8,128)(2,1)S(1)}, u32[]{:S(2)}, u32[]{:S(2)}) collective-permute-start(bf16[16,9216]{1,0:T(8,128)(2,1)} %get-tuple-element.8), channel_id=1, source_target_pairs={{0,8},{4,12},{8,0},{12,4},{16,24},{20,28},{24,16},{28,20},{1,9},{5... | collective-permute-start | bytes 884744 | tf_op jit(solution)/shard_map/ppermute | solution.py:140
  105.4 15.4 %collective-permute-start.14 = (bf16[16,9216]{1,0:T(8,128)(2,1)S(1)}, bf16[16,9216]{1,0:T(8,128)(2,1)S(1)}, u32[]{:S(2)}, u32[]{:S(2)}) collective-permute-start(bf16[16,9216]{1,0:T(8,128)(2,1)S(1)} %get-tuple-element.9), channel_id=1, source_target_pairs={{0,16},{4,20},{8,24},{12,28},{16,0},{20,4},{24,8},{28,12},{1,17},{... | collective-permute-start | bytes 884744 | tf_op jit(solution)/shard_map/ppermute | solution.py:140
  105.7 15.1 %collective-permute-start.15 = (bf16[16,9216]{1,0:T(8,128)(2,1)S(1)}, bf16[16,9216]{1,0:T(8,128)(2,1)}, u32[]{:S(2)}, u32[]{:S(2)}) collective-permute-start(bf16[16,9216]{1,0:T(8,128)(2,1)S(1)} %get-tuple-element.10), channel_id=1, source_target_pairs={{0,24},{4,28},{8,16},{12,20},{16,8},{20,12},{24,0},{28,4},{1,25},{... | collective-permute-start | bytes 884744 | tf_op jit(solution)/shard_map/ppermute | solution.py:140
  123.5 3.5 %copy-start.24 = (f32[3,128,512]{2,1,0:T(8,128)S(1)}, f32[3,128,512]{2,1,0:T(8,128)}, u32[]{:S(2)}) copy-start(f32[3,128,512]{2,1,0:T(8,128)} %fusion.115) | copy-start | bytes 2359300
  127.0 1.1 copy-start.23
  127.6 1.2 copy-start.22
  128.8 1.1 copy-start.21
  129.5 1.2 copy-start.14
  138.3 3.6 %copy-start.13 = (f32[3,128,512]{2,1,0:T(8,128)S(1)}, f32[3,128,512]{2,1,0:T(8,128)}, u32[]{:S(2)}) copy-start(f32[3,128,512]{2,1,0:T(8,128)} %fusion.105) | copy-start | bytes 2359300
  141.9 1.2 copy-start.7
  141.9 1.4 copy-start.20
  142.5 1.4 copy-start.5
  142.6 1.6 copy-start.19
  144.0 1.2 copy-start.18
  144.8 1.2 copy-start.17
  145.8 1.2 copy-start.16
  146.6 1.2 copy-start.15
  148.4 9.7 %copy-start.3 = (bf16[384,8192]{1,0:T(8,128)(2,1)}, bf16[384,8192]{1,0:T(8,128)(2,1)S(1)}, u32[]{:S(2)}) copy-start(bf16[384,8192]{1,0:T(8,128)(2,1)S(1)} %fusion.48) | copy-start | bytes 18874372
  148.4 9.6 %copy-start.1 = (s32[32]{0:T(128)S(1)}, s32[32]{0:T(128)}, u32[]{:S(2)}) copy-start(s32[32]{0:T(128)} %param.15) | copy-start | bytes 388

commit v4 on v3

--- a/solution.py
+++ b/solution.py
@@ -35,29 +35,33 @@
     relay_pairs = flat_pairs(lambda i, d, role: (i ^ (4 - 2 * role), d))
     partner_pairs = flat_pairs(lambda i, d, role: (i, d ^ 1))
     role = parity ^ (dp_index % 2)
+    sibling = me ^ 1
+    sibling_role = 1 - role
+    sources = [me, me ^ (2 + 2 * role), me ^ 6, me ^ (4 - 2 * role)]
+    sibling_sources = [sibling, sibling ^ (2 + 2 * sibling_role), sibling ^ 6,
+                       sibling ^ (4 - 2 * sibling_role)]
     rows = shard.shape[0] // WEIGHT_CHUNKS
-    chunks = []
+    result = []
+    previous = None
     for k in range(WEIGHT_CHUNKS):
         piece = shard[k * rows:(k + 1) * rows]
+        result.append((0.0, sources[0], k, piece))
+        result.append((1.0, sibling_sources[0], k, lax.ppermute(piece, "fsdp", xor_pairs(members, 1))))
+        if previous is not None:
+            piece, _ = lax.optimization_barrier((piece, previous))
         first = lax.ppermute(piece, ("fsdp", "dp"), first_pairs)
+        previous = first
+        result.append((2.0 + 2 * k, sources[1], k, first))
+        result.append((3.0 + 2 * k, sibling_sources[1], k, lax.ppermute(first, "fsdp", xor_pairs(members, 1))))
         relayed = lax.ppermute(first, ("fsdp", "dp"), relay_pairs)
         partner = lax.ppermute(first, ("fsdp", "dp"), partner_pairs)
-        own_four = jnp.stack([piece, first, relayed, partner])
-        sibling_four = lax.ppermute(own_four, "fsdp", xor_pairs(members, 1))
-        chunks.append((piece, first, relayed, partner, sibling_four))
-    sources = [me, me ^ (2 + 2 * role), me ^ 6, me ^ (4 - 2 * role)]
-    sibling = me ^ 1
-    sibling_role = 1 - role
-    sibling_sources = [sibling, sibling ^ (2 + 2 * sibling_role), sibling ^ 6,
-                       sibling ^ (4 - 2 * sibling_role)]
-    result = []
-    for k in range(WEIGHT_CHUNKS):
-        piece, first, relayed, partner, sibling_four = chunks[k]
-        for source, value in zip(sources, (piece, first, relayed, partner)):
-            result.append((source, k, value))
-        for index, source in enumerate(sibling_sources):
-            result.append((source, k, sibling_four[index]))
-    return result
+        result.append((4.5 + 2 * k, sources[2], k, relayed))
+        result.append((4.5 + 2 * k, sources[3], k, partner))
+        late = lax.ppermute(jnp.stack([relayed, partner]), "fsdp", xor_pairs(members, 1))
+        result.append((5.5 + 2 * k, sibling_sources[2], k, late[0]))
+        result.append((5.5 + 2 * k, sibling_sources[3], k, late[1]))
+    result.sort(key=lambda item: item[0])
+    return [item[1:] for item in result]
 
 
 def on_device(
@@ -157,9 +161,9 @@
         piece_rows = weight_piece.shape[0]
         column = source * shard_rows + chunk * piece_rows
         token_piece = lax.dynamic_slice_in_dim(tokens, column, piece_rows, axis=1)
-        output_total = output_total + jnp.dot(
+        output_total = lax.optimization_barrier(output_total + jnp.dot(
             token_piece, weight_piece, preferred_element_type=jnp.float32
-        )
+        ))
         down_piece = lax.dynamic_slice_in_dim(down_block, column, piece_rows, axis=2)
         backward_piece = lax.dot_general(
             masked_cot, weight_piece, (((1,), (1,)), ((), ())), preferred_element_type=jnp.float32

time: 159 us -> 132 us (0.83)
  matrix products: 70.4 us -> 41.7 us
  waiting for transfers between devices: 20.5 us -> 35.7 us
  local copies, waits for them, and re-layouts: 19.2 us -> 11 us
  other arithmetic: 14.5 us -> 7.58 us
  starting transfers between devices: 14.5 us -> 16.5 us
    dot_general x16, matrix products: 32.9 us -> 13.5 us  [on_device(): jnp.dot(token_piece, weight_piece, preferred_element_type=jnp.float32)]
    dot_general x16, matrix products: 19.4 us -> 9.36 us  [on_device(): jnp.einsum('uio,uof->uif', low_rank_gradient, down_piece, preferred_eleme...]
    ppermute x2, waiting for transfers between devices: 0.01 us -> 9.62 us  [relay_gather(): relayed = lax.ppermute(first, ('fsdp', 'dp'), relay_pairs)]
    ppermute x2, waiting for transfers between devices: 0.31 us -> 7.16 us  [relay_gather(): partner = lax.ppermute(first, ('fsdp', 'dp'), partner_pairs)]
    unnamed x70 -> x38, local copies, waits for them, and re-layouts: 11 us -> 4.55 us
    another operation x1 -> x0, local copies, waits for them, and re-layouts: 3.79 us -> none  [relay_gather(): own_four = jnp.stack([piece, first, relayed, partner])]
    another operation x2, other arithmetic: 4.13 us -> 0.39 us  [relay_gather(): jnp.stack([relayed, partner])]
    slice x0 -> x1, local copies, waits for them, and re-layouts: none -> 3.02 us  [relay_gather(): piece = shard[k * rows:(k + 1) * rows]]
  transfers between devices with their start and end apart: 16 -> 20, of which waited for: 4 -> 5; matrix products, arithmetic and copies ran while one was open for 46% -> 39% of each run, Pallas kernels for 0% -> 0%
where the time goes in v4:
time: 132 us; the launch traced here: 131 us
  matrix products  41.7 us (32%)
  waiting for transfers between devices  35.7 us (27%)
  between operations  19 us (14%)
  starting transfers between devices  16.5 us (12%)
  local copies, waits for them, and re-layouts  11 us (8%)
  other arithmetic  7.58 us (6%)
    dot_general x16, matrix products, on_device(): lax.dot_general(masked_cot, weight_piece, (((1,), (1,)), ((), ())), prefe...  15.2 us
    dot_general x16, matrix products, on_device(): jnp.dot(token_piece, weight_piece, preferred_element_type=jnp.float32)  13.5 us
    ppermute x3, waiting for transfers between devices, on_device(): lax.ppermute(sent, 'fsdp', xor_pairs(members, step)).astype(jnp.float32)  11.5 us
    ppermute x2, waiting for transfers between devices, relay_gather(): relayed = lax.ppermute(first, ('fsdp', 'dp'), relay_pairs)  9.62 us
    dot_general x16, matrix products, on_device(): jnp.einsum('uio,uof->uif', low_rank_gradient, down_piece, preferred_eleme...  9.36 us
    ppermute x3, waiting for transfers between devices, on_device(): by_step[step] = lax.ppermute(own_adapter, 'fsdp', xor_pairs(members, step))  7.39 us
    ppermute x2, waiting for transfers between devices, relay_gather(): partner = lax.ppermute(first, ('fsdp', 'dp'), partner_pairs)  7.16 us
    unnamed x38, local copies, waits for them, and re-layouts  4.55 us
  transfers between devices with their start and end apart: 20, of which 5 were waited for; matrix products, arithmetic and copies ran while one was open for 39% of the time, Pallas kernels for 0%

profile of v4, /device:TPU:0, one launch (start us, length us, event | category | flops | bytes accessed | tf_op | source)
XLA Modules:
  0.0 131.5 jit_solution(5991174013069027940)
XLA Ops:
  0.6 1.0 fusion.136
  1.7 3.0 %collective-permute-start = (bf16[16,9216]{1,0:T(8,128)(2,1)S(1)}, bf16[16,9216]{1,0:T(8,128)(2,1)S(1)}, u32[]{:S(2)}, u32[]{:S(2)}) collective-permute-start(bf16[16,9216]{1,0:T(8,128)(2,1)S(1)} %get-tuple-element.22), channel_id=1, source_target_pairs={{0,8},{4,12},{8,0},{12,4},{16,24},{20,28},{24,16},{28,20},{1,9},{5... | collective-permute-start | bytes 884744 | tf_op jit(solution)/shard_map/ppermute | solution.py:91
  4.7 1.5 %collective-permute-start.1 = (bf16[16,9216]{1,0:T(8,128)(2,1)S(1)}, bf16[16,9216]{1,0:T(8,128)(2,1)S(1)}, u32[]{:S(2)}, u32[]{:S(2)}) collective-permute-start(bf16[16,9216]{1,0:T(8,128)(2,1)S(1)} %get-tuple-element.22), channel_id=1, source_target_pairs={{0,16},{4,20},{8,24},{12,28},{16,0},{20,4},{24,8},{28,12},{1,17},{... | collective-permute-start | bytes 884744 | tf_op jit(solution)/shard_map/ppermute | solution.py:91
  6.2 3.0 %fusion.143 = (bf16[512,1024]{1,0:T(8,128)(2,1)}, bf16[512,1024]{1,0:T(8,128)(2,1)}) fusion(bf16[1024,1024]{1,0:T(8,128)(2,1)} %param.10), kind=kLoop, calls=%fused_computation.219 | loop fusion | bytes 4194304 | tf_op jit(solution)/shard_map/slice | solution.py:47
  9.3 1.9 %collective-permute-start.6 = (bf16[512,1024]{1,0:T(8,128)(2,1)}, bf16[512,1024]{1,0:T(8,128)(2,1)}, u32[]{:S(2)}, u32[]{:S(2)}) collective-permute-start(bf16[512,1024]{1,0:T(8,128)(2,1)} %get-tuple-element.17), channel_id=1, source_target_pairs={{0,8},{1,17},{2,10},{3,19},{4,20},{5,13},{6,22},{7,15},{8,0},{9,25... | collective-permute-start | bytes 3145736 | tf_op jit(solution)/shard_map/ppermute | solution.py:52
  11.2 0.7 constant_dynamic-update-slice_fusion.3
  12.0 0.6 gather_fusion
  12.9 7.4 %collective-permute-done.1 = bf16[16,9216]{1,0:T(8,128)(2,1)S(1)} collective-permute-done((bf16[16,9216]{1,0:T(8,128)(2,1)S(1)}, bf16[16,9216]{1,0:T(8,128)(2,1)S(1)}, u32[]{:S(2)}, u32[]{:S(2)}) %collective-permute-start.1) | collective-permute-done | bytes 294944 | tf_op jit(solution)/shard_map/ppermute | solution.py:91
  39.4 1.7 %collective-permute-start.7 = (bf16[512,1024]{1,0:T(8,128)(2,1)}, bf16[512,1024]{1,0:T(8,128)(2,1)S(1)}, u32[]{:S(2)}, u32[]{:S(2)}) collective-permute-start(bf16[512,1024]{1,0:T(8,128)(2,1)} %collective-permute-done.6), channel_id=1, source_target_pairs={{0,4},{4,0},{8,12},{12,8},{16,20},{20,16},{24,28},{28,24},{1,5},{5... | collective-permute-start | bytes 3145736 | tf_op jit(solution)/shard_map/ppermute | solution.py:55
  41.2 1.9 %fusion.58 = f32[384,1024]{1,0:T(8,128)S(1)} fusion(bf16[512,1024]{1,0:T(8,128)(2,1)} %collective-permute-done.6, bf16[384,8192]{1,0:T(8,128)(2,1)} %param.8, s32[]{:T(128)S(6)} %select_n.296), kind=kOutput, calls=%fused_computation.113 | convolution fusion | flops 402653184 | bytes 3014660 | tf_op jit(solution)/shard_map/dot_general | solution.py:164
  43.5 2.1 %fusion.60 = f32[384,1024]{1,0:T(8,128)S(1)} fusion(bf16[512,1024]{1,0:T(8,128)(2,1)} %collective-permute-done.5, bf16[384,8192]{1,0:T(8,128)(2,1)} %param.8, s32[]{:T(128)S(6)} %select_n.293), kind=kOutput, calls=%fused_computation.115 | convolution fusion | flops 402653184 | bytes 3014660 | tf_op jit(solution)/shard_map/dot_general | solution.py:164
  45.7 1.3 collective-permute-start.10
  47.5 1.1 copy-done.4
  48.9 1.2 fusion.92
  50.1 1.2 fusion.90
  51.3 0.9 fusion.145
  52.2 1.7 %fusion.32 = bf16[3,16,128]{2,1,0:T(8,128)(2,1)S(1)} fusion(bf16[3,128,8192]{2,1,0:T(8,128)(2,1)S(1)} %bitcast.122, f32[3,128]{1,0:T(4,128)S(1)} %get-tuple-element.24, bf16[3,16,9216]{2,1,0:T(8,128)(2,1)S(1)} %pad_maximum_fusion.4), kind=kOutput, calls=%fused_computation.69 | convolution fusion | flops 100675584 | bytes 7092224 | tf_op jit(solution)/shard_map/cvj,coj->cvo/dot_general | solution.py:111
  54.6 1.2 fusion.98
  55.8 1.2 fusion.96
  57.0 1.2 fusion.94
  61.3 0.7 broadcast_in_dim.44
  62.0 1.8 %fusion.1 = bf16[384,8192]{1,0:T(8,128)(2,1)S(1)} fusion(bf16[384,8192]{1,0:T(8,128)(2,1)S(1)} %broadcast_in_dim.44, s32[]{:T(128)S(6)} %select_n.290, f32[384,512]{1,0:T(8,128)} %bitcast.149, bf16[1024,1024]{1,0:T(8,128)(2,1)S(1)} %copy-done.2, bf16[384,1024]{1,0:T(8,128)(2,1)S(1)} %copy-done.4, f32[384]{0:T(512)S(1)} %get-tuple-element.23), kind=kOutput, calls=%fused_computation.33 | convolution fusion | flops 404226048 | bytes 3016708 | tf_op jit(solution)/shard_map/dot_general | solution.py:168
  63.9 0.6 fusion.3
  65.6 1.9 %convolution_add_fusion.3 = f32[384,1024]{1,0:T(8,128)S(1)} fusion(f32[384,1024]{1,0:T(8,128)S(1)} %convolution_add_fusion.4, bf16[512,1024]{1,0:T(8,128)(2,1)} %collective-permute-done.4, bf16[384,8192]{1,0:T(8,128)(2,1)S(1)} %bitcast.120, s32[]{:T(128)S(6)} %select_n.292), kind=kOutput, calls=%fused_computation.13 | convolution fusion | flops 403046400 | bytes 4587524 | tf_op jit(solution)/shard_map/dot_general | solution.py:164
  67.5 1.9 %fusion.5 = bf16[384,8192]{1,0:T(8,128)(2,1)S(1)} fusion(bf16[384,8192]{1,0:T(8,128)(2,1)S(1)} %fusion.3, s32[]{:T(128)S(6)} %select_n.292, f32[384,512]{1,0:T(8,128)S(1)} %bitcast.147, bf16[512,1024]{1,0:T(8,128)(2,1)} %collective-permute-done.4, bf16[384,1024]{1,0:T(8,128)(2,1)S(1)} %copy-done.4, f32[384]{0:T(512)S(1)} %get-tuple-element.23), kind=kOutput, calls=%fused_computation.37 | convolution fusion | flops 404226048 | bytes 3016708 | tf_op jit(solution)/shard_map/dot_general | solution.py:168
  69.5 2.0 %fusion.7 = bf16[384,8192]{1,0:T(8,128)(2,1)S(1)} fusion(bf16[384,8192]{1,0:T(8,128)(2,1)S(1)} %fusion.5, s32[]{:T(128)S(6)} %select_n.293, f32[384,512]{1,0:T(8,128)S(1)} %bitcast.146, bf16[512,1024]{1,0:T(8,128)(2,1)} %collective-permute-done.5, bf16[384,1024]{1,0:T(8,128)(2,1)S(1)} %copy-done.4, f32[384]{0:T(512)S(1)} %get-tuple-element.23), kind=kOutput, calls=%fused_computation.39 | convolution fusion | flops 404226048 | bytes 3016708 | tf_op jit(solution)/shard_map/dot_general | solution.py:168
  73.8 1.8 %fusion.9 = bf16[384,8192]{1,0:T(8,128)(2,1)S(1)} fusion(bf16[384,8192]{1,0:T(8,128)(2,1)S(1)} %fusion.7, s32[]{:T(128)S(6)} %select_n.296, f32[384,512]{1,0:T(8,128)S(1)} %bitcast.145, bf16[512,1024]{1,0:T(8,128)(2,1)} %collective-permute-done.6, bf16[384,1024]{1,0:T(8,128)(2,1)S(1)} %copy-done.4, f32[384]{0:T(512)S(1)} %get-tuple-element.23), kind=kOutput, calls=%fused_computation.41 | convolution fusion | flops 404226048 | bytes 3016708 | tf_op jit(solution)/shard_map/dot_general | solution.py:168
  79.4 0.6 fusion.11
  80.1 0.6 fusion.13
  80.7 0.6 fusion.15
  81.8 1.6 %collective-permute-start.17 = (bf16[16,9216]{1,0:T(8,128)(2,1)S(1)}, bf16[16,9216]{1,0:T(8,128)(2,1)S(1)}, u32[]{:S(2)}, u32[]{:S(2)}) collective-permute-start(bf16[16,9216]{1,0:T(8,128)(2,1)S(1)} %get-tuple-element.10), channel_id=1, source_target_pairs={{0,8},{4,12},{8,0},{12,4},{16,24},{20,28},{24,16},{28,20},{1,9},{5... | collective-permute-start | bytes 884744 | tf_op jit(solution)/shard_map/ppermute | solution.py:144
  83.8 1.5 %collective-permute-start.19 = (bf16[16,9216]{1,0:T(8,128)(2,1)S(1)}, bf16[16,9216]{1,0:T(8,128)(2,1)S(1)}, u32[]{:S(2)}, u32[]{:S(2)}) collective-permute-start(bf16[16,9216]{1,0:T(8,128)(2,1)S(1)} %get-tuple-element.12), channel_id=1, source_target_pairs={{0,24},{4,28},{8,16},{12,20},{16,8},{20,12},{24,0},{28,4},{1,25},{... | collective-permute-start | bytes 884744 | tf_op jit(solution)/shard_map/ppermute | solution.py:144
  85.3 0.6 fusion.17
  85.9 5.7 %collective-permute-done.17 = bf16[16,9216]{1,0:T(8,128)(2,1)S(1)} collective-permute-done((bf16[16,9216]{1,0:T(8,128)(2,1)S(1)}, bf16[16,9216]{1,0:T(8,128)(2,1)S(1)}, u32[]{:S(2)}, u32[]{:S(2)}) %collective-permute-start.17) | collective-permute-done | bytes 294944 | tf_op jit(solution)/shard_map/ppermute | solution.py:144
  91.6 1.3 collective-permute-start.13
  92.9 5.8 %collective-permute-done.18 = bf16[16,9216]{1,0:T(8,128)(2,1)S(1)} collective-permute-done((bf16[16,9216]{1,0:T(8,128)(2,1)S(1)}, bf16[16,9216]{1,0:T(8,128)(2,1)S(1)}, u32[]{:S(2)}, u32[]{:S(2)}) %collective-permute-start.18) | collective-permute-done | bytes 294944 | tf_op jit(solution)/shard_map/ppermute | solution.py:144
  99.0 0.7 slice_bitcast_fusion.12
  99.7 0.6 slice_bitcast_fusion.13
  100.3 9.6 %collective-permute-done.13 = bf16[512,1024]{1,0:T(8,128)(2,1)S(1)} collective-permute-done((bf16[512,1024]{1,0:T(8,128)(2,1)S(1)}, bf16[512,1024]{1,0:T(8,128)(2,1)S(1)}, u32[]{:S(2)}, u32[]{:S(2)}) %collective-permute-start.13) | collective-permute-done | bytes 1048608 | tf_op jit(solution)/shard_map/ppermute | solution.py:56
  109.9 7.2 %collective-permute-done.14 = bf16[512,1024]{1,0:T(8,128)(2,1)S(1)} collective-permute-done((bf16[512,1024]{1,0:T(8,128)(2,1)S(1)}, bf16[512,1024]{1,0:T(8,128)(2,1)S(1)}, u32[]{:S(2)}, u32[]{:S(2)}) %collective-permute-start.14) | collective-permute-done | bytes 1048608 | tf_op jit(solution)/shard_map/ppermute | solution.py:57
  118.8 0.6 fusion.19
  122.0 0.9 fusion.21
  122.9 0.6 fusion.23
  123.5 0.6 fusion.25
  124.2 0.6 fusion.27
  126.5 1.0 multiply_convert_fusion.1
  128.2 0.6 fusion.31
  128.8 2.7 %copy-done.3 = bf16[384,8192]{1,0:T(8,128)(2,1)} copy-done((bf16[384,8192]{1,0:T(8,128)(2,1)}, bf16[384,8192]{1,0:T(8,128)(2,1)S(1)}, u32[]{:S(2)}) %copy-start.3) | copy-done | bytes 6291480
  (121 shorter events, 21.5 us)
Async XLA Ops:
  0.6 11.3 %copy-start = (s32[32]{0:T(128)S(1)}, s32[32]{0:T(128)}, u32[]{:S(2)}) copy-start(s32[32]{0:T(128)} %param.15) | copy-start | bytes 388
  1.7 9.6 %copy-start.5 = (bf16[1,16,8192]{2,1,0:T(8,128)(2,1)S(1)}, bf16[1,16,8192]{2,1,0:T(8,128)(2,1)}, u32[]{:S(2)}) copy-start(bf16[1,16,8192]{2,1,0:T(8,128)(2,1)} %param.11) | copy-start | bytes 786436
  1.7 9.5 %copy-start.11 = (bf16[1,16,1024]{2,1,0:T(8,128)(2,1)S(1)}, bf16[1,16,1024]{2,1,0:T(8,128)(2,1)}, u32[]{:S(2)}) copy-start(bf16[1,16,1024]{2,1,0:T(8,128)(2,1)} %param.12) | copy-start | bytes 98308
  1.7 10.3 %copy-start.13 = (s32[3]{0:T(128)S(1)}, s32[3]{0:T(128)}, u32[]{:S(2)}) copy-start(s32[3]{0:T(128)} %param.13) | copy-start | bytes 40
  1.7 10.9 %collective-permute-start = (bf16[16,9216]{1,0:T(8,128)(2,1)S(1)}, bf16[16,9216]{1,0:T(8,128)(2,1)S(1)}, u32[]{:S(2)}, u32[]{:S(2)}) collective-permute-start(bf16[16,9216]{1,0:T(8,128)(2,1)S(1)} %get-tuple-element.22), channel_id=1, source_target_pairs={{0,8},{4,12},{8,0},{12,4},{16,24},{20,28},{24,16},{28,20},{1,9},{5... | collective-permute-start | bytes 884744 | tf_op jit(solution)/shard_map/ppermute | solution.py:91
  4.7 15.6 %collective-permute-start.1 = (bf16[16,9216]{1,0:T(8,128)(2,1)S(1)}, bf16[16,9216]{1,0:T(8,128)(2,1)S(1)}, u32[]{:S(2)}, u32[]{:S(2)}) collective-permute-start(bf16[16,9216]{1,0:T(8,128)(2,1)S(1)} %get-tuple-element.22), channel_id=1, source_target_pairs={{0,16},{4,20},{8,24},{12,28},{16,0},{20,4},{24,8},{28,12},{1,17},{... | collective-permute-start | bytes 884744 | tf_op jit(solution)/shard_map/ppermute | solution.py:91
  6.2 14.1 %collective-permute-start.2 = (bf16[16,9216]{1,0:T(8,128)(2,1)S(1)}, bf16[16,9216]{1,0:T(8,128)(2,1)S(1)}, u32[]{:S(2)}, u32[]{:S(2)}) collective-permute-start(bf16[16,9216]{1,0:T(8,128)(2,1)S(1)} %get-tuple-element.22), channel_id=1, source_target_pairs={{0,24},{4,28},{8,16},{12,20},{16,8},{20,12},{24,0},{28,4},{1,25},{... | collective-permute-start | bytes 884744 | tf_op jit(solution)/shard_map/ppermute | solution.py:91
  9.3 29.5 %copy-start.12 = (s32[3]{0:T(128)S(1)}, s32[3]{0:T(128)}, u32[]{:S(2)}) copy-start(s32[3]{0:T(128)} %param.14) | copy-start | bytes 40
  9.3 56.3 %collective-permute-start.4 = (bf16[512,1024]{1,0:T(8,128)(2,1)}, bf16[512,1024]{1,0:T(8,128)(2,1)}, u32[]{:S(2)}, u32[]{:S(2)}) collective-permute-start(bf16[512,1024]{1,0:T(8,128)(2,1)} %get-tuple-element.17), channel_id=1, source_target_pairs={{0,4},{4,0},{8,12},{12,8},{16,20},{20,16},{24,28},{28,24},{1,5},{5... | collective-permute-start | bytes 3145736 | tf_op jit(solution)/shard_map/ppermute | solution.py:49
  9.3 29.6 %collective-permute-start.6 = (bf16[512,1024]{1,0:T(8,128)(2,1)}, bf16[512,1024]{1,0:T(8,128)(2,1)}, u32[]{:S(2)}, u32[]{:S(2)}) collective-permute-start(bf16[512,1024]{1,0:T(8,128)(2,1)} %get-tuple-element.17), channel_id=1, source_target_pairs={{0,8},{1,17},{2,10},{3,19},{4,20},{5,13},{6,22},{7,15},{8,0},{9,25... | collective-permute-start | bytes 3145736 | tf_op jit(solution)/shard_map/ppermute | solution.py:52
  12.6 30.5 %collective-permute-start.5 = (bf16[512,1024]{1,0:T(8,128)(2,1)}, bf16[512,1024]{1,0:T(8,128)(2,1)}, u32[]{:S(2)}, u32[]{:S(2)}) collective-permute-start(bf16[512,1024]{1,0:T(8,128)(2,1)} %get-tuple-element.5), channel_id=1, source_target_pairs={{0,4},{4,0},{8,12},{12,8},{16,20},{20,16},{24,28},{28,24},{1,5},{5... | collective-permute-start | bytes 3145736 | tf_op jit(solution)/shard_map/ppermute | solution.py:49
  20.5 25.2 %collective-permute-start.3 = (bf16[4,16,9216]{2,1,0:T(8,128)(2,1)S(1)}, bf16[4,16,9216]{2,1,0:T(8,128)(2,1)S(1)}, u32[]{:S(2)}, u32[]{:S(2)}) collective-permute-start(bf16[4,16,9216]{2,1,0:T(8,128)(2,1)S(1)} %pad_maximum_fusion.2), channel_id=1, source_target_pairs={{0,4},{4,0},{8,12},{12,8},{16,20},{20,16},{24,28},{28,24},{1,5},{5... | collective-permute-start | bytes 3538952 | tf_op jit(solution)/shard_map/ppermute | solution.py:93
  38.9 38.1 %collective-permute-start.8 = (bf16[512,1024]{1,0:T(8,128)(2,1)}, bf16[512,1024]{1,0:T(8,128)(2,1)S(1)}, u32[]{:S(2)}, u32[]{:S(2)}) collective-permute-start(bf16[512,1024]{1,0:T(8,128)(2,1)} %get-tuple-element.5), channel_id=1, source_target_pairs={{0,8},{1,17},{2,10},{3,19},{4,20},{5,13},{6,22},{7,15},{8,0},{9,25... | collective-permute-start | bytes 3145736 | tf_op jit(solution)/shard_map/ppermute | solution.py:52
  39.4 37.0 %collective-permute-start.7 = (bf16[512,1024]{1,0:T(8,128)(2,1)}, bf16[512,1024]{1,0:T(8,128)(2,1)S(1)}, u32[]{:S(2)}, u32[]{:S(2)}) collective-permute-start(bf16[512,1024]{1,0:T(8,128)(2,1)} %collective-permute-done.6), channel_id=1, source_target_pairs={{0,4},{4,0},{8,12},{12,8},{16,20},{20,16},{24,28},{28,24},{1,5},{5... | collective-permute-start | bytes 3145736 | tf_op jit(solution)/shard_map/ppermute | solution.py:55
  43.1 3.9 %copy-start.10 = (bf16[8,16,9216]{2,1,0:T(8,128)(2,1)S(1)}, bf16[8,16,9216]{2,1,0:T(8,128)(2,1)}, u32[]{:S(2)}) copy-start(bf16[8,16,9216]{2,1,0:T(8,128)(2,1)} %constant_dynamic-update-slice_fusion.3) | copy-start | bytes 7077892
  43.1 32.6 %collective-permute-start.9 = (bf16[512,1024]{1,0:T(8,128)(2,1)}, bf16[512,1024]{1,0:T(8,128)(2,1)S(1)}, u32[]{:S(2)}, u32[]{:S(2)}) collective-permute-start(bf16[512,1024]{1,0:T(8,128)(2,1)} %collective-permute-done.6), channel_id=1, source_target_pairs={{0,16},{1,9},{2,18},{3,11},{4,12},{5,21},{6,14},{7,23},{8,24},{9,1... | collective-permute-start | bytes 3145736 | tf_op jit(solution)/shard_map/ppermute | solution.py:56
  43.5 7.7 %slice-start = ((s8[6291456]{0:T(1024)(128)(4,1)}), s8[4194304]{0:T(1024)(128)(4,1)S(1)}, s32[]{:S(2)}) async-start(s8[6291456]{0:T(1024)(128)(4,1)} %bitcast.119), calls=%async_computation | async-start | bytes 8388608
  45.7 30.0 %collective-permute-start.10 = (bf16[512,1024]{1,0:T(8,128)(2,1)}, bf16[512,1024]{1,0:T(8,128)(2,1)S(1)}, u32[]{:S(2)}, u32[]{:S(2)}) collective-permute-start(bf16[512,1024]{1,0:T(8,128)(2,1)} %collective-permute-done.6), channel_id=1, source_target_pairs={{0,1},{1,0},{2,3},{3,2},{4,5},{5,4},{6,7},{7,6},{8,9},{9,8},{10,11... | collective-permute-start | bytes 3145736 | tf_op jit(solution)/shard_map/ppermute | solution.py:57
  47.2 4.1 %slice-start.1 = ((s8[6291456]{0:T(1024)(128)(4,1)}), s8[2097152]{0:T(1024)(128)(4,1)S(1)}, s32[]{:S(2)}) async-start(s8[6291456]{0:T(1024)(128)(4,1)} %bitcast.119), calls=%async_computation.1 | async-start | bytes 4194304
  47.3 1.3 copy-start.4
  58.5 1.6 %copy-start.2 = (bf16[1024,1024]{1,0:T(8,128)(2,1)S(1)}, bf16[1024,1024]{1,0:T(8,128)(2,1)}, u32[]{:S(2)}) copy-start(bf16[1024,1024]{1,0:T(8,128)(2,1)} %param.10) | copy-start | bytes 6291460
  62.0 1.8 %copy-start.9 = (f32[3,128,512]{2,1,0:T(8,128)S(1)}, f32[3,128,512]{2,1,0:T(8,128)}, u32[]{:S(2)}) copy-start(f32[3,128,512]{2,1,0:T(8,128)} %fusion.96) | copy-start | bytes 2359300
  65.5 2.0 %copy-start.8 = (f32[3,128,512]{2,1,0:T(8,128)S(1)}, f32[3,128,512]{2,1,0:T(8,128)}, u32[]{:S(2)}) copy-start(f32[3,128,512]{2,1,0:T(8,128)} %fusion.94) | copy-start | bytes 2359300
  65.5 15.8 %collective-permute-start.16 = (bf16[4,16,9216]{2,1,0:T(8,128)(2,1)S(1)}, bf16[4,16,9216]{2,1,0:T(8,128)(2,1)S(1)}, u32[]{:S(2)}, u32[]{:S(2)}) collective-permute-start(bf16[4,16,9216]{2,1,0:T(8,128)(2,1)S(1)} %pad_maximum_fusion.3), channel_id=1, source_target_pairs={{0,4},{4,0},{8,12},{12,8},{16,20},{20,16},{24,28},{28,24},{1,5},{5... | collective-permute-start | bytes 3538952 | tf_op jit(solution)/shard_map/ppermute | solution.py:136
  67.5 1.9 %copy-start.7 = (f32[3,128,512]{2,1,0:T(8,128)S(1)}, f32[3,128,512]{2,1,0:T(8,128)}, u32[]{:S(2)}) copy-start(f32[3,128,512]{2,1,0:T(8,128)} %fusion.92) | copy-start | bytes 2359300
  72.7 1.1 copy-start.6
  75.9 43.6 %collective-permute-start.12 = (bf16[2,512,1024]{2,1,0:T(8,128)(2,1)S(1)}, bf16[2,512,1024]{2,1,0:T(8,128)(2,1)S(1)}, u32[]{:S(2)}, u32[]{:S(2)}) collective-permute-start(bf16[2,512,1024]{2,1,0:T(8,128)(2,1)S(1)} %pad_maximum_fusion), channel_id=1, source_target_pairs={{0,4},{4,0},{8,12},{12,8},{16,20},{20,16},{24,28},{28,24},{1,5},{5... | collective-permute-start | bytes 6291464 | tf_op jit(solution)/shard_map/ppermute | solution.py:60
  79.3 38.1 %collective-permute-start.11 = (bf16[512,1024]{1,0:T(8,128)(2,1)S(1)}, bf16[512,1024]{1,0:T(8,128)(2,1)S(1)}, u32[]{:S(2)}, u32[]{:S(2)}) collective-permute-start(bf16[512,1024]{1,0:T(8,128)(2,1)S(1)} %collective-permute-done.8), channel_id=1, source_target_pairs={{0,4},{4,0},{8,12},{12,8},{16,20},{20,16},{24,28},{28,24},{1,5},{5... | collective-permute-start | bytes 3145736 | tf_op jit(solution)/shard_map/ppermute | solution.py:55
  81.8 9.9 %collective-permute-start.17 = (bf16[16,9216]{1,0:T(8,128)(2,1)S(1)}, bf16[16,9216]{1,0:T(8,128)(2,1)S(1)}, u32[]{:S(2)}, u32[]{:S(2)}) collective-permute-start(bf16[16,9216]{1,0:T(8,128)(2,1)S(1)} %get-tuple-element.10), channel_id=1, source_target_pairs={{0,8},{4,12},{8,0},{12,4},{16,24},{20,28},{24,16},{28,20},{1,9},{5... | collective-permute-start | bytes 884744 | tf_op jit(solution)/shard_map/ppermute | solution.py:144
  83.3 15.4 %collective-permute-start.18 = (bf16[16,9216]{1,0:T(8,128)(2,1)S(1)}, bf16[16,9216]{1,0:T(8,128)(2,1)S(1)}, u32[]{:S(2)}, u32[]{:S(2)}) collective-permute-start(bf16[16,9216]{1,0:T(8,128)(2,1)S(1)} %get-tuple-element.11), channel_id=1, source_target_pairs={{0,16},{4,20},{8,24},{12,28},{16,0},{20,4},{24,8},{28,12},{1,17},{... | collective-permute-start | bytes 884744 | tf_op jit(solution)/shard_map/ppermute | solution.py:144
  83.8 14.9 %collective-permute-start.19 = (bf16[16,9216]{1,0:T(8,128)(2,1)S(1)}, bf16[16,9216]{1,0:T(8,128)(2,1)S(1)}, u32[]{:S(2)}, u32[]{:S(2)}) collective-permute-start(bf16[16,9216]{1,0:T(8,128)(2,1)S(1)} %get-tuple-element.12), channel_id=1, source_target_pairs={{0,24},{4,28},{8,16},{12,20},{16,8},{20,12},{24,0},{28,4},{1,25},{... | collective-permute-start | bytes 884744 | tf_op jit(solution)/shard_map/ppermute | solution.py:144
  91.6 18.3 %collective-permute-start.13 = (bf16[512,1024]{1,0:T(8,128)(2,1)S(1)}, bf16[512,1024]{1,0:T(8,128)(2,1)S(1)}, u32[]{:S(2)}, u32[]{:S(2)}) collective-permute-start(bf16[512,1024]{1,0:T(8,128)(2,1)S(1)} %collective-permute-done.8), channel_id=1, source_target_pairs={{0,16},{1,9},{2,18},{3,11},{4,12},{5,21},{6,14},{7,23},{8,24},{9,1... | collective-permute-start | bytes 3145736 | tf_op jit(solution)/shard_map/ppermute | solution.py:56
  98.7 18.4 %collective-permute-start.14 = (bf16[512,1024]{1,0:T(8,128)(2,1)S(1)}, bf16[512,1024]{1,0:T(8,128)(2,1)S(1)}, u32[]{:S(2)}, u32[]{:S(2)}) collective-permute-start(bf16[512,1024]{1,0:T(8,128)(2,1)S(1)} %collective-permute-done.8), channel_id=1, source_target_pairs={{0,1},{1,0},{2,3},{3,2},{4,5},{5,4},{6,7},{7,6},{8,9},{9,8},{10,11... | collective-permute-start | bytes 3145736 | tf_op jit(solution)/shard_map/ppermute | solution.py:57
  117.3 7.5 %collective-permute-start.15 = (bf16[2,512,1024]{2,1,0:T(8,128)(2,1)S(1)}, bf16[2,512,1024]{2,1,0:T(8,128)(2,1)S(1)}, u32[]{:S(2)}, u32[]{:S(2)}) collective-permute-start(bf16[2,512,1024]{2,1,0:T(8,128)(2,1)S(1)} %pad_maximum_fusion.1), channel_id=1, source_target_pairs={{0,4},{4,0},{8,12},{12,8},{16,20},{20,16},{24,28},{28,24},{1,5},{5... | collective-permute-start | bytes 6291464 | tf_op jit(solution)/shard_map/ppermute | solution.py:60
  127.5 4.0 %copy-start.1 = (s32[32]{0:T(128)S(1)}, s32[32]{0:T(128)}, u32[]{:S(2)}) copy-start(s32[32]{0:T(128)} %param.15) | copy-start | bytes 388
  128.8 2.7 %copy-start.3 = (bf16[384,8192]{1,0:T(8,128)(2,1)}, bf16[384,8192]{1,0:T(8,128)(2,1)S(1)}, u32[]{:S(2)}) copy-start(bf16[384,8192]{1,0:T(8,128)(2,1)S(1)} %fusion.31) | copy-start | bytes 18874372

commit v5 on v4

--- a/solution.py
+++ b/solution.py
@@ -43,7 +43,10 @@
     rows = shard.shape[0] // WEIGHT_CHUNKS
     result = []
     previous = None
-    for k in range(WEIGHT_CHUNKS):
+    offloaded = lax.all_gather(shard[rows:], "fsdp", axis=0, tiled=False)
+    for member in range(members):
+        result.append((4.0, member, 1, offloaded[member]))
+    for k in range(WEIGHT_CHUNKS - 1):
         piece = shard[k * rows:(k + 1) * rows]
         result.append((0.0, sources[0], k, piece))
         result.append((1.0, sibling_sources[0], k, lax.ppermute(piece, "fsdp", xor_pairs(members, 1))))

time: 132 us -> 158 us (1.20)
  matrix products: 41.7 us -> 68.4 us
  waiting for transfers between devices: 35.7 us -> 20.8 us
  between operations: 19 us -> 31.5 us
  local copies, waits for them, and re-layouts: 11 us -> 14.2 us
  starting transfers between devices: 16.5 us -> 14.9 us
    dot_general x16, matrix products: 13.5 us -> 27.7 us  [on_device(): jnp.dot(token_piece, weight_piece, preferred_element_type=jnp.float32)]
    ppermute x2 -> x1, waiting for transfers between devices: 0.01 us -> 9.85 us  [relay_gather(): first = lax.ppermute(piece, ('fsdp', 'dp'), first_pairs)]
    ppermute x2 -> x1, waiting for transfers between devices: 9.62 us -> 0.01 us  [relay_gather(): relayed = lax.ppermute(first, ('fsdp', 'dp'), relay_pairs)]
    ppermute x3, waiting for transfers between devices: 7.39 us -> 0.01 us  [on_device(): by_step[step] = lax.ppermute(own_adapter, 'fsdp', xor_pairs(members, step))]
    ppermute x2 -> x1, waiting for transfers between devices: 7.16 us -> 0.01 us  [relay_gather(): partner = lax.ppermute(first, ('fsdp', 'dp'), partner_pairs)]
    dot_general x16, matrix products: 9.36 us -> 15.7 us  [on_device(): jnp.einsum('uio,uof->uif', low_rank_gradient, down_piece, preferred_eleme...]
    dot_general x16, matrix products: 15.2 us -> 21.3 us  [on_device(): lax.dot_general(masked_cot, weight_piece, (((1,), (1,)), ((), ())), prefe...]
    unnamed x38 -> x78, local copies, waits for them, and re-layouts: 4.55 us -> 7.78 us
  transfers between devices with their start and end apart: 20 -> 15, of which waited for: 5 -> 4; matrix products, arithmetic and copies ran while one was open for 39% -> 30% of each run, Pallas kernels for 0% -> 0%
where the time goes in v5:
time: 158 us; the launch traced here: 157 us
  matrix products  68.4 us (43%)
  between operations  31.5 us (20%)
  waiting for transfers between devices  20.8 us (13%)
  starting transfers between devices  14.9 us (9%)
  local copies, waits for them, and re-layouts  14.2 us (9%)
  other arithmetic  7.63 us (5%)
    dot_general x16, matrix products, on_device(): jnp.dot(token_piece, weight_piece, preferred_element_type=jnp.float32)  27.7 us
    dot_general x16, matrix products, on_device(): lax.dot_general(masked_cot, weight_piece, (((1,), (1,)), ((), ())), prefe...  21.3 us
    dot_general x16, matrix products, on_device(): jnp.einsum('uio,uof->uif', low_rank_gradient, down_piece, preferred_eleme...  15.7 us
    ppermute x3, waiting for transfers between devices, on_device(): lax.ppermute(sent, 'fsdp', xor_pairs(members, step)).astype(jnp.float32)  10.9 us
    ppermute x1, waiting for transfers between devices, relay_gather(): first = lax.ppermute(piece, ('fsdp', 'dp'), first_pairs)  9.85 us
    unnamed x78, local copies, waits for them, and re-layouts  7.78 us
    ppermute x3, starting transfers between devices, on_device(): by_step[step] = lax.ppermute(own_adapter, 'fsdp', xor_pairs(members, step))  4.47 us
    ppermute x3, starting transfers between devices, on_device(): lax.ppermute(sent, 'fsdp', xor_pairs(members, step)).astype(jnp.float32)  3.61 us
  transfers between devices with their start and end apart: 15, of which 4 were waited for; matrix products, arithmetic and copies ran while one was open for 30% of the time, Pallas kernels for 0%

profile of v5, /device:TPU:0, one launch (start us, length us, event | category | flops | bytes accessed | tf_op | source)
XLA Modules:
  0.0 157.4 jit_solution(589913567929085013)
XLA Ops:
  7.2 1.7 %fusion.173 = (bf16[1,16,9216]{2,1,0:T(8,128)(2,1)S(1)}, bf16[16,9216]{1,0:T(8,128)(2,1)}) fusion(bf16[16,1024]{1,0:T(8,128)(2,1)} %bitcast.126, bf16[16,8192]{1,0:T(8,128)(2,1)} %bitcast.108), kind=kLoop, calls=%fused_computation.252 | loop fusion | flops 589824 | bytes 884736 | tf_op jit(solution)/shard_map/stack | solution.py:99
  9.0 2.9 %collective-permute-start = (bf16[16,9216]{1,0:T(8,128)(2,1)}, bf16[16,9216]{1,0:T(8,128)(2,1)S(1)}, u32[]{:S(2)}, u32[]{:S(2)}) collective-permute-start(bf16[16,9216]{1,0:T(8,128)(2,1)} %get-tuple-element.20), channel_id=1, source_target_pairs={{0,8},{4,12},{8,0},{12,4},{16,24},{20,28},{24,16},{28,20},{1,9},{5... | collective-permute-start | bytes 884744 | tf_op jit(solution)/shard_map/ppermute | solution.py:94
  11.9 1.5 collective-permute-start.1
  13.4 3.0 %fusion.178 = (bf16[512,1024]{1,0:T(8,128)(2,1)}, bf16[512,1024]{1,0:T(8,128)(2,1)}) fusion(bf16[1024,1024]{1,0:T(8,128)(2,1)} %param.10), kind=kLoop, calls=%fused_computation.255 | loop fusion | bytes 4194304 | tf_op jit(solution)/shard_map/slice | solution.py:46
  16.5 2.0 %collective-permute-start.5 = (bf16[512,1024]{1,0:T(8,128)(2,1)}, bf16[512,1024]{1,0:T(8,128)(2,1)}, u32[]{:S(2)}, u32[]{:S(2)}) collective-permute-start(bf16[512,1024]{1,0:T(8,128)(2,1)} %get-tuple-element.15), channel_id=1, source_target_pairs={{0,8},{1,17},{2,10},{3,19},{4,20},{5,13},{6,22},{7,15},{8,0},{9,25... | collective-permute-start | bytes 3145736 | tf_op jit(solution)/shard_map/ppermute | solution.py:55
  38.2 9.8 %collective-permute-done.5 = bf16[512,1024]{1,0:T(8,128)(2,1)} collective-permute-done((bf16[512,1024]{1,0:T(8,128)(2,1)}, bf16[512,1024]{1,0:T(8,128)(2,1)}, u32[]{:S(2)}, u32[]{:S(2)}) %collective-permute-start.5) | collective-permute-done | bytes 1048608 | tf_op jit(solution)/shard_map/ppermute | solution.py:55
  48.1 1.2 collective-permute-start.6
  49.3 1.5 collective-permute-start.7
  52.0 2.4 %fusion.72 = f32[384,1024]{1,0:T(8,128)S(1)} fusion(bf16[512,1024]{1,0:T(8,128)(2,1)} %collective-permute-done.5, bf16[384,8192]{1,0:T(8,128)(2,1)} %param.8, s32[]{:T(128)S(6)} %select_n.254), kind=kOutput, calls=%fused_computation.129 | convolution fusion | flops 402653184 | bytes 3014660 | tf_op jit(solution)/shard_map/dot_general | solution.py:167
  57.8 1.7 %fusion.32 = bf16[3,16,128]{2,1,0:T(8,128)(2,1)S(1)} fusion(bf16[3,128,8192]{2,1,0:T(8,128)(2,1)S(1)} %bitcast.100, f32[3,128]{1,0:T(4,128)S(1)} %get-tuple-element.22, bf16[3,16,9216]{2,1,0:T(8,128)(2,1)S(1)} %pad_maximum_fusion.3), kind=kOutput, calls=%fused_computation.73 | convolution fusion | flops 100675584 | bytes 7092224 | tf_op jit(solution)/shard_map/cvj,coj->cvo/dot_general | solution.py:114
  62.3 1.2 fusion.117
  65.9 1.2 fusion.99
  67.1 1.3 fusion.93
  69.6 1.2 fusion.81
  73.6 1.2 fusion.135
  77.4 1.8 %convolution_add_fusion.9 = f32[384,1024]{1,0:T(8,128)S(1)} fusion(f32[384,1024]{1,0:T(8,128)S(1)} %bitcast_add_fusion, bf16[512,1024]{1,0:T(8,128)(2,1)} %collective-permute-done.4, bf16[384,8192]{1,0:T(8,128)(2,1)S(1)} %bitcast.98, s32[]{:T(128)S(6)} %select_n.251), kind=kOutput, calls=%fused_computation.18 | convolution fusion | flops 403046400 | bytes 4587524 | tf_op jit(solution)/shard_map/dot_general | solution.py:167
  82.0 1.9 %fusion.3 = bf16[384,8192]{1,0:T(8,128)(2,1)S(1)} fusion(bf16[384,8192]{1,0:T(8,128)(2,1)S(1)} %fusion.1, s32[]{:T(128)S(6)} %select_n.251, f32[384,512]{1,0:T(8,128)S(1)} %bitcast.124, bf16[512,1024]{1,0:T(8,128)(2,1)} %collective-permute-done.4, bf16[384,1024]{1,0:T(8,128)(2,1)S(1)} %copy-done.11, f32[384]{0:T(512)S(1)} %get-tuple-element.21), kind=kOutput, calls=%fused_computation.39 | convolution fusion | flops 404226048 | bytes 3016708 | tf_op jit(solution)/shard_map/dot_general | solution.py:171
  83.9 1.9 %fusion.5 = bf16[384,8192]{1,0:T(8,128)(2,1)S(1)} fusion(bf16[384,8192]{1,0:T(8,128)(2,1)S(1)} %fusion.3, s32[]{:T(128)S(6)} %select_n.254, f32[384,512]{1,0:T(8,128)S(1)} %bitcast.123, bf16[512,1024]{1,0:T(8,128)(2,1)} %collective-permute-done.5, bf16[384,1024]{1,0:T(8,128)(2,1)S(1)} %copy-done.11, f32[384]{0:T(512)S(1)} %get-tuple-element.21), kind=kOutput, calls=%fused_computation.41 | convolution fusion | flops 404226048 | bytes 3016708 | tf_op jit(solution)/shard_map/dot_general | solution.py:171
  86.7 1.7 %convolution_add_fusion.8 = f32[384,1024]{1,0:T(8,128)} fusion(f32[384,1024]{1,0:T(8,128)S(1)} %add.261, bf16[512,1024]{1,0:T(8,128)(2,1)S(1)} %collective-permute-done.6, bf16[384,8192]{1,0:T(8,128)(2,1)S(1)} %bitcast.98, s32[]{:T(128)S(6)} %select_n.255), kind=kOutput, calls=%fused_computation.17 | convolution fusion | flops 403046400 | bytes 4587524 | tf_op jit(solution)/shard_map/dot_general | solution.py:167
  89.8 1.6 %collective-permute-start.12 = (bf16[16,9216]{1,0:T(8,128)(2,1)S(1)}, bf16[16,9216]{1,0:T(8,128)(2,1)S(1)}, u32[]{:S(2)}, u32[]{:S(2)}) collective-permute-start(bf16[16,9216]{1,0:T(8,128)(2,1)S(1)} %get-tuple-element.9), channel_id=1, source_target_pairs={{0,16},{4,20},{8,24},{12,28},{16,0},{20,4},{24,8},{28,12},{1,17},{... | collective-permute-start | bytes 884744 | tf_op jit(solution)/shard_map/ppermute | solution.py:147
  93.2 2.2 %fusion.60 = f32[384,1024]{1,0:T(8,128)} fusion(bf16[512,1024]{1,0:T(8,128)(2,1)S(1)} %collective-permute-done.8, bf16[384,8192]{1,0:T(8,128)(2,1)S(1)} %bitcast.98, s32[]{:T(128)S(6)} %select_n.257), kind=kOutput, calls=%fused_computation.117 | convolution fusion | flops 402653184 | bytes 3014660 | tf_op jit(solution)/shard_map/dot_general | solution.py:167
  95.4 3.5 %collective-permute-done.11 = bf16[16,9216]{1,0:T(8,128)(2,1)S(1)} collective-permute-done((bf16[16,9216]{1,0:T(8,128)(2,1)S(1)}, bf16[16,9216]{1,0:T(8,128)(2,1)S(1)}, u32[]{:S(2)}, u32[]{:S(2)}) %collective-permute-start.11) | collective-permute-done | bytes 294944 | tf_op jit(solution)/shard_map/ppermute | solution.py:147
  98.8 5.6 %collective-permute-done.12 = bf16[16,9216]{1,0:T(8,128)(2,1)S(1)} collective-permute-done((bf16[16,9216]{1,0:T(8,128)(2,1)S(1)}, bf16[16,9216]{1,0:T(8,128)(2,1)S(1)}, u32[]{:S(2)}, u32[]{:S(2)}) %collective-permute-start.12) | collective-permute-done | bytes 294944 | tf_op jit(solution)/shard_map/ppermute | solution.py:147
  104.5 1.8 %collective-permute-done.13 = bf16[16,9216]{1,0:T(8,128)(2,1)S(1)} collective-permute-done((bf16[16,9216]{1,0:T(8,128)(2,1)S(1)}, bf16[16,9216]{1,0:T(8,128)(2,1)S(1)}, u32[]{:S(2)}, u32[]{:S(2)}) %collective-permute-start.13) | collective-permute-done | bytes 294944 | tf_op jit(solution)/shard_map/ppermute | solution.py:147
  107.9 1.8 %fusion.34 = f32[384,1024]{1,0:T(8,128)} fusion(bf16[2,512,1024]{2,1,0:T(8,128)(2,1)S(1)} %collective-permute-done.9, bf16[384,8192]{1,0:T(8,128)(2,1)S(1)} %bitcast.98, s32[]{:T(128)S(6)} %select_n.258), kind=kOutput, calls=%fused_computation.77 | convolution fusion | flops 402653184 | bytes 3014660 | tf_op jit(solution)/shard_map/dot_general | solution.py:167
  109.7 1.8 %fusion.35 = f32[384,1024]{1,0:T(8,128)} fusion(bf16[2,512,1024]{2,1,0:T(8,128)(2,1)S(1)} %collective-permute-done.9, bf16[384,8192]{1,0:T(8,128)(2,1)S(1)} %bitcast.98, s32[]{:T(128)S(6)} %select_n.259), kind=kOutput, calls=%fused_computation.78 | convolution fusion | flops 402653184 | bytes 3014660 | tf_op jit(solution)/shard_map/dot_general | solution.py:167
  111.5 2.0 %fusion.50 = f32[384,1024]{1,0:T(8,128)S(1)} fusion(bf16[4096,1024]{1,0:T(8,128)(2,1)} %all-gather.3.cloned.1.call-done, bf16[384,8192]{1,0:T(8,128)(2,1)} %param.8), kind=kOutput, calls=%fused_computation.93 | convolution fusion | flops 402653184 | bytes 3014656 | tf_op jit(solution)/shard_map/dot_general | solution.py:167
  113.8 2.1 %convolution_add_fusion.7 = f32[384,1024]{1,0:T(8,128)S(1)} fusion(f32[384,1024]{1,0:T(8,128)S(1)} %add.265, bf16[4096,1024]{1,0:T(8,128)(2,1)} %all-gather.3.cloned.1.call-done, bf16[384,8192]{1,0:T(8,128)(2,1)} %param.8), kind=kOutput, calls=%fused_computation.16 | convolution fusion | flops 403046400 | bytes 4587520 | tf_op jit(solution)/shard_map/dot_general | solution.py:167
  115.9 1.4 copy-done.2
  117.4 1.6 %convolution_add_fusion.6 = f32[384,1024]{1,0:T(8,128)S(1)} fusion(f32[384,1024]{1,0:T(8,128)S(1)} %convolution_add_fusion.7, bf16[4096,1024]{1,0:T(8,128)(2,1)S(1)} %copy-done.2, bf16[384,8192]{1,0:T(8,128)(2,1)} %param.8), kind=kOutput, calls=%fused_computation.15 | convolution fusion | flops 403046400 | bytes 4587520 | tf_op jit(solution)/shard_map/dot_general | solution.py:167
  119.0 1.6 %convolution_add_fusion.5 = f32[384,1024]{1,0:T(8,128)S(1)} fusion(f32[384,1024]{1,0:T(8,128)S(1)} %convolution_add_fusion.6, bf16[4096,1024]{1,0:T(8,128)(2,1)S(1)} %copy-done.2, bf16[384,8192]{1,0:T(8,128)(2,1)} %param.8), kind=kOutput, calls=%fused_computation.14 | convolution fusion | flops 403046400 | bytes 4587520 | tf_op jit(solution)/shard_map/dot_general | solution.py:167
  120.6 1.6 %convolution_add_fusion.4 = f32[384,1024]{1,0:T(8,128)S(1)} fusion(f32[384,1024]{1,0:T(8,128)S(1)} %convolution_add_fusion.5, bf16[4096,1024]{1,0:T(8,128)(2,1)S(1)} %copy-done.2, bf16[384,8192]{1,0:T(8,128)(2,1)} %param.8), kind=kOutput, calls=%fused_computation.13 | convolution fusion | flops 403046400 | bytes 4587520 | tf_op jit(solution)/shard_map/dot_general | solution.py:167
  122.2 1.6 %convolution_add_fusion.3 = f32[384,1024]{1,0:T(8,128)S(1)} fusion(f32[384,1024]{1,0:T(8,128)S(1)} %convolution_add_fusion.4, bf16[4096,1024]{1,0:T(8,128)(2,1)S(1)} %copy-done.2, bf16[384,8192]{1,0:T(8,128)(2,1)} %param.8), kind=kOutput, calls=%fused_computation.12 | convolution fusion | flops 403046400 | bytes 4587520 | tf_op jit(solution)/shard_map/dot_general | solution.py:167
  123.8 1.6 %convolution_add_fusion.2 = f32[384,1024]{1,0:T(8,128)S(1)} fusion(f32[384,1024]{1,0:T(8,128)S(1)} %convolution_add_fusion.3, bf16[4096,1024]{1,0:T(8,128)(2,1)S(1)} %copy-done.2, bf16[384,8192]{1,0:T(8,128)(2,1)} %param.8), kind=kOutput, calls=%fused_computation.11 | convolution fusion | flops 403046400 | bytes 4587520 | tf_op jit(solution)/shard_map/dot_general | solution.py:167
  125.4 1.7 %convolution_add_fusion.1 = f32[384,1024]{1,0:T(8,128)S(1)} fusion(f32[384,1024]{1,0:T(8,128)S(1)} %convolution_add_fusion.2, bf16[4096,1024]{1,0:T(8,128)(2,1)S(1)} %copy-done.2, bf16[384,8192]{1,0:T(8,128)(2,1)} %param.8), kind=kOutput, calls=%fused_computation.10 | convolution fusion | flops 403046400 | bytes 4587520 | tf_op jit(solution)/shard_map/dot_general | solution.py:167
  127.1 1.7 %convolution_add_fusion = f32[384,1024]{1,0:T(8,128)S(1)} fusion(f32[384,1024]{1,0:T(8,128)S(1)} %convolution_add_fusion.1, bf16[512,1024]{1,0:T(8,128)(2,1)S(1)} %copy-done.10, bf16[384,8192]{1,0:T(8,128)(2,1)} %param.8, s32[]{:T(128)S(6)} %select_n.256), kind=kOutput, calls=%fused_computation.9 | convolution fusion | flops 403046400 | bytes 4587524 | tf_op jit(solution)/shard_map/dot_general | solution.py:167
  133.7 1.4 fusion.9
  135.0 1.4 fusion.11
  136.4 1.4 fusion.13
  137.8 1.4 fusion.15
  139.1 1.4 fusion.17
  140.5 1.4 fusion.19
  141.9 1.4 fusion.21
  143.2 1.4 fusion.23
  144.6 1.4 fusion.25
  146.0 1.4 fusion.27
  147.9 1.4 fusion.29
  149.2 1.4 fusion.31
  (145 shorter events, 33.2 us)
Async XLA Ops:
  7.2 11.3 %copy-start = (s32[32]{0:T(128)S(1)}, s32[32]{0:T(128)}, u32[]{:S(2)}) copy-start(s32[32]{0:T(128)} %param.15) | copy-start | bytes 388
  7.2 104.3 %all-gather.3.cloned.1.call-start = ((), (), s32[]{:S(2)}) async-start(), calls=%async_computation | async-start | bytes 9437184 | tf_op jit(solution)/shard_map/all_gather | solution.py:46
  9.0 9.5 %copy-start.33 = (s32[3]{0:T(128)S(1)}, s32[3]{0:T(128)}, u32[]{:S(2)}) copy-start(s32[3]{0:T(128)} %param.13) | copy-start | bytes 40
  9.0 10.2 %copy-start.32 = (s32[3]{0:T(128)S(1)}, s32[3]{0:T(128)}, u32[]{:S(2)}) copy-start(s32[3]{0:T(128)} %param.14) | copy-start | bytes 40
  9.0 27.8 %collective-permute-start = (bf16[16,9216]{1,0:T(8,128)(2,1)}, bf16[16,9216]{1,0:T(8,128)(2,1)S(1)}, u32[]{:S(2)}, u32[]{:S(2)}) collective-permute-start(bf16[16,9216]{1,0:T(8,128)(2,1)} %get-tuple-element.20), channel_id=1, source_target_pairs={{0,8},{4,12},{8,0},{12,4},{16,24},{20,28},{24,16},{28,20},{1,9},{5... | collective-permute-start | bytes 884744 | tf_op jit(solution)/shard_map/ppermute | solution.py:94
  11.9 24.8 %collective-permute-start.1 = (bf16[16,9216]{1,0:T(8,128)(2,1)}, bf16[16,9216]{1,0:T(8,128)(2,1)S(1)}, u32[]{:S(2)}, u32[]{:S(2)}) collective-permute-start(bf16[16,9216]{1,0:T(8,128)(2,1)} %get-tuple-element.20), channel_id=1, source_target_pairs={{0,16},{4,20},{8,24},{12,28},{16,0},{20,4},{24,8},{28,12},{1,17},{... | collective-permute-start | bytes 884744 | tf_op jit(solution)/shard_map/ppermute | solution.py:94
  13.4 23.3 %collective-permute-start.2 = (bf16[16,9216]{1,0:T(8,128)(2,1)}, bf16[16,9216]{1,0:T(8,128)(2,1)S(1)}, u32[]{:S(2)}, u32[]{:S(2)}) collective-permute-start(bf16[16,9216]{1,0:T(8,128)(2,1)} %get-tuple-element.20), channel_id=1, source_target_pairs={{0,24},{4,28},{8,16},{12,20},{16,8},{20,12},{24,0},{28,4},{1,25},{... | collective-permute-start | bytes 884744 | tf_op jit(solution)/shard_map/ppermute | solution.py:94
  16.5 61.0 %collective-permute-start.4 = (bf16[512,1024]{1,0:T(8,128)(2,1)}, bf16[512,1024]{1,0:T(8,128)(2,1)}, u32[]{:S(2)}, u32[]{:S(2)}) collective-permute-start(bf16[512,1024]{1,0:T(8,128)(2,1)} %get-tuple-element.15), channel_id=1, source_target_pairs={{0,4},{4,0},{8,12},{12,8},{16,20},{20,16},{24,28},{28,24},{1,5},{5... | collective-permute-start | bytes 3145736 | tf_op jit(solution)/shard_map/ppermute | solution.py:52
  16.5 31.6 %collective-permute-start.5 = (bf16[512,1024]{1,0:T(8,128)(2,1)}, bf16[512,1024]{1,0:T(8,128)(2,1)}, u32[]{:S(2)}, u32[]{:S(2)}) collective-permute-start(bf16[512,1024]{1,0:T(8,128)(2,1)} %get-tuple-element.15), channel_id=1, source_target_pairs={{0,8},{1,17},{2,10},{3,19},{4,20},{5,13},{6,22},{7,15},{8,0},{9,25... | collective-permute-start | bytes 3145736 | tf_op jit(solution)/shard_map/ppermute | solution.py:55
  18.4 18.8 %copy-start.31 = (bf16[1,16,1024]{2,1,0:T(8,128)(2,1)S(1)}, bf16[1,16,1024]{2,1,0:T(8,128)(2,1)}, u32[]{:S(2)}) copy-start(bf16[1,16,1024]{2,1,0:T(8,128)(2,1)} %param.12) | copy-start | bytes 98308
  18.5 37.7 %slice-start = ((s8[6291456]{0:T(1024)(128)(4,1)}), s8[2097152]{0:T(1024)(128)(4,1)S(1)}, s32[]{:S(2)}) async-start(s8[6291456]{0:T(1024)(128)(4,1)} %bitcast.97), calls=%async_computation.1 | async-start | bytes 4194304
  36.7 12.6 %copy-start.17 = (bf16[16,9216]{1,0:T(8,128)(2,1)}, bf16[16,9216]{1,0:T(8,128)(2,1)S(1)}, u32[]{:S(2)}) copy-start(bf16[16,9216]{1,0:T(8,128)(2,1)S(1)} %collective-permute-done) | copy-start | bytes 884740
  36.7 12.6 %copy-start.15 = (bf16[16,9216]{1,0:T(8,128)(2,1)}, bf16[16,9216]{1,0:T(8,128)(2,1)S(1)}, u32[]{:S(2)}) copy-start(bf16[16,9216]{1,0:T(8,128)(2,1)S(1)} %collective-permute-done.1) | copy-start | bytes 884740
  36.9 17.4 %collective-permute-start.3 = (bf16[4,16,9216]{2,1,0:T(8,128)(2,1)S(1)}, bf16[4,16,9216]{2,1,0:T(8,128)(2,1)S(1)}, u32[]{:S(2)}, u32[]{:S(2)}) collective-permute-start(bf16[4,16,9216]{2,1,0:T(8,128)(2,1)S(1)} %pad_maximum_fusion.1), channel_id=1, source_target_pairs={{0,4},{4,0},{8,12},{12,8},{16,20},{20,16},{24,28},{28,24},{1,5},{5... | collective-permute-start | bytes 3538952 | tf_op jit(solution)/shard_map/ppermute | solution.py:96
  48.1 38.7 %collective-permute-start.6 = (bf16[512,1024]{1,0:T(8,128)(2,1)}, bf16[512,1024]{1,0:T(8,128)(2,1)S(1)}, u32[]{:S(2)}, u32[]{:S(2)}) collective-permute-start(bf16[512,1024]{1,0:T(8,128)(2,1)} %collective-permute-done.5), channel_id=1, source_target_pairs={{0,4},{4,0},{8,12},{12,8},{16,20},{20,16},{24,28},{28,24},{1,5},{5... | collective-permute-start | bytes 3145736 | tf_op jit(solution)/shard_map/ppermute | solution.py:58
  49.3 36.4 %collective-permute-start.7 = (bf16[512,1024]{1,0:T(8,128)(2,1)}, bf16[512,1024]{1,0:T(8,128)(2,1)S(1)}, u32[]{:S(2)}, u32[]{:S(2)}) collective-permute-start(bf16[512,1024]{1,0:T(8,128)(2,1)} %collective-permute-done.5), channel_id=1, source_target_pairs={{0,16},{1,9},{2,18},{3,11},{4,12},{5,21},{6,14},{7,23},{8,24},{9,1... | collective-permute-start | bytes 3145736 | tf_op jit(solution)/shard_map/ppermute | solution.py:59
  50.8 3.6 %copy-start.18 = (bf16[16,9216]{1,0:T(8,128)(2,1)S(1)}, bf16[16,9216]{1,0:T(8,128)(2,1)}, u32[]{:S(2)}) copy-start(bf16[16,9216]{1,0:T(8,128)(2,1)} %copy-done.17) | copy-start | bytes 884740
  50.8 3.6 %copy-start.16 = (bf16[16,9216]{1,0:T(8,128)(2,1)S(1)}, bf16[16,9216]{1,0:T(8,128)(2,1)}, u32[]{:S(2)}) copy-start(bf16[16,9216]{1,0:T(8,128)(2,1)} %copy-done.15) | copy-start | bytes 884740
  50.8 34.9 %collective-permute-start.8 = (bf16[512,1024]{1,0:T(8,128)(2,1)}, bf16[512,1024]{1,0:T(8,128)(2,1)S(1)}, u32[]{:S(2)}, u32[]{:S(2)}) collective-permute-start(bf16[512,1024]{1,0:T(8,128)(2,1)} %collective-permute-done.5), channel_id=1, source_target_pairs={{0,1},{1,0},{2,3},{3,2},{4,5},{5,4},{6,7},{7,6},{8,9},{9,8},{10,11... | collective-permute-start | bytes 3145736 | tf_op jit(solution)/shard_map/ppermute | solution.py:60
  54.4 2.4 %slice-start.1 = ((s8[6291456]{0:T(1024)(128)(4,1)}), s8[4194304]{0:T(1024)(128)(4,1)S(1)}, s32[]{:S(2)}) async-start(s8[6291456]{0:T(1024)(128)(4,1)} %bitcast.97), calls=%async_computation.2 | async-start | bytes 8388608
  60.5 28.0 %collective-permute-start.10 = (bf16[4,16,9216]{2,1,0:T(8,128)(2,1)S(1)}, bf16[4,16,9216]{2,1,0:T(8,128)(2,1)S(1)}, u32[]{:S(2)}, u32[]{:S(2)}) collective-permute-start(bf16[4,16,9216]{2,1,0:T(8,128)(2,1)S(1)} %pad_maximum_fusion.2), channel_id=1, source_target_pairs={{0,4},{4,0},{8,12},{12,8},{16,20},{20,16},{24,28},{28,24},{1,5},{5... | collective-permute-start | bytes 3538952 | tf_op jit(solution)/shard_map/ppermute | solution.py:139
  70.8 1.6 %copy-start.8 = (bf16[1024,1024]{1,0:T(8,128)(2,1)S(1)}, bf16[1024,1024]{1,0:T(8,128)(2,1)}, u32[]{:S(2)}) copy-start(bf16[1024,1024]{1,0:T(8,128)(2,1)} %param.10) | copy-start | bytes 6291460
  86.7 21.2 %collective-permute-start.9 = (bf16[2,512,1024]{2,1,0:T(8,128)(2,1)S(1)}, bf16[2,512,1024]{2,1,0:T(8,128)(2,1)S(1)}, u32[]{:S(2)}, u32[]{:S(2)}) collective-permute-start(bf16[2,512,1024]{2,1,0:T(8,128)(2,1)S(1)} %pad_maximum_fusion), channel_id=1, source_target_pairs={{0,4},{4,0},{8,12},{12,8},{16,20},{20,16},{24,28},{28,24},{1,5},{5... | collective-permute-start | bytes 6291464 | tf_op jit(solution)/shard_map/ppermute | solution.py:63
  88.9 9.9 %collective-permute-start.11 = (bf16[16,9216]{1,0:T(8,128)(2,1)S(1)}, bf16[16,9216]{1,0:T(8,128)(2,1)S(1)}, u32[]{:S(2)}, u32[]{:S(2)}) collective-permute-start(bf16[16,9216]{1,0:T(8,128)(2,1)S(1)} %get-tuple-element.8), channel_id=1, source_target_pairs={{0,8},{4,12},{8,0},{12,4},{16,24},{20,28},{24,16},{28,20},{1,9},{5... | collective-permute-start | bytes 884744 | tf_op jit(solution)/shard_map/ppermute | solution.py:147
  89.8 14.6 %collective-permute-start.12 = (bf16[16,9216]{1,0:T(8,128)(2,1)S(1)}, bf16[16,9216]{1,0:T(8,128)(2,1)S(1)}, u32[]{:S(2)}, u32[]{:S(2)}) collective-permute-start(bf16[16,9216]{1,0:T(8,128)(2,1)S(1)} %get-tuple-element.9), channel_id=1, source_target_pairs={{0,16},{4,20},{8,24},{12,28},{16,0},{20,4},{24,8},{28,12},{1,17},{... | collective-permute-start | bytes 884744 | tf_op jit(solution)/shard_map/ppermute | solution.py:147
  91.4 14.8 %collective-permute-start.13 = (bf16[16,9216]{1,0:T(8,128)(2,1)S(1)}, bf16[16,9216]{1,0:T(8,128)(2,1)S(1)}, u32[]{:S(2)}, u32[]{:S(2)}) collective-permute-start(bf16[16,9216]{1,0:T(8,128)(2,1)S(1)} %get-tuple-element.10), channel_id=1, source_target_pairs={{0,24},{4,28},{8,16},{12,20},{16,8},{20,12},{24,0},{28,4},{1,25},{... | collective-permute-start | bytes 884744 | tf_op jit(solution)/shard_map/ppermute | solution.py:147
  93.2 13.4 %copy-start.3 = (bf16[384,8192]{1,0:T(8,128)(2,1)}, bf16[384,8192]{1,0:T(8,128)(2,1)S(1)}, u32[]{:S(2)}) copy-start(bf16[384,8192]{1,0:T(8,128)(2,1)S(1)} %fusion.7) | copy-start | bytes 18874372
  107.9 1.8 %copy-start.13 = (bf16[2,512,1024]{2,1,0:T(8,128)(2,1)}, bf16[2,512,1024]{2,1,0:T(8,128)(2,1)S(1)}, u32[]{:S(2)}) copy-start(bf16[2,512,1024]{2,1,0:T(8,128)(2,1)S(1)} %collective-permute-done.9) | copy-start | bytes 6291460
  111.5 2.0 %copy-start.4 = (f32[384,1024]{1,0:T(8,128)S(1)}, f32[384,1024]{1,0:T(8,128)}, u32[]{:S(2)}) copy-start(f32[384,1024]{1,0:T(8,128)} %convolution_add_fusion.8) | copy-start | bytes 4718596
  113.5 3.8 %copy-start.2 = (bf16[4096,1024]{1,0:T(8,128)(2,1)S(1)}, bf16[4096,1024]{1,0:T(8,128)(2,1)}, u32[]{:S(2)}) copy-start(bf16[4096,1024]{1,0:T(8,128)(2,1)} %all-gather.3.cloned.1.call-done) | copy-start | bytes 25165828
  125.4 1.7 %copy-start.10 = (bf16[512,1024]{1,0:T(8,128)(2,1)S(1)}, bf16[512,1024]{1,0:T(8,128)(2,1)}, u32[]{:S(2)}) copy-start(bf16[512,1024]{1,0:T(8,128)(2,1)} %copy-done.9) | copy-start | bytes 3145732
  127.1 1.7 %copy-start.5 = (f32[384,1024]{1,0:T(8,128)S(1)}, f32[384,1024]{1,0:T(8,128)}, u32[]{:S(2)}) copy-start(f32[384,1024]{1,0:T(8,128)} %fusion.60) | copy-start | bytes 4718596
  128.8 1.4 copy-start.7
  130.2 1.4 copy-start.6
  132.0 1.6 %copy-start.30 = (f32[3,128,512]{2,1,0:T(8,128)S(1)}, f32[3,128,512]{2,1,0:T(8,128)}, u32[]{:S(2)}) copy-start(f32[3,128,512]{2,1,0:T(8,128)} %fusion.123) | copy-start | bytes 2359300
  133.1 2.0 %copy-start.28 = (f32[3,128,512]{2,1,0:T(8,128)S(1)}, f32[3,128,512]{2,1,0:T(8,128)}, u32[]{:S(2)}) copy-start(f32[3,128,512]{2,1,0:T(8,128)} %fusion.117) | copy-start | bytes 2359300
  135.0 1.4 copy-start.27
  136.4 1.4 copy-start.25
  137.8 1.4 copy-start.23
  139.1 1.4 copy-start.22
  140.5 1.4 copy-start.20
  141.9 1.4 copy-start.19
  143.2 1.4 copy-start.24
  144.6 1.4 copy-start.21
  146.0 1.6 %copy-start.14 = (bf16[2,512,1024]{2,1,0:T(8,128)(2,1)S(1)}, bf16[2,512,1024]{2,1,0:T(8,128)(2,1)}, u32[]{:S(2)}) copy-start(bf16[2,512,1024]{2,1,0:T(8,128)(2,1)} %copy-done.13) | copy-start | bytes 6291460
  146.0 1.9 %copy-start.29 = (f32[3,128,512]{2,1,0:T(8,128)S(1)}, f32[3,128,512]{2,1,0:T(8,128)}, u32[]{:S(2)}) copy-start(f32[3,128,512]{2,1,0:T(8,128)} %fusion.131) | copy-start | bytes 2359300
  147.3 1.9 %copy-start.26 = (f32[3,128,512]{2,1,0:T(8,128)S(1)}, f32[3,128,512]{2,1,0:T(8,128)}, u32[]{:S(2)}) copy-start(f32[3,128,512]{2,1,0:T(8,128)} %fusion.129) | copy-start | bytes 2359300
  147.9 2.7 %copy-start.1 = (s32[32]{0:T(128)S(1)}, s32[32]{0:T(128)}, u32[]{:S(2)}) copy-start(s32[32]{0:T(128)} %param.15) | copy-start | bytes 388
  (3 other events, 3.5 us)
Sparse Core Ops, SparseCore 0:
  18.6 72.7 all-gather.2

commit v6 on v4

--- a/solution.py
+++ b/solution.py
@@ -138,17 +138,19 @@
         table_row(me ^ step).astype(jnp.float32) + from_sibling[index].astype(jnp.float32)
         for index, step in enumerate(range(0, members, 2))
     ]
+    weight_pieces = relay_gather(frozen_value_weight, members, groups, me, dp_index)
+    if weight_pieces and len(weight_pieces[0]) == 2:
+        weight_pieces = [(source, 0, value) for source, value in weight_pieces]
+    last_pieces = tuple(value for _, _, value in weight_pieces[-4:])
     grad_sum = pair_sums[0]
     for index, step in enumerate(even_steps):
         sent = pair_sums[index + 1].astype(jnp.bfloat16)
+        sent, _ = lax.optimization_barrier((sent, last_pieces))
         grad_sum = grad_sum + lax.ppermute(sent, "fsdp", xor_pairs(members, step)).astype(jnp.float32)
     grad_sum = grad_sum.astype(jnp.bfloat16)
     grad_down = grad_sum[None, :, :model_width]
     grad_up = grad_sum[None, :, model_width:]
 
-    weight_pieces = relay_gather(frozen_value_weight, members, groups, me, dp_index)
-    if weight_pieces and len(weight_pieces[0]) == 2:
-        weight_pieces = [(source, 0, value) for source, value in weight_pieces]
     adapter_output = jnp.einsum(
         "znr,zrm->znm", low_rank_state, up_block, preferred_element_type=jnp.float32
     ).reshape(tok_rows, value_width)

time: 132 us -> 132 us (level)
  local copies, waits for them, and re-layouts: 11 us -> 8.32 us
  waiting for transfers between devices: 35.7 us -> 37.3 us
    ppermute x2, waiting for transfers between devices: 7.16 us -> 11.6 us  [relay_gather(): partner = lax.ppermute(first, ('fsdp', 'dp'), partner_pairs)]
    ppermute x3, waiting for transfers between devices: 11.5 us -> 8.38 us  [on_device(): lax.ppermute(sent, 'fsdp', xor_pairs(members, step)).astype(jnp.float32)]
    unnamed x38, local copies, waits for them, and re-layouts: 4.55 us -> 1.86 us
  transfers between devices with their start and end apart: 20 -> 20, of which waited for: 5 -> 5; matrix products, arithmetic and copies ran while one was open for 39% -> 41% of each run, Pallas kernels for 0% -> 0%
where the time goes in v6:
time: 132 us; the launch traced here: 131 us
  matrix products  41.6 us (32%)
  waiting for transfers between devices  37.3 us (28%)
  between operations  19.1 us (14%)
  starting transfers between devices  17.1 us (13%)
  local copies, waits for them, and re-layouts  8.32 us (6%)
  other arithmetic  7.81 us (6%)
    dot_general x16, matrix products, on_device(): lax.dot_general(masked_cot, weight_piece, (((1,), (1,)), ((), ())), prefe...  15.3 us
    dot_general x16, matrix products, on_device(): jnp.dot(token_piece, weight_piece, preferred_element_type=jnp.float32)  13.4 us
    ppermute x2, waiting for transfers between devices, relay_gather(): partner = lax.ppermute(first, ('fsdp', 'dp'), partner_pairs)  11.6 us
    ppermute x2, waiting for transfers between devices, relay_gather(): relayed = lax.ppermute(first, ('fsdp', 'dp'), relay_pairs)  9.54 us
    dot_general x16, matrix products, on_device(): jnp.einsum('uio,uof->uif', low_rank_gradient, down_piece, preferred_eleme...  9.36 us
    ppermute x3, waiting for transfers between devices, on_device(): lax.ppermute(sent, 'fsdp', xor_pairs(members, step)).astype(jnp.float32)  8.38 us
    ppermute x3, waiting for transfers between devices, on_device(): by_step[step] = lax.ppermute(own_adapter, 'fsdp', xor_pairs(members, step))  7.79 us
    ppermute x3, starting transfers between devices, on_device(): by_step[step] = lax.ppermute(own_adapter, 'fsdp', xor_pairs(members, step))  4.54 us
  transfers between devices with their start and end apart: 20, of which 5 were waited for; matrix products, arithmetic and copies ran while one was open for 41% of the time, Pallas kernels for 0%

profile of v6, /device:TPU:0, one launch (start us, length us, event | category | flops | bytes accessed | tf_op | source)
XLA Modules:
  0.0 131.2 jit_solution(2833530360860330954)
XLA Ops:
  0.6 1.0 fusion.136
  1.7 3.0 %collective-permute-start = (bf16[16,9216]{1,0:T(8,128)(2,1)S(1)}, bf16[16,9216]{1,0:T(8,128)(2,1)S(1)}, u32[]{:S(2)}, u32[]{:S(2)}) collective-permute-start(bf16[16,9216]{1,0:T(8,128)(2,1)S(1)} %get-tuple-element.30), channel_id=1, source_target_pairs={{0,8},{4,12},{8,0},{12,4},{16,24},{20,28},{24,16},{28,20},{1,9},{5... | collective-permute-start | bytes 884744 | tf_op jit(solution)/shard_map/ppermute | solution.py:91
  4.7 1.5 %collective-permute-start.1 = (bf16[16,9216]{1,0:T(8,128)(2,1)S(1)}, bf16[16,9216]{1,0:T(8,128)(2,1)S(1)}, u32[]{:S(2)}, u32[]{:S(2)}) collective-permute-start(bf16[16,9216]{1,0:T(8,128)(2,1)S(1)} %get-tuple-element.30), channel_id=1, source_target_pairs={{0,16},{4,20},{8,24},{12,28},{16,0},{20,4},{24,8},{28,12},{1,17},{... | collective-permute-start | bytes 884744 | tf_op jit(solution)/shard_map/ppermute | solution.py:91
  6.2 3.0 %fusion.143 = (bf16[512,1024]{1,0:T(8,128)(2,1)}, bf16[512,1024]{1,0:T(8,128)(2,1)}) fusion(bf16[1024,1024]{1,0:T(8,128)(2,1)} %param.10), kind=kLoop, calls=%fused_computation.219 | loop fusion | bytes 4194304 | tf_op jit(solution)/shard_map/slice | solution.py:47
  9.3 1.9 %collective-permute-start.6 = (bf16[512,1024]{1,0:T(8,128)(2,1)}, bf16[512,1024]{1,0:T(8,128)(2,1)}, u32[]{:S(2)}, u32[]{:S(2)}) collective-permute-start(bf16[512,1024]{1,0:T(8,128)(2,1)} %get-tuple-element.25), channel_id=1, source_target_pairs={{0,8},{1,17},{2,10},{3,19},{4,20},{5,13},{6,22},{7,15},{8,0},{9,25... | collective-permute-start | bytes 3145736 | tf_op jit(solution)/shard_map/ppermute | solution.py:52
  11.2 0.7 constant_dynamic-update-slice_fusion.3
  12.0 0.6 gather_fusion
  13.2 7.8 %collective-permute-done.1 = bf16[16,9216]{1,0:T(8,128)(2,1)S(1)} collective-permute-done((bf16[16,9216]{1,0:T(8,128)(2,1)S(1)}, bf16[16,9216]{1,0:T(8,128)(2,1)S(1)}, u32[]{:S(2)}, u32[]{:S(2)}) %collective-permute-start.1) | collective-permute-done | bytes 294944 | tf_op jit(solution)/shard_map/ppermute | solution.py:91
  39.6 1.7 %collective-permute-start.7 = (bf16[512,1024]{1,0:T(8,128)(2,1)}, bf16[512,1024]{1,0:T(8,128)(2,1)S(1)}, u32[]{:S(2)}, u32[]{:S(2)}) collective-permute-start(bf16[512,1024]{1,0:T(8,128)(2,1)} %collective-permute-done.6), channel_id=1, source_target_pairs={{0,4},{4,0},{8,12},{12,8},{16,20},{20,16},{24,28},{28,24},{1,5},{5... | collective-permute-start | bytes 3145736 | tf_op jit(solution)/shard_map/ppermute | solution.py:55
  41.3 1.9 %fusion.58 = f32[384,1024]{1,0:T(8,128)S(1)} fusion(bf16[512,1024]{1,0:T(8,128)(2,1)} %collective-permute-done.6, bf16[384,8192]{1,0:T(8,128)(2,1)} %param.8, s32[]{:T(128)S(6)} %select_n.296), kind=kOutput, calls=%fused_computation.113 | convolution fusion | flops 402653184 | bytes 3014660 | tf_op jit(solution)/shard_map/dot_general | solution.py:166
  43.8 2.1 %fusion.60 = f32[384,1024]{1,0:T(8,128)S(1)} fusion(bf16[512,1024]{1,0:T(8,128)(2,1)} %collective-permute-done.5, bf16[384,8192]{1,0:T(8,128)(2,1)} %param.8, s32[]{:T(128)S(6)} %select_n.293), kind=kOutput, calls=%fused_computation.115 | convolution fusion | flops 402653184 | bytes 3014660 | tf_op jit(solution)/shard_map/dot_general | solution.py:166
  45.9 1.1 collective-permute-start.10
  47.5 1.1 copy-done.4
  48.9 1.2 fusion.92
  50.1 1.2 fusion.90
  51.3 0.9 fusion.145
  52.2 1.7 %fusion.32 = bf16[3,16,128]{2,1,0:T(8,128)(2,1)S(1)} fusion(bf16[3,128,8192]{2,1,0:T(8,128)(2,1)S(1)} %bitcast.122, f32[3,128]{1,0:T(4,128)S(1)} %get-tuple-element.32, bf16[3,16,9216]{2,1,0:T(8,128)(2,1)S(1)} %pad_maximum_fusion.4), kind=kOutput, calls=%fused_computation.69 | convolution fusion | flops 100675584 | bytes 7092224 | tf_op jit(solution)/shard_map/cvj,coj->cvo/dot_general | solution.py:111
  54.6 1.2 fusion.98
  55.8 1.2 fusion.96
  57.0 1.2 fusion.94
  61.3 0.7 broadcast_in_dim.44
  62.0 1.8 %fusion.1 = bf16[384,8192]{1,0:T(8,128)(2,1)S(1)} fusion(bf16[384,8192]{1,0:T(8,128)(2,1)S(1)} %broadcast_in_dim.44, s32[]{:T(128)S(6)} %select_n.290, f32[384,512]{1,0:T(8,128)} %bitcast.149, bf16[1024,1024]{1,0:T(8,128)(2,1)S(1)} %copy-done.2, bf16[384,1024]{1,0:T(8,128)(2,1)S(1)} %copy-done.4, f32[384]{0:T(512)S(1)} %get-tuple-element.31), kind=kOutput, calls=%fused_computation.33 | convolution fusion | flops 404226048 | bytes 3016708 | tf_op jit(solution)/shard_map/dot_general | solution.py:170
  63.9 0.6 fusion.3
  65.6 1.9 %convolution_add_fusion.3 = f32[384,1024]{1,0:T(8,128)S(1)} fusion(f32[384,1024]{1,0:T(8,128)S(1)} %convolution_add_fusion.4, bf16[512,1024]{1,0:T(8,128)(2,1)} %collective-permute-done.4, bf16[384,8192]{1,0:T(8,128)(2,1)S(1)} %bitcast.120, s32[]{:T(128)S(6)} %select_n.292), kind=kOutput, calls=%fused_computation.13 | convolution fusion | flops 403046400 | bytes 4587524 | tf_op jit(solution)/shard_map/dot_general | solution.py:166
  67.5 1.9 %fusion.5 = bf16[384,8192]{1,0:T(8,128)(2,1)S(1)} fusion(bf16[384,8192]{1,0:T(8,128)(2,1)S(1)} %fusion.3, s32[]{:T(128)S(6)} %select_n.292, f32[384,512]{1,0:T(8,128)S(1)} %bitcast.147, bf16[512,1024]{1,0:T(8,128)(2,1)} %collective-permute-done.4, bf16[384,1024]{1,0:T(8,128)(2,1)S(1)} %copy-done.4, f32[384]{0:T(512)S(1)} %get-tuple-element.31), kind=kOutput, calls=%fused_computation.37 | convolution fusion | flops 404226048 | bytes 3016708 | tf_op jit(solution)/shard_map/dot_general | solution.py:170
  69.5 2.0 %fusion.7 = bf16[384,8192]{1,0:T(8,128)(2,1)S(1)} fusion(bf16[384,8192]{1,0:T(8,128)(2,1)S(1)} %fusion.5, s32[]{:T(128)S(6)} %select_n.293, f32[384,512]{1,0:T(8,128)S(1)} %bitcast.146, bf16[512,1024]{1,0:T(8,128)(2,1)} %collective-permute-done.5, bf16[384,1024]{1,0:T(8,128)(2,1)S(1)} %copy-done.4, f32[384]{0:T(512)S(1)} %get-tuple-element.31), kind=kOutput, calls=%fused_computation.39 | convolution fusion | flops 404226048 | bytes 3016708 | tf_op jit(solution)/shard_map/dot_general | solution.py:170
  73.8 1.8 %fusion.9 = bf16[384,8192]{1,0:T(8,128)(2,1)S(1)} fusion(bf16[384,8192]{1,0:T(8,128)(2,1)S(1)} %fusion.7, s32[]{:T(128)S(6)} %select_n.296, f32[384,512]{1,0:T(8,128)S(1)} %bitcast.145, bf16[512,1024]{1,0:T(8,128)(2,1)} %collective-permute-done.6, bf16[384,1024]{1,0:T(8,128)(2,1)S(1)} %copy-done.4, f32[384]{0:T(512)S(1)} %get-tuple-element.31), kind=kOutput, calls=%fused_computation.41 | convolution fusion | flops 404226048 | bytes 3016708 | tf_op jit(solution)/shard_map/dot_general | solution.py:170
  79.3 1.3 %collective-permute-start.13 = (bf16[512,1024]{1,0:T(8,128)(2,1)S(1)}, bf16[512,1024]{1,0:T(8,128)(2,1)S(1)}, u32[]{:S(2)}, u32[]{:S(2)}) collective-permute-start(bf16[512,1024]{1,0:T(8,128)(2,1)S(1)} %collective-permute-done.8), channel_id=1, source_target_pairs={{0,16},{1,9},{2,18},{3,11},{4,12},{5,21},{6,14},{7,23},{8,24},{9,1... | collective-permute-start | bytes 3145736 | tf_op jit(solution)/shard_map/ppermute | solution.py:56
  80.6 1.0 collective-permute-start.14
  81.7 0.6 fusion.11
  82.3 0.6 fusion.13
  82.9 0.6 fusion.15
  83.5 0.6 fusion.17
  84.6 9.5 %collective-permute-done.13 = bf16[512,1024]{1,0:T(8,128)(2,1)S(1)} collective-permute-done((bf16[512,1024]{1,0:T(8,128)(2,1)S(1)}, bf16[512,1024]{1,0:T(8,128)(2,1)S(1)}, u32[]{:S(2)}, u32[]{:S(2)}) %collective-permute-start.13) | collective-permute-done | bytes 1048608 | tf_op jit(solution)/shard_map/ppermute | solution.py:56
  94.2 11.6 %collective-permute-done.14 = bf16[512,1024]{1,0:T(8,128)(2,1)S(1)} collective-permute-done((bf16[512,1024]{1,0:T(8,128)(2,1)S(1)}, bf16[512,1024]{1,0:T(8,128)(2,1)S(1)}, u32[]{:S(2)}, u32[]{:S(2)}) %collective-permute-start.14) | collective-permute-done | bytes 1048608 | tf_op jit(solution)/shard_map/ppermute | solution.py:57
  107.5 0.6 fusion.19
  110.8 0.6 fusion.21
  111.4 0.9 fusion.23
  112.3 0.6 fusion.25
  112.9 0.6 fusion.27
  114.2 1.3 collective-permute-start.18
  115.4 1.7 %collective-permute-start.19 = (bf16[16,9216]{1,0:T(8,128)(2,1)S(1)}, bf16[16,9216]{1,0:T(8,128)(2,1)S(1)}, u32[]{:S(2)}, u32[]{:S(2)}) collective-permute-start(bf16[16,9216]{1,0:T(8,128)(2,1)S(1)} %get-tuple-element.11), channel_id=1, source_target_pairs={{0,24},{4,28},{8,16},{12,20},{16,8},{20,12},{24,0},{28,4},{1,25},{... | collective-permute-start | bytes 884744 | tf_op jit(solution)/shard_map/ppermute | solution.py:149
  118.9 1.0 multiply_convert_fusion.1
  120.6 0.6 fusion.31
  121.2 2.2 %collective-permute-done.17 = bf16[16,9216]{1,0:T(8,128)(2,1)S(1)} collective-permute-done((bf16[16,9216]{1,0:T(8,128)(2,1)S(1)}, bf16[16,9216]{1,0:T(8,128)(2,1)S(1)}, u32[]{:S(2)}, u32[]{:S(2)}) %collective-permute-start.17) | collective-permute-done | bytes 294944 | tf_op jit(solution)/shard_map/ppermute | solution.py:149
  123.4 6.2 %collective-permute-done.18 = bf16[16,9216]{1,0:T(8,128)(2,1)S(1)} collective-permute-done((bf16[16,9216]{1,0:T(8,128)(2,1)S(1)}, bf16[16,9216]{1,0:T(8,128)(2,1)S(1)}, u32[]{:S(2)}, u32[]{:S(2)}) %collective-permute-start.18) | collective-permute-done | bytes 294944 | tf_op jit(solution)/shard_map/ppermute | solution.py:149
  129.9 0.7 slice_bitcast_fusion.8
  130.6 0.6 slice_bitcast_fusion.9
  (121 shorter events, 21.5 us)
Async XLA Ops:
  0.6 11.3 %copy-start = (s32[32]{0:T(128)S(1)}, s32[32]{0:T(128)}, u32[]{:S(2)}) copy-start(s32[32]{0:T(128)} %param.15) | copy-start | bytes 388
  1.7 9.6 %copy-start.5 = (bf16[1,16,8192]{2,1,0:T(8,128)(2,1)S(1)}, bf16[1,16,8192]{2,1,0:T(8,128)(2,1)}, u32[]{:S(2)}) copy-start(bf16[1,16,8192]{2,1,0:T(8,128)(2,1)} %param.11) | copy-start | bytes 786436
  1.7 9.5 %copy-start.11 = (bf16[1,16,1024]{2,1,0:T(8,128)(2,1)S(1)}, bf16[1,16,1024]{2,1,0:T(8,128)(2,1)}, u32[]{:S(2)}) copy-start(bf16[1,16,1024]{2,1,0:T(8,128)(2,1)} %param.12) | copy-start | bytes 98308
  1.7 10.3 %copy-start.13 = (s32[3]{0:T(128)S(1)}, s32[3]{0:T(128)}, u32[]{:S(2)}) copy-start(s32[3]{0:T(128)} %param.13) | copy-start | bytes 40
  1.7 10.9 %collective-permute-start = (bf16[16,9216]{1,0:T(8,128)(2,1)S(1)}, bf16[16,9216]{1,0:T(8,128)(2,1)S(1)}, u32[]{:S(2)}, u32[]{:S(2)}) collective-permute-start(bf16[16,9216]{1,0:T(8,128)(2,1)S(1)} %get-tuple-element.30), channel_id=1, source_target_pairs={{0,8},{4,12},{8,0},{12,4},{16,24},{20,28},{24,16},{28,20},{1,9},{5... | collective-permute-start | bytes 884744 | tf_op jit(solution)/shard_map/ppermute | solution.py:91
  4.7 16.3 %collective-permute-start.1 = (bf16[16,9216]{1,0:T(8,128)(2,1)S(1)}, bf16[16,9216]{1,0:T(8,128)(2,1)S(1)}, u32[]{:S(2)}, u32[]{:S(2)}) collective-permute-start(bf16[16,9216]{1,0:T(8,128)(2,1)S(1)} %get-tuple-element.30), channel_id=1, source_target_pairs={{0,16},{4,20},{8,24},{12,28},{16,0},{20,4},{24,8},{28,12},{1,17},{... | collective-permute-start | bytes 884744 | tf_op jit(solution)/shard_map/ppermute | solution.py:91
  6.2 14.7 %collective-permute-start.2 = (bf16[16,9216]{1,0:T(8,128)(2,1)S(1)}, bf16[16,9216]{1,0:T(8,128)(2,1)S(1)}, u32[]{:S(2)}, u32[]{:S(2)}) collective-permute-start(bf16[16,9216]{1,0:T(8,128)(2,1)S(1)} %get-tuple-element.30), channel_id=1, source_target_pairs={{0,24},{4,28},{8,16},{12,20},{16,8},{20,12},{24,0},{28,4},{1,25},{... | collective-permute-start | bytes 884744 | tf_op jit(solution)/shard_map/ppermute | solution.py:91
  9.3 30.1 %copy-start.12 = (s32[3]{0:T(128)S(1)}, s32[3]{0:T(128)}, u32[]{:S(2)}) copy-start(s32[3]{0:T(128)} %param.14) | copy-start | bytes 40
  9.3 30.3 %collective-permute-start.6 = (bf16[512,1024]{1,0:T(8,128)(2,1)}, bf16[512,1024]{1,0:T(8,128)(2,1)}, u32[]{:S(2)}, u32[]{:S(2)}) collective-permute-start(bf16[512,1024]{1,0:T(8,128)(2,1)} %get-tuple-element.25), channel_id=1, source_target_pairs={{0,8},{1,17},{2,10},{3,19},{4,20},{5,13},{6,22},{7,15},{8,0},{9,25... | collective-permute-start | bytes 3145736 | tf_op jit(solution)/shard_map/ppermute | solution.py:52
  11.2 54.3 %collective-permute-start.4 = (bf16[512,1024]{1,0:T(8,128)(2,1)}, bf16[512,1024]{1,0:T(8,128)(2,1)}, u32[]{:S(2)}, u32[]{:S(2)}) collective-permute-start(bf16[512,1024]{1,0:T(8,128)(2,1)} %get-tuple-element.25), channel_id=1, source_target_pairs={{0,4},{4,0},{8,12},{12,8},{16,20},{20,16},{24,28},{28,24},{1,5},{5... | collective-permute-start | bytes 3145736 | tf_op jit(solution)/shard_map/ppermute | solution.py:49
  12.6 30.6 %collective-permute-start.5 = (bf16[512,1024]{1,0:T(8,128)(2,1)}, bf16[512,1024]{1,0:T(8,128)(2,1)}, u32[]{:S(2)}, u32[]{:S(2)}) collective-permute-start(bf16[512,1024]{1,0:T(8,128)(2,1)} %get-tuple-element.8), channel_id=1, source_target_pairs={{0,4},{4,0},{8,12},{12,8},{16,20},{20,16},{24,28},{28,24},{1,5},{5... | collective-permute-start | bytes 3145736 | tf_op jit(solution)/shard_map/ppermute | solution.py:49
  21.1 24.8 %collective-permute-start.3 = (bf16[4,16,9216]{2,1,0:T(8,128)(2,1)S(1)}, bf16[4,16,9216]{2,1,0:T(8,128)(2,1)S(1)}, u32[]{:S(2)}, u32[]{:S(2)}) collective-permute-start(bf16[4,16,9216]{2,1,0:T(8,128)(2,1)S(1)} %pad_maximum_fusion.2), channel_id=1, source_target_pairs={{0,4},{4,0},{8,12},{12,8},{16,20},{20,16},{24,28},{28,24},{1,5},{5... | collective-permute-start | bytes 3538952 | tf_op jit(solution)/shard_map/ppermute | solution.py:93
  39.6 37.4 %collective-permute-start.8 = (bf16[512,1024]{1,0:T(8,128)(2,1)}, bf16[512,1024]{1,0:T(8,128)(2,1)S(1)}, u32[]{:S(2)}, u32[]{:S(2)}) collective-permute-start(bf16[512,1024]{1,0:T(8,128)(2,1)} %get-tuple-element.8), channel_id=1, source_target_pairs={{0,8},{1,17},{2,10},{3,19},{4,20},{5,13},{6,22},{7,15},{8,0},{9,25... | collective-permute-start | bytes 3145736 | tf_op jit(solution)/shard_map/ppermute | solution.py:52
  39.6 36.8 %collective-permute-start.7 = (bf16[512,1024]{1,0:T(8,128)(2,1)}, bf16[512,1024]{1,0:T(8,128)(2,1)S(1)}, u32[]{:S(2)}, u32[]{:S(2)}) collective-permute-start(bf16[512,1024]{1,0:T(8,128)(2,1)} %collective-permute-done.6), channel_id=1, source_target_pairs={{0,4},{4,0},{8,12},{12,8},{16,20},{20,16},{24,28},{28,24},{1,5},{5... | collective-permute-start | bytes 3145736 | tf_op jit(solution)/shard_map/ppermute | solution.py:55
  43.2 3.8 %copy-start.10 = (bf16[8,16,9216]{2,1,0:T(8,128)(2,1)S(1)}, bf16[8,16,9216]{2,1,0:T(8,128)(2,1)}, u32[]{:S(2)}) copy-start(bf16[8,16,9216]{2,1,0:T(8,128)(2,1)} %constant_dynamic-update-slice_fusion.3) | copy-start | bytes 7077892
  43.2 32.4 %collective-permute-start.9 = (bf16[512,1024]{1,0:T(8,128)(2,1)}, bf16[512,1024]{1,0:T(8,128)(2,1)S(1)}, u32[]{:S(2)}, u32[]{:S(2)}) collective-permute-start(bf16[512,1024]{1,0:T(8,128)(2,1)} %collective-permute-done.6), channel_id=1, source_target_pairs={{0,16},{1,9},{2,18},{3,11},{4,12},{5,21},{6,14},{7,23},{8,24},{9,1... | collective-permute-start | bytes 3145736 | tf_op jit(solution)/shard_map/ppermute | solution.py:56
  43.8 7.5 %slice-start = ((s8[6291456]{0:T(1024)(128)(4,1)}), s8[4194304]{0:T(1024)(128)(4,1)S(1)}, s32[]{:S(2)}) async-start(s8[6291456]{0:T(1024)(128)(4,1)} %bitcast.119), calls=%async_computation | async-start | bytes 8388608
  45.9 29.8 %collective-permute-start.10 = (bf16[512,1024]{1,0:T(8,128)(2,1)}, bf16[512,1024]{1,0:T(8,128)(2,1)S(1)}, u32[]{:S(2)}, u32[]{:S(2)}) collective-permute-start(bf16[512,1024]{1,0:T(8,128)(2,1)} %collective-permute-done.6), channel_id=1, source_target_pairs={{0,1},{1,0},{2,3},{3,2},{4,5},{5,4},{6,7},{7,6},{8,9},{9,8},{10,11... | collective-permute-start | bytes 3145736 | tf_op jit(solution)/shard_map/ppermute | solution.py:57
  47.2 4.1 %slice-start.1 = ((s8[6291456]{0:T(1024)(128)(4,1)}), s8[2097152]{0:T(1024)(128)(4,1)S(1)}, s32[]{:S(2)}) async-start(s8[6291456]{0:T(1024)(128)(4,1)} %bitcast.119), calls=%async_computation.1 | async-start | bytes 4194304
  47.3 1.3 copy-start.4
  58.5 1.6 %copy-start.2 = (bf16[1024,1024]{1,0:T(8,128)(2,1)S(1)}, bf16[1024,1024]{1,0:T(8,128)(2,1)}, u32[]{:S(2)}) copy-start(bf16[1024,1024]{1,0:T(8,128)(2,1)} %param.10) | copy-start | bytes 6291460
  62.0 1.8 %copy-start.9 = (f32[3,128,512]{2,1,0:T(8,128)S(1)}, f32[3,128,512]{2,1,0:T(8,128)}, u32[]{:S(2)}) copy-start(f32[3,128,512]{2,1,0:T(8,128)} %fusion.96) | copy-start | bytes 2359300
  65.5 2.0 %copy-start.8 = (f32[3,128,512]{2,1,0:T(8,128)S(1)}, f32[3,128,512]{2,1,0:T(8,128)}, u32[]{:S(2)}) copy-start(f32[3,128,512]{2,1,0:T(8,128)} %fusion.94) | copy-start | bytes 2359300
  65.5 18.6 %collective-permute-start.16 = (bf16[4,16,9216]{2,1,0:T(8,128)(2,1)S(1)}, bf16[4,16,9216]{2,1,0:T(8,128)(2,1)S(1)}, u32[]{:S(2)}, u32[]{:S(2)}) collective-permute-start(bf16[4,16,9216]{2,1,0:T(8,128)(2,1)S(1)} %pad_maximum_fusion.3), channel_id=1, source_target_pairs={{0,4},{4,0},{8,12},{12,8},{16,20},{20,16},{24,28},{28,24},{1,5},{5... | collective-permute-start | bytes 3538952 | tf_op jit(solution)/shard_map/ppermute | solution.py:136
  67.5 1.9 %copy-start.7 = (f32[3,128,512]{2,1,0:T(8,128)S(1)}, f32[3,128,512]{2,1,0:T(8,128)}, u32[]{:S(2)}) copy-start(f32[3,128,512]{2,1,0:T(8,128)} %fusion.92) | copy-start | bytes 2359300
  72.7 1.1 copy-start.6
  75.9 32.2 %collective-permute-start.12 = (bf16[2,512,1024]{2,1,0:T(8,128)(2,1)S(1)}, bf16[2,512,1024]{2,1,0:T(8,128)(2,1)S(1)}, u32[]{:S(2)}, u32[]{:S(2)}) collective-permute-start(bf16[2,512,1024]{2,1,0:T(8,128)(2,1)S(1)} %pad_maximum_fusion), channel_id=1, source_target_pairs={{0,4},{4,0},{8,12},{12,8},{16,20},{20,16},{24,28},{28,24},{1,5},{5... | collective-permute-start | bytes 6291464 | tf_op jit(solution)/shard_map/ppermute | solution.py:60
  79.3 14.9 %collective-permute-start.13 = (bf16[512,1024]{1,0:T(8,128)(2,1)S(1)}, bf16[512,1024]{1,0:T(8,128)(2,1)S(1)}, u32[]{:S(2)}, u32[]{:S(2)}) collective-permute-start(bf16[512,1024]{1,0:T(8,128)(2,1)S(1)} %collective-permute-done.8), channel_id=1, source_target_pairs={{0,16},{1,9},{2,18},{3,11},{4,12},{5,21},{6,14},{7,23},{8,24},{9,1... | collective-permute-start | bytes 3145736 | tf_op jit(solution)/shard_map/ppermute | solution.py:56
  80.6 25.1 %collective-permute-start.14 = (bf16[512,1024]{1,0:T(8,128)(2,1)S(1)}, bf16[512,1024]{1,0:T(8,128)(2,1)S(1)}, u32[]{:S(2)}, u32[]{:S(2)}) collective-permute-start(bf16[512,1024]{1,0:T(8,128)(2,1)S(1)} %collective-permute-done.8), channel_id=1, source_target_pairs={{0,1},{1,0},{2,3},{3,2},{4,5},{5,4},{6,7},{7,6},{8,9},{9,8},{10,11... | collective-permute-start | bytes 3145736 | tf_op jit(solution)/shard_map/ppermute | solution.py:57
  81.7 24.3 %collective-permute-start.11 = (bf16[512,1024]{1,0:T(8,128)(2,1)S(1)}, bf16[512,1024]{1,0:T(8,128)(2,1)S(1)}, u32[]{:S(2)}, u32[]{:S(2)}) collective-permute-start(bf16[512,1024]{1,0:T(8,128)(2,1)S(1)} %collective-permute-done.8), channel_id=1, source_target_pairs={{0,4},{4,0},{8,12},{12,8},{16,20},{20,16},{24,28},{28,24},{1,5},{5... | collective-permute-start | bytes 3145736 | tf_op jit(solution)/shard_map/ppermute | solution.py:55
  105.9 7.6 %collective-permute-start.15 = (bf16[2,512,1024]{2,1,0:T(8,128)(2,1)S(1)}, bf16[2,512,1024]{2,1,0:T(8,128)(2,1)S(1)}, u32[]{:S(2)}, u32[]{:S(2)}) collective-permute-start(bf16[2,512,1024]{2,1,0:T(8,128)(2,1)S(1)} %pad_maximum_fusion.1), channel_id=1, source_target_pairs={{0,4},{4,0},{8,12},{12,8},{16,20},{20,16},{24,28},{28,24},{1,5},{5... | collective-permute-start | bytes 6291464 | tf_op jit(solution)/shard_map/ppermute | solution.py:60
  113.6 9.9 %collective-permute-start.17 = (bf16[16,9216]{1,0:T(8,128)(2,1)S(1)}, bf16[16,9216]{1,0:T(8,128)(2,1)S(1)}, u32[]{:S(2)}, u32[]{:S(2)}) collective-permute-start(bf16[16,9216]{1,0:T(8,128)(2,1)S(1)} %get-tuple-element.9), channel_id=1, source_target_pairs={{0,8},{4,12},{8,0},{12,4},{16,24},{20,28},{24,16},{28,20},{1,9},{5... | collective-permute-start | bytes 884744 | tf_op jit(solution)/shard_map/ppermute | solution.py:149
  114.2 15.4 %collective-permute-start.18 = (bf16[16,9216]{1,0:T(8,128)(2,1)S(1)}, bf16[16,9216]{1,0:T(8,128)(2,1)S(1)}, u32[]{:S(2)}, u32[]{:S(2)}) collective-permute-start(bf16[16,9216]{1,0:T(8,128)(2,1)S(1)} %get-tuple-element.10), channel_id=1, source_target_pairs={{0,16},{4,20},{8,24},{12,28},{16,0},{20,4},{24,8},{28,12},{1,17},{... | collective-permute-start | bytes 884744 | tf_op jit(solution)/shard_map/ppermute | solution.py:149
  115.4 14.2 %collective-permute-start.19 = (bf16[16,9216]{1,0:T(8,128)(2,1)S(1)}, bf16[16,9216]{1,0:T(8,128)(2,1)S(1)}, u32[]{:S(2)}, u32[]{:S(2)}) collective-permute-start(bf16[16,9216]{1,0:T(8,128)(2,1)S(1)} %get-tuple-element.11), channel_id=1, source_target_pairs={{0,24},{4,28},{8,16},{12,20},{16,8},{20,12},{24,0},{28,4},{1,25},{... | collective-permute-start | bytes 884744 | tf_op jit(solution)/shard_map/ppermute | solution.py:149
  120.6 10.6 %copy-start.1 = (s32[32]{0:T(128)S(1)}, s32[32]{0:T(128)}, u32[]{:S(2)}) copy-start(s32[32]{0:T(128)} %param.15) | copy-start | bytes 388
  121.2 10.0 %copy-start.3 = (bf16[384,8192]{1,0:T(8,128)(2,1)}, bf16[384,8192]{1,0:T(8,128)(2,1)S(1)}, u32[]{:S(2)}) copy-start(bf16[384,8192]{1,0:T(8,128)(2,1)S(1)} %fusion.31) | copy-start | bytes 18874372

commit v7 on v6

--- a/solution.py
+++ b/solution.py
@@ -86,19 +86,39 @@
     even_steps = list(range(2, members, 2))
 
     own_adapter = jnp.concatenate([adapter_down_maps[0], adapter_up_maps[0]], axis=1)
-    by_step = {0: own_adapter}
-    for step in even_steps:
-        by_step[step] = lax.ppermute(own_adapter, "fsdp", xor_pairs(members, step))
-    same_parity = jnp.stack([by_step[step] for step in range(0, members, 2)])
-    other_parity = lax.ppermute(same_parity, "fsdp", xor_pairs(members, 1))
-    for index, step in enumerate(range(0, members, 2)):
-        by_step[step ^ 1] = other_parity[index]
-    adapter_stack = jnp.stack([by_step[step] for step in range(members)])
-
     slot_ids = jnp.take(tenant_owner_slot, block_tenant_ids)
     member_ids = slot_ids // groups
-    picked = jnp.stack([lax.dynamic_index_in_dim(adapter_stack, me ^ member_ids[b], 0, keepdims=False)
-                        for b in range(blocks)])
+    parity = me % 2
+    doubling = members == 8
+    if doubling:
+        first_axis = 2 + 2 * parity
+        second_axis = 6 - first_axis
+        first_pairs = [(src, src ^ (2 + 2 * (src % 2))) for src in range(members)]
+        second_pairs = [(src, src ^ (4 - 2 * (src % 2))) for src in range(members)]
+        got_first = lax.ppermute(own_adapter, "fsdp", first_pairs)
+        got_second = lax.ppermute(jnp.stack([own_adapter, got_first]), "fsdp", second_pairs)
+        same_parity = jnp.stack([own_adapter, got_first, got_second[0], got_second[1]])
+        same_members = [me, me ^ first_axis, me ^ second_axis, me ^ 6]
+    else:
+        same_list = [own_adapter] + [
+            lax.ppermute(own_adapter, "fsdp", xor_pairs(members, step)) for step in even_steps
+        ]
+        same_parity = jnp.stack(same_list)
+        same_members = [me ^ step for step in range(0, members, 2)]
+    other_parity = lax.ppermute(same_parity, "fsdp", xor_pairs(members, 1))
+    adapter_stack = jnp.concatenate([same_parity, other_parity])
+    sibling_parity = 1 - parity
+    if doubling:
+        sibling_first = 2 + 2 * sibling_parity
+        other_members = [me ^ 1, me ^ 1 ^ sibling_first, me ^ 1 ^ (6 - sibling_first), me ^ 7]
+    else:
+        other_members = [me ^ 1 ^ step for step in range(0, members, 2)]
+    stack_members = jnp.stack([jnp.asarray(m, jnp.int32) for m in same_members + other_members])
+    picked = jnp.stack([
+        lax.dynamic_index_in_dim(
+            adapter_stack, jnp.argmax(stack_members == member_ids[b]).astype(jnp.int32), 0,
+            keepdims=False)
+        for b in range(blocks)])
     down_block = picked[:, :, :model_width]
     up_block = picked[:, :, model_width:]
 
@@ -142,11 +162,23 @@
     if weight_pieces and len(weight_pieces[0]) == 2:
         weight_pieces = [(source, 0, value) for source, value in weight_pieces]
     last_pieces = tuple(value for _, _, value in weight_pieces[-4:])
-    grad_sum = pair_sums[0]
-    for index, step in enumerate(even_steps):
-        sent = pair_sums[index + 1].astype(jnp.bfloat16)
-        sent, _ = lax.optimization_barrier((sent, last_pieces))
-        grad_sum = grad_sum + lax.ppermute(sent, "fsdp", xor_pairs(members, step)).astype(jnp.float32)
+    if doubling:
+        by_axis = jnp.stack(pair_sums)
+        keep_first = lax.dynamic_index_in_dim(by_axis, second_axis // 2, 0, keepdims=False)
+        send_first = jnp.stack([
+            lax.dynamic_index_in_dim(by_axis, first_axis // 2, 0, keepdims=False), pair_sums[3]
+        ]).astype(jnp.bfloat16)
+        send_first, _ = lax.optimization_barrier((send_first, last_pieces))
+        got = lax.ppermute(send_first, "fsdp", first_pairs).astype(jnp.float32)
+        mine = pair_sums[0] + got[0]
+        send_second = (keep_first + got[1]).astype(jnp.bfloat16)
+        grad_sum = mine + lax.ppermute(send_second, "fsdp", second_pairs).astype(jnp.float32)
+    else:
+        grad_sum = pair_sums[0]
+        for index, step in enumerate(even_steps):
+            sent = pair_sums[index + 1].astype(jnp.bfloat16)
+            sent, _ = lax.optimization_barrier((sent, last_pieces))
+            grad_sum = grad_sum + lax.ppermute(sent, "fsdp", xor_pairs(members, step)).astype(jnp.float32)
     grad_sum = grad_sum.astype(jnp.bfloat16)
     grad_down = grad_sum[None, :, :model_width]
     grad_up = grad_sum[None, :, model_width:]

time: 132 us -> 149 us (1.13)
  waiting for transfers between devices: 37.3 us -> 45.3 us
  between operations: 19.1 us -> 22.9 us
  other arithmetic: 7.81 us -> 10.8 us
  local copies, waits for them, and re-layouts: 8.32 us -> 11.1 us
    ppermute x6 -> x4, waiting for transfers between devices: 16.2 us -> 26.1 us  [the longest x1 13.6 us: on_device(): got_first = lax.ppermute(own_adapter, 'fsdp', first_pairs)]
    another operation x3 -> x9, other arithmetic: 1.26 us -> 4.6 us  [the longest x3 4.08 us: on_device(): jnp.argmax(stack_members == member_ids[b]).astype(jnp.int32)]
    ppermute x2, starting transfers between devices: 1.96 us -> 4.93 us  [relay_gather(): first = lax.ppermute(piece, ('fsdp', 'dp'), first_pairs)]
    unnamed x38 -> x30, local copies, waits for them, and re-layouts: 1.86 us -> 4.38 us
    ppermute x6 -> x4, starting transfers between devices: 8.1 us -> 6.06 us  [the longest x1 2.12 us: on_device(): lax.ppermute(jnp.stack([own_adapter, got_first]), 'fsdp', second_pairs)]
  transfers between devices with their start and end apart: 20 -> 18, of which waited for: 5 -> 6; matrix products, arithmetic and copies ran while one was open for 41% -> 35% of each run, Pallas kernels for 0% -> 0%
where the time goes in v7:
time: 149 us; the launch traced here: 148 us
  waiting for transfers between devices  45.3 us (30%)
  matrix products  41.4 us (28%)
  between operations  22.9 us (15%)
  starting transfers between devices  16.9 us (11%)
  local copies, waits for them, and re-layouts  11.1 us (7%)
  other arithmetic  10.8 us (7%)
    dot_general x16, matrix products, on_device(): lax.dot_general(masked_cot, weight_piece, (((1,), (1,)), ((), ())), prefe...  15 us
    ppermute x1, waiting for transfers between devices, on_device(): got_first = lax.ppermute(own_adapter, 'fsdp', first_pairs)  13.6 us
    dot_general x16, matrix products, on_device(): jnp.dot(token_piece, weight_piece, preferred_element_type=jnp.float32)  13.4 us
    ppermute x2, waiting for transfers between devices, relay_gather(): partner = lax.ppermute(first, ('fsdp', 'dp'), partner_pairs)  11 us
    dot_general x16, matrix products, on_device(): jnp.einsum('uio,uof->uif', low_rank_gradient, down_piece, preferred_eleme...  9.39 us
    ppermute x2, waiting for transfers between devices, relay_gather(): relayed = lax.ppermute(first, ('fsdp', 'dp'), relay_pairs)  8.11 us
    ppermute x1, waiting for transfers between devices, on_device(): got = lax.ppermute(send_first, 'fsdp', first_pairs).astype(jnp.float32)  6.64 us
    ppermute x2, starting transfers between devices, relay_gather(): first = lax.ppermute(piece, ('fsdp', 'dp'), first_pairs)  4.93 us
  transfers between devices with their start and end apart: 18, of which 6 were waited for; matrix products, arithmetic and copies ran while one was open for 35% of the time, Pallas kernels for 0%

profile of v7, /device:TPU:0, one launch (start us, length us, event | category | flops | bytes accessed | tf_op | source)
XLA Modules:
  0.0 148.3 jit_solution(12271782276073219407)
XLA Ops:
  0.7 3.1 %fusion.143 = (bf16[512,1024]{1,0:T(8,128)(2,1)}, bf16[512,1024]{1,0:T(8,128)(2,1)}) fusion(bf16[1024,1024]{1,0:T(8,128)(2,1)} %param.10), kind=kLoop, calls=%fused_computation.221 | loop fusion | bytes 4194304 | tf_op jit(solution)/shard_map/slice | solution.py:47
  3.8 2.9 %collective-permute-start.5 = (bf16[512,1024]{1,0:T(8,128)(2,1)}, bf16[512,1024]{1,0:T(8,128)(2,1)}, u32[]{:S(2)}, u32[]{:S(2)}) collective-permute-start(bf16[512,1024]{1,0:T(8,128)(2,1)} %get-tuple-element.29), channel_id=1, source_target_pairs={{0,8},{1,17},{2,10},{3,19},{4,20},{5,13},{6,22},{7,15},{8,0},{9,25... | collective-permute-start | bytes 3145736 | tf_op jit(solution)/shard_map/ppermute | solution.py:52
  6.8 1.1 collective-permute-start
  7.9 0.7 collective-permute-start.4
  8.6 0.6 gather_fusion
  9.3 13.6 %collective-permute-done = bf16[16,9216]{1,0:T(8,128)(2,1)S(1)} collective-permute-done((bf16[16,9216]{1,0:T(8,128)(2,1)S(1)}, bf16[16,9216]{1,0:T(8,128)(2,1)S(1)}, u32[]{:S(2)}, u32[]{:S(2)}) %collective-permute-start) | collective-permute-done | bytes 294944 | tf_op jit(solution)/shard_map/ppermute | solution.py:98
  22.9 2.1 %collective-permute-start.1 = (bf16[2,16,9216]{2,1,0:T(8,128)(2,1)S(1)}, bf16[2,16,9216]{2,1,0:T(8,128)(2,1)S(1)}, u32[]{:S(2)}, u32[]{:S(2)}) collective-permute-start(bf16[2,16,9216]{2,1,0:T(8,128)(2,1)S(1)} %pad_maximum_fusion.8), channel_id=1, source_target_pairs={{0,16},{4,12},{8,24},{12,4},{16,0},{20,28},{24,8},{28,20},{1,17},{... | collective-permute-start | bytes 1769480 | tf_op jit(solution)/shard_map/ppermute | solution.py:99
  25.2 0.7 fusion.144
  25.8 1.4 compare_reduce_fusion.2
  28.6 1.3 compare_reduce_fusion.1
  31.0 1.9 %collective-permute-done.1 = bf16[2,16,9216]{2,1,0:T(8,128)(2,1)S(1)} collective-permute-done((bf16[2,16,9216]{2,1,0:T(8,128)(2,1)S(1)}, bf16[2,16,9216]{2,1,0:T(8,128)(2,1)S(1)}, u32[]{:S(2)}, u32[]{:S(2)}) %collective-permute-start.1) | collective-permute-done | bytes 589856 | tf_op jit(solution)/shard_map/ppermute | solution.py:99
  33.1 1.4 compare_reduce_fusion
  53.6 2.0 %collective-permute-start.7 = (bf16[512,1024]{1,0:T(8,128)(2,1)}, bf16[512,1024]{1,0:T(8,128)(2,1)S(1)}, u32[]{:S(2)}, u32[]{:S(2)}) collective-permute-start(bf16[512,1024]{1,0:T(8,128)(2,1)} %get-tuple-element.12), channel_id=1, source_target_pairs={{0,8},{1,17},{2,10},{3,19},{4,20},{5,13},{6,22},{7,15},{8,0},{9,25... | collective-permute-start | bytes 3145736 | tf_op jit(solution)/shard_map/ppermute | solution.py:52
  55.8 1.9 %fusion.59 = f32[384,1024]{1,0:T(8,128)S(1)} fusion(bf16[512,1024]{1,0:T(8,128)(2,1)} %collective-permute-done.5, bf16[384,8192]{1,0:T(8,128)(2,1)} %param.8, s32[]{:T(128)S(6)} %select_n.323), kind=kOutput, calls=%fused_computation.121 | convolution fusion | flops 402653184 | bytes 3014660 | tf_op jit(solution)/shard_map/dot_general | solution.py:198
  57.7 1.3 collective-permute-start.8
  59.1 2.1 %fusion.61 = f32[384,1024]{1,0:T(8,128)S(1)} fusion(bf16[512,1024]{1,0:T(8,128)(2,1)} %collective-permute-done.4, bf16[384,8192]{1,0:T(8,128)(2,1)} %param.8, s32[]{:T(128)S(6)} %select_n.321), kind=kOutput, calls=%fused_computation.123 | convolution fusion | flops 402653184 | bytes 3014660 | tf_op jit(solution)/shard_map/dot_general | solution.py:198
  61.8 1.1 copy-done.4
  63.5 1.2 fusion.89
  64.7 0.9 fusion.145
  65.6 1.7 %fusion.32 = bf16[3,16,128]{2,1,0:T(8,128)(2,1)S(1)} fusion(bf16[3,128,8192]{2,1,0:T(8,128)(2,1)S(1)} %bitcast.118, f32[3,128]{1,0:T(4,128)S(1)} %get-tuple-element.36, bf16[3,16,9216]{2,1,0:T(8,128)(2,1)S(1)} %pad_maximum_fusion.6), kind=kOutput, calls=%fused_computation.71 | convolution fusion | flops 100675584 | bytes 7092224 | tf_op jit(solution)/shard_map/cvj,coj->cvo/dot_general | solution.py:131
  68.0 1.2 fusion.97
  69.2 1.2 fusion.95
  70.7 1.2 fusion.87
  71.9 1.2 fusion.85
  75.6 0.7 broadcast_in_dim.44
  76.3 1.8 %fusion.1 = bf16[384,8192]{1,0:T(8,128)(2,1)S(1)} fusion(bf16[384,8192]{1,0:T(8,128)(2,1)S(1)} %broadcast_in_dim.44, s32[]{:T(128)S(6)} %select_n.318, f32[384,512]{1,0:T(8,128)} %bitcast.143, bf16[1024,1024]{1,0:T(8,128)(2,1)S(1)} %copy-done.2, bf16[384,1024]{1,0:T(8,128)(2,1)S(1)} %copy-done.4, f32[384]{0:T(512)S(1)} %get-tuple-element.35), kind=kOutput, calls=%fused_computation.35 | convolution fusion | flops 404226048 | bytes 3016708 | tf_op jit(solution)/shard_map/dot_general | solution.py:202
  78.2 0.6 fusion.3
  79.9 1.8 %convolution_add_fusion.3 = f32[384,1024]{1,0:T(8,128)S(1)} fusion(f32[384,1024]{1,0:T(8,128)S(1)} %convolution_add_fusion.4, bf16[512,1024]{1,0:T(8,128)(2,1)} %collective-permute-done.3, bf16[384,8192]{1,0:T(8,128)(2,1)S(1)} %bitcast.116, s32[]{:T(128)S(6)} %select_n.320), kind=kOutput, calls=%fused_computation.15 | convolution fusion | flops 403046400 | bytes 4587524 | tf_op jit(solution)/shard_map/dot_general | solution.py:198
  81.7 1.9 %fusion.5 = bf16[384,8192]{1,0:T(8,128)(2,1)S(1)} fusion(bf16[384,8192]{1,0:T(8,128)(2,1)S(1)} %fusion.3, s32[]{:T(128)S(6)} %select_n.320, f32[384,512]{1,0:T(8,128)S(1)} %bitcast.141, bf16[512,1024]{1,0:T(8,128)(2,1)} %collective-permute-done.3, bf16[384,1024]{1,0:T(8,128)(2,1)S(1)} %copy-done.4, f32[384]{0:T(512)S(1)} %get-tuple-element.35), kind=kOutput, calls=%fused_computation.39 | convolution fusion | flops 404226048 | bytes 3016708 | tf_op jit(solution)/shard_map/dot_general | solution.py:202
  83.6 1.8 %fusion.7 = bf16[384,8192]{1,0:T(8,128)(2,1)S(1)} fusion(bf16[384,8192]{1,0:T(8,128)(2,1)S(1)} %fusion.5, s32[]{:T(128)S(6)} %select_n.321, f32[384,512]{1,0:T(8,128)S(1)} %bitcast.140, bf16[512,1024]{1,0:T(8,128)(2,1)} %collective-permute-done.4, bf16[384,1024]{1,0:T(8,128)(2,1)S(1)} %copy-done.4, f32[384]{0:T(512)S(1)} %get-tuple-element.35), kind=kOutput, calls=%fused_computation.41 | convolution fusion | flops 404226048 | bytes 3016708 | tf_op jit(solution)/shard_map/dot_general | solution.py:202
  88.0 1.8 %fusion.9 = bf16[384,8192]{1,0:T(8,128)(2,1)S(1)} fusion(bf16[384,8192]{1,0:T(8,128)(2,1)S(1)} %fusion.7, s32[]{:T(128)S(6)} %select_n.323, f32[384,512]{1,0:T(8,128)S(1)} %bitcast.139, bf16[512,1024]{1,0:T(8,128)(2,1)} %collective-permute-done.5, bf16[384,1024]{1,0:T(8,128)(2,1)S(1)} %copy-done.4, f32[384]{0:T(512)S(1)} %get-tuple-element.35), kind=kOutput, calls=%fused_computation.43 | convolution fusion | flops 404226048 | bytes 3016708 | tf_op jit(solution)/shard_map/dot_general | solution.py:202
  92.1 0.8 collective-permute-start.12
  92.9 2.0 %collective-permute-start.13 = (bf16[512,1024]{1,0:T(8,128)(2,1)S(1)}, bf16[512,1024]{1,0:T(8,128)(2,1)S(1)}, u32[]{:S(2)}, u32[]{:S(2)}) collective-permute-start(bf16[512,1024]{1,0:T(8,128)(2,1)S(1)} %collective-permute-done.7), channel_id=1, source_target_pairs={{0,1},{1,0},{2,3},{3,2},{4,5},{5,4},{6,7},{7,6},{8,9},{9,8},{10,11... | collective-permute-start | bytes 3145736 | tf_op jit(solution)/shard_map/ppermute | solution.py:57
  95.5 0.6 fusion.13
  96.7 0.6 fusion.17
  98.8 8.1 %collective-permute-done.12 = bf16[512,1024]{1,0:T(8,128)(2,1)S(1)} collective-permute-done((bf16[512,1024]{1,0:T(8,128)(2,1)S(1)}, bf16[512,1024]{1,0:T(8,128)(2,1)S(1)}, u32[]{:S(2)}, u32[]{:S(2)}) %collective-permute-start.12) | collective-permute-done | bytes 1048608 | tf_op jit(solution)/shard_map/ppermute | solution.py:56
  106.9 11.0 %collective-permute-done.13 = bf16[512,1024]{1,0:T(8,128)(2,1)S(1)} collective-permute-done((bf16[512,1024]{1,0:T(8,128)(2,1)S(1)}, bf16[512,1024]{1,0:T(8,128)(2,1)S(1)}, u32[]{:S(2)}, u32[]{:S(2)}) %collective-permute-start.13) | collective-permute-done | bytes 1048608 | tf_op jit(solution)/shard_map/ppermute | solution.py:57
  117.9 1.5 collective-permute-start.16
  120.6 0.6 fusion.19
  121.2 6.6 %collective-permute-done.16 = bf16[2,16,9216]{2,1,0:T(8,128)(2,1)S(1)} collective-permute-done((bf16[2,16,9216]{2,1,0:T(8,128)(2,1)S(1)}, bf16[2,16,9216]{2,1,0:T(8,128)(2,1)S(1)}, u32[]{:S(2)}, u32[]{:S(2)}) %collective-permute-start.16) | collective-permute-done | bytes 589856 | tf_op jit(solution)/shard_map/ppermute | solution.py:172
  128.0 1.3 collective-permute-start.17
  130.8 4.0 %collective-permute-done.17 = bf16[16,9216]{1,0:T(8,128)(2,1)S(1)} collective-permute-done((bf16[16,9216]{1,0:T(8,128)(2,1)S(1)}, bf16[16,9216]{1,0:T(8,128)(2,1)S(1)}, u32[]{:S(2)}, u32[]{:S(2)}) %collective-permute-start.17) | collective-permute-done | bytes 294944 | tf_op jit(solution)/shard_map/ppermute | solution.py:175
  134.8 0.6 slice_bitcast_fusion.9
  135.5 0.7 slice_bitcast_fusion.8
  139.5 0.9 fusion.23
  140.3 0.6 fusion.25
  143.3 1.0 multiply_convert_fusion.1
  145.6 2.7 %copy-done.3 = bf16[384,8192]{1,0:T(8,128)(2,1)} copy-done((bf16[384,8192]{1,0:T(8,128)(2,1)}, bf16[384,8192]{1,0:T(8,128)(2,1)S(1)}, u32[]{:S(2)}) %copy-start.3) | copy-done | bytes 6291480
  (118 shorter events, 23.2 us)
Async XLA Ops:
  0.6 8.0 %copy-start = (s32[32]{0:T(128)S(1)}, s32[32]{0:T(128)}, u32[]{:S(2)}) copy-start(s32[32]{0:T(128)} %param.15) | copy-start | bytes 388
  0.6 6.1 %copy-start.9 = (bf16[1,16,8192]{2,1,0:T(8,128)(2,1)S(1)}, bf16[1,16,8192]{2,1,0:T(8,128)(2,1)}, u32[]{:S(2)}) copy-start(bf16[1,16,8192]{2,1,0:T(8,128)(2,1)} %param.11) | copy-start | bytes 786436
  0.7 6.1 %copy-start.10 = (bf16[1,16,1024]{2,1,0:T(8,128)(2,1)S(1)}, bf16[1,16,1024]{2,1,0:T(8,128)(2,1)}, u32[]{:S(2)}) copy-start(bf16[1,16,1024]{2,1,0:T(8,128)(2,1)} %param.12) | copy-start | bytes 98308
  0.7 7.9 %copy-start.12 = (s32[3]{0:T(128)S(1)}, s32[3]{0:T(128)}, u32[]{:S(2)}) copy-start(s32[3]{0:T(128)} %param.13) | copy-start | bytes 40
  3.8 49.8 %collective-permute-start.5 = (bf16[512,1024]{1,0:T(8,128)(2,1)}, bf16[512,1024]{1,0:T(8,128)(2,1)}, u32[]{:S(2)}, u32[]{:S(2)}) collective-permute-start(bf16[512,1024]{1,0:T(8,128)(2,1)} %get-tuple-element.29), channel_id=1, source_target_pairs={{0,8},{1,17},{2,10},{3,19},{4,20},{5,13},{6,22},{7,15},{8,0},{9,25... | collective-permute-start | bytes 3145736 | tf_op jit(solution)/shard_map/ppermute | solution.py:52
  6.7 73.1 %collective-permute-start.3 = (bf16[512,1024]{1,0:T(8,128)(2,1)}, bf16[512,1024]{1,0:T(8,128)(2,1)}, u32[]{:S(2)}, u32[]{:S(2)}) collective-permute-start(bf16[512,1024]{1,0:T(8,128)(2,1)} %get-tuple-element.29), channel_id=1, source_target_pairs={{0,4},{4,0},{8,12},{12,8},{16,20},{20,16},{24,28},{28,24},{1,5},{5... | collective-permute-start | bytes 3145736 | tf_op jit(solution)/shard_map/ppermute | solution.py:49
  6.8 16.1 %collective-permute-start = (bf16[16,9216]{1,0:T(8,128)(2,1)S(1)}, bf16[16,9216]{1,0:T(8,128)(2,1)S(1)}, u32[]{:S(2)}, u32[]{:S(2)}) collective-permute-start(bf16[16,9216]{1,0:T(8,128)(2,1)S(1)} %get-tuple-element.34), channel_id=1, source_target_pairs={{0,8},{4,20},{8,0},{12,28},{16,24},{20,4},{24,16},{28,12},{1,9},{5... | collective-permute-start | bytes 884744 | tf_op jit(solution)/shard_map/ppermute | solution.py:98
  7.9 49.8 %collective-permute-start.4 = (bf16[512,1024]{1,0:T(8,128)(2,1)}, bf16[512,1024]{1,0:T(8,128)(2,1)}, u32[]{:S(2)}, u32[]{:S(2)}) collective-permute-start(bf16[512,1024]{1,0:T(8,128)(2,1)} %get-tuple-element.12), channel_id=1, source_target_pairs={{0,4},{4,0},{8,12},{12,8},{16,20},{20,16},{24,28},{28,24},{1,5},{5... | collective-permute-start | bytes 3145736 | tf_op jit(solution)/shard_map/ppermute | solution.py:49
  9.3 44.1 %copy-start.11 = (s32[3]{0:T(128)S(1)}, s32[3]{0:T(128)}, u32[]{:S(2)}) copy-start(s32[3]{0:T(128)} %param.14) | copy-start | bytes 40
  22.9 10.0 %collective-permute-start.1 = (bf16[2,16,9216]{2,1,0:T(8,128)(2,1)S(1)}, bf16[2,16,9216]{2,1,0:T(8,128)(2,1)S(1)}, u32[]{:S(2)}, u32[]{:S(2)}) collective-permute-start(bf16[2,16,9216]{2,1,0:T(8,128)(2,1)S(1)} %pad_maximum_fusion.8), channel_id=1, source_target_pairs={{0,16},{4,12},{8,24},{12,4},{16,0},{20,28},{24,8},{28,20},{1,17},{... | collective-permute-start | bytes 1769480 | tf_op jit(solution)/shard_map/ppermute | solution.py:99
  33.0 28.1 %collective-permute-start.2 = (bf16[4,16,9216]{2,1,0:T(8,128)(2,1)S(1)}, bf16[4,16,9216]{2,1,0:T(8,128)(2,1)S(1)}, u32[]{:S(2)}, u32[]{:S(2)}) collective-permute-start(bf16[4,16,9216]{2,1,0:T(8,128)(2,1)S(1)} %pad_maximum_fusion.4), channel_id=1, source_target_pairs={{0,4},{4,0},{8,12},{12,8},{16,20},{20,16},{24,28},{28,24},{1,5},{5... | collective-permute-start | bytes 3538952 | tf_op jit(solution)/shard_map/ppermute | solution.py:108
  53.6 37.6 %collective-permute-start.7 = (bf16[512,1024]{1,0:T(8,128)(2,1)}, bf16[512,1024]{1,0:T(8,128)(2,1)S(1)}, u32[]{:S(2)}, u32[]{:S(2)}) collective-permute-start(bf16[512,1024]{1,0:T(8,128)(2,1)} %get-tuple-element.12), channel_id=1, source_target_pairs={{0,8},{1,17},{2,10},{3,19},{4,20},{5,13},{6,22},{7,15},{8,0},{9,25... | collective-permute-start | bytes 3145736 | tf_op jit(solution)/shard_map/ppermute | solution.py:52
  55.5 35.0 %collective-permute-start.6 = (bf16[512,1024]{1,0:T(8,128)(2,1)}, bf16[512,1024]{1,0:T(8,128)(2,1)S(1)}, u32[]{:S(2)}, u32[]{:S(2)}) collective-permute-start(bf16[512,1024]{1,0:T(8,128)(2,1)} %collective-permute-done.5), channel_id=1, source_target_pairs={{0,4},{4,0},{8,12},{12,8},{16,20},{20,16},{24,28},{28,24},{1,5},{5... | collective-permute-start | bytes 3145736 | tf_op jit(solution)/shard_map/ppermute | solution.py:55
  57.7 32.1 %collective-permute-start.8 = (bf16[512,1024]{1,0:T(8,128)(2,1)}, bf16[512,1024]{1,0:T(8,128)(2,1)S(1)}, u32[]{:S(2)}, u32[]{:S(2)}) collective-permute-start(bf16[512,1024]{1,0:T(8,128)(2,1)} %collective-permute-done.5), channel_id=1, source_target_pairs={{0,16},{1,9},{2,18},{3,11},{4,12},{5,21},{6,14},{7,23},{8,24},{9,1... | collective-permute-start | bytes 3145736 | tf_op jit(solution)/shard_map/ppermute | solution.py:56
  59.1 5.6 %slice-start = ((s8[6291456]{0:T(1024)(128)(4,1)}), s8[4194304]{0:T(1024)(128)(4,1)S(1)}, s32[]{:S(2)}) async-start(s8[6291456]{0:T(1024)(128)(4,1)} %bitcast.115), calls=%async_computation | async-start | bytes 8388608
  61.2 28.7 %collective-permute-start.9 = (bf16[512,1024]{1,0:T(8,128)(2,1)}, bf16[512,1024]{1,0:T(8,128)(2,1)S(1)}, u32[]{:S(2)}, u32[]{:S(2)}) collective-permute-start(bf16[512,1024]{1,0:T(8,128)(2,1)} %collective-permute-done.5), channel_id=1, source_target_pairs={{0,1},{1,0},{2,3},{3,2},{4,5},{5,4},{6,7},{7,6},{8,9},{9,8},{10,11... | collective-permute-start | bytes 3145736 | tf_op jit(solution)/shard_map/ppermute | solution.py:57
  61.5 3.2 %slice-start.1 = ((s8[6291456]{0:T(1024)(128)(4,1)}), s8[2097152]{0:T(1024)(128)(4,1)S(1)}, s32[]{:S(2)}) async-start(s8[6291456]{0:T(1024)(128)(4,1)} %bitcast.115), calls=%async_computation.1 | async-start | bytes 4194304
  61.6 1.3 copy-start.4
  71.9 2.5 %copy-start.2 = (bf16[1024,1024]{1,0:T(8,128)(2,1)S(1)}, bf16[1024,1024]{1,0:T(8,128)(2,1)}, u32[]{:S(2)}) copy-start(bf16[1024,1024]{1,0:T(8,128)(2,1)} %param.10) | copy-start | bytes 6291460
  76.3 1.8 %copy-start.8 = (f32[3,128,512]{2,1,0:T(8,128)S(1)}, f32[3,128,512]{2,1,0:T(8,128)}, u32[]{:S(2)}) copy-start(f32[3,128,512]{2,1,0:T(8,128)} %fusion.95) | copy-start | bytes 2359300
  79.8 18.2 %collective-permute-start.15 = (bf16[4,16,9216]{2,1,0:T(8,128)(2,1)S(1)}, bf16[4,16,9216]{2,1,0:T(8,128)(2,1)S(1)}, u32[]{:S(2)}, u32[]{:S(2)}) collective-permute-start(bf16[4,16,9216]{2,1,0:T(8,128)(2,1)S(1)} %pad_maximum_fusion.5), channel_id=1, source_target_pairs={{0,4},{4,0},{8,12},{12,8},{16,20},{20,16},{24,28},{28,24},{1,5},{5... | collective-permute-start | bytes 3538952 | tf_op jit(solution)/shard_map/ppermute | solution.py:156
  86.8 1.1 copy-start.7
  90.0 46.2 %collective-permute-start.11 = (bf16[2,512,1024]{2,1,0:T(8,128)(2,1)S(1)}, bf16[2,512,1024]{2,1,0:T(8,128)(2,1)S(1)}, u32[]{:S(2)}, u32[]{:S(2)}) collective-permute-start(bf16[2,512,1024]{2,1,0:T(8,128)(2,1)S(1)} %pad_maximum_fusion.2), channel_id=1, source_target_pairs={{0,4},{4,0},{8,12},{12,8},{16,20},{20,16},{24,28},{28,24},{1,5},{5... | collective-permute-start | bytes 6291464 | tf_op jit(solution)/shard_map/ppermute | solution.py:60
  91.8 3.1 %copy-start.6 = (f32[3,128,512]{2,1,0:T(8,128)S(1)}, f32[3,128,512]{2,1,0:T(8,128)}, u32[]{:S(2)}) copy-start(f32[3,128,512]{2,1,0:T(8,128)} %fusion.87) | copy-start | bytes 2359300
  92.0 3.4 %copy-start.5 = (f32[3,128,512]{2,1,0:T(8,128)S(1)}, f32[3,128,512]{2,1,0:T(8,128)}, u32[]{:S(2)}) copy-start(f32[3,128,512]{2,1,0:T(8,128)} %fusion.85) | copy-start | bytes 2359300
  92.1 14.9 %collective-permute-start.12 = (bf16[512,1024]{1,0:T(8,128)(2,1)S(1)}, bf16[512,1024]{1,0:T(8,128)(2,1)S(1)}, u32[]{:S(2)}, u32[]{:S(2)}) collective-permute-start(bf16[512,1024]{1,0:T(8,128)(2,1)S(1)} %collective-permute-done.7), channel_id=1, source_target_pairs={{0,16},{1,9},{2,18},{3,11},{4,12},{5,21},{6,14},{7,23},{8,24},{9,1... | collective-permute-start | bytes 3145736 | tf_op jit(solution)/shard_map/ppermute | solution.py:56
  92.9 25.1 %collective-permute-start.13 = (bf16[512,1024]{1,0:T(8,128)(2,1)S(1)}, bf16[512,1024]{1,0:T(8,128)(2,1)S(1)}, u32[]{:S(2)}, u32[]{:S(2)}) collective-permute-start(bf16[512,1024]{1,0:T(8,128)(2,1)S(1)} %collective-permute-done.7), channel_id=1, source_target_pairs={{0,1},{1,0},{2,3},{3,2},{4,5},{5,4},{6,7},{7,6},{8,9},{9,8},{10,11... | collective-permute-start | bytes 3145736 | tf_op jit(solution)/shard_map/ppermute | solution.py:57
  94.9 25.7 %collective-permute-start.10 = (bf16[512,1024]{1,0:T(8,128)(2,1)S(1)}, bf16[512,1024]{1,0:T(8,128)(2,1)S(1)}, u32[]{:S(2)}, u32[]{:S(2)}) collective-permute-start(bf16[512,1024]{1,0:T(8,128)(2,1)S(1)} %collective-permute-done.7), channel_id=1, source_target_pairs={{0,4},{4,0},{8,12},{12,8},{16,20},{20,16},{24,28},{28,24},{1,5},{5... | collective-permute-start | bytes 3145736 | tf_op jit(solution)/shard_map/ppermute | solution.py:55
  117.9 9.9 %collective-permute-start.16 = (bf16[2,16,9216]{2,1,0:T(8,128)(2,1)S(1)}, bf16[2,16,9216]{2,1,0:T(8,128)(2,1)S(1)}, u32[]{:S(2)}, u32[]{:S(2)}) collective-permute-start(bf16[2,16,9216]{2,1,0:T(8,128)(2,1)S(1)} %pad_maximum_fusion.9), channel_id=1, source_target_pairs={{0,8},{4,20},{8,0},{12,28},{16,24},{20,4},{24,16},{28,12},{1,9},{5... | collective-permute-start | bytes 1769480 | tf_op jit(solution)/shard_map/ppermute | solution.py:172
  120.5 21.1 %collective-permute-start.14 = (bf16[2,512,1024]{2,1,0:T(8,128)(2,1)S(1)}, bf16[2,512,1024]{2,1,0:T(8,128)(2,1)S(1)}, u32[]{:S(2)}, u32[]{:S(2)}) collective-permute-start(bf16[2,512,1024]{2,1,0:T(8,128)(2,1)S(1)} %pad_maximum_fusion.3), channel_id=1, source_target_pairs={{0,4},{4,0},{8,12},{12,8},{16,20},{20,16},{24,28},{28,24},{1,5},{5... | collective-permute-start | bytes 6291464 | tf_op jit(solution)/shard_map/ppermute | solution.py:60
  128.0 6.8 %collective-permute-start.17 = (bf16[16,9216]{1,0:T(8,128)(2,1)S(1)}, bf16[16,9216]{1,0:T(8,128)(2,1)S(1)}, u32[]{:S(2)}, u32[]{:S(2)}) collective-permute-start(bf16[16,9216]{1,0:T(8,128)(2,1)S(1)} %fusion.66), channel_id=1, source_target_pairs={{0,16},{4,12},{8,24},{12,4},{16,0},{20,28},{24,8},{28,20},{1,17},{... | collective-permute-start | bytes 884744 | tf_op jit(solution)/shard_map/ppermute | solution.py:175
  144.4 4.0 %copy-start.1 = (s32[32]{0:T(128)S(1)}, s32[32]{0:T(128)}, u32[]{:S(2)}) copy-start(s32[32]{0:T(128)} %param.15) | copy-start | bytes 388
  145.6 2.7 %copy-start.3 = (bf16[384,8192]{1,0:T(8,128)(2,1)}, bf16[384,8192]{1,0:T(8,128)(2,1)S(1)}, u32[]{:S(2)}) copy-start(bf16[384,8192]{1,0:T(8,128)(2,1)S(1)} %fusion.31) | copy-start | bytes 18874372

commit v8 on v6

--- a/solution.py
+++ b/solution.py
@@ -141,7 +141,7 @@
     weight_pieces = relay_gather(frozen_value_weight, members, groups, me, dp_index)
     if weight_pieces and len(weight_pieces[0]) == 2:
         weight_pieces = [(source, 0, value) for source, value in weight_pieces]
-    last_pieces = tuple(value for _, _, value in weight_pieces[-4:])
+    last_pieces = tuple(value for _, _, value in weight_pieces[-4:-2])
     grad_sum = pair_sums[0]
     for index, step in enumerate(even_steps):
         sent = pair_sums[index + 1].astype(jnp.bfloat16)

time: 132 us -> 135 us (1.023)
  local copies, waits for them, and re-layouts: 8.32 us -> 11 us
    unnamed x38, local copies, waits for them, and re-layouts: 1.86 us -> 4.55 us
  transfers between devices with their start and end apart: 20 -> 20, of which waited for: 5 -> 5; matrix products, arithmetic and copies ran while one was open for 41% -> 38% of each run, Pallas kernels for 0% -> 0%
where the time goes in v8:
time: 135 us; the launch traced here: 134 us
  matrix products  41.6 us (31%)
  waiting for transfers between devices  37.4 us (28%)
  between operations  19 us (14%)
  starting transfers between devices  17 us (13%)
  local copies, waits for them, and re-layouts  11 us (8%)
  other arithmetic  7.79 us (6%)
    dot_general x16, matrix products, on_device(): lax.dot_general(masked_cot, weight_piece, (((1,), (1,)), ((), ())), prefe...  15.2 us
    dot_general x16, matrix products, on_device(): jnp.dot(token_piece, weight_piece, preferred_element_type=jnp.float32)  13.4 us
    ppermute x2, waiting for transfers between devices, relay_gather(): partner = lax.ppermute(first, ('fsdp', 'dp'), partner_pairs)  11.6 us
    ppermute x2, waiting for transfers between devices, relay_gather(): relayed = lax.ppermute(first, ('fsdp', 'dp'), relay_pairs)  9.54 us
    dot_general x16, matrix products, on_device(): jnp.einsum('uio,uof->uif', low_rank_gradient, down_piece, preferred_eleme...  9.36 us
    ppermute x3, waiting for transfers between devices, on_device(): lax.ppermute(sent, 'fsdp', xor_pairs(members, step)).astype(jnp.float32)  8.5 us
    ppermute x3, waiting for transfers between devices, on_device(): by_step[step] = lax.ppermute(own_adapter, 'fsdp', xor_pairs(members, step))  7.79 us
    unnamed x38, local copies, waits for them, and re-layouts  4.55 us
  transfers between devices with their start and end apart: 20, of which 5 were waited for; matrix products, arithmetic and copies ran while one was open for 38% of the time, Pallas kernels for 0%

profile of v8, /device:TPU:0, one launch (start us, length us, event | category | flops | bytes accessed | tf_op | source)
XLA Modules:
  0.0 133.9 jit_solution(13699411964291340561)
XLA Ops:
  0.6 1.0 fusion.136
  1.7 3.0 %collective-permute-start = (bf16[16,9216]{1,0:T(8,128)(2,1)S(1)}, bf16[16,9216]{1,0:T(8,128)(2,1)S(1)}, u32[]{:S(2)}, u32[]{:S(2)}) collective-permute-start(bf16[16,9216]{1,0:T(8,128)(2,1)S(1)} %get-tuple-element.28), channel_id=1, source_target_pairs={{0,8},{4,12},{8,0},{12,4},{16,24},{20,28},{24,16},{28,20},{1,9},{5... | collective-permute-start | bytes 884744 | tf_op jit(solution)/shard_map/ppermute | solution.py:91
  4.7 1.5 %collective-permute-start.1 = (bf16[16,9216]{1,0:T(8,128)(2,1)S(1)}, bf16[16,9216]{1,0:T(8,128)(2,1)S(1)}, u32[]{:S(2)}, u32[]{:S(2)}) collective-permute-start(bf16[16,9216]{1,0:T(8,128)(2,1)S(1)} %get-tuple-element.28), channel_id=1, source_target_pairs={{0,16},{4,20},{8,24},{12,28},{16,0},{20,4},{24,8},{28,12},{1,17},{... | collective-permute-start | bytes 884744 | tf_op jit(solution)/shard_map/ppermute | solution.py:91
  6.2 3.0 %fusion.143 = (bf16[512,1024]{1,0:T(8,128)(2,1)}, bf16[512,1024]{1,0:T(8,128)(2,1)}) fusion(bf16[1024,1024]{1,0:T(8,128)(2,1)} %param.10), kind=kLoop, calls=%fused_computation.219 | loop fusion | bytes 4194304 | tf_op jit(solution)/shard_map/slice | solution.py:47
  9.3 1.9 %collective-permute-start.6 = (bf16[512,1024]{1,0:T(8,128)(2,1)}, bf16[512,1024]{1,0:T(8,128)(2,1)}, u32[]{:S(2)}, u32[]{:S(2)}) collective-permute-start(bf16[512,1024]{1,0:T(8,128)(2,1)} %get-tuple-element.23), channel_id=1, source_target_pairs={{0,8},{1,17},{2,10},{3,19},{4,20},{5,13},{6,22},{7,15},{8,0},{9,25... | collective-permute-start | bytes 3145736 | tf_op jit(solution)/shard_map/ppermute | solution.py:52
  11.2 0.7 constant_dynamic-update-slice_fusion.3
  12.0 0.6 gather_fusion
  13.2 7.8 %collective-permute-done.1 = bf16[16,9216]{1,0:T(8,128)(2,1)S(1)} collective-permute-done((bf16[16,9216]{1,0:T(8,128)(2,1)S(1)}, bf16[16,9216]{1,0:T(8,128)(2,1)S(1)}, u32[]{:S(2)}, u32[]{:S(2)}) %collective-permute-start.1) | collective-permute-done | bytes 294944 | tf_op jit(solution)/shard_map/ppermute | solution.py:91
  39.6 1.7 %collective-permute-start.7 = (bf16[512,1024]{1,0:T(8,128)(2,1)}, bf16[512,1024]{1,0:T(8,128)(2,1)S(1)}, u32[]{:S(2)}, u32[]{:S(2)}) collective-permute-start(bf16[512,1024]{1,0:T(8,128)(2,1)} %collective-permute-done.6), channel_id=1, source_target_pairs={{0,4},{4,0},{8,12},{12,8},{16,20},{20,16},{24,28},{28,24},{1,5},{5... | collective-permute-start | bytes 3145736 | tf_op jit(solution)/shard_map/ppermute | solution.py:55
  41.3 1.9 %fusion.58 = f32[384,1024]{1,0:T(8,128)S(1)} fusion(bf16[512,1024]{1,0:T(8,128)(2,1)} %collective-permute-done.6, bf16[384,8192]{1,0:T(8,128)(2,1)} %param.8, s32[]{:T(128)S(6)} %select_n.296), kind=kOutput, calls=%fused_computation.113 | convolution fusion | flops 402653184 | bytes 3014660 | tf_op jit(solution)/shard_map/dot_general | solution.py:166
  43.8 2.1 %fusion.60 = f32[384,1024]{1,0:T(8,128)S(1)} fusion(bf16[512,1024]{1,0:T(8,128)(2,1)} %collective-permute-done.5, bf16[384,8192]{1,0:T(8,128)(2,1)} %param.8, s32[]{:T(128)S(6)} %select_n.293), kind=kOutput, calls=%fused_computation.115 | convolution fusion | flops 402653184 | bytes 3014660 | tf_op jit(solution)/shard_map/dot_general | solution.py:166
  45.9 1.1 collective-permute-start.10
  47.5 1.1 copy-done.4
  48.9 1.2 fusion.92
  50.1 1.2 fusion.90
  51.3 0.9 fusion.145
  52.2 1.7 %fusion.32 = bf16[3,16,128]{2,1,0:T(8,128)(2,1)S(1)} fusion(bf16[3,128,8192]{2,1,0:T(8,128)(2,1)S(1)} %bitcast.122, f32[3,128]{1,0:T(4,128)S(1)} %get-tuple-element.30, bf16[3,16,9216]{2,1,0:T(8,128)(2,1)S(1)} %pad_maximum_fusion.4), kind=kOutput, calls=%fused_computation.69 | convolution fusion | flops 100675584 | bytes 7092224 | tf_op jit(solution)/shard_map/cvj,coj->cvo/dot_general | solution.py:111
  54.6 1.2 fusion.98
  55.8 1.2 fusion.96
  57.0 1.2 fusion.94
  61.3 0.7 broadcast_in_dim.44
  62.0 1.8 %fusion.1 = bf16[384,8192]{1,0:T(8,128)(2,1)S(1)} fusion(bf16[384,8192]{1,0:T(8,128)(2,1)S(1)} %broadcast_in_dim.44, s32[]{:T(128)S(6)} %select_n.290, f32[384,512]{1,0:T(8,128)} %bitcast.149, bf16[1024,1024]{1,0:T(8,128)(2,1)S(1)} %copy-done.2, bf16[384,1024]{1,0:T(8,128)(2,1)S(1)} %copy-done.4, f32[384]{0:T(512)S(1)} %get-tuple-element.29), kind=kOutput, calls=%fused_computation.33 | convolution fusion | flops 404226048 | bytes 3016708 | tf_op jit(solution)/shard_map/dot_general | solution.py:170
  63.9 0.6 fusion.3
  65.6 1.9 %convolution_add_fusion.3 = f32[384,1024]{1,0:T(8,128)S(1)} fusion(f32[384,1024]{1,0:T(8,128)S(1)} %convolution_add_fusion.4, bf16[512,1024]{1,0:T(8,128)(2,1)} %collective-permute-done.4, bf16[384,8192]{1,0:T(8,128)(2,1)S(1)} %bitcast.120, s32[]{:T(128)S(6)} %select_n.292), kind=kOutput, calls=%fused_computation.13 | convolution fusion | flops 403046400 | bytes 4587524 | tf_op jit(solution)/shard_map/dot_general | solution.py:166
  67.5 1.9 %fusion.5 = bf16[384,8192]{1,0:T(8,128)(2,1)S(1)} fusion(bf16[384,8192]{1,0:T(8,128)(2,1)S(1)} %fusion.3, s32[]{:T(128)S(6)} %select_n.292, f32[384,512]{1,0:T(8,128)S(1)} %bitcast.147, bf16[512,1024]{1,0:T(8,128)(2,1)} %collective-permute-done.4, bf16[384,1024]{1,0:T(8,128)(2,1)S(1)} %copy-done.4, f32[384]{0:T(512)S(1)} %get-tuple-element.29), kind=kOutput, calls=%fused_computation.37 | convolution fusion | flops 404226048 | bytes 3016708 | tf_op jit(solution)/shard_map/dot_general | solution.py:170
  69.5 2.0 %fusion.7 = bf16[384,8192]{1,0:T(8,128)(2,1)S(1)} fusion(bf16[384,8192]{1,0:T(8,128)(2,1)S(1)} %fusion.5, s32[]{:T(128)S(6)} %select_n.293, f32[384,512]{1,0:T(8,128)S(1)} %bitcast.146, bf16[512,1024]{1,0:T(8,128)(2,1)} %collective-permute-done.5, bf16[384,1024]{1,0:T(8,128)(2,1)S(1)} %copy-done.4, f32[384]{0:T(512)S(1)} %get-tuple-element.29), kind=kOutput, calls=%fused_computation.39 | convolution fusion | flops 404226048 | bytes 3016708 | tf_op jit(solution)/shard_map/dot_general | solution.py:170
  73.8 1.8 %fusion.9 = bf16[384,8192]{1,0:T(8,128)(2,1)S(1)} fusion(bf16[384,8192]{1,0:T(8,128)(2,1)S(1)} %fusion.7, s32[]{:T(128)S(6)} %select_n.296, f32[384,512]{1,0:T(8,128)S(1)} %bitcast.145, bf16[512,1024]{1,0:T(8,128)(2,1)} %collective-permute-done.6, bf16[384,1024]{1,0:T(8,128)(2,1)S(1)} %copy-done.4, f32[384]{0:T(512)S(1)} %get-tuple-element.29), kind=kOutput, calls=%fused_computation.41 | convolution fusion | flops 404226048 | bytes 3016708 | tf_op jit(solution)/shard_map/dot_general | solution.py:170
  79.3 1.3 %collective-permute-start.13 = (bf16[512,1024]{1,0:T(8,128)(2,1)S(1)}, bf16[512,1024]{1,0:T(8,128)(2,1)S(1)}, u32[]{:S(2)}, u32[]{:S(2)}) collective-permute-start(bf16[512,1024]{1,0:T(8,128)(2,1)S(1)} %collective-permute-done.8), channel_id=1, source_target_pairs={{0,16},{1,9},{2,18},{3,11},{4,12},{5,21},{6,14},{7,23},{8,24},{9,1... | collective-permute-start | bytes 3145736 | tf_op jit(solution)/shard_map/ppermute | solution.py:56
  80.6 1.0 collective-permute-start.14
  82.3 0.6 fusion.13
  82.9 0.6 fusion.15
  83.5 0.6 fusion.17
  84.6 9.5 %collective-permute-done.13 = bf16[512,1024]{1,0:T(8,128)(2,1)S(1)} collective-permute-done((bf16[512,1024]{1,0:T(8,128)(2,1)S(1)}, bf16[512,1024]{1,0:T(8,128)(2,1)S(1)}, u32[]{:S(2)}, u32[]{:S(2)}) %collective-permute-start.13) | collective-permute-done | bytes 1048608 | tf_op jit(solution)/shard_map/ppermute | solution.py:56
  94.2 11.6 %collective-permute-done.14 = bf16[512,1024]{1,0:T(8,128)(2,1)S(1)} collective-permute-done((bf16[512,1024]{1,0:T(8,128)(2,1)S(1)}, bf16[512,1024]{1,0:T(8,128)(2,1)S(1)}, u32[]{:S(2)}, u32[]{:S(2)}) %collective-permute-start.14) | collective-permute-done | bytes 1048608 | tf_op jit(solution)/shard_map/ppermute | solution.py:57
  106.2 1.3 collective-permute-start.18
  107.5 1.7 %collective-permute-start.19 = (bf16[16,9216]{1,0:T(8,128)(2,1)S(1)}, bf16[16,9216]{1,0:T(8,128)(2,1)S(1)}, u32[]{:S(2)}, u32[]{:S(2)}) collective-permute-start(bf16[16,9216]{1,0:T(8,128)(2,1)S(1)} %get-tuple-element.11), channel_id=1, source_target_pairs={{0,24},{4,28},{8,16},{12,20},{16,8},{20,12},{24,0},{28,4},{1,25},{... | collective-permute-start | bytes 884744 | tf_op jit(solution)/shard_map/ppermute | solution.py:149
  109.5 0.6 fusion.19
  111.7 4.0 %collective-permute-done.17 = bf16[16,9216]{1,0:T(8,128)(2,1)S(1)} collective-permute-done((bf16[16,9216]{1,0:T(8,128)(2,1)S(1)}, bf16[16,9216]{1,0:T(8,128)(2,1)S(1)}, u32[]{:S(2)}, u32[]{:S(2)}) %collective-permute-start.17) | collective-permute-done | bytes 294944 | tf_op jit(solution)/shard_map/ppermute | solution.py:149
  115.7 4.5 %collective-permute-done.18 = bf16[16,9216]{1,0:T(8,128)(2,1)S(1)} collective-permute-done((bf16[16,9216]{1,0:T(8,128)(2,1)S(1)}, bf16[16,9216]{1,0:T(8,128)(2,1)S(1)}, u32[]{:S(2)}, u32[]{:S(2)}) %collective-permute-start.18) | collective-permute-done | bytes 294944 | tf_op jit(solution)/shard_map/ppermute | solution.py:149
  120.4 0.6 slice_bitcast_fusion.13
  121.0 0.7 slice_bitcast_fusion.12
  124.4 0.8 fusion.21
  125.2 0.6 fusion.23
  125.8 0.6 fusion.25
  126.5 0.6 fusion.27
  128.9 1.0 multiply_convert_fusion.1
  130.6 0.6 fusion.31
  131.2 2.7 %copy-done.3 = bf16[384,8192]{1,0:T(8,128)(2,1)} copy-done((bf16[384,8192]{1,0:T(8,128)(2,1)}, bf16[384,8192]{1,0:T(8,128)(2,1)S(1)}, u32[]{:S(2)}) %copy-start.3) | copy-done | bytes 6291480
  (121 shorter events, 22.0 us)
Async XLA Ops:
  0.6 11.3 %copy-start = (s32[32]{0:T(128)S(1)}, s32[32]{0:T(128)}, u32[]{:S(2)}) copy-start(s32[32]{0:T(128)} %param.15) | copy-start | bytes 388
  1.7 9.6 %copy-start.5 = (bf16[1,16,8192]{2,1,0:T(8,128)(2,1)S(1)}, bf16[1,16,8192]{2,1,0:T(8,128)(2,1)}, u32[]{:S(2)}) copy-start(bf16[1,16,8192]{2,1,0:T(8,128)(2,1)} %param.11) | copy-start | bytes 786436
  1.7 9.5 %copy-start.11 = (bf16[1,16,1024]{2,1,0:T(8,128)(2,1)S(1)}, bf16[1,16,1024]{2,1,0:T(8,128)(2,1)}, u32[]{:S(2)}) copy-start(bf16[1,16,1024]{2,1,0:T(8,128)(2,1)} %param.12) | copy-start | bytes 98308
  1.7 10.3 %copy-start.13 = (s32[3]{0:T(128)S(1)}, s32[3]{0:T(128)}, u32[]{:S(2)}) copy-start(s32[3]{0:T(128)} %param.13) | copy-start | bytes 40
  1.7 10.9 %collective-permute-start = (bf16[16,9216]{1,0:T(8,128)(2,1)S(1)}, bf16[16,9216]{1,0:T(8,128)(2,1)S(1)}, u32[]{:S(2)}, u32[]{:S(2)}) collective-permute-start(bf16[16,9216]{1,0:T(8,128)(2,1)S(1)} %get-tuple-element.28), channel_id=1, source_target_pairs={{0,8},{4,12},{8,0},{12,4},{16,24},{20,28},{24,16},{28,20},{1,9},{5... | collective-permute-start | bytes 884744 | tf_op jit(solution)/shard_map/ppermute | solution.py:91
  4.7 16.3 %collective-permute-start.1 = (bf16[16,9216]{1,0:T(8,128)(2,1)S(1)}, bf16[16,9216]{1,0:T(8,128)(2,1)S(1)}, u32[]{:S(2)}, u32[]{:S(2)}) collective-permute-start(bf16[16,9216]{1,0:T(8,128)(2,1)S(1)} %get-tuple-element.28), channel_id=1, source_target_pairs={{0,16},{4,20},{8,24},{12,28},{16,0},{20,4},{24,8},{28,12},{1,17},{... | collective-permute-start | bytes 884744 | tf_op jit(solution)/shard_map/ppermute | solution.py:91
  6.2 14.7 %collective-permute-start.2 = (bf16[16,9216]{1,0:T(8,128)(2,1)S(1)}, bf16[16,9216]{1,0:T(8,128)(2,1)S(1)}, u32[]{:S(2)}, u32[]{:S(2)}) collective-permute-start(bf16[16,9216]{1,0:T(8,128)(2,1)S(1)} %get-tuple-element.28), channel_id=1, source_target_pairs={{0,24},{4,28},{8,16},{12,20},{16,8},{20,12},{24,0},{28,4},{1,25},{... | collective-permute-start | bytes 884744 | tf_op jit(solution)/shard_map/ppermute | solution.py:91
  9.3 30.1 %copy-start.12 = (s32[3]{0:T(128)S(1)}, s32[3]{0:T(128)}, u32[]{:S(2)}) copy-start(s32[3]{0:T(128)} %param.14) | copy-start | bytes 40
  9.3 30.3 %collective-permute-start.6 = (bf16[512,1024]{1,0:T(8,128)(2,1)}, bf16[512,1024]{1,0:T(8,128)(2,1)}, u32[]{:S(2)}, u32[]{:S(2)}) collective-permute-start(bf16[512,1024]{1,0:T(8,128)(2,1)} %get-tuple-element.23), channel_id=1, source_target_pairs={{0,8},{1,17},{2,10},{3,19},{4,20},{5,13},{6,22},{7,15},{8,0},{9,25... | collective-permute-start | bytes 3145736 | tf_op jit(solution)/shard_map/ppermute | solution.py:52
  11.2 54.3 %collective-permute-start.4 = (bf16[512,1024]{1,0:T(8,128)(2,1)}, bf16[512,1024]{1,0:T(8,128)(2,1)}, u32[]{:S(2)}, u32[]{:S(2)}) collective-permute-start(bf16[512,1024]{1,0:T(8,128)(2,1)} %get-tuple-element.23), channel_id=1, source_target_pairs={{0,4},{4,0},{8,12},{12,8},{16,20},{20,16},{24,28},{28,24},{1,5},{5... | collective-permute-start | bytes 3145736 | tf_op jit(solution)/shard_map/ppermute | solution.py:49
  12.6 30.6 %collective-permute-start.5 = (bf16[512,1024]{1,0:T(8,128)(2,1)}, bf16[512,1024]{1,0:T(8,128)(2,1)}, u32[]{:S(2)}, u32[]{:S(2)}) collective-permute-start(bf16[512,1024]{1,0:T(8,128)(2,1)} %get-tuple-element.8), channel_id=1, source_target_pairs={{0,4},{4,0},{8,12},{12,8},{16,20},{20,16},{24,28},{28,24},{1,5},{5... | collective-permute-start | bytes 3145736 | tf_op jit(solution)/shard_map/ppermute | solution.py:49
  21.1 24.8 %collective-permute-start.3 = (bf16[4,16,9216]{2,1,0:T(8,128)(2,1)S(1)}, bf16[4,16,9216]{2,1,0:T(8,128)(2,1)S(1)}, u32[]{:S(2)}, u32[]{:S(2)}) collective-permute-start(bf16[4,16,9216]{2,1,0:T(8,128)(2,1)S(1)} %pad_maximum_fusion.2), channel_id=1, source_target_pairs={{0,4},{4,0},{8,12},{12,8},{16,20},{20,16},{24,28},{28,24},{1,5},{5... | collective-permute-start | bytes 3538952 | tf_op jit(solution)/shard_map/ppermute | solution.py:93
  39.6 37.4 %collective-permute-start.8 = (bf16[512,1024]{1,0:T(8,128)(2,1)}, bf16[512,1024]{1,0:T(8,128)(2,1)S(1)}, u32[]{:S(2)}, u32[]{:S(2)}) collective-permute-start(bf16[512,1024]{1,0:T(8,128)(2,1)} %get-tuple-element.8), channel_id=1, source_target_pairs={{0,8},{1,17},{2,10},{3,19},{4,20},{5,13},{6,22},{7,15},{8,0},{9,25... | collective-permute-start | bytes 3145736 | tf_op jit(solution)/shard_map/ppermute | solution.py:52
  39.6 36.8 %collective-permute-start.7 = (bf16[512,1024]{1,0:T(8,128)(2,1)}, bf16[512,1024]{1,0:T(8,128)(2,1)S(1)}, u32[]{:S(2)}, u32[]{:S(2)}) collective-permute-start(bf16[512,1024]{1,0:T(8,128)(2,1)} %collective-permute-done.6), channel_id=1, source_target_pairs={{0,4},{4,0},{8,12},{12,8},{16,20},{20,16},{24,28},{28,24},{1,5},{5... | collective-permute-start | bytes 3145736 | tf_op jit(solution)/shard_map/ppermute | solution.py:55
  43.2 3.8 %copy-start.10 = (bf16[8,16,9216]{2,1,0:T(8,128)(2,1)S(1)}, bf16[8,16,9216]{2,1,0:T(8,128)(2,1)}, u32[]{:S(2)}) copy-start(bf16[8,16,9216]{2,1,0:T(8,128)(2,1)} %constant_dynamic-update-slice_fusion.3) | copy-start | bytes 7077892
  43.2 32.4 %collective-permute-start.9 = (bf16[512,1024]{1,0:T(8,128)(2,1)}, bf16[512,1024]{1,0:T(8,128)(2,1)S(1)}, u32[]{:S(2)}, u32[]{:S(2)}) collective-permute-start(bf16[512,1024]{1,0:T(8,128)(2,1)} %collective-permute-done.6), channel_id=1, source_target_pairs={{0,16},{1,9},{2,18},{3,11},{4,12},{5,21},{6,14},{7,23},{8,24},{9,1... | collective-permute-start | bytes 3145736 | tf_op jit(solution)/shard_map/ppermute | solution.py:56
  43.8 7.5 %slice-start = ((s8[6291456]{0:T(1024)(128)(4,1)}), s8[4194304]{0:T(1024)(128)(4,1)S(1)}, s32[]{:S(2)}) async-start(s8[6291456]{0:T(1024)(128)(4,1)} %bitcast.119), calls=%async_computation | async-start | bytes 8388608
  45.9 29.8 %collective-permute-start.10 = (bf16[512,1024]{1,0:T(8,128)(2,1)}, bf16[512,1024]{1,0:T(8,128)(2,1)S(1)}, u32[]{:S(2)}, u32[]{:S(2)}) collective-permute-start(bf16[512,1024]{1,0:T(8,128)(2,1)} %collective-permute-done.6), channel_id=1, source_target_pairs={{0,1},{1,0},{2,3},{3,2},{4,5},{5,4},{6,7},{7,6},{8,9},{9,8},{10,11... | collective-permute-start | bytes 3145736 | tf_op jit(solution)/shard_map/ppermute | solution.py:57
  47.2 4.1 %slice-start.1 = ((s8[6291456]{0:T(1024)(128)(4,1)}), s8[2097152]{0:T(1024)(128)(4,1)S(1)}, s32[]{:S(2)}) async-start(s8[6291456]{0:T(1024)(128)(4,1)} %bitcast.119), calls=%async_computation.1 | async-start | bytes 4194304
  47.3 1.3 copy-start.4
  58.5 1.6 %copy-start.2 = (bf16[1024,1024]{1,0:T(8,128)(2,1)S(1)}, bf16[1024,1024]{1,0:T(8,128)(2,1)}, u32[]{:S(2)}) copy-start(bf16[1024,1024]{1,0:T(8,128)(2,1)} %param.10) | copy-start | bytes 6291460
  62.0 1.8 %copy-start.9 = (f32[3,128,512]{2,1,0:T(8,128)S(1)}, f32[3,128,512]{2,1,0:T(8,128)}, u32[]{:S(2)}) copy-start(f32[3,128,512]{2,1,0:T(8,128)} %fusion.96) | copy-start | bytes 2359300
  65.5 2.0 %copy-start.8 = (f32[3,128,512]{2,1,0:T(8,128)S(1)}, f32[3,128,512]{2,1,0:T(8,128)}, u32[]{:S(2)}) copy-start(f32[3,128,512]{2,1,0:T(8,128)} %fusion.94) | copy-start | bytes 2359300
  65.5 18.6 %collective-permute-start.16 = (bf16[4,16,9216]{2,1,0:T(8,128)(2,1)S(1)}, bf16[4,16,9216]{2,1,0:T(8,128)(2,1)S(1)}, u32[]{:S(2)}, u32[]{:S(2)}) collective-permute-start(bf16[4,16,9216]{2,1,0:T(8,128)(2,1)S(1)} %pad_maximum_fusion.3), channel_id=1, source_target_pairs={{0,4},{4,0},{8,12},{12,8},{16,20},{20,16},{24,28},{28,24},{1,5},{5... | collective-permute-start | bytes 3538952 | tf_op jit(solution)/shard_map/ppermute | solution.py:136
  67.5 1.9 %copy-start.7 = (f32[3,128,512]{2,1,0:T(8,128)S(1)}, f32[3,128,512]{2,1,0:T(8,128)}, u32[]{:S(2)}) copy-start(f32[3,128,512]{2,1,0:T(8,128)} %fusion.92) | copy-start | bytes 2359300
  72.7 1.1 copy-start.6
  75.9 45.9 %collective-permute-start.12 = (bf16[2,512,1024]{2,1,0:T(8,128)(2,1)S(1)}, bf16[2,512,1024]{2,1,0:T(8,128)(2,1)S(1)}, u32[]{:S(2)}, u32[]{:S(2)}) collective-permute-start(bf16[2,512,1024]{2,1,0:T(8,128)(2,1)S(1)} %pad_maximum_fusion), channel_id=1, source_target_pairs={{0,4},{4,0},{8,12},{12,8},{16,20},{20,16},{24,28},{28,24},{1,5},{5... | collective-permute-start | bytes 6291464 | tf_op jit(solution)/shard_map/ppermute | solution.py:60
  79.3 14.9 %collective-permute-start.13 = (bf16[512,1024]{1,0:T(8,128)(2,1)S(1)}, bf16[512,1024]{1,0:T(8,128)(2,1)S(1)}, u32[]{:S(2)}, u32[]{:S(2)}) collective-permute-start(bf16[512,1024]{1,0:T(8,128)(2,1)S(1)} %collective-permute-done.8), channel_id=1, source_target_pairs={{0,16},{1,9},{2,18},{3,11},{4,12},{5,21},{6,14},{7,23},{8,24},{9,1... | collective-permute-start | bytes 3145736 | tf_op jit(solution)/shard_map/ppermute | solution.py:56
  80.6 25.1 %collective-permute-start.14 = (bf16[512,1024]{1,0:T(8,128)(2,1)S(1)}, bf16[512,1024]{1,0:T(8,128)(2,1)S(1)}, u32[]{:S(2)}, u32[]{:S(2)}) collective-permute-start(bf16[512,1024]{1,0:T(8,128)(2,1)S(1)} %collective-permute-done.8), channel_id=1, source_target_pairs={{0,1},{1,0},{2,3},{3,2},{4,5},{5,4},{6,7},{7,6},{8,9},{9,8},{10,11... | collective-permute-start | bytes 3145736 | tf_op jit(solution)/shard_map/ppermute | solution.py:57
  81.7 27.8 %collective-permute-start.11 = (bf16[512,1024]{1,0:T(8,128)(2,1)S(1)}, bf16[512,1024]{1,0:T(8,128)(2,1)S(1)}, u32[]{:S(2)}, u32[]{:S(2)}) collective-permute-start(bf16[512,1024]{1,0:T(8,128)(2,1)S(1)} %collective-permute-done.8), channel_id=1, source_target_pairs={{0,4},{4,0},{8,12},{12,8},{16,20},{20,16},{24,28},{28,24},{1,5},{5... | collective-permute-start | bytes 3145736 | tf_op jit(solution)/shard_map/ppermute | solution.py:55
  105.7 9.9 %collective-permute-start.17 = (bf16[16,9216]{1,0:T(8,128)(2,1)S(1)}, bf16[16,9216]{1,0:T(8,128)(2,1)S(1)}, u32[]{:S(2)}, u32[]{:S(2)}) collective-permute-start(bf16[16,9216]{1,0:T(8,128)(2,1)S(1)} %get-tuple-element.9), channel_id=1, source_target_pairs={{0,8},{4,12},{8,0},{12,4},{16,24},{20,28},{24,16},{28,20},{1,9},{5... | collective-permute-start | bytes 884744 | tf_op jit(solution)/shard_map/ppermute | solution.py:149
  106.2 13.9 %collective-permute-start.18 = (bf16[16,9216]{1,0:T(8,128)(2,1)S(1)}, bf16[16,9216]{1,0:T(8,128)(2,1)S(1)}, u32[]{:S(2)}, u32[]{:S(2)}) collective-permute-start(bf16[16,9216]{1,0:T(8,128)(2,1)S(1)} %get-tuple-element.10), channel_id=1, source_target_pairs={{0,16},{4,20},{8,24},{12,28},{16,0},{20,4},{24,8},{28,12},{1,17},{... | collective-permute-start | bytes 884744 | tf_op jit(solution)/shard_map/ppermute | solution.py:149
  107.5 12.6 %collective-permute-start.19 = (bf16[16,9216]{1,0:T(8,128)(2,1)S(1)}, bf16[16,9216]{1,0:T(8,128)(2,1)S(1)}, u32[]{:S(2)}, u32[]{:S(2)}) collective-permute-start(bf16[16,9216]{1,0:T(8,128)(2,1)S(1)} %get-tuple-element.11), channel_id=1, source_target_pairs={{0,24},{4,28},{8,16},{12,20},{16,8},{20,12},{24,0},{28,4},{1,25},{... | collective-permute-start | bytes 884744 | tf_op jit(solution)/shard_map/ppermute | solution.py:149
  109.4 17.7 %collective-permute-start.15 = (bf16[2,512,1024]{2,1,0:T(8,128)(2,1)S(1)}, bf16[2,512,1024]{2,1,0:T(8,128)(2,1)S(1)}, u32[]{:S(2)}, u32[]{:S(2)}) collective-permute-start(bf16[2,512,1024]{2,1,0:T(8,128)(2,1)S(1)} %pad_maximum_fusion.1), channel_id=1, source_target_pairs={{0,4},{4,0},{8,12},{12,8},{16,20},{20,16},{24,28},{28,24},{1,5},{5... | collective-permute-start | bytes 6291464 | tf_op jit(solution)/shard_map/ppermute | solution.py:60
  129.9 4.0 %copy-start.1 = (s32[32]{0:T(128)S(1)}, s32[32]{0:T(128)}, u32[]{:S(2)}) copy-start(s32[32]{0:T(128)} %param.15) | copy-start | bytes 388
  131.2 2.7 %copy-start.3 = (bf16[384,8192]{1,0:T(8,128)(2,1)}, bf16[384,8192]{1,0:T(8,128)(2,1)S(1)}, u32[]{:S(2)}) copy-start(bf16[384,8192]{1,0:T(8,128)(2,1)S(1)} %fusion.31) | copy-start | bytes 18874372

commit v9 on v6

--- a/solution.py
+++ b/solution.py
@@ -4,7 +4,6 @@
 from jax.sharding import PartitionSpec as P
 
 ADAPTER_SCALE = 2.0
-WEIGHT_CHUNKS = 2
 
 
 def xor_pairs(count, step):
@@ -40,26 +39,26 @@
     sources = [me, me ^ (2 + 2 * role), me ^ 6, me ^ (4 - 2 * role)]
     sibling_sources = [sibling, sibling ^ (2 + 2 * sibling_role), sibling ^ 6,
                        sibling ^ (4 - 2 * sibling_role)]
-    rows = shard.shape[0] // WEIGHT_CHUNKS
+    bounds = [0, shard.shape[0] // 4, shard.shape[0]]
     result = []
     previous = None
-    for k in range(WEIGHT_CHUNKS):
-        piece = shard[k * rows:(k + 1) * rows]
-        result.append((0.0, sources[0], k, piece))
-        result.append((1.0, sibling_sources[0], k, lax.ppermute(piece, "fsdp", xor_pairs(members, 1))))
+    for k in range(len(bounds) - 1):
+        piece = shard[bounds[k]:bounds[k + 1]]
+        result.append((0.0, sources[0], bounds[k], piece))
+        result.append((1.0, sibling_sources[0], bounds[k], lax.ppermute(piece, "fsdp", xor_pairs(members, 1))))
         if previous is not None:
             piece, _ = lax.optimization_barrier((piece, previous))
         first = lax.ppermute(piece, ("fsdp", "dp"), first_pairs)
         previous = first
-        result.append((2.0 + 2 * k, sources[1], k, first))
-        result.append((3.0 + 2 * k, sibling_sources[1], k, lax.ppermute(first, "fsdp", xor_pairs(members, 1))))
+        result.append((2.0 + 2 * k, sources[1], bounds[k], first))
+        result.append((3.0 + 2 * k, sibling_sources[1], bounds[k], lax.ppermute(first, "fsdp", xor_pairs(members, 1))))
         relayed = lax.ppermute(first, ("fsdp", "dp"), relay_pairs)
         partner = lax.ppermute(first, ("fsdp", "dp"), partner_pairs)
-        result.append((4.5 + 2 * k, sources[2], k, relayed))
-        result.append((4.5 + 2 * k, sources[3], k, partner))
+        result.append((4.5 + 2 * k, sources[2], bounds[k], relayed))
+        result.append((4.5 + 2 * k, sources[3], bounds[k], partner))
         late = lax.ppermute(jnp.stack([relayed, partner]), "fsdp", xor_pairs(members, 1))
-        result.append((5.5 + 2 * k, sibling_sources[2], k, late[0]))
-        result.append((5.5 + 2 * k, sibling_sources[3], k, late[1]))
+        result.append((5.5 + 2 * k, sibling_sources[2], bounds[k], late[0]))
+        result.append((5.5 + 2 * k, sibling_sources[3], bounds[k], late[1]))
     result.sort(key=lambda item: item[0])
     return [item[1:] for item in result]
 
@@ -161,7 +160,7 @@
     token_gradient = jnp.zeros((tok_rows, model_width), jnp.bfloat16)
     for source, chunk, weight_piece in weight_pieces:
         piece_rows = weight_piece.shape[0]
-        column = source * shard_rows + chunk * piece_rows
+        column = source * shard_rows + chunk
         token_piece = lax.dynamic_slice_in_dim(tokens, column, piece_rows, axis=1)
         output_total = lax.optimization_barrier(output_total + jnp.dot(
             token_piece, weight_piece, preferred_element_type=jnp.float32

time: 132 us -> 161 us (1.22)
  matrix products: 41.6 us -> 52.4 us
  waiting for transfers between devices: 37.3 us -> 44.7 us
  local copies, waits for them, and re-layouts: 8.32 us -> 14.1 us
  other arithmetic: 7.81 us -> 11.6 us
    dot_general x16, matrix products: 13.4 us -> 18.7 us  [on_device(): jnp.dot(token_piece, weight_piece, preferred_element_type=jnp.float32)]
    ppermute x2, waiting for transfers between devices: 11.6 us -> 16.6 us  [relay_gather(): partner = lax.ppermute(first, ('fsdp', 'dp'), partner_pairs)]
    unnamed x38 -> x50, local copies, waits for them, and re-layouts: 1.86 us -> 6.47 us
    dot_general x16, matrix products: 15.3 us -> 19.7 us  [on_device(): lax.dot_general(masked_cot, weight_piece, (((1,), (1,)), ((), ())), prefe...]
    ppermute x2, waiting for transfers between devices: 9.54 us -> 11.5 us  [relay_gather(): relayed = lax.ppermute(first, ('fsdp', 'dp'), relay_pairs)]
    ppermute x2, starting transfers between devices: 1.72 us -> 0.07 us  [relay_gather(): lax.ppermute(first, 'fsdp', xor_pairs(members, 1))]
    ppermute x2, waiting for transfers between devices: 0.01 us -> 1.65 us  [relay_gather(): first = lax.ppermute(piece, ('fsdp', 'dp'), first_pairs)]
  transfers between devices with their start and end apart: 20 -> 20, of which waited for: 5 -> 6; matrix products, arithmetic and copies ran while one was open for 41% -> 45% of each run, Pallas kernels for 0% -> 0%
where the time goes in v9:
time: 161 us; the launch traced here: 160 us
  matrix products  52.4 us (33%)
  waiting for transfers between devices  44.7 us (28%)
  between operations  18.7 us (12%)
  starting transfers between devices  18 us (11%)
  local copies, waits for them, and re-layouts  14.1 us (9%)
  other arithmetic  11.6 us (7%)
    dot_general x16, matrix products, on_device(): lax.dot_general(masked_cot, weight_piece, (((1,), (1,)), ((), ())), prefe...  19.7 us
    dot_general x16, matrix products, on_device(): jnp.dot(token_piece, weight_piece, preferred_element_type=jnp.float32)  18.7 us
    ppermute x2, waiting for transfers between devices, relay_gather(): partner = lax.ppermute(first, ('fsdp', 'dp'), partner_pairs)  16.6 us
    ppermute x2, waiting for transfers between devices, relay_gather(): relayed = lax.ppermute(first, ('fsdp', 'dp'), relay_pairs)  11.5 us
    dot_general x16, matrix products, on_device(): jnp.einsum('uio,uof->uif', low_rank_gradient, down_piece, preferred_eleme...  10.4 us
    ppermute x3, waiting for transfers between devices, on_device(): by_step[step] = lax.ppermute(own_adapter, 'fsdp', xor_pairs(members, step))  7.79 us
    ppermute x3, waiting for transfers between devices, on_device(): lax.ppermute(sent, 'fsdp', xor_pairs(members, step)).astype(jnp.float32)  7.17 us
    unnamed x50, local copies, waits for them, and re-layouts  6.47 us
  transfers between devices with their start and end apart: 20, of which 6 were waited for; matrix products, arithmetic and copies ran while one was open for 45% of the time, Pallas kernels for 0%

profile of v9, /device:TPU:0, one launch (start us, length us, event | category | flops | bytes accessed | tf_op | source)
XLA Modules:
  0.0 159.5 jit_solution(1192038311471357406)
XLA Ops:
  0.7 1.9 %fusion.138 = (bf16[1,16,9216]{2,1,0:T(8,128)(2,1)S(1)}, bf16[16,9216]{1,0:T(8,128)(2,1)}) fusion(bf16[16,1024]{1,0:T(8,128)(2,1)} %bitcast.150, bf16[16,8192]{1,0:T(8,128)(2,1)} %bitcast.140), kind=kLoop, calls=%fused_computation.216 | loop fusion | flops 589824 | bytes 884736 | tf_op jit(solution)/shard_map/stack | solution.py:95
  2.6 2.9 %collective-permute-start = (bf16[16,9216]{1,0:T(8,128)(2,1)}, bf16[16,9216]{1,0:T(8,128)(2,1)S(1)}, u32[]{:S(2)}, u32[]{:S(2)}) collective-permute-start(bf16[16,9216]{1,0:T(8,128)(2,1)} %get-tuple-element.28), channel_id=1, source_target_pairs={{0,8},{4,12},{8,0},{12,4},{16,24},{20,28},{24,16},{28,20},{1,9},{5... | collective-permute-start | bytes 884744 | tf_op jit(solution)/shard_map/ppermute | solution.py:90
  5.5 1.5 collective-permute-start.1
  7.0 1.9 %slice.57 = bf16[256,1024]{1,0:T(8,128)(2,1)} slice(bf16[1024,1024]{1,0:T(8,128)(2,1)} %param.10), slice={[0:256], [0:1024]} | slice | bytes 1048576 | tf_op jit(solution)/shard_map/slice | solution.py:46
  8.9 2.0 %collective-permute-start.6 = (bf16[256,1024]{1,0:T(8,128)(2,1)}, bf16[256,1024]{1,0:T(8,128)(2,1)}, u32[]{:S(2)}, u32[]{:S(2)}) collective-permute-start(bf16[256,1024]{1,0:T(8,128)(2,1)} %slice.57), channel_id=1, source_target_pairs={{0,8},{1,17},{2,10},{3,19},{4,20},{5,13},{6,22},{7,15},{8,0},{9,25... | collective-permute-start | bytes 1572872 | tf_op jit(solution)/shard_map/ppermute | solution.py:51
  11.6 1.3 slice.58
  14.2 7.8 %collective-permute-done.1 = bf16[16,9216]{1,0:T(8,128)(2,1)S(1)} collective-permute-done((bf16[16,9216]{1,0:T(8,128)(2,1)}, bf16[16,9216]{1,0:T(8,128)(2,1)S(1)}, u32[]{:S(2)}, u32[]{:S(2)}) %collective-permute-start.1) | collective-permute-done | bytes 294944 | tf_op jit(solution)/shard_map/ppermute | solution.py:90
  22.0 1.2 pad_maximum_fusion.1
  23.2 1.6 %collective-permute-done.6 = bf16[256,1024]{1,0:T(8,128)(2,1)} collective-permute-done((bf16[256,1024]{1,0:T(8,128)(2,1)}, bf16[256,1024]{1,0:T(8,128)(2,1)}, u32[]{:S(2)}, u32[]{:S(2)}) %collective-permute-start.6) | collective-permute-done | bytes 524320 | tf_op jit(solution)/shard_map/ppermute | solution.py:51
  24.8 1.8 %collective-permute-start.9 = (bf16[256,1024]{1,0:T(8,128)(2,1)}, bf16[256,1024]{1,0:T(8,128)(2,1)S(1)}, u32[]{:S(2)}, u32[]{:S(2)}) collective-permute-start(bf16[256,1024]{1,0:T(8,128)(2,1)} %collective-permute-done.6), channel_id=1, source_target_pairs={{0,16},{1,9},{2,18},{3,11},{4,12},{5,21},{6,14},{7,23},{8,24},{9,1... | collective-permute-start | bytes 1572872 | tf_op jit(solution)/shard_map/ppermute | solution.py:55
  26.6 1.8 %collective-permute-start.10 = (bf16[256,1024]{1,0:T(8,128)(2,1)}, bf16[256,1024]{1,0:T(8,128)(2,1)S(1)}, u32[]{:S(2)}, u32[]{:S(2)}) collective-permute-start(bf16[256,1024]{1,0:T(8,128)(2,1)} %collective-permute-done.6), channel_id=1, source_target_pairs={{0,1},{1,0},{2,3},{3,2},{4,5},{5,4},{6,7},{7,6},{8,9},{9,8},{10,11... | collective-permute-start | bytes 1572872 | tf_op jit(solution)/shard_map/ppermute | solution.py:56
  46.3 1.6 %fusion.64 = f32[384,1024]{1,0:T(8,128)S(1)} fusion(bf16[256,1024]{1,0:T(8,128)(2,1)} %collective-permute-done.6, bf16[384,8192]{1,0:T(8,128)(2,1)} %param.8, s32[]{:T(128)S(6)} %select_n.296), kind=kOutput, calls=%fused_computation.125 | convolution fusion | flops 201326592 | bytes 2293764 | tf_op jit(solution)/shard_map/dot_general | solution.py:165
  47.9 1.6 collective-permute-start.8
  49.5 1.1 pad_maximum_fusion.3
  50.6 1.5 fusion.60
  53.7 1.0 slice_dynamic-update-slice_fusion.2
  57.0 1.1 copy-done.4
  59.9 1.7 %fusion.32 = bf16[3,16,128]{2,1,0:T(8,128)(2,1)S(1)} fusion(bf16[3,128,8192]{2,1,0:T(8,128)(2,1)S(1)} %bitcast.122, f32[3,128]{1,0:T(4,128)S(1)} %get-tuple-element.30, bf16[3,16,9216]{2,1,0:T(8,128)(2,1)S(1)} %pad_maximum_fusion.4), kind=kOutput, calls=%fused_computation.70 | convolution fusion | flops 100675584 | bytes 7092224 | tf_op jit(solution)/shard_map/cvj,coj->cvo/dot_general | solution.py:110
  62.3 1.0 fusion.98
  63.3 1.4 fusion.82
  64.7 1.0 fusion.96
  65.7 1.5 fusion.80
  67.2 1.0 fusion.92
  68.2 1.4 fusion.78
  73.4 1.4 fusion.17
  75.4 1.2 pad_maximum_fusion.2
  78.1 1.6 %fusion.19 = bf16[384,8192]{1,0:T(8,128)(2,1)S(1)} fusion(bf16[384,8192]{1,0:T(8,128)(2,1)S(1)} %fusion.1, s32[]{:T(128)S(6)} %select_n.292, f32[384,256]{1,0:T(8,128)S(1)} %bitcast.148, bf16[256,1024]{1,0:T(8,128)(2,1)} %collective-permute-done.4, bf16[384,1024]{1,0:T(8,128)(2,1)S(1)} %copy-done.4, f32[384]{0:T(512)S(1)} %get-tuple-element.29), kind=kOutput, calls=%fused_computation.54 | convolution fusion | flops 202702848 | bytes 1902596 | tf_op jit(solution)/shard_map/dot_general | solution.py:169
  79.7 1.4 convolution_add_fusion.4
  81.4 2.2 %fusion.50 = f32[384,1024]{1,0:T(8,128)S(1)} fusion(bf16[768,1024]{1,0:T(8,128)(2,1)} %collective-permute-done.5, bf16[384,8192]{1,0:T(8,128)(2,1)S(1)} %bitcast.120, s32[]{:T(128)S(6)} %select_n.293), kind=kOutput, calls=%fused_computation.103 | convolution fusion | flops 603979776 | bytes 3735556 | tf_op jit(solution)/shard_map/dot_general | solution.py:165
  84.2 1.5 convolution_add_fusion.3
  85.8 2.2 %fusion.3 = bf16[384,8192]{1,0:T(8,128)(2,1)S(1)} fusion(bf16[384,8192]{1,0:T(8,128)(2,1)S(1)} %fusion.19, s32[]{:T(128)S(6)} %select_n.293, f32[384,768]{1,0:T(8,128)S(1)} %bitcast.138, bf16[768,1024]{1,0:T(8,128)(2,1)} %collective-permute-done.5, bf16[384,1024]{1,0:T(8,128)(2,1)S(1)} %copy-done.4, f32[384]{0:T(512)S(1)} %get-tuple-element.29), kind=kOutput, calls=%fused_computation.28 | convolution fusion | flops 605749248 | bytes 4130820 | tf_op jit(solution)/shard_map/dot_general | solution.py:169
  88.0 1.5 fusion.21
  89.6 1.5 fusion.23
  91.1 2.2 %fusion.48 = f32[384,1024]{1,0:T(8,128)S(1)} fusion(bf16[768,1024]{1,0:T(8,128)(2,1)} %collective-permute-done.8, bf16[384,8192]{1,0:T(8,128)(2,1)S(1)} %bitcast.120, s32[]{:T(128)S(6)} %select_n.298), kind=kOutput, calls=%fused_computation.101 | convolution fusion | flops 603979776 | bytes 3735556 | tf_op jit(solution)/shard_map/dot_general | solution.py:165
  93.6 1.6 collective-permute-start.13
  96.8 2.2 %fusion.5 = bf16[384,8192]{1,0:T(8,128)(2,1)S(1)} fusion(bf16[384,8192]{1,0:T(8,128)(2,1)S(1)} %fusion.23, s32[]{:T(128)S(6)} %select_n.298, f32[384,768]{1,0:T(8,128)S(1)} %bitcast.137, bf16[768,1024]{1,0:T(8,128)(2,1)} %collective-permute-done.8, bf16[384,1024]{1,0:T(8,128)(2,1)S(1)} %copy-done.4, f32[384]{0:T(512)S(1)} %get-tuple-element.29), kind=kOutput, calls=%fused_computation.30 | convolution fusion | flops 605749248 | bytes 4130820 | tf_op jit(solution)/shard_map/dot_general | solution.py:169
  99.9 1.4 fusion.53
  101.4 1.4 fusion.54
  102.8 11.5 %collective-permute-done.13 = bf16[768,1024]{1,0:T(8,128)(2,1)S(1)} collective-permute-done((bf16[768,1024]{1,0:T(8,128)(2,1)}, bf16[768,1024]{1,0:T(8,128)(2,1)S(1)}, u32[]{:S(2)}, u32[]{:S(2)}) %collective-permute-start.13) | collective-permute-done | bytes 1572896 | tf_op jit(solution)/shard_map/ppermute | solution.py:55
  114.3 16.6 %collective-permute-done.14 = bf16[768,1024]{1,0:T(8,128)(2,1)S(1)} collective-permute-done((bf16[768,1024]{1,0:T(8,128)(2,1)}, bf16[768,1024]{1,0:T(8,128)(2,1)S(1)}, u32[]{:S(2)}, u32[]{:S(2)}) %collective-permute-start.14) | collective-permute-done | bytes 1572896 | tf_op jit(solution)/shard_map/ppermute | solution.py:56
  136.0 1.5 fusion.29
  137.5 1.5 fusion.31
  139.0 1.1 fusion.9
  140.9 1.5 collective-permute-start.17
  142.5 1.2 collective-permute-start.18
  148.4 1.3 copy-done.3
  149.7 1.0 multiply_convert_fusion.1
  150.8 7.1 %collective-permute-done.18 = bf16[16,9216]{1,0:T(8,128)(2,1)S(1)} collective-permute-done((bf16[16,9216]{1,0:T(8,128)(2,1)S(1)}, bf16[16,9216]{1,0:T(8,128)(2,1)S(1)}, u32[]{:S(2)}, u32[]{:S(2)}) %collective-permute-start.18) | collective-permute-done | bytes 294944 | tf_op jit(solution)/shard_map/ppermute | solution.py:148
  (134 shorter events, 30.6 us)
Async XLA Ops:
  0.6 12.3 %copy-start = (s32[32]{0:T(128)S(1)}, s32[32]{0:T(128)}, u32[]{:S(2)}) copy-start(s32[32]{0:T(128)} %param.15) | copy-start | bytes 388
  0.6 10.2 %copy-start.13 = (bf16[1,16,8192]{2,1,0:T(8,128)(2,1)S(1)}, bf16[1,16,8192]{2,1,0:T(8,128)(2,1)}, u32[]{:S(2)}) copy-start(bf16[1,16,8192]{2,1,0:T(8,128)(2,1)} %param.11) | copy-start | bytes 786436
  0.7 10.2 %copy-start.17 = (bf16[1,16,1024]{2,1,0:T(8,128)(2,1)S(1)}, bf16[1,16,1024]{2,1,0:T(8,128)(2,1)}, u32[]{:S(2)}) copy-start(bf16[1,16,1024]{2,1,0:T(8,128)(2,1)} %param.12) | copy-start | bytes 98308
  0.7 11.0 %copy-start.2 = (bf16[1024,1024]{1,0:T(8,128)(2,1)S(1)}, bf16[1024,1024]{1,0:T(8,128)(2,1)}, u32[]{:S(2)}) copy-start(bf16[1024,1024]{1,0:T(8,128)(2,1)} %param.10) | copy-start | bytes 6291460
  2.6 11.1 %collective-permute-start = (bf16[16,9216]{1,0:T(8,128)(2,1)}, bf16[16,9216]{1,0:T(8,128)(2,1)S(1)}, u32[]{:S(2)}, u32[]{:S(2)}) collective-permute-start(bf16[16,9216]{1,0:T(8,128)(2,1)} %get-tuple-element.28), channel_id=1, source_target_pairs={{0,8},{4,12},{8,0},{12,4},{16,24},{20,28},{24,16},{28,20},{1,9},{5... | collective-permute-start | bytes 884744 | tf_op jit(solution)/shard_map/ppermute | solution.py:90
  5.5 16.5 %collective-permute-start.1 = (bf16[16,9216]{1,0:T(8,128)(2,1)}, bf16[16,9216]{1,0:T(8,128)(2,1)S(1)}, u32[]{:S(2)}, u32[]{:S(2)}) collective-permute-start(bf16[16,9216]{1,0:T(8,128)(2,1)} %get-tuple-element.28), channel_id=1, source_target_pairs={{0,16},{4,20},{8,24},{12,28},{16,0},{20,4},{24,8},{28,12},{1,17},{... | collective-permute-start | bytes 884744 | tf_op jit(solution)/shard_map/ppermute | solution.py:90
  7.0 14.9 %collective-permute-start.2 = (bf16[16,9216]{1,0:T(8,128)(2,1)}, bf16[16,9216]{1,0:T(8,128)(2,1)S(1)}, u32[]{:S(2)}, u32[]{:S(2)}) collective-permute-start(bf16[16,9216]{1,0:T(8,128)(2,1)} %get-tuple-element.28), channel_id=1, source_target_pairs={{0,24},{4,28},{8,16},{12,20},{16,8},{20,12},{24,0},{28,4},{1,25},{... | collective-permute-start | bytes 884744 | tf_op jit(solution)/shard_map/ppermute | solution.py:90
  8.9 15.9 %collective-permute-start.6 = (bf16[256,1024]{1,0:T(8,128)(2,1)}, bf16[256,1024]{1,0:T(8,128)(2,1)}, u32[]{:S(2)}, u32[]{:S(2)}) collective-permute-start(bf16[256,1024]{1,0:T(8,128)(2,1)} %slice.57), channel_id=1, source_target_pairs={{0,8},{1,17},{2,10},{3,19},{4,20},{5,13},{6,22},{7,15},{8,0},{9,25... | collective-permute-start | bytes 1572872 | tf_op jit(solution)/shard_map/ppermute | solution.py:51
  10.9 67.0 %collective-permute-start.4 = (bf16[256,1024]{1,0:T(8,128)(2,1)}, bf16[256,1024]{1,0:T(8,128)(2,1)}, u32[]{:S(2)}, u32[]{:S(2)}) collective-permute-start(bf16[256,1024]{1,0:T(8,128)(2,1)} %slice.57), channel_id=1, source_target_pairs={{0,4},{4,0},{8,12},{12,8},{16,20},{20,16},{24,28},{28,24},{1,5},{5... | collective-permute-start | bytes 1572872 | tf_op jit(solution)/shard_map/ppermute | solution.py:48
  11.6 1.3 copy-start.19
  11.6 2.0 %copy-start.18 = (s32[3]{0:T(128)S(1)}, s32[3]{0:T(128)}, u32[]{:S(2)}) copy-start(s32[3]{0:T(128)} %param.14) | copy-start | bytes 40
  13.7 9.5 %copy-start.8 = (bf16[16,9216]{1,0:T(8,128)(2,1)}, bf16[16,9216]{1,0:T(8,128)(2,1)S(1)}, u32[]{:S(2)}) copy-start(bf16[16,9216]{1,0:T(8,128)(2,1)S(1)} %collective-permute-done) | copy-start | bytes 884740
  13.7 67.7 %collective-permute-start.5 = (bf16[768,1024]{1,0:T(8,128)(2,1)}, bf16[768,1024]{1,0:T(8,128)(2,1)}, u32[]{:S(2)}, u32[]{:S(2)}) collective-permute-start(bf16[768,1024]{1,0:T(8,128)(2,1)} %slice.58), channel_id=1, source_target_pairs={{0,4},{4,0},{8,12},{12,8},{16,20},{20,16},{24,28},{28,24},{1,5},{5... | collective-permute-start | bytes 4718600 | tf_op jit(solution)/shard_map/ppermute | solution.py:48
  22.0 1.2 copy-start.6
  23.1 28.9 %collective-permute-start.3 = (bf16[4,16,9216]{2,1,0:T(8,128)(2,1)}, bf16[4,16,9216]{2,1,0:T(8,128)(2,1)}, u32[]{:S(2)}, u32[]{:S(2)}) collective-permute-start(bf16[4,16,9216]{2,1,0:T(8,128)(2,1)} %pad_maximum_fusion.1), channel_id=1, source_target_pairs={{0,4},{4,0},{8,12},{12,8},{16,20},{20,16},{24,28},{28,24},{1,5},{5... | collective-permute-start | bytes 3538952 | tf_op jit(solution)/shard_map/ppermute | solution.py:92
  24.8 23.1 %collective-permute-start.9 = (bf16[256,1024]{1,0:T(8,128)(2,1)}, bf16[256,1024]{1,0:T(8,128)(2,1)S(1)}, u32[]{:S(2)}, u32[]{:S(2)}) collective-permute-start(bf16[256,1024]{1,0:T(8,128)(2,1)} %collective-permute-done.6), channel_id=1, source_target_pairs={{0,16},{1,9},{2,18},{3,11},{4,12},{5,21},{6,14},{7,23},{8,24},{9,1... | collective-permute-start | bytes 1572872 | tf_op jit(solution)/shard_map/ppermute | solution.py:55
  26.6 22.9 %collective-permute-start.10 = (bf16[256,1024]{1,0:T(8,128)(2,1)}, bf16[256,1024]{1,0:T(8,128)(2,1)S(1)}, u32[]{:S(2)}, u32[]{:S(2)}) collective-permute-start(bf16[256,1024]{1,0:T(8,128)(2,1)} %collective-permute-done.6), channel_id=1, source_target_pairs={{0,1},{1,0},{2,3},{3,2},{4,5},{5,4},{6,7},{7,6},{8,9},{9,8},{10,11... | collective-permute-start | bytes 1572872 | tf_op jit(solution)/shard_map/ppermute | solution.py:56
  46.2 1.7 %copy-start.5 = (bf16[768,1024]{1,0:T(8,128)(2,1)S(1)}, bf16[768,1024]{1,0:T(8,128)(2,1)}, u32[]{:S(2)}) copy-start(bf16[768,1024]{1,0:T(8,128)(2,1)} %slice.58) | copy-start | bytes 4718596
  47.9 43.1 %collective-permute-start.8 = (bf16[768,1024]{1,0:T(8,128)(2,1)S(1)}, bf16[768,1024]{1,0:T(8,128)(2,1)}, u32[]{:S(2)}, u32[]{:S(2)}) collective-permute-start(bf16[768,1024]{1,0:T(8,128)(2,1)S(1)} %copy-done.5), channel_id=1, source_target_pairs={{0,8},{1,17},{2,10},{3,19},{4,20},{5,13},{6,22},{7,15},{8,0},{9,25... | collective-permute-start | bytes 4718600 | tf_op jit(solution)/shard_map/ppermute | solution.py:51
  49.5 34.7 %collective-permute-start.7 = (bf16[256,1024]{1,0:T(8,128)(2,1)}, bf16[256,1024]{1,0:T(8,128)(2,1)}, u32[]{:S(2)}, u32[]{:S(2)}) collective-permute-start(bf16[256,1024]{1,0:T(8,128)(2,1)} %collective-permute-done.6), channel_id=1, source_target_pairs={{0,4},{4,0},{8,12},{12,8},{16,20},{20,16},{24,28},{28,24},{1,5},{5... | collective-permute-start | bytes 1572872 | tf_op jit(solution)/shard_map/ppermute | solution.py:54
  49.5 3.2 %copy-start.14 = (bf16[8,16,9216]{2,1,0:T(8,128)(2,1)S(1)}, bf16[8,16,9216]{2,1,0:T(8,128)(2,1)}, u32[]{:S(2)}) copy-start(bf16[8,16,9216]{2,1,0:T(8,128)(2,1)} %constant_dynamic-update-slice_fusion.3) | copy-start | bytes 7077892
  49.5 4.1 %copy-start.9 = (bf16[16,9216]{1,0:T(8,128)(2,1)S(1)}, bf16[16,9216]{1,0:T(8,128)(2,1)}, u32[]{:S(2)}) copy-start(bf16[16,9216]{1,0:T(8,128)(2,1)} %copy-done.8) | copy-start | bytes 884740
  49.5 5.2 %copy-start.7 = (bf16[16,9216]{1,0:T(8,128)(2,1)S(1)}, bf16[16,9216]{1,0:T(8,128)(2,1)}, u32[]{:S(2)}) copy-start(bf16[16,9216]{1,0:T(8,128)(2,1)} %copy-done.6) | copy-start | bytes 884740
  50.6 8.3 %slice-start = ((s8[6291456]{0:T(1024)(128)(4,1)}), s8[4194304]{0:T(1024)(128)(4,1)S(1)}, s32[]{:S(2)}) async-start(s8[6291456]{0:T(1024)(128)(4,1)} %bitcast.119), calls=%async_computation | async-start | bytes 8388608
  52.1 47.8 %collective-permute-start.12 = (bf16[2,256,1024]{2,1,0:T(8,128)(2,1)}, bf16[2,256,1024]{2,1,0:T(8,128)(2,1)}, u32[]{:S(2)}, u32[]{:S(2)}) collective-permute-start(bf16[2,256,1024]{2,1,0:T(8,128)(2,1)} %pad_maximum_fusion.3), channel_id=1, source_target_pairs={{0,4},{4,0},{8,12},{12,8},{16,20},{20,16},{24,28},{28,24},{1,5},{5... | collective-permute-start | bytes 3145736 | tf_op jit(solution)/shard_map/ppermute | solution.py:59
  56.7 2.2 %slice-start.1 = ((s8[6291456]{0:T(1024)(128)(4,1)}), s8[2097152]{0:T(1024)(128)(4,1)S(1)}, s32[]{:S(2)}) async-start(s8[6291456]{0:T(1024)(128)(4,1)} %bitcast.119), calls=%async_computation.1 | async-start | bytes 4194304
  56.8 1.3 copy-start.4
  75.4 1.7 %copy-start.12 = (f32[3,128,768]{2,1,0:T(8,128)S(1)}, f32[3,128,768]{2,1,0:T(8,128)}, u32[]{:S(2)}) copy-start(f32[3,128,768]{2,1,0:T(8,128)} %fusion.82) | copy-start | bytes 3538948
  77.1 1.0 copy-start.16
  77.9 53.3 %collective-permute-start.16 = (bf16[4,16,9216]{2,1,0:T(8,128)(2,1)}, bf16[4,16,9216]{2,1,0:T(8,128)(2,1)S(1)}, u32[]{:S(2)}, u32[]{:S(2)}) collective-permute-start(bf16[4,16,9216]{2,1,0:T(8,128)(2,1)} %pad_maximum_fusion.2), channel_id=1, source_target_pairs={{0,4},{4,0},{8,12},{12,8},{16,20},{20,16},{24,28},{28,24},{1,5},{5... | collective-permute-start | bytes 3538952 | tf_op jit(solution)/shard_map/ppermute | solution.py:135
  84.2 1.5 copy-start.11
  88.0 1.5 copy-start.15
  93.6 20.7 %collective-permute-start.13 = (bf16[768,1024]{1,0:T(8,128)(2,1)}, bf16[768,1024]{1,0:T(8,128)(2,1)S(1)}, u32[]{:S(2)}, u32[]{:S(2)}) collective-permute-start(bf16[768,1024]{1,0:T(8,128)(2,1)} %collective-permute-done.8), channel_id=1, source_target_pairs={{0,16},{1,9},{2,18},{3,11},{4,12},{5,21},{6,14},{7,23},{8,24},{9,1... | collective-permute-start | bytes 4718600 | tf_op jit(solution)/shard_map/ppermute | solution.py:55
  95.2 35.7 %collective-permute-start.14 = (bf16[768,1024]{1,0:T(8,128)(2,1)}, bf16[768,1024]{1,0:T(8,128)(2,1)S(1)}, u32[]{:S(2)}, u32[]{:S(2)}) collective-permute-start(bf16[768,1024]{1,0:T(8,128)(2,1)} %collective-permute-done.8), channel_id=1, source_target_pairs={{0,1},{1,0},{2,3},{3,2},{4,5},{5,4},{6,7},{7,6},{8,9},{9,8},{10,11... | collective-permute-start | bytes 4718600 | tf_op jit(solution)/shard_map/ppermute | solution.py:56
  95.5 1.3 copy-start.10
  95.8 35.9 %collective-permute-start.11 = (bf16[768,1024]{1,0:T(8,128)(2,1)}, bf16[768,1024]{1,0:T(8,128)(2,1)S(1)}, u32[]{:S(2)}, u32[]{:S(2)}) collective-permute-start(bf16[768,1024]{1,0:T(8,128)(2,1)} %collective-permute-done.8), channel_id=1, source_target_pairs={{0,4},{4,0},{8,12},{12,8},{16,20},{20,16},{24,28},{28,24},{1,5},{5... | collective-permute-start | bytes 4718600 | tf_op jit(solution)/shard_map/ppermute | solution.py:54
  131.2 9.8 %collective-permute-start.15 = (bf16[2,768,1024]{2,1,0:T(8,128)(2,1)S(1)}, bf16[2,768,1024]{2,1,0:T(8,128)(2,1)S(1)}, u32[]{:S(2)}, u32[]{:S(2)}) collective-permute-start(bf16[2,768,1024]{2,1,0:T(8,128)(2,1)S(1)} %pad_maximum_fusion), channel_id=1, source_target_pairs={{0,4},{4,0},{8,12},{12,8},{16,20},{20,16},{24,28},{28,24},{1,5},{5... | collective-permute-start | bytes 9437192 | tf_op jit(solution)/shard_map/ppermute | solution.py:59
  140.9 9.9 %collective-permute-start.17 = (bf16[16,9216]{1,0:T(8,128)(2,1)S(1)}, bf16[16,9216]{1,0:T(8,128)(2,1)S(1)}, u32[]{:S(2)}, u32[]{:S(2)}) collective-permute-start(bf16[16,9216]{1,0:T(8,128)(2,1)S(1)} %get-tuple-element.9), channel_id=1, source_target_pairs={{0,8},{4,12},{8,0},{12,4},{16,24},{20,28},{24,16},{28,20},{1,9},{5... | collective-permute-start | bytes 884744 | tf_op jit(solution)/shard_map/ppermute | solution.py:148
  142.5 15.4 %collective-permute-start.18 = (bf16[16,9216]{1,0:T(8,128)(2,1)S(1)}, bf16[16,9216]{1,0:T(8,128)(2,1)S(1)}, u32[]{:S(2)}, u32[]{:S(2)}) collective-permute-start(bf16[16,9216]{1,0:T(8,128)(2,1)S(1)} %get-tuple-element.10), channel_id=1, source_target_pairs={{0,16},{4,20},{8,24},{12,28},{16,0},{20,4},{24,8},{28,12},{1,17},{... | collective-permute-start | bytes 884744 | tf_op jit(solution)/shard_map/ppermute | solution.py:148
  143.7 14.2 %collective-permute-start.19 = (bf16[16,9216]{1,0:T(8,128)(2,1)S(1)}, bf16[16,9216]{1,0:T(8,128)(2,1)S(1)}, u32[]{:S(2)}, u32[]{:S(2)}) collective-permute-start(bf16[16,9216]{1,0:T(8,128)(2,1)S(1)} %get-tuple-element.11), channel_id=1, source_target_pairs={{0,24},{4,28},{8,16},{12,20},{16,8},{20,12},{24,0},{28,4},{1,25},{... | collective-permute-start | bytes 884744 | tf_op jit(solution)/shard_map/ppermute | solution.py:148
  147.0 2.7 %copy-start.3 = (bf16[384,8192]{1,0:T(8,128)(2,1)}, bf16[384,8192]{1,0:T(8,128)(2,1)S(1)}, u32[]{:S(2)}) copy-start(bf16[384,8192]{1,0:T(8,128)(2,1)S(1)} %fusion.15) | copy-start | bytes 18874372
  149.7 9.8 %copy-start.1 = (s32[32]{0:T(128)S(1)}, s32[32]{0:T(128)}, u32[]{:S(2)}) copy-start(s32[32]{0:T(128)} %param.15) | copy-start | bytes 388

commit v10 on v6

--- a/solution.py
+++ b/solution.py
@@ -85,7 +85,12 @@
     dp_index = lax.axis_index("dp")
     even_steps = list(range(2, members, 2))
 
+    weight_pieces = relay_gather(frozen_value_weight, members, groups, me, dp_index)
+    if weight_pieces and len(weight_pieces[0]) == 2:
+        weight_pieces = [(source, 0, value) for source, value in weight_pieces]
+
     own_adapter = jnp.concatenate([adapter_down_maps[0], adapter_up_maps[0]], axis=1)
+    own_adapter, _ = lax.optimization_barrier((own_adapter, weight_pieces[4][2]))
     by_step = {0: own_adapter}
     for step in even_steps:
         by_step[step] = lax.ppermute(own_adapter, "fsdp", xor_pairs(members, step))
@@ -138,9 +143,6 @@
         table_row(me ^ step).astype(jnp.float32) + from_sibling[index].astype(jnp.float32)
         for index, step in enumerate(range(0, members, 2))
     ]
-    weight_pieces = relay_gather(frozen_value_weight, members, groups, me, dp_index)
-    if weight_pieces and len(weight_pieces[0]) == 2:
-        weight_pieces = [(source, 0, value) for source, value in weight_pieces]
     last_pieces = tuple(value for _, _, value in weight_pieces[-4:])
     grad_sum = pair_sums[0]
     for index, step in enumerate(even_steps):

time: 132 us -> 148 us (1.12)
  matrix products: 41.6 us -> 52.7 us
  local copies, waits for them, and re-layouts: 8.32 us -> 11.3 us
  waiting for transfers between devices: 37.3 us -> 39.6 us
    ppermute x2, waiting for transfers between devices: 11.6 us -> 2.3 us  [relay_gather(): partner = lax.ppermute(first, ('fsdp', 'dp'), partner_pairs)]
    dot_general x16, matrix products: 9.36 us -> 17.6 us  [on_device(): jnp.einsum('uio,uof->uif', low_rank_gradient, down_piece, preferred_eleme...]
    ppermute x2, waiting for transfers between devices: 9.54 us -> 16.3 us  [relay_gather(): relayed = lax.ppermute(first, ('fsdp', 'dp'), relay_pairs)]
    ppermute x3, waiting for transfers between devices: 7.79 us -> 11.1 us  [on_device(): by_step[step] = lax.ppermute(own_adapter, 'fsdp', xor_pairs(members, step))]
    unnamed x38 -> x61, local copies, waits for them, and re-layouts: 1.86 us -> 4.75 us
    ppermute x2, starting transfers between devices: 1.96 us -> 4.08 us  [relay_gather(): first = lax.ppermute(piece, ('fsdp', 'dp'), first_pairs)]
    dot_general x16, matrix products: 13.4 us -> 15.2 us  [on_device(): jnp.dot(token_piece, weight_piece, preferred_element_type=jnp.float32)]
    ppermute x2, starting transfers between devices: 2.13 us -> 3.76 us  [relay_gather(): partner = lax.ppermute(first, ('fsdp', 'dp'), partner_pairs)]
  transfers between devices with their start and end apart: 20 -> 20, of which waited for: 5 -> 6; matrix products, arithmetic and copies ran while one was open for 41% -> 42% of each run, Pallas kernels for 0% -> 0%
where the time goes in v10:
time: 148 us; the launch traced here: 147 us
  matrix products  52.7 us (36%)
  waiting for transfers between devices  39.6 us (27%)
  between operations  19.2 us (13%)
  starting transfers between devices  18 us (12%)
  local copies, waits for them, and re-layouts  11.3 us (8%)
  other arithmetic  6.42 us (4%)
    dot_general x16, matrix products, on_device(): jnp.einsum('uio,uof->uif', low_rank_gradient, down_piece, preferred_eleme...  17.6 us
    dot_general x16, matrix products, on_device(): lax.dot_general(masked_cot, weight_piece, (((1,), (1,)), ((), ())), prefe...  16.3 us
    ppermute x2, waiting for transfers between devices, relay_gather(): relayed = lax.ppermute(first, ('fsdp', 'dp'), relay_pairs)  16.3 us
    dot_general x16, matrix products, on_device(): jnp.dot(token_piece, weight_piece, preferred_element_type=jnp.float32)  15.2 us
    ppermute x3, waiting for transfers between devices, on_device(): by_step[step] = lax.ppermute(own_adapter, 'fsdp', xor_pairs(members, step))  11.1 us
    ppermute x3, waiting for transfers between devices, on_device(): lax.ppermute(sent, 'fsdp', xor_pairs(members, step)).astype(jnp.float32)  9.84 us
    unnamed x61, local copies, waits for them, and re-layouts  4.75 us
    ppermute x2, starting transfers between devices, relay_gather(): first = lax.ppermute(piece, ('fsdp', 'dp'), first_pairs)  4.08 us
  transfers between devices with their start and end apart: 20, of which 6 were waited for; matrix products, arithmetic and copies ran while one was open for 42% of the time, Pallas kernels for 0%

profile of v10, /device:TPU:0, one launch (start us, length us, event | category | flops | bytes accessed | tf_op | source)
XLA Modules:
  0.0 147.2 jit_solution(8656165688057507658)
XLA Ops:
  0.7 3.1 %fusion.142 = (bf16[512,1024]{1,0:T(8,128)(2,1)}, bf16[512,1024]{1,0:T(8,128)(2,1)}) fusion(bf16[1024,1024]{1,0:T(8,128)(2,1)} %param.10), kind=kLoop, calls=%fused_computation.218 | loop fusion | bytes 4194304 | tf_op jit(solution)/shard_map/slice | solution.py:47
  3.8 2.9 %collective-permute-start = (bf16[512,1024]{1,0:T(8,128)(2,1)}, bf16[512,1024]{1,0:T(8,128)(2,1)S(1)}, u32[]{:S(2)}, u32[]{:S(2)}) collective-permute-start(bf16[512,1024]{1,0:T(8,128)(2,1)} %get-tuple-element.27), channel_id=1, source_target_pairs={{0,8},{1,17},{2,10},{3,19},{4,20},{5,13},{6,22},{7,15},{8,0},{9,25... | collective-permute-start | bytes 3145736 | tf_op jit(solution)/shard_map/ppermute | solution.py:52
  25.8 1.1 collective-permute-start.1
  27.0 1.0 collective-permute-start.2
  27.9 1.4 collective-permute-start.3
  29.4 1.1 collective-permute-start.8
  30.5 5.2 %collective-permute-done.1 = bf16[16,9216]{1,0:T(8,128)(2,1)S(1)} collective-permute-done((bf16[16,9216]{1,0:T(8,128)(2,1)S(1)}, bf16[16,9216]{1,0:T(8,128)(2,1)S(1)}, u32[]{:S(2)}, u32[]{:S(2)}) %collective-permute-start.1) | collective-permute-done | bytes 294944 | tf_op jit(solution)/shard_map/ppermute | solution.py:96
  35.7 1.5 %collective-permute-start.9 = (bf16[512,1024]{1,0:T(8,128)(2,1)S(1)}, bf16[512,1024]{1,0:T(8,128)(2,1)S(1)}, u32[]{:S(2)}, u32[]{:S(2)}) collective-permute-start(bf16[512,1024]{1,0:T(8,128)(2,1)S(1)} %collective-permute-done), channel_id=1, source_target_pairs={{0,16},{1,9},{2,18},{3,11},{4,12},{5,21},{6,14},{7,23},{8,24},{9,1... | collective-permute-start | bytes 3145736 | tf_op jit(solution)/shard_map/ppermute | solution.py:56
  37.2 6.0 %collective-permute-done.2 = bf16[16,9216]{1,0:T(8,128)(2,1)S(1)} collective-permute-done((bf16[16,9216]{1,0:T(8,128)(2,1)S(1)}, bf16[16,9216]{1,0:T(8,128)(2,1)S(1)}, u32[]{:S(2)}, u32[]{:S(2)}) %collective-permute-start.2) | collective-permute-done | bytes 294944 | tf_op jit(solution)/shard_map/ppermute | solution.py:96
  43.2 2.0 %collective-permute-start.10 = (bf16[512,1024]{1,0:T(8,128)(2,1)S(1)}, bf16[512,1024]{1,0:T(8,128)(2,1)S(1)}, u32[]{:S(2)}, u32[]{:S(2)}) collective-permute-start(bf16[512,1024]{1,0:T(8,128)(2,1)S(1)} %collective-permute-done), channel_id=1, source_target_pairs={{0,1},{1,0},{2,3},{3,2},{4,5},{5,4},{6,7},{7,6},{8,9},{9,8},{10,11... | collective-permute-start | bytes 3145736 | tf_op jit(solution)/shard_map/ppermute | solution.py:57
  45.4 1.6 %fusion.58 = f32[384,1024]{1,0:T(8,128)S(1)} fusion(bf16[512,1024]{1,0:T(8,128)(2,1)S(1)} %collective-permute-done, bf16[384,8192]{1,0:T(8,128)(2,1)} %param.8, s32[]{:T(128)S(6)} %select_n.296), kind=kOutput, calls=%fused_computation.113 | convolution fusion | flops 402653184 | bytes 3014660 | tf_op jit(solution)/shard_map/dot_general | solution.py:168
  48.1 16.3 %collective-permute-done.9 = bf16[512,1024]{1,0:T(8,128)(2,1)S(1)} collective-permute-done((bf16[512,1024]{1,0:T(8,128)(2,1)S(1)}, bf16[512,1024]{1,0:T(8,128)(2,1)S(1)}, u32[]{:S(2)}, u32[]{:S(2)}) %collective-permute-start.9) | collective-permute-done | bytes 1048608 | tf_op jit(solution)/shard_map/ppermute | solution.py:56
  64.4 2.3 %collective-permute-done.10 = bf16[512,1024]{1,0:T(8,128)(2,1)S(1)} collective-permute-done((bf16[512,1024]{1,0:T(8,128)(2,1)S(1)}, bf16[512,1024]{1,0:T(8,128)(2,1)S(1)}, u32[]{:S(2)}, u32[]{:S(2)}) %collective-permute-start.10) | collective-permute-done | bytes 1048608 | tf_op jit(solution)/shard_map/ppermute | solution.py:57
  67.1 1.8 %fusion.55 = f32[384,1024]{1,0:T(8,128)S(1)} fusion(bf16[512,1024]{1,0:T(8,128)(2,1)} %collective-permute-done.8, bf16[384,8192]{1,0:T(8,128)(2,1)S(1)} %copy-done.2, s32[]{:T(128)S(6)} %select_n.298), kind=kOutput, calls=%fused_computation.110 | convolution fusion | flops 402653184 | bytes 3014660 | tf_op jit(solution)/shard_map/dot_general | solution.py:168
  69.5 1.8 %collective-permute-start.14 = (bf16[512,1024]{1,0:T(8,128)(2,1)}, bf16[512,1024]{1,0:T(8,128)(2,1)S(1)}, u32[]{:S(2)}, u32[]{:S(2)}) collective-permute-start(bf16[512,1024]{1,0:T(8,128)(2,1)} %collective-permute-done.8), channel_id=1, source_target_pairs={{0,1},{1,0},{2,3},{3,2},{4,5},{5,4},{6,7},{7,6},{8,9},{9,8},{10,11... | collective-permute-start | bytes 3145736 | tf_op jit(solution)/shard_map/ppermute | solution.py:57
  71.8 0.9 copy-done.5
  73.0 1.2 fusion.92
  74.2 1.2 fusion.90
  75.4 1.3 fusion.86
  76.7 1.2 fusion.82
  77.9 0.9 fusion.144
  78.8 1.7 %fusion.32 = bf16[3,16,128]{2,1,0:T(8,128)(2,1)S(1)} fusion(bf16[3,128,8192]{2,1,0:T(8,128)(2,1)S(1)} %bitcast.119, f32[3,128]{1,0:T(4,128)S(1)} %get-tuple-element.32, bf16[3,16,9216]{2,1,0:T(8,128)(2,1)S(1)} %pad_maximum_fusion.4), kind=kOutput, calls=%fused_computation.69 | convolution fusion | flops 100675584 | bytes 7092224 | tf_op jit(solution)/shard_map/cvj,coj->cvo/dot_general | solution.py:116
  81.2 1.2 fusion.98
  82.4 1.2 fusion.96
  83.6 1.2 fusion.94
  84.8 1.2 fusion.88
  87.7 1.2 fusion.84
  89.0 1.2 fusion.80
  90.2 1.3 fusion.78
  91.4 1.2 fusion.76
  92.6 1.2 fusion.74
  94.0 1.8 %convolution_add_fusion.3 = f32[384,1024]{1,0:T(8,128)S(1)} fusion(f32[384,1024]{1,0:T(8,128)S(1)} %convolution_add_fusion.4, bf16[512,1024]{1,0:T(8,128)(2,1)} %collective-permute-done.5, bf16[384,8192]{1,0:T(8,128)(2,1)S(1)} %copy-done.2, s32[]{:T(128)S(6)} %select_n.292), kind=kOutput, calls=%fused_computation.13 | convolution fusion | flops 403046400 | bytes 4587524 | tf_op jit(solution)/shard_map/dot_general | solution.py:168
  95.8 1.3 fusion.72
  98.4 1.8 %convolution_add_fusion.2 = f32[384,1024]{1,0:T(8,128)S(1)} fusion(f32[384,1024]{1,0:T(8,128)S(1)} %add.347, bf16[512,1024]{1,0:T(8,128)(2,1)} %collective-permute-done.7, bf16[384,8192]{1,0:T(8,128)(2,1)S(1)} %copy-done.2, s32[]{:T(128)S(6)} %select_n.297), kind=kOutput, calls=%fused_computation.12 | convolution fusion | flops 403046400 | bytes 4587524 | tf_op jit(solution)/shard_map/dot_general | solution.py:168
  101.3 1.8 %fusion.1 = bf16[384,8192]{1,0:T(8,128)(2,1)S(1)} fusion(bf16[384,8192]{1,0:T(8,128)(2,1)S(1)} %broadcast_in_dim.44, s32[]{:T(128)S(6)} %select_n.290, f32[384,512]{1,0:T(8,128)} %bitcast.145, bf16[1024,1024]{1,0:T(8,128)(2,1)S(1)} %copy-done.3, bf16[384,1024]{1,0:T(8,128)(2,1)S(1)} %copy-done.5, f32[384]{0:T(512)S(1)} %get-tuple-element.31), kind=kOutput, calls=%fused_computation.33 | convolution fusion | flops 404226048 | bytes 3016708 | tf_op jit(solution)/shard_map/dot_general | solution.py:172
  104.9 1.9 %fusion.5 = bf16[384,8192]{1,0:T(8,128)(2,1)S(1)} fusion(bf16[384,8192]{1,0:T(8,128)(2,1)S(1)} %fusion.3, s32[]{:T(128)S(6)} %select_n.292, f32[384,512]{1,0:T(8,128)S(1)} %bitcast.142, bf16[512,1024]{1,0:T(8,128)(2,1)} %collective-permute-done.5, bf16[384,1024]{1,0:T(8,128)(2,1)S(1)} %copy-done.5, f32[384]{0:T(512)S(1)} %get-tuple-element.31), kind=kOutput, calls=%fused_computation.37 | convolution fusion | flops 404226048 | bytes 3016708 | tf_op jit(solution)/shard_map/dot_general | solution.py:172
  108.9 1.9 %fusion.11 = bf16[384,8192]{1,0:T(8,128)(2,1)S(1)} fusion(bf16[384,8192]{1,0:T(8,128)(2,1)S(1)} %fusion.9, s32[]{:T(128)S(6)} %select_n.297, f32[384,512]{1,0:T(8,128)S(1)} %bitcast.141, bf16[512,1024]{1,0:T(8,128)(2,1)} %collective-permute-done.7, bf16[384,1024]{1,0:T(8,128)(2,1)S(1)} %copy-done.5, f32[384]{0:T(512)S(1)} %get-tuple-element.31), kind=kOutput, calls=%fused_computation.43 | convolution fusion | flops 404226048 | bytes 3016708 | tf_op jit(solution)/shard_map/dot_general | solution.py:172
  110.8 1.9 %fusion.13 = bf16[384,8192]{1,0:T(8,128)(2,1)S(1)} fusion(bf16[384,8192]{1,0:T(8,128)(2,1)S(1)} %fusion.11, s32[]{:T(128)S(6)} %select_n.298, f32[384,512]{1,0:T(8,128)S(1)} %bitcast.136, bf16[512,1024]{1,0:T(8,128)(2,1)} %collective-permute-done.8, bf16[384,1024]{1,0:T(8,128)(2,1)S(1)} %copy-done.5, f32[384]{0:T(512)S(1)} %get-tuple-element.31), kind=kOutput, calls=%fused_computation.45 | convolution fusion | flops 404226048 | bytes 3016708 | tf_op jit(solution)/shard_map/dot_general | solution.py:172
  113.3 0.8 copy-done.21
  116.1 1.8 %fusion.50 = f32[384,1024]{1,0:T(8,128)S(1)} fusion(bf16[512,1024]{1,0:T(8,128)(2,1)} %collective-permute-done.11, bf16[384,8192]{1,0:T(8,128)(2,1)S(1)} %copy-done.2, s32[]{:T(128)S(6)} %select_n.301), kind=kOutput, calls=%fused_computation.105 | convolution fusion | flops 402653184 | bytes 3014660 | tf_op jit(solution)/shard_map/dot_general | solution.py:168
  118.0 1.9 %fusion.19 = bf16[384,8192]{1,0:T(8,128)(2,1)S(1)} fusion(bf16[384,8192]{1,0:T(8,128)(2,1)S(1)} %fusion.17, s32[]{:T(128)S(6)} %select_n.301, f32[384,512]{1,0:T(8,128)S(1)} %bitcast.138, bf16[512,1024]{1,0:T(8,128)(2,1)} %collective-permute-done.11, bf16[384,1024]{1,0:T(8,128)(2,1)S(1)} %copy-done.5, f32[384]{0:T(512)S(1)} %get-tuple-element.31), kind=kOutput, calls=%fused_computation.51 | convolution fusion | flops 404226048 | bytes 3016708 | tf_op jit(solution)/shard_map/dot_general | solution.py:172
  124.0 0.8 copy-done.13
  125.5 0.9 fusion.23
  128.2 2.0 %collective-permute-start.17 = (bf16[16,9216]{1,0:T(8,128)(2,1)S(1)}, bf16[16,9216]{1,0:T(8,128)(2,1)S(1)}, u32[]{:S(2)}, u32[]{:S(2)}) collective-permute-start(bf16[16,9216]{1,0:T(8,128)(2,1)S(1)} %get-tuple-element.11), channel_id=1, source_target_pairs={{0,8},{4,12},{8,0},{12,4},{16,24},{20,28},{24,16},{28,20},{1,9},{5... | collective-permute-start | bytes 884744 | tf_op jit(solution)/shard_map/ppermute | solution.py:151
  130.2 1.6 %collective-permute-start.19 = (bf16[16,9216]{1,0:T(8,128)(2,1)S(1)}, bf16[16,9216]{1,0:T(8,128)(2,1)S(1)}, u32[]{:S(2)}, u32[]{:S(2)}) collective-permute-start(bf16[16,9216]{1,0:T(8,128)(2,1)S(1)} %get-tuple-element.13), channel_id=1, source_target_pairs={{0,24},{4,28},{8,16},{12,20},{16,8},{20,12},{24,0},{28,4},{1,25},{... | collective-permute-start | bytes 884744 | tf_op jit(solution)/shard_map/ppermute | solution.py:151
  133.4 1.0 multiply_convert_fusion.1
  135.7 2.3 %collective-permute-done.17 = bf16[16,9216]{1,0:T(8,128)(2,1)S(1)} collective-permute-done((bf16[16,9216]{1,0:T(8,128)(2,1)S(1)}, bf16[16,9216]{1,0:T(8,128)(2,1)S(1)}, u32[]{:S(2)}, u32[]{:S(2)}) %collective-permute-start.17) | collective-permute-done | bytes 294944 | tf_op jit(solution)/shard_map/ppermute | solution.py:151
  138.0 7.5 %collective-permute-done.18 = bf16[16,9216]{1,0:T(8,128)(2,1)S(1)} collective-permute-done((bf16[16,9216]{1,0:T(8,128)(2,1)S(1)}, bf16[16,9216]{1,0:T(8,128)(2,1)S(1)}, u32[]{:S(2)}, u32[]{:S(2)}) %collective-permute-start.18) | collective-permute-done | bytes 294944 | tf_op jit(solution)/shard_map/ppermute | solution.py:151
  (142 shorter events, 26.6 us)
Async XLA Ops:
  0.6 6.3 %copy-start = (s32[32]{0:T(128)S(1)}, s32[32]{0:T(128)}, u32[]{:S(2)}) copy-start(s32[32]{0:T(128)} %param.15) | copy-start | bytes 388
  0.6 6.1 %copy-start.25 = (s32[3]{0:T(128)S(1)}, s32[3]{0:T(128)}, u32[]{:S(2)}) copy-start(s32[3]{0:T(128)} %param.14) | copy-start | bytes 40
  0.7 6.2 %copy-start.26 = (s32[3]{0:T(128)S(1)}, s32[3]{0:T(128)}, u32[]{:S(2)}) copy-start(s32[3]{0:T(128)} %param.13) | copy-start | bytes 40
  0.7 25.1 %copy-start.23 = (bf16[1,16,8192]{2,1,0:T(8,128)(2,1)S(1)}, bf16[1,16,8192]{2,1,0:T(8,128)(2,1)}, u32[]{:S(2)}) copy-start(bf16[1,16,8192]{2,1,0:T(8,128)(2,1)} %param.11) | copy-start | bytes 786436
  0.7 25.1 %copy-start.24 = (bf16[1,16,1024]{2,1,0:T(8,128)(2,1)S(1)}, bf16[1,16,1024]{2,1,0:T(8,128)(2,1)}, u32[]{:S(2)}) copy-start(bf16[1,16,1024]{2,1,0:T(8,128)(2,1)} %param.12) | copy-start | bytes 98308
  3.8 22.0 %collective-permute-start = (bf16[512,1024]{1,0:T(8,128)(2,1)}, bf16[512,1024]{1,0:T(8,128)(2,1)S(1)}, u32[]{:S(2)}, u32[]{:S(2)}) collective-permute-start(bf16[512,1024]{1,0:T(8,128)(2,1)} %get-tuple-element.27), channel_id=1, source_target_pairs={{0,8},{1,17},{2,10},{3,19},{4,20},{5,13},{6,22},{7,15},{8,0},{9,25... | collective-permute-start | bytes 3145736 | tf_op jit(solution)/shard_map/ppermute | solution.py:52
  6.7 40.2 %collective-permute-start.6 = (bf16[512,1024]{1,0:T(8,128)(2,1)}, bf16[512,1024]{1,0:T(8,128)(2,1)S(1)}, u32[]{:S(2)}, u32[]{:S(2)}) collective-permute-start(bf16[512,1024]{1,0:T(8,128)(2,1)} %get-tuple-element.10), channel_id=1, source_target_pairs={{0,4},{4,0},{8,12},{12,8},{16,20},{20,16},{24,28},{28,24},{1,5},{5... | collective-permute-start | bytes 3145736 | tf_op jit(solution)/shard_map/ppermute | solution.py:49
  25.8 21.8 %copy-start.2 = (bf16[384,8192]{1,0:T(8,128)(2,1)S(1)}, bf16[384,8192]{1,0:T(8,128)(2,1)}, u32[]{:S(2)}) copy-start(bf16[384,8192]{1,0:T(8,128)(2,1)} %param.8) | copy-start | bytes 18874372
  25.8 38.6 %copy-start.6 = (bf16[512,1024]{1,0:T(8,128)(2,1)}, bf16[512,1024]{1,0:T(8,128)(2,1)S(1)}, u32[]{:S(2)}) copy-start(bf16[512,1024]{1,0:T(8,128)(2,1)S(1)} %collective-permute-done) | copy-start | bytes 3145732
  25.8 9.9 %collective-permute-start.1 = (bf16[16,9216]{1,0:T(8,128)(2,1)S(1)}, bf16[16,9216]{1,0:T(8,128)(2,1)S(1)}, u32[]{:S(2)}, u32[]{:S(2)}) collective-permute-start(bf16[16,9216]{1,0:T(8,128)(2,1)S(1)} %pad_maximum_fusion.6), channel_id=1, source_target_pairs={{0,8},{4,12},{8,0},{12,4},{16,24},{20,28},{24,16},{28,20},{1,9},{5... | collective-permute-start | bytes 884744 | tf_op jit(solution)/shard_map/ppermute | solution.py:96
  27.0 16.2 %collective-permute-start.2 = (bf16[16,9216]{1,0:T(8,128)(2,1)S(1)}, bf16[16,9216]{1,0:T(8,128)(2,1)S(1)}, u32[]{:S(2)}, u32[]{:S(2)}) collective-permute-start(bf16[16,9216]{1,0:T(8,128)(2,1)S(1)} %pad_maximum_fusion.6), channel_id=1, source_target_pairs={{0,16},{4,20},{8,24},{12,28},{16,0},{20,4},{24,8},{28,12},{1,17},{... | collective-permute-start | bytes 884744 | tf_op jit(solution)/shard_map/ppermute | solution.py:96
  27.9 17.2 %collective-permute-start.3 = (bf16[16,9216]{1,0:T(8,128)(2,1)S(1)}, bf16[16,9216]{1,0:T(8,128)(2,1)S(1)}, u32[]{:S(2)}, u32[]{:S(2)}) collective-permute-start(bf16[16,9216]{1,0:T(8,128)(2,1)S(1)} %pad_maximum_fusion.6), channel_id=1, source_target_pairs={{0,24},{4,28},{8,16},{12,20},{16,8},{20,12},{24,0},{28,4},{1,25},{... | collective-permute-start | bytes 884744 | tf_op jit(solution)/shard_map/ppermute | solution.py:96
  29.4 37.6 %collective-permute-start.8 = (bf16[512,1024]{1,0:T(8,128)(2,1)}, bf16[512,1024]{1,0:T(8,128)(2,1)}, u32[]{:S(2)}, u32[]{:S(2)}) collective-permute-start(bf16[512,1024]{1,0:T(8,128)(2,1)} %get-tuple-element.10), channel_id=1, source_target_pairs={{0,8},{1,17},{2,10},{3,19},{4,20},{5,13},{6,22},{7,15},{8,0},{9,25... | collective-permute-start | bytes 3145736 | tf_op jit(solution)/shard_map/ppermute | solution.py:52
  35.7 28.7 %collective-permute-start.9 = (bf16[512,1024]{1,0:T(8,128)(2,1)S(1)}, bf16[512,1024]{1,0:T(8,128)(2,1)S(1)}, u32[]{:S(2)}, u32[]{:S(2)}) collective-permute-start(bf16[512,1024]{1,0:T(8,128)(2,1)S(1)} %collective-permute-done), channel_id=1, source_target_pairs={{0,16},{1,9},{2,18},{3,11},{4,12},{5,21},{6,14},{7,23},{8,24},{9,1... | collective-permute-start | bytes 3145736 | tf_op jit(solution)/shard_map/ppermute | solution.py:56
  43.2 23.5 %collective-permute-start.10 = (bf16[512,1024]{1,0:T(8,128)(2,1)S(1)}, bf16[512,1024]{1,0:T(8,128)(2,1)S(1)}, u32[]{:S(2)}, u32[]{:S(2)}) collective-permute-start(bf16[512,1024]{1,0:T(8,128)(2,1)S(1)} %collective-permute-done), channel_id=1, source_target_pairs={{0,1},{1,0},{2,3},{3,2},{4,5},{5,4},{6,7},{7,6},{8,9},{9,8},{10,11... | collective-permute-start | bytes 3145736 | tf_op jit(solution)/shard_map/ppermute | solution.py:57
  45.3 24.2 %collective-permute-start.4 = (bf16[4,16,9216]{2,1,0:T(8,128)(2,1)S(1)}, bf16[4,16,9216]{2,1,0:T(8,128)(2,1)S(1)}, u32[]{:S(2)}, u32[]{:S(2)}) collective-permute-start(bf16[4,16,9216]{2,1,0:T(8,128)(2,1)S(1)} %pad_maximum_fusion.2), channel_id=1, source_target_pairs={{0,4},{4,0},{8,12},{12,8},{16,20},{20,16},{24,28},{28,24},{1,5},{5... | collective-permute-start | bytes 3538952 | tf_op jit(solution)/shard_map/ppermute | solution.py:98
  47.0 19.9 %copy-start.8 = (bf16[512,1024]{1,0:T(8,128)(2,1)}, bf16[512,1024]{1,0:T(8,128)(2,1)S(1)}, u32[]{:S(2)}) copy-start(bf16[512,1024]{1,0:T(8,128)(2,1)S(1)} %collective-permute-done.6) | copy-start | bytes 3145732
  47.0 46.8 %collective-permute-start.5 = (bf16[512,1024]{1,0:T(8,128)(2,1)}, bf16[512,1024]{1,0:T(8,128)(2,1)}, u32[]{:S(2)}, u32[]{:S(2)}) collective-permute-start(bf16[512,1024]{1,0:T(8,128)(2,1)} %get-tuple-element.27), channel_id=1, source_target_pairs={{0,4},{4,0},{8,12},{12,8},{16,20},{20,16},{24,28},{28,24},{1,5},{5... | collective-permute-start | bytes 3145736 | tf_op jit(solution)/shard_map/ppermute | solution.py:49
  64.4 33.6 %collective-permute-start.7 = (bf16[512,1024]{1,0:T(8,128)(2,1)S(1)}, bf16[512,1024]{1,0:T(8,128)(2,1)}, u32[]{:S(2)}, u32[]{:S(2)}) collective-permute-start(bf16[512,1024]{1,0:T(8,128)(2,1)S(1)} %collective-permute-done), channel_id=1, source_target_pairs={{0,4},{4,0},{8,12},{12,8},{16,20},{20,16},{24,28},{28,24},{1,5},{5... | collective-permute-start | bytes 3145736 | tf_op jit(solution)/shard_map/ppermute | solution.py:55
  66.9 54.3 %collective-permute-start.12 = (bf16[2,512,1024]{2,1,0:T(8,128)(2,1)S(1)}, bf16[2,512,1024]{2,1,0:T(8,128)(2,1)S(1)}, u32[]{:S(2)}, u32[]{:S(2)}) collective-permute-start(bf16[2,512,1024]{2,1,0:T(8,128)(2,1)S(1)} %pad_maximum_fusion), channel_id=1, source_target_pairs={{0,4},{4,0},{8,12},{12,8},{16,20},{20,16},{24,28},{28,24},{1,5},{5... | collective-permute-start | bytes 6291464 | tf_op jit(solution)/shard_map/ppermute | solution.py:60
  67.0 48.7 %collective-permute-start.13 = (bf16[512,1024]{1,0:T(8,128)(2,1)}, bf16[512,1024]{1,0:T(8,128)(2,1)S(1)}, u32[]{:S(2)}, u32[]{:S(2)}) collective-permute-start(bf16[512,1024]{1,0:T(8,128)(2,1)} %collective-permute-done.8), channel_id=1, source_target_pairs={{0,16},{1,9},{2,18},{3,11},{4,12},{5,21},{6,14},{7,23},{8,24},{9,1... | collective-permute-start | bytes 3145736 | tf_op jit(solution)/shard_map/ppermute | solution.py:56
  69.5 46.2 %collective-permute-start.14 = (bf16[512,1024]{1,0:T(8,128)(2,1)}, bf16[512,1024]{1,0:T(8,128)(2,1)S(1)}, u32[]{:S(2)}, u32[]{:S(2)}) collective-permute-start(bf16[512,1024]{1,0:T(8,128)(2,1)} %collective-permute-done.8), channel_id=1, source_target_pairs={{0,1},{1,0},{2,3},{3,2},{4,5},{5,4},{6,7},{7,6},{8,9},{9,8},{10,11... | collective-permute-start | bytes 3145736 | tf_op jit(solution)/shard_map/ppermute | solution.py:57
  71.6 1.1 copy-start.5
  81.2 4.8 %copy-start.3 = (bf16[1024,1024]{1,0:T(8,128)(2,1)S(1)}, bf16[1024,1024]{1,0:T(8,128)(2,1)}, u32[]{:S(2)}) copy-start(bf16[1024,1024]{1,0:T(8,128)(2,1)} %param.10) | copy-start | bytes 6291460
  93.8 22.3 %collective-permute-start.11 = (bf16[512,1024]{1,0:T(8,128)(2,1)}, bf16[512,1024]{1,0:T(8,128)(2,1)}, u32[]{:S(2)}, u32[]{:S(2)}) collective-permute-start(bf16[512,1024]{1,0:T(8,128)(2,1)} %collective-permute-done.8), channel_id=1, source_target_pairs={{0,4},{4,0},{8,12},{12,8},{16,20},{20,16},{24,28},{28,24},{1,5},{5... | collective-permute-start | bytes 3145736 | tf_op jit(solution)/shard_map/ppermute | solution.py:55
  97.9 22.8 %collective-permute-start.16 = (bf16[4,16,9216]{2,1,0:T(8,128)(2,1)S(1)}, bf16[4,16,9216]{2,1,0:T(8,128)(2,1)S(1)}, u32[]{:S(2)}, u32[]{:S(2)}) collective-permute-start(bf16[4,16,9216]{2,1,0:T(8,128)(2,1)S(1)} %pad_maximum_fusion.3), channel_id=1, source_target_pairs={{0,4},{4,0},{8,12},{12,8},{16,20},{20,16},{24,28},{28,24},{1,5},{5... | collective-permute-start | bytes 3538952 | tf_op jit(solution)/shard_map/ppermute | solution.py:141
  101.3 1.8 %copy-start.22 = (f32[3,128,512]{2,1,0:T(8,128)S(1)}, f32[3,128,512]{2,1,0:T(8,128)}, u32[]{:S(2)}) copy-start(f32[3,128,512]{2,1,0:T(8,128)} %fusion.96) | copy-start | bytes 2359300
  103.8 1.1 copy-start.20
  104.4 2.4 %copy-start.9 = (bf16[512,1024]{1,0:T(8,128)(2,1)S(1)}, bf16[512,1024]{1,0:T(8,128)(2,1)}, u32[]{:S(2)}) copy-start(bf16[512,1024]{1,0:T(8,128)(2,1)} %copy-done.8) | copy-start | bytes 3145732
  104.4 2.4 %copy-start.18 = (f32[3,128,512]{2,1,0:T(8,128)S(1)}, f32[3,128,512]{2,1,0:T(8,128)}, u32[]{:S(2)}) copy-start(f32[3,128,512]{2,1,0:T(8,128)} %fusion.92) | copy-start | bytes 2359300
  106.8 1.2 copy-start.7
  106.8 1.4 copy-start.17
  107.5 1.4 copy-start.19
  108.9 2.0 %copy-start.15 = (f32[3,128,512]{2,1,0:T(8,128)S(1)}, f32[3,128,512]{2,1,0:T(8,128)}, u32[]{:S(2)}) copy-start(f32[3,128,512]{2,1,0:T(8,128)} %fusion.86) | copy-start | bytes 2359300
  113.0 1.1 copy-start.21
  113.3 1.5 %copy-start.14 = (f32[3,128,512]{2,1,0:T(8,128)S(1)}, f32[3,128,512]{2,1,0:T(8,128)}, u32[]{:S(2)}) copy-start(f32[3,128,512]{2,1,0:T(8,128)} %fusion.82) | copy-start | bytes 2359300
  115.9 2.1 %copy-start.16 = (f32[3,128,512]{2,1,0:T(8,128)S(1)}, f32[3,128,512]{2,1,0:T(8,128)}, u32[]{:S(2)}) copy-start(f32[3,128,512]{2,1,0:T(8,128)} %fusion.80) | copy-start | bytes 2359300
  115.9 12.2 %collective-permute-start.15 = (bf16[2,512,1024]{2,1,0:T(8,128)(2,1)S(1)}, bf16[2,512,1024]{2,1,0:T(8,128)(2,1)S(1)}, u32[]{:S(2)}, u32[]{:S(2)}) collective-permute-start(bf16[2,512,1024]{2,1,0:T(8,128)(2,1)S(1)} %pad_maximum_fusion.1), channel_id=1, source_target_pairs={{0,4},{4,0},{8,12},{12,8},{16,20},{20,16},{24,28},{28,24},{1,5},{5... | collective-permute-start | bytes 6291464 | tf_op jit(solution)/shard_map/ppermute | solution.py:60
  123.7 1.1 copy-start.13
  124.0 1.5 %copy-start.11 = (f32[3,128,512]{2,1,0:T(8,128)S(1)}, f32[3,128,512]{2,1,0:T(8,128)}, u32[]{:S(2)}) copy-start(f32[3,128,512]{2,1,0:T(8,128)} %fusion.76) | copy-start | bytes 2359300
  125.5 1.1 copy-start.10
  126.3 1.2 copy-start.12
  128.2 9.9 %collective-permute-start.17 = (bf16[16,9216]{1,0:T(8,128)(2,1)S(1)}, bf16[16,9216]{1,0:T(8,128)(2,1)S(1)}, u32[]{:S(2)}, u32[]{:S(2)}) collective-permute-start(bf16[16,9216]{1,0:T(8,128)(2,1)S(1)} %get-tuple-element.11), channel_id=1, source_target_pairs={{0,8},{4,12},{8,0},{12,4},{16,24},{20,28},{24,16},{28,20},{1,9},{5... | collective-permute-start | bytes 884744 | tf_op jit(solution)/shard_map/ppermute | solution.py:151
  130.2 15.4 %collective-permute-start.18 = (bf16[16,9216]{1,0:T(8,128)(2,1)S(1)}, bf16[16,9216]{1,0:T(8,128)(2,1)S(1)}, u32[]{:S(2)}, u32[]{:S(2)}) collective-permute-start(bf16[16,9216]{1,0:T(8,128)(2,1)S(1)} %get-tuple-element.12), channel_id=1, source_target_pairs={{0,16},{4,20},{8,24},{12,28},{16,0},{20,4},{24,8},{28,12},{1,17},{... | collective-permute-start | bytes 884744 | tf_op jit(solution)/shard_map/ppermute | solution.py:151
  130.2 15.4 %collective-permute-start.19 = (bf16[16,9216]{1,0:T(8,128)(2,1)S(1)}, bf16[16,9216]{1,0:T(8,128)(2,1)S(1)}, u32[]{:S(2)}, u32[]{:S(2)}) collective-permute-start(bf16[16,9216]{1,0:T(8,128)(2,1)S(1)} %get-tuple-element.13), channel_id=1, source_target_pairs={{0,24},{4,28},{8,16},{12,20},{16,8},{20,12},{24,0},{28,4},{1,25},{... | collective-permute-start | bytes 884744 | tf_op jit(solution)/shard_map/ppermute | solution.py:151
  135.1 12.1 %copy-start.1 = (s32[32]{0:T(128)S(1)}, s32[32]{0:T(128)}, u32[]{:S(2)}) copy-start(s32[32]{0:T(128)} %param.15) | copy-start | bytes 388
  135.7 11.5 %copy-start.4 = (bf16[384,8192]{1,0:T(8,128)(2,1)}, bf16[384,8192]{1,0:T(8,128)(2,1)S(1)}, u32[]{:S(2)}) copy-start(bf16[384,8192]{1,0:T(8,128)(2,1)S(1)} %fusion.31) | copy-start | bytes 18874372

commit v11 on v8

--- a/solution.py
+++ b/solution.py
@@ -141,7 +141,7 @@
     weight_pieces = relay_gather(frozen_value_weight, members, groups, me, dp_index)
     if weight_pieces and len(weight_pieces[0]) == 2:
         weight_pieces = [(source, 0, value) for source, value in weight_pieces]
-    last_pieces = tuple(value for _, _, value in weight_pieces[-4:-2])
+    last_pieces = (weight_pieces[6][2],)
     grad_sum = pair_sums[0]
     for index, step in enumerate(even_steps):
         sent = pair_sums[index + 1].astype(jnp.bfloat16)

time: 135 us -> 132 us (0.978)
    ppermute x2, waiting for transfers between devices: 11.6 us -> 7.16 us  [relay_gather(): partner = lax.ppermute(first, ('fsdp', 'dp'), partner_pairs)]
    ppermute x3, waiting for transfers between devices: 8.5 us -> 11.5 us  [on_device(): lax.ppermute(sent, 'fsdp', xor_pairs(members, step)).astype(jnp.float32)]
  transfers between devices with their start and end apart: 20 -> 20, of which waited for: 5 -> 5; matrix products, arithmetic and copies ran while one was open for 38% -> 39% of each run, Pallas kernels for 0% -> 0%
where the time goes in v11:
time: 132 us; the launch traced here: 131 us
  matrix products  41.6 us (32%)
  waiting for transfers between devices  36.1 us (27%)
  between operations  19 us (14%)
  starting transfers between devices  16.1 us (12%)
  local copies, waits for them, and re-layouts  11 us (8%)
  other arithmetic  7.58 us (6%)
    dot_general x16, matrix products, on_device(): lax.dot_general(masked_cot, weight_piece, (((1,), (1,)), ((), ())), prefe...  15.2 us
    dot_general x16, matrix products, on_device(): jnp.dot(token_piece, weight_piece, preferred_element_type=jnp.float32)  13.4 us
    ppermute x3, waiting for transfers between devices, on_device(): lax.ppermute(sent, 'fsdp', xor_pairs(members, step)).astype(jnp.float32)  11.5 us
    ppermute x2, waiting for transfers between devices, relay_gather(): relayed = lax.ppermute(first, ('fsdp', 'dp'), relay_pairs)  9.62 us
    dot_general x16, matrix products, on_device(): jnp.einsum('uio,uof->uif', low_rank_gradient, down_piece, preferred_eleme...  9.36 us
    ppermute x3, waiting for transfers between devices, on_device(): by_step[step] = lax.ppermute(own_adapter, 'fsdp', xor_pairs(members, step))  7.79 us
    ppermute x2, waiting for transfers between devices, relay_gather(): partner = lax.ppermute(first, ('fsdp', 'dp'), partner_pairs)  7.16 us
    unnamed x38, local copies, waits for them, and re-layouts  4.55 us
  transfers between devices with their start and end apart: 20, of which 5 were waited for; matrix products, arithmetic and copies ran while one was open for 39% of the time, Pallas kernels for 0%

profile of v11, /device:TPU:0, one launch (start us, length us, event | category | flops | bytes accessed | tf_op | source)
XLA Modules:
  0.0 131.5 jit_solution(11547865301870257398)
XLA Ops:
  0.6 1.0 fusion.136
  1.7 3.0 %collective-permute-start = (bf16[16,9216]{1,0:T(8,128)(2,1)S(1)}, bf16[16,9216]{1,0:T(8,128)(2,1)S(1)}, u32[]{:S(2)}, u32[]{:S(2)}) collective-permute-start(bf16[16,9216]{1,0:T(8,128)(2,1)S(1)} %get-tuple-element.28), channel_id=1, source_target_pairs={{0,8},{4,12},{8,0},{12,4},{16,24},{20,28},{24,16},{28,20},{1,9},{5... | collective-permute-start | bytes 884744 | tf_op jit(solution)/shard_map/ppermute | solution.py:91
  4.7 1.5 %collective-permute-start.1 = (bf16[16,9216]{1,0:T(8,128)(2,1)S(1)}, bf16[16,9216]{1,0:T(8,128)(2,1)S(1)}, u32[]{:S(2)}, u32[]{:S(2)}) collective-permute-start(bf16[16,9216]{1,0:T(8,128)(2,1)S(1)} %get-tuple-element.28), channel_id=1, source_target_pairs={{0,16},{4,20},{8,24},{12,28},{16,0},{20,4},{24,8},{28,12},{1,17},{... | collective-permute-start | bytes 884744 | tf_op jit(solution)/shard_map/ppermute | solution.py:91
  6.2 3.0 %fusion.143 = (bf16[512,1024]{1,0:T(8,128)(2,1)}, bf16[512,1024]{1,0:T(8,128)(2,1)}) fusion(bf16[1024,1024]{1,0:T(8,128)(2,1)} %param.10), kind=kLoop, calls=%fused_computation.219 | loop fusion | bytes 4194304 | tf_op jit(solution)/shard_map/slice | solution.py:47
  9.3 1.9 %collective-permute-start.6 = (bf16[512,1024]{1,0:T(8,128)(2,1)}, bf16[512,1024]{1,0:T(8,128)(2,1)}, u32[]{:S(2)}, u32[]{:S(2)}) collective-permute-start(bf16[512,1024]{1,0:T(8,128)(2,1)} %get-tuple-element.23), channel_id=1, source_target_pairs={{0,8},{1,17},{2,10},{3,19},{4,20},{5,13},{6,22},{7,15},{8,0},{9,25... | collective-permute-start | bytes 3145736 | tf_op jit(solution)/shard_map/ppermute | solution.py:52
  11.2 0.7 constant_dynamic-update-slice_fusion.3
  12.0 0.6 gather_fusion
  13.2 7.8 %collective-permute-done.1 = bf16[16,9216]{1,0:T(8,128)(2,1)S(1)} collective-permute-done((bf16[16,9216]{1,0:T(8,128)(2,1)S(1)}, bf16[16,9216]{1,0:T(8,128)(2,1)S(1)}, u32[]{:S(2)}, u32[]{:S(2)}) %collective-permute-start.1) | collective-permute-done | bytes 294944 | tf_op jit(solution)/shard_map/ppermute | solution.py:91
  39.6 1.7 %collective-permute-start.7 = (bf16[512,1024]{1,0:T(8,128)(2,1)}, bf16[512,1024]{1,0:T(8,128)(2,1)S(1)}, u32[]{:S(2)}, u32[]{:S(2)}) collective-permute-start(bf16[512,1024]{1,0:T(8,128)(2,1)} %collective-permute-done.6), channel_id=1, source_target_pairs={{0,4},{4,0},{8,12},{12,8},{16,20},{20,16},{24,28},{28,24},{1,5},{5... | collective-permute-start | bytes 3145736 | tf_op jit(solution)/shard_map/ppermute | solution.py:55
  41.3 1.9 %fusion.58 = f32[384,1024]{1,0:T(8,128)S(1)} fusion(bf16[512,1024]{1,0:T(8,128)(2,1)} %collective-permute-done.6, bf16[384,8192]{1,0:T(8,128)(2,1)} %param.8, s32[]{:T(128)S(6)} %select_n.296), kind=kOutput, calls=%fused_computation.113 | convolution fusion | flops 402653184 | bytes 3014660 | tf_op jit(solution)/shard_map/dot_general | solution.py:166
  43.8 2.1 %fusion.60 = f32[384,1024]{1,0:T(8,128)S(1)} fusion(bf16[512,1024]{1,0:T(8,128)(2,1)} %collective-permute-done.5, bf16[384,8192]{1,0:T(8,128)(2,1)} %param.8, s32[]{:T(128)S(6)} %select_n.293), kind=kOutput, calls=%fused_computation.115 | convolution fusion | flops 402653184 | bytes 3014660 | tf_op jit(solution)/shard_map/dot_general | solution.py:166
  45.9 1.1 collective-permute-start.10
  47.5 1.1 copy-done.4
  48.9 1.2 fusion.92
  50.1 1.2 fusion.90
  51.3 0.9 fusion.145
  52.2 1.7 %fusion.32 = bf16[3,16,128]{2,1,0:T(8,128)(2,1)S(1)} fusion(bf16[3,128,8192]{2,1,0:T(8,128)(2,1)S(1)} %bitcast.122, f32[3,128]{1,0:T(4,128)S(1)} %get-tuple-element.30, bf16[3,16,9216]{2,1,0:T(8,128)(2,1)S(1)} %pad_maximum_fusion.4), kind=kOutput, calls=%fused_computation.69 | convolution fusion | flops 100675584 | bytes 7092224 | tf_op jit(solution)/shard_map/cvj,coj->cvo/dot_general | solution.py:111
  54.6 1.2 fusion.98
  55.8 1.2 fusion.96
  57.0 1.2 fusion.94
  61.3 0.7 broadcast_in_dim.44
  62.0 1.8 %fusion.1 = bf16[384,8192]{1,0:T(8,128)(2,1)S(1)} fusion(bf16[384,8192]{1,0:T(8,128)(2,1)S(1)} %broadcast_in_dim.44, s32[]{:T(128)S(6)} %select_n.290, f32[384,512]{1,0:T(8,128)} %bitcast.149, bf16[1024,1024]{1,0:T(8,128)(2,1)S(1)} %copy-done.2, bf16[384,1024]{1,0:T(8,128)(2,1)S(1)} %copy-done.4, f32[384]{0:T(512)S(1)} %get-tuple-element.29), kind=kOutput, calls=%fused_computation.33 | convolution fusion | flops 404226048 | bytes 3016708 | tf_op jit(solution)/shard_map/dot_general | solution.py:170
  63.9 0.6 fusion.3
  65.6 1.9 %convolution_add_fusion.3 = f32[384,1024]{1,0:T(8,128)S(1)} fusion(f32[384,1024]{1,0:T(8,128)S(1)} %convolution_add_fusion.4, bf16[512,1024]{1,0:T(8,128)(2,1)} %collective-permute-done.4, bf16[384,8192]{1,0:T(8,128)(2,1)S(1)} %bitcast.120, s32[]{:T(128)S(6)} %select_n.292), kind=kOutput, calls=%fused_computation.13 | convolution fusion | flops 403046400 | bytes 4587524 | tf_op jit(solution)/shard_map/dot_general | solution.py:166
  67.5 1.9 %fusion.5 = bf16[384,8192]{1,0:T(8,128)(2,1)S(1)} fusion(bf16[384,8192]{1,0:T(8,128)(2,1)S(1)} %fusion.3, s32[]{:T(128)S(6)} %select_n.292, f32[384,512]{1,0:T(8,128)S(1)} %bitcast.147, bf16[512,1024]{1,0:T(8,128)(2,1)} %collective-permute-done.4, bf16[384,1024]{1,0:T(8,128)(2,1)S(1)} %copy-done.4, f32[384]{0:T(512)S(1)} %get-tuple-element.29), kind=kOutput, calls=%fused_computation.37 | convolution fusion | flops 404226048 | bytes 3016708 | tf_op jit(solution)/shard_map/dot_general | solution.py:170
  69.5 2.0 %fusion.7 = bf16[384,8192]{1,0:T(8,128)(2,1)S(1)} fusion(bf16[384,8192]{1,0:T(8,128)(2,1)S(1)} %fusion.5, s32[]{:T(128)S(6)} %select_n.293, f32[384,512]{1,0:T(8,128)S(1)} %bitcast.146, bf16[512,1024]{1,0:T(8,128)(2,1)} %collective-permute-done.5, bf16[384,1024]{1,0:T(8,128)(2,1)S(1)} %copy-done.4, f32[384]{0:T(512)S(1)} %get-tuple-element.29), kind=kOutput, calls=%fused_computation.39 | convolution fusion | flops 404226048 | bytes 3016708 | tf_op jit(solution)/shard_map/dot_general | solution.py:170
  73.8 1.8 %fusion.9 = bf16[384,8192]{1,0:T(8,128)(2,1)S(1)} fusion(bf16[384,8192]{1,0:T(8,128)(2,1)S(1)} %fusion.7, s32[]{:T(128)S(6)} %select_n.296, f32[384,512]{1,0:T(8,128)S(1)} %bitcast.145, bf16[512,1024]{1,0:T(8,128)(2,1)} %collective-permute-done.6, bf16[384,1024]{1,0:T(8,128)(2,1)S(1)} %copy-done.4, f32[384]{0:T(512)S(1)} %get-tuple-element.29), kind=kOutput, calls=%fused_computation.41 | convolution fusion | flops 404226048 | bytes 3016708 | tf_op jit(solution)/shard_map/dot_general | solution.py:170
  79.4 0.6 fusion.11
  80.1 0.6 fusion.13
  80.7 0.6 fusion.15
  81.8 1.6 %collective-permute-start.17 = (bf16[16,9216]{1,0:T(8,128)(2,1)S(1)}, bf16[16,9216]{1,0:T(8,128)(2,1)S(1)}, u32[]{:S(2)}, u32[]{:S(2)}) collective-permute-start(bf16[16,9216]{1,0:T(8,128)(2,1)S(1)} %get-tuple-element.9), channel_id=1, source_target_pairs={{0,8},{4,12},{8,0},{12,4},{16,24},{20,28},{24,16},{28,20},{1,9},{5... | collective-permute-start | bytes 884744 | tf_op jit(solution)/shard_map/ppermute | solution.py:149
  83.8 1.5 %collective-permute-start.19 = (bf16[16,9216]{1,0:T(8,128)(2,1)S(1)}, bf16[16,9216]{1,0:T(8,128)(2,1)S(1)}, u32[]{:S(2)}, u32[]{:S(2)}) collective-permute-start(bf16[16,9216]{1,0:T(8,128)(2,1)S(1)} %get-tuple-element.11), channel_id=1, source_target_pairs={{0,24},{4,28},{8,16},{12,20},{16,8},{20,12},{24,0},{28,4},{1,25},{... | collective-permute-start | bytes 884744 | tf_op jit(solution)/shard_map/ppermute | solution.py:149
  85.3 0.6 fusion.17
  85.9 5.7 %collective-permute-done.17 = bf16[16,9216]{1,0:T(8,128)(2,1)S(1)} collective-permute-done((bf16[16,9216]{1,0:T(8,128)(2,1)S(1)}, bf16[16,9216]{1,0:T(8,128)(2,1)S(1)}, u32[]{:S(2)}, u32[]{:S(2)}) %collective-permute-start.17) | collective-permute-done | bytes 294944 | tf_op jit(solution)/shard_map/ppermute | solution.py:149
  91.6 1.3 collective-permute-start.13
  92.9 5.8 %collective-permute-done.18 = bf16[16,9216]{1,0:T(8,128)(2,1)S(1)} collective-permute-done((bf16[16,9216]{1,0:T(8,128)(2,1)S(1)}, bf16[16,9216]{1,0:T(8,128)(2,1)S(1)}, u32[]{:S(2)}, u32[]{:S(2)}) %collective-permute-start.18) | collective-permute-done | bytes 294944 | tf_op jit(solution)/shard_map/ppermute | solution.py:149
  99.0 0.7 slice_bitcast_fusion.12
  99.7 0.6 slice_bitcast_fusion.13
  100.3 9.6 %collective-permute-done.13 = bf16[512,1024]{1,0:T(8,128)(2,1)S(1)} collective-permute-done((bf16[512,1024]{1,0:T(8,128)(2,1)S(1)}, bf16[512,1024]{1,0:T(8,128)(2,1)S(1)}, u32[]{:S(2)}, u32[]{:S(2)}) %collective-permute-start.13) | collective-permute-done | bytes 1048608 | tf_op jit(solution)/shard_map/ppermute | solution.py:56
  109.9 7.2 %collective-permute-done.14 = bf16[512,1024]{1,0:T(8,128)(2,1)S(1)} collective-permute-done((bf16[512,1024]{1,0:T(8,128)(2,1)S(1)}, bf16[512,1024]{1,0:T(8,128)(2,1)S(1)}, u32[]{:S(2)}, u32[]{:S(2)}) %collective-permute-start.14) | collective-permute-done | bytes 1048608 | tf_op jit(solution)/shard_map/ppermute | solution.py:57
  118.8 0.6 fusion.19
  122.0 0.9 fusion.21
  122.9 0.6 fusion.23
  123.5 0.6 fusion.25
  124.2 0.6 fusion.27
  126.5 1.0 multiply_convert_fusion.1
  128.2 0.6 fusion.31
  128.8 2.7 %copy-done.3 = bf16[384,8192]{1,0:T(8,128)(2,1)} copy-done((bf16[384,8192]{1,0:T(8,128)(2,1)}, bf16[384,8192]{1,0:T(8,128)(2,1)S(1)}, u32[]{:S(2)}) %copy-start.3) | copy-done | bytes 6291480
  (121 shorter events, 21.4 us)
Async XLA Ops:
  0.6 11.3 %copy-start = (s32[32]{0:T(128)S(1)}, s32[32]{0:T(128)}, u32[]{:S(2)}) copy-start(s32[32]{0:T(128)} %param.15) | copy-start | bytes 388
  1.7 9.6 %copy-start.5 = (bf16[1,16,8192]{2,1,0:T(8,128)(2,1)S(1)}, bf16[1,16,8192]{2,1,0:T(8,128)(2,1)}, u32[]{:S(2)}) copy-start(bf16[1,16,8192]{2,1,0:T(8,128)(2,1)} %param.11) | copy-start | bytes 786436
  1.7 9.5 %copy-start.11 = (bf16[1,16,1024]{2,1,0:T(8,128)(2,1)S(1)}, bf16[1,16,1024]{2,1,0:T(8,128)(2,1)}, u32[]{:S(2)}) copy-start(bf16[1,16,1024]{2,1,0:T(8,128)(2,1)} %param.12) | copy-start | bytes 98308
  1.7 10.3 %copy-start.13 = (s32[3]{0:T(128)S(1)}, s32[3]{0:T(128)}, u32[]{:S(2)}) copy-start(s32[3]{0:T(128)} %param.13) | copy-start | bytes 40
  1.7 10.9 %collective-permute-start = (bf16[16,9216]{1,0:T(8,128)(2,1)S(1)}, bf16[16,9216]{1,0:T(8,128)(2,1)S(1)}, u32[]{:S(2)}, u32[]{:S(2)}) collective-permute-start(bf16[16,9216]{1,0:T(8,128)(2,1)S(1)} %get-tuple-element.28), channel_id=1, source_target_pairs={{0,8},{4,12},{8,0},{12,4},{16,24},{20,28},{24,16},{28,20},{1,9},{5... | collective-permute-start | bytes 884744 | tf_op jit(solution)/shard_map/ppermute | solution.py:91
  4.7 16.3 %collective-permute-start.1 = (bf16[16,9216]{1,0:T(8,128)(2,1)S(1)}, bf16[16,9216]{1,0:T(8,128)(2,1)S(1)}, u32[]{:S(2)}, u32[]{:S(2)}) collective-permute-start(bf16[16,9216]{1,0:T(8,128)(2,1)S(1)} %get-tuple-element.28), channel_id=1, source_target_pairs={{0,16},{4,20},{8,24},{12,28},{16,0},{20,4},{24,8},{28,12},{1,17},{... | collective-permute-start | bytes 884744 | tf_op jit(solution)/shard_map/ppermute | solution.py:91
  6.2 14.7 %collective-permute-start.2 = (bf16[16,9216]{1,0:T(8,128)(2,1)S(1)}, bf16[16,9216]{1,0:T(8,128)(2,1)S(1)}, u32[]{:S(2)}, u32[]{:S(2)}) collective-permute-start(bf16[16,9216]{1,0:T(8,128)(2,1)S(1)} %get-tuple-element.28), channel_id=1, source_target_pairs={{0,24},{4,28},{8,16},{12,20},{16,8},{20,12},{24,0},{28,4},{1,25},{... | collective-permute-start | bytes 884744 | tf_op jit(solution)/shard_map/ppermute | solution.py:91
  9.3 30.1 %copy-start.12 = (s32[3]{0:T(128)S(1)}, s32[3]{0:T(128)}, u32[]{:S(2)}) copy-start(s32[3]{0:T(128)} %param.14) | copy-start | bytes 40
  9.3 30.3 %collective-permute-start.6 = (bf16[512,1024]{1,0:T(8,128)(2,1)}, bf16[512,1024]{1,0:T(8,128)(2,1)}, u32[]{:S(2)}, u32[]{:S(2)}) collective-permute-start(bf16[512,1024]{1,0:T(8,128)(2,1)} %get-tuple-element.23), channel_id=1, source_target_pairs={{0,8},{1,17},{2,10},{3,19},{4,20},{5,13},{6,22},{7,15},{8,0},{9,25... | collective-permute-start | bytes 3145736 | tf_op jit(solution)/shard_map/ppermute | solution.py:52
  11.2 54.3 %collective-permute-start.4 = (bf16[512,1024]{1,0:T(8,128)(2,1)}, bf16[512,1024]{1,0:T(8,128)(2,1)}, u32[]{:S(2)}, u32[]{:S(2)}) collective-permute-start(bf16[512,1024]{1,0:T(8,128)(2,1)} %get-tuple-element.23), channel_id=1, source_target_pairs={{0,4},{4,0},{8,12},{12,8},{16,20},{20,16},{24,28},{28,24},{1,5},{5... | collective-permute-start | bytes 3145736 | tf_op jit(solution)/shard_map/ppermute | solution.py:49
  12.6 30.6 %collective-permute-start.5 = (bf16[512,1024]{1,0:T(8,128)(2,1)}, bf16[512,1024]{1,0:T(8,128)(2,1)}, u32[]{:S(2)}, u32[]{:S(2)}) collective-permute-start(bf16[512,1024]{1,0:T(8,128)(2,1)} %get-tuple-element.8), channel_id=1, source_target_pairs={{0,4},{4,0},{8,12},{12,8},{16,20},{20,16},{24,28},{28,24},{1,5},{5... | collective-permute-start | bytes 3145736 | tf_op jit(solution)/shard_map/ppermute | solution.py:49
  21.1 24.8 %collective-permute-start.3 = (bf16[4,16,9216]{2,1,0:T(8,128)(2,1)S(1)}, bf16[4,16,9216]{2,1,0:T(8,128)(2,1)S(1)}, u32[]{:S(2)}, u32[]{:S(2)}) collective-permute-start(bf16[4,16,9216]{2,1,0:T(8,128)(2,1)S(1)} %pad_maximum_fusion.2), channel_id=1, source_target_pairs={{0,4},{4,0},{8,12},{12,8},{16,20},{20,16},{24,28},{28,24},{1,5},{5... | collective-permute-start | bytes 3538952 | tf_op jit(solution)/shard_map/ppermute | solution.py:93
  39.6 37.4 %collective-permute-start.8 = (bf16[512,1024]{1,0:T(8,128)(2,1)}, bf16[512,1024]{1,0:T(8,128)(2,1)S(1)}, u32[]{:S(2)}, u32[]{:S(2)}) collective-permute-start(bf16[512,1024]{1,0:T(8,128)(2,1)} %get-tuple-element.8), channel_id=1, source_target_pairs={{0,8},{1,17},{2,10},{3,19},{4,20},{5,13},{6,22},{7,15},{8,0},{9,25... | collective-permute-start | bytes 3145736 | tf_op jit(solution)/shard_map/ppermute | solution.py:52
  39.6 36.8 %collective-permute-start.7 = (bf16[512,1024]{1,0:T(8,128)(2,1)}, bf16[512,1024]{1,0:T(8,128)(2,1)S(1)}, u32[]{:S(2)}, u32[]{:S(2)}) collective-permute-start(bf16[512,1024]{1,0:T(8,128)(2,1)} %collective-permute-done.6), channel_id=1, source_target_pairs={{0,4},{4,0},{8,12},{12,8},{16,20},{20,16},{24,28},{28,24},{1,5},{5... | collective-permute-start | bytes 3145736 | tf_op jit(solution)/shard_map/ppermute | solution.py:55
  43.2 3.8 %copy-start.10 = (bf16[8,16,9216]{2,1,0:T(8,128)(2,1)S(1)}, bf16[8,16,9216]{2,1,0:T(8,128)(2,1)}, u32[]{:S(2)}) copy-start(bf16[8,16,9216]{2,1,0:T(8,128)(2,1)} %constant_dynamic-update-slice_fusion.3) | copy-start | bytes 7077892
  43.2 32.4 %collective-permute-start.9 = (bf16[512,1024]{1,0:T(8,128)(2,1)}, bf16[512,1024]{1,0:T(8,128)(2,1)S(1)}, u32[]{:S(2)}, u32[]{:S(2)}) collective-permute-start(bf16[512,1024]{1,0:T(8,128)(2,1)} %collective-permute-done.6), channel_id=1, source_target_pairs={{0,16},{1,9},{2,18},{3,11},{4,12},{5,21},{6,14},{7,23},{8,24},{9,1... | collective-permute-start | bytes 3145736 | tf_op jit(solution)/shard_map/ppermute | solution.py:56
  43.8 7.5 %slice-start = ((s8[6291456]{0:T(1024)(128)(4,1)}), s8[4194304]{0:T(1024)(128)(4,1)S(1)}, s32[]{:S(2)}) async-start(s8[6291456]{0:T(1024)(128)(4,1)} %bitcast.119), calls=%async_computation | async-start | bytes 8388608
  45.9 29.8 %collective-permute-start.10 = (bf16[512,1024]{1,0:T(8,128)(2,1)}, bf16[512,1024]{1,0:T(8,128)(2,1)S(1)}, u32[]{:S(2)}, u32[]{:S(2)}) collective-permute-start(bf16[512,1024]{1,0:T(8,128)(2,1)} %collective-permute-done.6), channel_id=1, source_target_pairs={{0,1},{1,0},{2,3},{3,2},{4,5},{5,4},{6,7},{7,6},{8,9},{9,8},{10,11... | collective-permute-start | bytes 3145736 | tf_op jit(solution)/shard_map/ppermute | solution.py:57
  47.2 4.1 %slice-start.1 = ((s8[6291456]{0:T(1024)(128)(4,1)}), s8[2097152]{0:T(1024)(128)(4,1)S(1)}, s32[]{:S(2)}) async-start(s8[6291456]{0:T(1024)(128)(4,1)} %bitcast.119), calls=%async_computation.1 | async-start | bytes 4194304
  47.3 1.3 copy-start.4
  58.5 1.6 %copy-start.2 = (bf16[1024,1024]{1,0:T(8,128)(2,1)S(1)}, bf16[1024,1024]{1,0:T(8,128)(2,1)}, u32[]{:S(2)}) copy-start(bf16[1024,1024]{1,0:T(8,128)(2,1)} %param.10) | copy-start | bytes 6291460
  62.0 1.8 %copy-start.9 = (f32[3,128,512]{2,1,0:T(8,128)S(1)}, f32[3,128,512]{2,1,0:T(8,128)}, u32[]{:S(2)}) copy-start(f32[3,128,512]{2,1,0:T(8,128)} %fusion.96) | copy-start | bytes 2359300
  65.5 2.0 %copy-start.8 = (f32[3,128,512]{2,1,0:T(8,128)S(1)}, f32[3,128,512]{2,1,0:T(8,128)}, u32[]{:S(2)}) copy-start(f32[3,128,512]{2,1,0:T(8,128)} %fusion.94) | copy-start | bytes 2359300
  65.5 15.8 %collective-permute-start.16 = (bf16[4,16,9216]{2,1,0:T(8,128)(2,1)S(1)}, bf16[4,16,9216]{2,1,0:T(8,128)(2,1)S(1)}, u32[]{:S(2)}, u32[]{:S(2)}) collective-permute-start(bf16[4,16,9216]{2,1,0:T(8,128)(2,1)S(1)} %pad_maximum_fusion.3), channel_id=1, source_target_pairs={{0,4},{4,0},{8,12},{12,8},{16,20},{20,16},{24,28},{28,24},{1,5},{5... | collective-permute-start | bytes 3538952 | tf_op jit(solution)/shard_map/ppermute | solution.py:136
  67.5 1.9 %copy-start.7 = (f32[3,128,512]{2,1,0:T(8,128)S(1)}, f32[3,128,512]{2,1,0:T(8,128)}, u32[]{:S(2)}) copy-start(f32[3,128,512]{2,1,0:T(8,128)} %fusion.92) | copy-start | bytes 2359300
  72.7 1.1 copy-start.6
  75.9 43.6 %collective-permute-start.12 = (bf16[2,512,1024]{2,1,0:T(8,128)(2,1)S(1)}, bf16[2,512,1024]{2,1,0:T(8,128)(2,1)S(1)}, u32[]{:S(2)}, u32[]{:S(2)}) collective-permute-start(bf16[2,512,1024]{2,1,0:T(8,128)(2,1)S(1)} %pad_maximum_fusion), channel_id=1, source_target_pairs={{0,4},{4,0},{8,12},{12,8},{16,20},{20,16},{24,28},{28,24},{1,5},{5... | collective-permute-start | bytes 6291464 | tf_op jit(solution)/shard_map/ppermute | solution.py:60
  79.3 38.1 %collective-permute-start.11 = (bf16[512,1024]{1,0:T(8,128)(2,1)S(1)}, bf16[512,1024]{1,0:T(8,128)(2,1)S(1)}, u32[]{:S(2)}, u32[]{:S(2)}) collective-permute-start(bf16[512,1024]{1,0:T(8,128)(2,1)S(1)} %collective-permute-done.8), channel_id=1, source_target_pairs={{0,4},{4,0},{8,12},{12,8},{16,20},{20,16},{24,28},{28,24},{1,5},{5... | collective-permute-start | bytes 3145736 | tf_op jit(solution)/shard_map/ppermute | solution.py:55
  81.8 9.9 %collective-permute-start.17 = (bf16[16,9216]{1,0:T(8,128)(2,1)S(1)}, bf16[16,9216]{1,0:T(8,128)(2,1)S(1)}, u32[]{:S(2)}, u32[]{:S(2)}) collective-permute-start(bf16[16,9216]{1,0:T(8,128)(2,1)S(1)} %get-tuple-element.9), channel_id=1, source_target_pairs={{0,8},{4,12},{8,0},{12,4},{16,24},{20,28},{24,16},{28,20},{1,9},{5... | collective-permute-start | bytes 884744 | tf_op jit(solution)/shard_map/ppermute | solution.py:149
  83.3 15.4 %collective-permute-start.18 = (bf16[16,9216]{1,0:T(8,128)(2,1)S(1)}, bf16[16,9216]{1,0:T(8,128)(2,1)S(1)}, u32[]{:S(2)}, u32[]{:S(2)}) collective-permute-start(bf16[16,9216]{1,0:T(8,128)(2,1)S(1)} %get-tuple-element.10), channel_id=1, source_target_pairs={{0,16},{4,20},{8,24},{12,28},{16,0},{20,4},{24,8},{28,12},{1,17},{... | collective-permute-start | bytes 884744 | tf_op jit(solution)/shard_map/ppermute | solution.py:149
  83.8 14.9 %collective-permute-start.19 = (bf16[16,9216]{1,0:T(8,128)(2,1)S(1)}, bf16[16,9216]{1,0:T(8,128)(2,1)S(1)}, u32[]{:S(2)}, u32[]{:S(2)}) collective-permute-start(bf16[16,9216]{1,0:T(8,128)(2,1)S(1)} %get-tuple-element.11), channel_id=1, source_target_pairs={{0,24},{4,28},{8,16},{12,20},{16,8},{20,12},{24,0},{28,4},{1,25},{... | collective-permute-start | bytes 884744 | tf_op jit(solution)/shard_map/ppermute | solution.py:149
  91.6 18.3 %collective-permute-start.13 = (bf16[512,1024]{1,0:T(8,128)(2,1)S(1)}, bf16[512,1024]{1,0:T(8,128)(2,1)S(1)}, u32[]{:S(2)}, u32[]{:S(2)}) collective-permute-start(bf16[512,1024]{1,0:T(8,128)(2,1)S(1)} %collective-permute-done.8), channel_id=1, source_target_pairs={{0,16},{1,9},{2,18},{3,11},{4,12},{5,21},{6,14},{7,23},{8,24},{9,1... | collective-permute-start | bytes 3145736 | tf_op jit(solution)/shard_map/ppermute | solution.py:56
  98.7 18.4 %collective-permute-start.14 = (bf16[512,1024]{1,0:T(8,128)(2,1)S(1)}, bf16[512,1024]{1,0:T(8,128)(2,1)S(1)}, u32[]{:S(2)}, u32[]{:S(2)}) collective-permute-start(bf16[512,1024]{1,0:T(8,128)(2,1)S(1)} %collective-permute-done.8), channel_id=1, source_target_pairs={{0,1},{1,0},{2,3},{3,2},{4,5},{5,4},{6,7},{7,6},{8,9},{9,8},{10,11... | collective-permute-start | bytes 3145736 | tf_op jit(solution)/shard_map/ppermute | solution.py:57
  117.3 7.5 %collective-permute-start.15 = (bf16[2,512,1024]{2,1,0:T(8,128)(2,1)S(1)}, bf16[2,512,1024]{2,1,0:T(8,128)(2,1)S(1)}, u32[]{:S(2)}, u32[]{:S(2)}) collective-permute-start(bf16[2,512,1024]{2,1,0:T(8,128)(2,1)S(1)} %pad_maximum_fusion.1), channel_id=1, source_target_pairs={{0,4},{4,0},{8,12},{12,8},{16,20},{20,16},{24,28},{28,24},{1,5},{5... | collective-permute-start | bytes 6291464 | tf_op jit(solution)/shard_map/ppermute | solution.py:60
  127.5 4.0 %copy-start.1 = (s32[32]{0:T(128)S(1)}, s32[32]{0:T(128)}, u32[]{:S(2)}) copy-start(s32[32]{0:T(128)} %param.15) | copy-start | bytes 388
  128.8 2.7 %copy-start.3 = (bf16[384,8192]{1,0:T(8,128)(2,1)}, bf16[384,8192]{1,0:T(8,128)(2,1)S(1)}, u32[]{:S(2)}) copy-start(bf16[384,8192]{1,0:T(8,128)(2,1)S(1)} %fusion.31) | copy-start | bytes 18874372

commit v12 on v11

--- a/solution.py
+++ b/solution.py
@@ -141,7 +141,7 @@
     weight_pieces = relay_gather(frozen_value_weight, members, groups, me, dp_index)
     if weight_pieces and len(weight_pieces[0]) == 2:
         weight_pieces = [(source, 0, value) for source, value in weight_pieces]
-    last_pieces = (weight_pieces[6][2],)
+    last_pieces = (weight_pieces[-4][2],)
     grad_sum = pair_sums[0]
     for index, step in enumerate(even_steps):
         sent = pair_sums[index + 1].astype(jnp.bfloat16)

time: 132 us -> 130 us (0.985)
  waiting for transfers between devices: 36.1 us -> 32.8 us
    ppermute x3, waiting for transfers between devices: 11.5 us -> 5.38 us  [on_device(): lax.ppermute(sent, 'fsdp', xor_pairs(members, step)).astype(jnp.float32)]
    ppermute x2, waiting for transfers between devices: 7.16 us -> 10.1 us  [relay_gather(): partner = lax.ppermute(first, ('fsdp', 'dp'), partner_pairs)]
  transfers between devices with their start and end apart: 20 -> 20, of which waited for: 5 -> 4; matrix products, arithmetic and copies ran while one was open for 39% -> 39% of each run, Pallas kernels for 0% -> 0%
where the time goes in v12:
time: 130 us; the launch traced here: 129 us
  matrix products  41.6 us (32%)
  waiting for transfers between devices  32.8 us (25%)
  between operations  19.1 us (15%)
  starting transfers between devices  17.2 us (13%)
  local copies, waits for them, and re-layouts  11 us (8%)
  other arithmetic  7.79 us (6%)
    dot_general x16, matrix products, on_device(): lax.dot_general(masked_cot, weight_piece, (((1,), (1,)), ((), ())), prefe...  15.3 us
    dot_general x16, matrix products, on_device(): jnp.dot(token_piece, weight_piece, preferred_element_type=jnp.float32)  13.4 us
    ppermute x2, waiting for transfers between devices, relay_gather(): partner = lax.ppermute(first, ('fsdp', 'dp'), partner_pairs)  10.1 us
    ppermute x2, waiting for transfers between devices, relay_gather(): relayed = lax.ppermute(first, ('fsdp', 'dp'), relay_pairs)  9.54 us
    dot_general x16, matrix products, on_device(): jnp.einsum('uio,uof->uif', low_rank_gradient, down_piece, preferred_eleme...  9.36 us
    ppermute x3, waiting for transfers between devices, on_device(): by_step[step] = lax.ppermute(own_adapter, 'fsdp', xor_pairs(members, step))  7.79 us
    ppermute x3, waiting for transfers between devices, on_device(): lax.ppermute(sent, 'fsdp', xor_pairs(members, step)).astype(jnp.float32)  5.38 us
    unnamed x38, local copies, waits for them, and re-layouts  4.55 us
  transfers between devices with their start and end apart: 20, of which 4 were waited for; matrix products, arithmetic and copies ran while one was open for 39% of the time, Pallas kernels for 0%

profile of v12, /device:TPU:0, one launch (start us, length us, event | category | flops | bytes accessed | tf_op | source)
XLA Modules:
  0.0 129.5 jit_solution(16095756114770967990)
XLA Ops:
  0.6 1.0 fusion.136
  1.7 3.0 %collective-permute-start = (bf16[16,9216]{1,0:T(8,128)(2,1)S(1)}, bf16[16,9216]{1,0:T(8,128)(2,1)S(1)}, u32[]{:S(2)}, u32[]{:S(2)}) collective-permute-start(bf16[16,9216]{1,0:T(8,128)(2,1)S(1)} %get-tuple-element.28), channel_id=1, source_target_pairs={{0,8},{4,12},{8,0},{12,4},{16,24},{20,28},{24,16},{28,20},{1,9},{5... | collective-permute-start | bytes 884744 | tf_op jit(solution)/shard_map/ppermute | solution.py:91
  4.7 1.5 %collective-permute-start.1 = (bf16[16,9216]{1,0:T(8,128)(2,1)S(1)}, bf16[16,9216]{1,0:T(8,128)(2,1)S(1)}, u32[]{:S(2)}, u32[]{:S(2)}) collective-permute-start(bf16[16,9216]{1,0:T(8,128)(2,1)S(1)} %get-tuple-element.28), channel_id=1, source_target_pairs={{0,16},{4,20},{8,24},{12,28},{16,0},{20,4},{24,8},{28,12},{1,17},{... | collective-permute-start | bytes 884744 | tf_op jit(solution)/shard_map/ppermute | solution.py:91
  6.2 3.0 %fusion.143 = (bf16[512,1024]{1,0:T(8,128)(2,1)}, bf16[512,1024]{1,0:T(8,128)(2,1)}) fusion(bf16[1024,1024]{1,0:T(8,128)(2,1)} %param.10), kind=kLoop, calls=%fused_computation.219 | loop fusion | bytes 4194304 | tf_op jit(solution)/shard_map/slice | solution.py:47
  9.3 1.9 %collective-permute-start.6 = (bf16[512,1024]{1,0:T(8,128)(2,1)}, bf16[512,1024]{1,0:T(8,128)(2,1)}, u32[]{:S(2)}, u32[]{:S(2)}) collective-permute-start(bf16[512,1024]{1,0:T(8,128)(2,1)} %get-tuple-element.23), channel_id=1, source_target_pairs={{0,8},{1,17},{2,10},{3,19},{4,20},{5,13},{6,22},{7,15},{8,0},{9,25... | collective-permute-start | bytes 3145736 | tf_op jit(solution)/shard_map/ppermute | solution.py:52
  11.2 0.7 constant_dynamic-update-slice_fusion.3
  12.0 0.6 gather_fusion
  13.2 7.8 %collective-permute-done.1 = bf16[16,9216]{1,0:T(8,128)(2,1)S(1)} collective-permute-done((bf16[16,9216]{1,0:T(8,128)(2,1)S(1)}, bf16[16,9216]{1,0:T(8,128)(2,1)S(1)}, u32[]{:S(2)}, u32[]{:S(2)}) %collective-permute-start.1) | collective-permute-done | bytes 294944 | tf_op jit(solution)/shard_map/ppermute | solution.py:91
  39.6 1.7 %collective-permute-start.7 = (bf16[512,1024]{1,0:T(8,128)(2,1)}, bf16[512,1024]{1,0:T(8,128)(2,1)S(1)}, u32[]{:S(2)}, u32[]{:S(2)}) collective-permute-start(bf16[512,1024]{1,0:T(8,128)(2,1)} %collective-permute-done.6), channel_id=1, source_target_pairs={{0,4},{4,0},{8,12},{12,8},{16,20},{20,16},{24,28},{28,24},{1,5},{5... | collective-permute-start | bytes 3145736 | tf_op jit(solution)/shard_map/ppermute | solution.py:55
  41.3 1.9 %fusion.58 = f32[384,1024]{1,0:T(8,128)S(1)} fusion(bf16[512,1024]{1,0:T(8,128)(2,1)} %collective-permute-done.6, bf16[384,8192]{1,0:T(8,128)(2,1)} %param.8, s32[]{:T(128)S(6)} %select_n.296), kind=kOutput, calls=%fused_computation.113 | convolution fusion | flops 402653184 | bytes 3014660 | tf_op jit(solution)/shard_map/dot_general | solution.py:166
  43.8 2.1 %fusion.60 = f32[384,1024]{1,0:T(8,128)S(1)} fusion(bf16[512,1024]{1,0:T(8,128)(2,1)} %collective-permute-done.5, bf16[384,8192]{1,0:T(8,128)(2,1)} %param.8, s32[]{:T(128)S(6)} %select_n.293), kind=kOutput, calls=%fused_computation.115 | convolution fusion | flops 402653184 | bytes 3014660 | tf_op jit(solution)/shard_map/dot_general | solution.py:166
  45.9 1.1 collective-permute-start.10
  47.5 1.1 copy-done.4
  48.9 1.2 fusion.92
  50.1 1.2 fusion.90
  51.3 0.9 fusion.145
  52.2 1.7 %fusion.32 = bf16[3,16,128]{2,1,0:T(8,128)(2,1)S(1)} fusion(bf16[3,128,8192]{2,1,0:T(8,128)(2,1)S(1)} %bitcast.122, f32[3,128]{1,0:T(4,128)S(1)} %get-tuple-element.30, bf16[3,16,9216]{2,1,0:T(8,128)(2,1)S(1)} %pad_maximum_fusion.4), kind=kOutput, calls=%fused_computation.69 | convolution fusion | flops 100675584 | bytes 7092224 | tf_op jit(solution)/shard_map/cvj,coj->cvo/dot_general | solution.py:111
  54.6 1.2 fusion.98
  55.8 1.2 fusion.96
  57.0 1.2 fusion.94
  61.3 0.7 broadcast_in_dim.44
  62.0 1.8 %fusion.1 = bf16[384,8192]{1,0:T(8,128)(2,1)S(1)} fusion(bf16[384,8192]{1,0:T(8,128)(2,1)S(1)} %broadcast_in_dim.44, s32[]{:T(128)S(6)} %select_n.290, f32[384,512]{1,0:T(8,128)} %bitcast.149, bf16[1024,1024]{1,0:T(8,128)(2,1)S(1)} %copy-done.2, bf16[384,1024]{1,0:T(8,128)(2,1)S(1)} %copy-done.4, f32[384]{0:T(512)S(1)} %get-tuple-element.29), kind=kOutput, calls=%fused_computation.33 | convolution fusion | flops 404226048 | bytes 3016708 | tf_op jit(solution)/shard_map/dot_general | solution.py:170
  63.9 0.6 fusion.3
  65.6 1.9 %convolution_add_fusion.3 = f32[384,1024]{1,0:T(8,128)S(1)} fusion(f32[384,1024]{1,0:T(8,128)S(1)} %convolution_add_fusion.4, bf16[512,1024]{1,0:T(8,128)(2,1)} %collective-permute-done.4, bf16[384,8192]{1,0:T(8,128)(2,1)S(1)} %bitcast.120, s32[]{:T(128)S(6)} %select_n.292), kind=kOutput, calls=%fused_computation.13 | convolution fusion | flops 403046400 | bytes 4587524 | tf_op jit(solution)/shard_map/dot_general | solution.py:166
  67.5 1.9 %fusion.5 = bf16[384,8192]{1,0:T(8,128)(2,1)S(1)} fusion(bf16[384,8192]{1,0:T(8,128)(2,1)S(1)} %fusion.3, s32[]{:T(128)S(6)} %select_n.292, f32[384,512]{1,0:T(8,128)S(1)} %bitcast.147, bf16[512,1024]{1,0:T(8,128)(2,1)} %collective-permute-done.4, bf16[384,1024]{1,0:T(8,128)(2,1)S(1)} %copy-done.4, f32[384]{0:T(512)S(1)} %get-tuple-element.29), kind=kOutput, calls=%fused_computation.37 | convolution fusion | flops 404226048 | bytes 3016708 | tf_op jit(solution)/shard_map/dot_general | solution.py:170
  69.5 2.0 %fusion.7 = bf16[384,8192]{1,0:T(8,128)(2,1)S(1)} fusion(bf16[384,8192]{1,0:T(8,128)(2,1)S(1)} %fusion.5, s32[]{:T(128)S(6)} %select_n.293, f32[384,512]{1,0:T(8,128)S(1)} %bitcast.146, bf16[512,1024]{1,0:T(8,128)(2,1)} %collective-permute-done.5, bf16[384,1024]{1,0:T(8,128)(2,1)S(1)} %copy-done.4, f32[384]{0:T(512)S(1)} %get-tuple-element.29), kind=kOutput, calls=%fused_computation.39 | convolution fusion | flops 404226048 | bytes 3016708 | tf_op jit(solution)/shard_map/dot_general | solution.py:170
  73.8 1.8 %fusion.9 = bf16[384,8192]{1,0:T(8,128)(2,1)S(1)} fusion(bf16[384,8192]{1,0:T(8,128)(2,1)S(1)} %fusion.7, s32[]{:T(128)S(6)} %select_n.296, f32[384,512]{1,0:T(8,128)S(1)} %bitcast.145, bf16[512,1024]{1,0:T(8,128)(2,1)} %collective-permute-done.6, bf16[384,1024]{1,0:T(8,128)(2,1)S(1)} %copy-done.4, f32[384]{0:T(512)S(1)} %get-tuple-element.29), kind=kOutput, calls=%fused_computation.41 | convolution fusion | flops 404226048 | bytes 3016708 | tf_op jit(solution)/shard_map/dot_general | solution.py:170
  79.3 1.3 %collective-permute-start.13 = (bf16[512,1024]{1,0:T(8,128)(2,1)S(1)}, bf16[512,1024]{1,0:T(8,128)(2,1)S(1)}, u32[]{:S(2)}, u32[]{:S(2)}) collective-permute-start(bf16[512,1024]{1,0:T(8,128)(2,1)S(1)} %collective-permute-done.8), channel_id=1, source_target_pairs={{0,16},{1,9},{2,18},{3,11},{4,12},{5,21},{6,14},{7,23},{8,24},{9,1... | collective-permute-start | bytes 3145736 | tf_op jit(solution)/shard_map/ppermute | solution.py:56
  80.7 1.0 collective-permute-start.14
  81.7 0.6 fusion.11
  82.3 0.6 fusion.13
  82.9 0.6 fusion.15
  83.5 0.6 fusion.17
  84.6 9.5 %collective-permute-done.13 = bf16[512,1024]{1,0:T(8,128)(2,1)S(1)} collective-permute-done((bf16[512,1024]{1,0:T(8,128)(2,1)S(1)}, bf16[512,1024]{1,0:T(8,128)(2,1)S(1)}, u32[]{:S(2)}, u32[]{:S(2)}) %collective-permute-start.13) | collective-permute-done | bytes 1048608 | tf_op jit(solution)/shard_map/ppermute | solution.py:56
  94.2 1.5 %collective-permute-start.17 = (bf16[16,9216]{1,0:T(8,128)(2,1)S(1)}, bf16[16,9216]{1,0:T(8,128)(2,1)S(1)}, u32[]{:S(2)}, u32[]{:S(2)}) collective-permute-start(bf16[16,9216]{1,0:T(8,128)(2,1)S(1)} %get-tuple-element.9), channel_id=1, source_target_pairs={{0,8},{4,12},{8,0},{12,4},{16,24},{20,28},{24,16},{28,20},{1,9},{5... | collective-permute-start | bytes 884744 | tf_op jit(solution)/shard_map/ppermute | solution.py:149
  96.2 10.1 %collective-permute-done.14 = bf16[512,1024]{1,0:T(8,128)(2,1)S(1)} collective-permute-done((bf16[512,1024]{1,0:T(8,128)(2,1)S(1)}, bf16[512,1024]{1,0:T(8,128)(2,1)S(1)}, u32[]{:S(2)}, u32[]{:S(2)}) %collective-permute-start.14) | collective-permute-done | bytes 1048608 | tf_op jit(solution)/shard_map/ppermute | solution.py:57
  106.2 1.7 %collective-permute-start.19 = (bf16[16,9216]{1,0:T(8,128)(2,1)S(1)}, bf16[16,9216]{1,0:T(8,128)(2,1)S(1)}, u32[]{:S(2)}, u32[]{:S(2)}) collective-permute-start(bf16[16,9216]{1,0:T(8,128)(2,1)S(1)} %get-tuple-element.11), channel_id=1, source_target_pairs={{0,24},{4,28},{8,16},{12,20},{16,8},{20,12},{24,0},{28,4},{1,25},{... | collective-permute-start | bytes 884744 | tf_op jit(solution)/shard_map/ppermute | solution.py:149
  108.2 0.6 fusion.19
  110.4 5.4 %collective-permute-done.19 = bf16[16,9216]{1,0:T(8,128)(2,1)S(1)} collective-permute-done((bf16[16,9216]{1,0:T(8,128)(2,1)S(1)}, bf16[16,9216]{1,0:T(8,128)(2,1)S(1)}, u32[]{:S(2)}, u32[]{:S(2)}) %collective-permute-start.19) | collective-permute-done | bytes 294944 | tf_op jit(solution)/shard_map/ppermute | solution.py:149
  116.0 0.6 slice_bitcast_fusion.13
  116.6 0.7 slice_bitcast_fusion.12
  119.9 0.9 fusion.21
  120.8 0.6 fusion.23
  121.4 0.6 fusion.25
  122.0 0.6 fusion.27
  124.5 1.0 multiply_convert_fusion.1
  126.1 0.6 fusion.31
  126.8 2.7 %copy-done.3 = bf16[384,8192]{1,0:T(8,128)(2,1)} copy-done((bf16[384,8192]{1,0:T(8,128)(2,1)}, bf16[384,8192]{1,0:T(8,128)(2,1)S(1)}, u32[]{:S(2)}) %copy-start.3) | copy-done | bytes 6291480
  (121 shorter events, 21.4 us)
Async XLA Ops:
  0.6 11.3 %copy-start = (s32[32]{0:T(128)S(1)}, s32[32]{0:T(128)}, u32[]{:S(2)}) copy-start(s32[32]{0:T(128)} %param.15) | copy-start | bytes 388
  1.7 9.6 %copy-start.5 = (bf16[1,16,8192]{2,1,0:T(8,128)(2,1)S(1)}, bf16[1,16,8192]{2,1,0:T(8,128)(2,1)}, u32[]{:S(2)}) copy-start(bf16[1,16,8192]{2,1,0:T(8,128)(2,1)} %param.11) | copy-start | bytes 786436
  1.7 9.5 %copy-start.11 = (bf16[1,16,1024]{2,1,0:T(8,128)(2,1)S(1)}, bf16[1,16,1024]{2,1,0:T(8,128)(2,1)}, u32[]{:S(2)}) copy-start(bf16[1,16,1024]{2,1,0:T(8,128)(2,1)} %param.12) | copy-start | bytes 98308
  1.7 10.3 %copy-start.13 = (s32[3]{0:T(128)S(1)}, s32[3]{0:T(128)}, u32[]{:S(2)}) copy-start(s32[3]{0:T(128)} %param.13) | copy-start | bytes 40
  1.7 10.9 %collective-permute-start = (bf16[16,9216]{1,0:T(8,128)(2,1)S(1)}, bf16[16,9216]{1,0:T(8,128)(2,1)S(1)}, u32[]{:S(2)}, u32[]{:S(2)}) collective-permute-start(bf16[16,9216]{1,0:T(8,128)(2,1)S(1)} %get-tuple-element.28), channel_id=1, source_target_pairs={{0,8},{4,12},{8,0},{12,4},{16,24},{20,28},{24,16},{28,20},{1,9},{5... | collective-permute-start | bytes 884744 | tf_op jit(solution)/shard_map/ppermute | solution.py:91
  4.7 16.3 %collective-permute-start.1 = (bf16[16,9216]{1,0:T(8,128)(2,1)S(1)}, bf16[16,9216]{1,0:T(8,128)(2,1)S(1)}, u32[]{:S(2)}, u32[]{:S(2)}) collective-permute-start(bf16[16,9216]{1,0:T(8,128)(2,1)S(1)} %get-tuple-element.28), channel_id=1, source_target_pairs={{0,16},{4,20},{8,24},{12,28},{16,0},{20,4},{24,8},{28,12},{1,17},{... | collective-permute-start | bytes 884744 | tf_op jit(solution)/shard_map/ppermute | solution.py:91
  6.2 14.7 %collective-permute-start.2 = (bf16[16,9216]{1,0:T(8,128)(2,1)S(1)}, bf16[16,9216]{1,0:T(8,128)(2,1)S(1)}, u32[]{:S(2)}, u32[]{:S(2)}) collective-permute-start(bf16[16,9216]{1,0:T(8,128)(2,1)S(1)} %get-tuple-element.28), channel_id=1, source_target_pairs={{0,24},{4,28},{8,16},{12,20},{16,8},{20,12},{24,0},{28,4},{1,25},{... | collective-permute-start | bytes 884744 | tf_op jit(solution)/shard_map/ppermute | solution.py:91
  9.3 30.1 %copy-start.12 = (s32[3]{0:T(128)S(1)}, s32[3]{0:T(128)}, u32[]{:S(2)}) copy-start(s32[3]{0:T(128)} %param.14) | copy-start | bytes 40
  9.3 30.3 %collective-permute-start.6 = (bf16[512,1024]{1,0:T(8,128)(2,1)}, bf16[512,1024]{1,0:T(8,128)(2,1)}, u32[]{:S(2)}, u32[]{:S(2)}) collective-permute-start(bf16[512,1024]{1,0:T(8,128)(2,1)} %get-tuple-element.23), channel_id=1, source_target_pairs={{0,8},{1,17},{2,10},{3,19},{4,20},{5,13},{6,22},{7,15},{8,0},{9,25... | collective-permute-start | bytes 3145736 | tf_op jit(solution)/shard_map/ppermute | solution.py:52
  11.2 54.3 %collective-permute-start.4 = (bf16[512,1024]{1,0:T(8,128)(2,1)}, bf16[512,1024]{1,0:T(8,128)(2,1)}, u32[]{:S(2)}, u32[]{:S(2)}) collective-permute-start(bf16[512,1024]{1,0:T(8,128)(2,1)} %get-tuple-element.23), channel_id=1, source_target_pairs={{0,4},{4,0},{8,12},{12,8},{16,20},{20,16},{24,28},{28,24},{1,5},{5... | collective-permute-start | bytes 3145736 | tf_op jit(solution)/shard_map/ppermute | solution.py:49
  12.6 30.6 %collective-permute-start.5 = (bf16[512,1024]{1,0:T(8,128)(2,1)}, bf16[512,1024]{1,0:T(8,128)(2,1)}, u32[]{:S(2)}, u32[]{:S(2)}) collective-permute-start(bf16[512,1024]{1,0:T(8,128)(2,1)} %get-tuple-element.8), channel_id=1, source_target_pairs={{0,4},{4,0},{8,12},{12,8},{16,20},{20,16},{24,28},{28,24},{1,5},{5... | collective-permute-start | bytes 3145736 | tf_op jit(solution)/shard_map/ppermute | solution.py:49
  21.1 24.8 %collective-permute-start.3 = (bf16[4,16,9216]{2,1,0:T(8,128)(2,1)S(1)}, bf16[4,16,9216]{2,1,0:T(8,128)(2,1)S(1)}, u32[]{:S(2)}, u32[]{:S(2)}) collective-permute-start(bf16[4,16,9216]{2,1,0:T(8,128)(2,1)S(1)} %pad_maximum_fusion.2), channel_id=1, source_target_pairs={{0,4},{4,0},{8,12},{12,8},{16,20},{20,16},{24,28},{28,24},{1,5},{5... | collective-permute-start | bytes 3538952 | tf_op jit(solution)/shard_map/ppermute | solution.py:93
  39.6 37.4 %collective-permute-start.8 = (bf16[512,1024]{1,0:T(8,128)(2,1)}, bf16[512,1024]{1,0:T(8,128)(2,1)S(1)}, u32[]{:S(2)}, u32[]{:S(2)}) collective-permute-start(bf16[512,1024]{1,0:T(8,128)(2,1)} %get-tuple-element.8), channel_id=1, source_target_pairs={{0,8},{1,17},{2,10},{3,19},{4,20},{5,13},{6,22},{7,15},{8,0},{9,25... | collective-permute-start | bytes 3145736 | tf_op jit(solution)/shard_map/ppermute | solution.py:52
  39.6 36.8 %collective-permute-start.7 = (bf16[512,1024]{1,0:T(8,128)(2,1)}, bf16[512,1024]{1,0:T(8,128)(2,1)S(1)}, u32[]{:S(2)}, u32[]{:S(2)}) collective-permute-start(bf16[512,1024]{1,0:T(8,128)(2,1)} %collective-permute-done.6), channel_id=1, source_target_pairs={{0,4},{4,0},{8,12},{12,8},{16,20},{20,16},{24,28},{28,24},{1,5},{5... | collective-permute-start | bytes 3145736 | tf_op jit(solution)/shard_map/ppermute | solution.py:55
  43.2 3.8 %copy-start.10 = (bf16[8,16,9216]{2,1,0:T(8,128)(2,1)S(1)}, bf16[8,16,9216]{2,1,0:T(8,128)(2,1)}, u32[]{:S(2)}) copy-start(bf16[8,16,9216]{2,1,0:T(8,128)(2,1)} %constant_dynamic-update-slice_fusion.3) | copy-start | bytes 7077892
  43.2 32.4 %collective-permute-start.9 = (bf16[512,1024]{1,0:T(8,128)(2,1)}, bf16[512,1024]{1,0:T(8,128)(2,1)S(1)}, u32[]{:S(2)}, u32[]{:S(2)}) collective-permute-start(bf16[512,1024]{1,0:T(8,128)(2,1)} %collective-permute-done.6), channel_id=1, source_target_pairs={{0,16},{1,9},{2,18},{3,11},{4,12},{5,21},{6,14},{7,23},{8,24},{9,1... | collective-permute-start | bytes 3145736 | tf_op jit(solution)/shard_map/ppermute | solution.py:56
  43.8 7.5 %slice-start = ((s8[6291456]{0:T(1024)(128)(4,1)}), s8[4194304]{0:T(1024)(128)(4,1)S(1)}, s32[]{:S(2)}) async-start(s8[6291456]{0:T(1024)(128)(4,1)} %bitcast.119), calls=%async_computation | async-start | bytes 8388608
  45.9 29.8 %collective-permute-start.10 = (bf16[512,1024]{1,0:T(8,128)(2,1)}, bf16[512,1024]{1,0:T(8,128)(2,1)S(1)}, u32[]{:S(2)}, u32[]{:S(2)}) collective-permute-start(bf16[512,1024]{1,0:T(8,128)(2,1)} %collective-permute-done.6), channel_id=1, source_target_pairs={{0,1},{1,0},{2,3},{3,2},{4,5},{5,4},{6,7},{7,6},{8,9},{9,8},{10,11... | collective-permute-start | bytes 3145736 | tf_op jit(solution)/shard_map/ppermute | solution.py:57
  47.2 4.1 %slice-start.1 = ((s8[6291456]{0:T(1024)(128)(4,1)}), s8[2097152]{0:T(1024)(128)(4,1)S(1)}, s32[]{:S(2)}) async-start(s8[6291456]{0:T(1024)(128)(4,1)} %bitcast.119), calls=%async_computation.1 | async-start | bytes 4194304
  47.3 1.3 copy-start.4
  58.5 1.6 %copy-start.2 = (bf16[1024,1024]{1,0:T(8,128)(2,1)S(1)}, bf16[1024,1024]{1,0:T(8,128)(2,1)}, u32[]{:S(2)}) copy-start(bf16[1024,1024]{1,0:T(8,128)(2,1)} %param.10) | copy-start | bytes 6291460
  62.0 1.8 %copy-start.9 = (f32[3,128,512]{2,1,0:T(8,128)S(1)}, f32[3,128,512]{2,1,0:T(8,128)}, u32[]{:S(2)}) copy-start(f32[3,128,512]{2,1,0:T(8,128)} %fusion.96) | copy-start | bytes 2359300
  65.5 2.0 %copy-start.8 = (f32[3,128,512]{2,1,0:T(8,128)S(1)}, f32[3,128,512]{2,1,0:T(8,128)}, u32[]{:S(2)}) copy-start(f32[3,128,512]{2,1,0:T(8,128)} %fusion.94) | copy-start | bytes 2359300
  65.5 18.6 %collective-permute-start.16 = (bf16[4,16,9216]{2,1,0:T(8,128)(2,1)S(1)}, bf16[4,16,9216]{2,1,0:T(8,128)(2,1)S(1)}, u32[]{:S(2)}, u32[]{:S(2)}) collective-permute-start(bf16[4,16,9216]{2,1,0:T(8,128)(2,1)S(1)} %pad_maximum_fusion.3), channel_id=1, source_target_pairs={{0,4},{4,0},{8,12},{12,8},{16,20},{20,16},{24,28},{28,24},{1,5},{5... | collective-permute-start | bytes 3538952 | tf_op jit(solution)/shard_map/ppermute | solution.py:136
  67.5 1.9 %copy-start.7 = (f32[3,128,512]{2,1,0:T(8,128)S(1)}, f32[3,128,512]{2,1,0:T(8,128)}, u32[]{:S(2)}) copy-start(f32[3,128,512]{2,1,0:T(8,128)} %fusion.92) | copy-start | bytes 2359300
  72.7 1.1 copy-start.6
  75.9 41.4 %collective-permute-start.12 = (bf16[2,512,1024]{2,1,0:T(8,128)(2,1)S(1)}, bf16[2,512,1024]{2,1,0:T(8,128)(2,1)S(1)}, u32[]{:S(2)}, u32[]{:S(2)}) collective-permute-start(bf16[2,512,1024]{2,1,0:T(8,128)(2,1)S(1)} %pad_maximum_fusion), channel_id=1, source_target_pairs={{0,4},{4,0},{8,12},{12,8},{16,20},{20,16},{24,28},{28,24},{1,5},{5... | collective-permute-start | bytes 6291464 | tf_op jit(solution)/shard_map/ppermute | solution.py:60
  79.3 14.9 %collective-permute-start.13 = (bf16[512,1024]{1,0:T(8,128)(2,1)S(1)}, bf16[512,1024]{1,0:T(8,128)(2,1)S(1)}, u32[]{:S(2)}, u32[]{:S(2)}) collective-permute-start(bf16[512,1024]{1,0:T(8,128)(2,1)S(1)} %collective-permute-done.8), channel_id=1, source_target_pairs={{0,16},{1,9},{2,18},{3,11},{4,12},{5,21},{6,14},{7,23},{8,24},{9,1... | collective-permute-start | bytes 3145736 | tf_op jit(solution)/shard_map/ppermute | solution.py:56
  80.6 27.5 %collective-permute-start.11 = (bf16[512,1024]{1,0:T(8,128)(2,1)S(1)}, bf16[512,1024]{1,0:T(8,128)(2,1)S(1)}, u32[]{:S(2)}, u32[]{:S(2)}) collective-permute-start(bf16[512,1024]{1,0:T(8,128)(2,1)S(1)} %collective-permute-done.8), channel_id=1, source_target_pairs={{0,4},{4,0},{8,12},{12,8},{16,20},{20,16},{24,28},{28,24},{1,5},{5... | collective-permute-start | bytes 3145736 | tf_op jit(solution)/shard_map/ppermute | solution.py:55
  80.7 25.6 %collective-permute-start.14 = (bf16[512,1024]{1,0:T(8,128)(2,1)S(1)}, bf16[512,1024]{1,0:T(8,128)(2,1)S(1)}, u32[]{:S(2)}, u32[]{:S(2)}) collective-permute-start(bf16[512,1024]{1,0:T(8,128)(2,1)S(1)} %collective-permute-done.8), channel_id=1, source_target_pairs={{0,1},{1,0},{2,3},{3,2},{4,5},{5,4},{6,7},{7,6},{8,9},{9,8},{10,11... | collective-permute-start | bytes 3145736 | tf_op jit(solution)/shard_map/ppermute | solution.py:57
  94.2 16.2 %collective-permute-start.17 = (bf16[16,9216]{1,0:T(8,128)(2,1)S(1)}, bf16[16,9216]{1,0:T(8,128)(2,1)S(1)}, u32[]{:S(2)}, u32[]{:S(2)}) collective-permute-start(bf16[16,9216]{1,0:T(8,128)(2,1)S(1)} %get-tuple-element.9), channel_id=1, source_target_pairs={{0,8},{4,12},{8,0},{12,4},{16,24},{20,28},{24,16},{28,20},{1,9},{5... | collective-permute-start | bytes 884744 | tf_op jit(solution)/shard_map/ppermute | solution.py:149
  95.7 14.7 %collective-permute-start.18 = (bf16[16,9216]{1,0:T(8,128)(2,1)S(1)}, bf16[16,9216]{1,0:T(8,128)(2,1)S(1)}, u32[]{:S(2)}, u32[]{:S(2)}) collective-permute-start(bf16[16,9216]{1,0:T(8,128)(2,1)S(1)} %get-tuple-element.10), channel_id=1, source_target_pairs={{0,16},{4,20},{8,24},{12,28},{16,0},{20,4},{24,8},{28,12},{1,17},{... | collective-permute-start | bytes 884744 | tf_op jit(solution)/shard_map/ppermute | solution.py:149
  106.2 9.5 %collective-permute-start.19 = (bf16[16,9216]{1,0:T(8,128)(2,1)S(1)}, bf16[16,9216]{1,0:T(8,128)(2,1)S(1)}, u32[]{:S(2)}, u32[]{:S(2)}) collective-permute-start(bf16[16,9216]{1,0:T(8,128)(2,1)S(1)} %get-tuple-element.11), channel_id=1, source_target_pairs={{0,24},{4,28},{8,16},{12,20},{16,8},{20,12},{24,0},{28,4},{1,25},{... | collective-permute-start | bytes 884744 | tf_op jit(solution)/shard_map/ppermute | solution.py:149
  108.1 14.6 %collective-permute-start.15 = (bf16[2,512,1024]{2,1,0:T(8,128)(2,1)S(1)}, bf16[2,512,1024]{2,1,0:T(8,128)(2,1)S(1)}, u32[]{:S(2)}, u32[]{:S(2)}) collective-permute-start(bf16[2,512,1024]{2,1,0:T(8,128)(2,1)S(1)} %pad_maximum_fusion.1), channel_id=1, source_target_pairs={{0,4},{4,0},{8,12},{12,8},{16,20},{20,16},{24,28},{28,24},{1,5},{5... | collective-permute-start | bytes 6291464 | tf_op jit(solution)/shard_map/ppermute | solution.py:60
  125.5 4.0 %copy-start.1 = (s32[32]{0:T(128)S(1)}, s32[32]{0:T(128)}, u32[]{:S(2)}) copy-start(s32[32]{0:T(128)} %param.15) | copy-start | bytes 388
  126.8 2.7 %copy-start.3 = (bf16[384,8192]{1,0:T(8,128)(2,1)}, bf16[384,8192]{1,0:T(8,128)(2,1)S(1)}, u32[]{:S(2)}) copy-start(bf16[384,8192]{1,0:T(8,128)(2,1)S(1)} %fusion.31) | copy-start | bytes 18874372

commit v13 on v12

--- a/solution.py
+++ b/solution.py
@@ -57,9 +57,10 @@
         partner = lax.ppermute(first, ("fsdp", "dp"), partner_pairs)
         result.append((4.5 + 2 * k, sources[2], k, relayed))
         result.append((4.5 + 2 * k, sources[3], k, partner))
-        late = lax.ppermute(jnp.stack([relayed, partner]), "fsdp", xor_pairs(members, 1))
-        result.append((5.5 + 2 * k, sibling_sources[2], k, late[0]))
-        result.append((5.5 + 2 * k, sibling_sources[3], k, late[1]))
+        result.append((5.5 + 2 * k, sibling_sources[2], k,
+                       lax.ppermute(relayed, "fsdp", xor_pairs(members, 1))))
+        result.append((5.5 + 2 * k, sibling_sources[3], k,
+                       lax.ppermute(partner, "fsdp", xor_pairs(members, 1))))
     result.sort(key=lambda item: item[0])
     return [item[1:] for item in result]
 

time: 130 us -> 124 us (0.954)
  waiting for transfers between devices: 32.8 us -> 24.9 us
    ppermute x3, waiting for transfers between devices: 5.38 us -> 0.01 us  [on_device(): lax.ppermute(sent, 'fsdp', xor_pairs(members, step)).astype(jnp.float32)]
    ppermute x2, waiting for transfers between devices: 10.1 us -> 8.15 us  [relay_gather(): partner = lax.ppermute(first, ('fsdp', 'dp'), partner_pairs)]
    unnamed x38 -> x40, local copies, waits for them, and re-layouts: 4.55 us -> 4.9 us
    add x10 -> x9, other arithmetic: 2.81 us -> 3.08 us  [on_device(): output_total + jnp.dot(token_piece, weight_piece, preferred_element_type=...]
  transfers between devices with their start and end apart: 20 -> 22, of which waited for: 4 -> 3; matrix products, arithmetic and copies ran while one was open for 39% -> 43% of each run, Pallas kernels for 0% -> 0%
where the time goes in v13:
time: 124 us; the launch traced here: 123 us
  matrix products  42.6 us (34%)
  waiting for transfers between devices  24.9 us (20%)
  between operations  19.1 us (15%)
  starting transfers between devices  17.7 us (14%)
  local copies, waits for them, and re-layouts  11.4 us (9%)
  other arithmetic  7.66 us (6%)
    dot_general x16, matrix products, on_device(): lax.dot_general(masked_cot, weight_piece, (((1,), (1,)), ((), ())), prefe...  15.3 us
    dot_general x16, matrix products, on_device(): jnp.dot(token_piece, weight_piece, preferred_element_type=jnp.float32)  13.3 us
    dot_general x16, matrix products, on_device(): jnp.einsum('uio,uof->uif', low_rank_gradient, down_piece, preferred_eleme...  10.3 us
    ppermute x2, waiting for transfers between devices, relay_gather(): relayed = lax.ppermute(first, ('fsdp', 'dp'), relay_pairs)  8.97 us
    ppermute x2, waiting for transfers between devices, relay_gather(): partner = lax.ppermute(first, ('fsdp', 'dp'), partner_pairs)  8.15 us
    ppermute x3, waiting for transfers between devices, on_device(): by_step[step] = lax.ppermute(own_adapter, 'fsdp', xor_pairs(members, step))  7.71 us
    unnamed x40, local copies, waits for them, and re-layouts  4.9 us
    ppermute x3, starting transfers between devices, on_device(): by_step[step] = lax.ppermute(own_adapter, 'fsdp', xor_pairs(members, step))  4.54 us
  transfers between devices with their start and end apart: 22, of which 3 were waited for; matrix products, arithmetic and copies ran while one was open for 43% of the time, Pallas kernels for 0%

profile of v13, /device:TPU:0, one launch (start us, length us, event | category | flops | bytes accessed | tf_op | source)
XLA Modules:
  0.0 123.3 jit_solution(17613048123968937111)
XLA Ops:
  0.6 1.0 fusion.135
  1.7 3.0 %collective-permute-start = (bf16[16,9216]{1,0:T(8,128)(2,1)S(1)}, bf16[16,9216]{1,0:T(8,128)(2,1)S(1)}, u32[]{:S(2)}, u32[]{:S(2)}) collective-permute-start(bf16[16,9216]{1,0:T(8,128)(2,1)S(1)} %get-tuple-element.28), channel_id=1, source_target_pairs={{0,8},{4,12},{8,0},{12,4},{16,24},{20,28},{24,16},{28,20},{1,9},{5... | collective-permute-start | bytes 884744 | tf_op jit(solution)/shard_map/ppermute | solution.py:92
  4.7 1.5 %collective-permute-start.1 = (bf16[16,9216]{1,0:T(8,128)(2,1)S(1)}, bf16[16,9216]{1,0:T(8,128)(2,1)S(1)}, u32[]{:S(2)}, u32[]{:S(2)}) collective-permute-start(bf16[16,9216]{1,0:T(8,128)(2,1)S(1)} %get-tuple-element.28), channel_id=1, source_target_pairs={{0,16},{4,20},{8,24},{12,28},{16,0},{20,4},{24,8},{28,12},{1,17},{... | collective-permute-start | bytes 884744 | tf_op jit(solution)/shard_map/ppermute | solution.py:92
  6.2 3.1 %fusion.142 = (bf16[512,1024]{1,0:T(8,128)(2,1)}, bf16[512,1024]{1,0:T(8,128)(2,1)}) fusion(bf16[1024,1024]{1,0:T(8,128)(2,1)} %param.10), kind=kLoop, calls=%fused_computation.213 | loop fusion | bytes 4194304 | tf_op jit(solution)/shard_map/slice | solution.py:47
  9.3 1.9 %collective-permute-start.6 = (bf16[512,1024]{1,0:T(8,128)(2,1)}, bf16[512,1024]{1,0:T(8,128)(2,1)}, u32[]{:S(2)}, u32[]{:S(2)}) collective-permute-start(bf16[512,1024]{1,0:T(8,128)(2,1)} %get-tuple-element.23), channel_id=1, source_target_pairs={{0,8},{1,17},{2,10},{3,19},{4,20},{5,13},{6,22},{7,15},{8,0},{9,25... | collective-permute-start | bytes 3145736 | tf_op jit(solution)/shard_map/ppermute | solution.py:52
  11.3 0.7 constant_dynamic-update-slice_fusion.3
  12.1 0.6 gather_fusion
  13.2 7.7 %collective-permute-done.1 = bf16[16,9216]{1,0:T(8,128)(2,1)S(1)} collective-permute-done((bf16[16,9216]{1,0:T(8,128)(2,1)S(1)}, bf16[16,9216]{1,0:T(8,128)(2,1)S(1)}, u32[]{:S(2)}, u32[]{:S(2)}) %collective-permute-start.1) | collective-permute-done | bytes 294944 | tf_op jit(solution)/shard_map/ppermute | solution.py:92
  39.6 1.7 %collective-permute-start.7 = (bf16[512,1024]{1,0:T(8,128)(2,1)}, bf16[512,1024]{1,0:T(8,128)(2,1)S(1)}, u32[]{:S(2)}, u32[]{:S(2)}) collective-permute-start(bf16[512,1024]{1,0:T(8,128)(2,1)} %collective-permute-done.6), channel_id=1, source_target_pairs={{0,4},{4,0},{8,12},{12,8},{16,20},{20,16},{24,28},{28,24},{1,5},{5... | collective-permute-start | bytes 3145736 | tf_op jit(solution)/shard_map/ppermute | solution.py:55
  41.3 1.9 %fusion.57 = f32[384,1024]{1,0:T(8,128)S(1)} fusion(bf16[512,1024]{1,0:T(8,128)(2,1)} %collective-permute-done.6, bf16[384,8192]{1,0:T(8,128)(2,1)} %param.8, s32[]{:T(128)S(6)} %select_n.296), kind=kOutput, calls=%fused_computation.107 | convolution fusion | flops 402653184 | bytes 3014660 | tf_op jit(solution)/shard_map/dot_general | solution.py:167
  43.8 2.1 %fusion.59 = f32[384,1024]{1,0:T(8,128)S(1)} fusion(bf16[512,1024]{1,0:T(8,128)(2,1)} %collective-permute-done.5, bf16[384,8192]{1,0:T(8,128)(2,1)} %param.8, s32[]{:T(128)S(6)} %select_n.293), kind=kOutput, calls=%fused_computation.109 | convolution fusion | flops 402653184 | bytes 3014660 | tf_op jit(solution)/shard_map/dot_general | solution.py:167
  45.9 1.1 collective-permute-start.10
  47.5 1.1 copy-done.4
  48.9 1.2 fusion.91
  50.1 1.2 fusion.89
  51.4 0.9 fusion.144
  52.3 1.7 %fusion.32 = bf16[3,16,128]{2,1,0:T(8,128)(2,1)S(1)} fusion(bf16[3,128,8192]{2,1,0:T(8,128)(2,1)S(1)} %bitcast.110, f32[3,128]{1,0:T(4,128)S(1)} %get-tuple-element.30, bf16[3,16,9216]{2,1,0:T(8,128)(2,1)S(1)} %pad_maximum_fusion.2), kind=kOutput, calls=%fused_computation.68 | convolution fusion | flops 100675584 | bytes 7092224 | tf_op jit(solution)/shard_map/cvj,coj->cvo/dot_general | solution.py:112
  54.7 1.2 fusion.97
  55.9 1.2 fusion.95
  57.0 1.2 %fusion.93 = f32[3,128,512]{2,1,0:T(8,128)} fusion(bf16[3,16,128]{2,1,0:T(8,128)(2,1)S(1)} %fusion.33, bf16[3,16,8192]{2,1,0:T(8,128)(2,1)S(1)} %slice.131, s32[]{:T(128)S(6)} %select_n.292), kind=kOutput, calls=%fused_computation.150 | convolution fusion | flops 6291456 | bytes 847876 | tf_op jit(solution)/shard_map/uio,uof->uif/dot_general | solution.py:173
  58.3 1.2 fusion.87
  62.9 0.7 broadcast_in_dim.44
  63.6 1.8 %fusion.1 = bf16[384,8192]{1,0:T(8,128)(2,1)S(1)} fusion(bf16[384,8192]{1,0:T(8,128)(2,1)S(1)} %broadcast_in_dim.44, s32[]{:T(128)S(6)} %select_n.290, f32[384,512]{1,0:T(8,128)} %bitcast.133, bf16[1024,1024]{1,0:T(8,128)(2,1)S(1)} %copy-done.2, bf16[384,1024]{1,0:T(8,128)(2,1)S(1)} %copy-done.4, f32[384]{0:T(512)S(1)} %get-tuple-element.29), kind=kOutput, calls=%fused_computation.32 | convolution fusion | flops 404226048 | bytes 3016708 | tf_op jit(solution)/shard_map/dot_general | solution.py:171
  65.5 0.6 fusion.3
  67.8 1.9 %fusion.5 = bf16[384,8192]{1,0:T(8,128)(2,1)S(1)} fusion(bf16[384,8192]{1,0:T(8,128)(2,1)S(1)} %fusion.3, s32[]{:T(128)S(6)} %select_n.292, f32[384,512]{1,0:T(8,128)S(1)} %bitcast.131, bf16[512,1024]{1,0:T(8,128)(2,1)} %collective-permute-done.4, bf16[384,1024]{1,0:T(8,128)(2,1)S(1)} %copy-done.4, f32[384]{0:T(512)S(1)} %get-tuple-element.29), kind=kOutput, calls=%fused_computation.36 | convolution fusion | flops 404226048 | bytes 3016708 | tf_op jit(solution)/shard_map/dot_general | solution.py:171
  69.7 2.1 %fusion.7 = bf16[384,8192]{1,0:T(8,128)(2,1)S(1)} fusion(bf16[384,8192]{1,0:T(8,128)(2,1)S(1)} %fusion.5, s32[]{:T(128)S(6)} %select_n.293, f32[384,512]{1,0:T(8,128)S(1)} %bitcast.130, bf16[512,1024]{1,0:T(8,128)(2,1)} %collective-permute-done.5, bf16[384,1024]{1,0:T(8,128)(2,1)S(1)} %copy-done.4, f32[384]{0:T(512)S(1)} %get-tuple-element.29), kind=kOutput, calls=%fused_computation.38 | convolution fusion | flops 404226048 | bytes 3016708 | tf_op jit(solution)/shard_map/dot_general | solution.py:171
  71.9 1.8 %fusion.9 = bf16[384,8192]{1,0:T(8,128)(2,1)S(1)} fusion(bf16[384,8192]{1,0:T(8,128)(2,1)S(1)} %fusion.7, s32[]{:T(128)S(6)} %select_n.296, f32[384,512]{1,0:T(8,128)S(1)} %bitcast.129, bf16[512,1024]{1,0:T(8,128)(2,1)} %collective-permute-done.6, bf16[384,1024]{1,0:T(8,128)(2,1)S(1)} %copy-done.4, f32[384]{0:T(512)S(1)} %get-tuple-element.29), kind=kOutput, calls=%fused_computation.40 | convolution fusion | flops 404226048 | bytes 3016708 | tf_op jit(solution)/shard_map/dot_general | solution.py:171
  73.7 1.8 %convolution_add_fusion.4 = f32[384,1024]{1,0:T(8,128)S(1)} fusion(f32[384,1024]{1,0:T(8,128)S(1)} %convolution_add_fusion.5, bf16[512,1024]{1,0:T(8,128)(2,1)} %collective-permute-done.4, bf16[384,8192]{1,0:T(8,128)(2,1)S(1)} %bitcast.108, s32[]{:T(128)S(6)} %select_n.292), kind=kOutput, calls=%fused_computation.12 | convolution fusion | flops 403046400 | bytes 4587524 | tf_op jit(solution)/shard_map/dot_general | solution.py:167
  80.3 1.3 %collective-permute-start.14 = (bf16[512,1024]{1,0:T(8,128)(2,1)S(1)}, bf16[512,1024]{1,0:T(8,128)(2,1)S(1)}, u32[]{:S(2)}, u32[]{:S(2)}) collective-permute-start(bf16[512,1024]{1,0:T(8,128)(2,1)S(1)} %collective-permute-done.8), channel_id=1, source_target_pairs={{0,16},{1,9},{2,18},{3,11},{4,12},{5,21},{6,14},{7,23},{8,24},{9,1... | collective-permute-start | bytes 3145736 | tf_op jit(solution)/shard_map/ppermute | solution.py:56
  82.2 0.6 fusion.11
  82.8 0.6 fusion.13
  83.4 0.6 fusion.15
  84.0 0.6 fusion.17
  84.7 1.1 collective-permute-start.15
  86.2 9.0 %collective-permute-done.14 = bf16[512,1024]{1,0:T(8,128)(2,1)S(1)} collective-permute-done((bf16[512,1024]{1,0:T(8,128)(2,1)S(1)}, bf16[512,1024]{1,0:T(8,128)(2,1)S(1)}, u32[]{:S(2)}, u32[]{:S(2)}) %collective-permute-start.14) | collective-permute-done | bytes 1048608 | tf_op jit(solution)/shard_map/ppermute | solution.py:56
  95.2 1.5 %collective-permute-start.19 = (bf16[16,9216]{1,0:T(8,128)(2,1)S(1)}, bf16[16,9216]{1,0:T(8,128)(2,1)S(1)}, u32[]{:S(2)}, u32[]{:S(2)}) collective-permute-start(bf16[16,9216]{1,0:T(8,128)(2,1)S(1)} %get-tuple-element.9), channel_id=1, source_target_pairs={{0,8},{4,12},{8,0},{12,4},{16,24},{20,28},{24,16},{28,20},{1,9},{5... | collective-permute-start | bytes 884744 | tf_op jit(solution)/shard_map/ppermute | solution.py:150
  98.1 1.5 %collective-permute-start.21 = (bf16[16,9216]{1,0:T(8,128)(2,1)S(1)}, bf16[16,9216]{1,0:T(8,128)(2,1)S(1)}, u32[]{:S(2)}, u32[]{:S(2)}) collective-permute-start(bf16[16,9216]{1,0:T(8,128)(2,1)S(1)} %get-tuple-element.11), channel_id=1, source_target_pairs={{0,24},{4,28},{8,16},{12,20},{16,8},{20,12},{24,0},{28,4},{1,25},{... | collective-permute-start | bytes 884744 | tf_op jit(solution)/shard_map/ppermute | solution.py:150
  102.2 8.1 %collective-permute-done.15 = bf16[512,1024]{1,0:T(8,128)(2,1)S(1)} collective-permute-done((bf16[512,1024]{1,0:T(8,128)(2,1)S(1)}, bf16[512,1024]{1,0:T(8,128)(2,1)S(1)}, u32[]{:S(2)}, u32[]{:S(2)}) %collective-permute-start.15) | collective-permute-done | bytes 1048608 | tf_op jit(solution)/shard_map/ppermute | solution.py:57
  112.5 0.6 fusion.21
  113.1 0.9 fusion.23
  114.0 0.6 fusion.25
  114.6 0.6 fusion.27
  115.5 0.7 slice_bitcast_fusion
  116.2 0.6 slice_bitcast_fusion.1
  118.3 1.0 multiply_convert_fusion.1
  119.3 0.6 fusion.29
  120.0 0.6 fusion.31
  120.6 2.7 %copy-done.3 = bf16[384,8192]{1,0:T(8,128)(2,1)} copy-done((bf16[384,8192]{1,0:T(8,128)(2,1)}, bf16[384,8192]{1,0:T(8,128)(2,1)S(1)}, u32[]{:S(2)}) %copy-start.3) | copy-done | bytes 6291480
  (124 shorter events, 21.8 us)
Async XLA Ops:
  0.6 11.4 %copy-start = (s32[32]{0:T(128)S(1)}, s32[32]{0:T(128)}, u32[]{:S(2)}) copy-start(s32[32]{0:T(128)} %param.15) | copy-start | bytes 388
  1.7 9.6 %copy-start.5 = (bf16[1,16,8192]{2,1,0:T(8,128)(2,1)S(1)}, bf16[1,16,8192]{2,1,0:T(8,128)(2,1)}, u32[]{:S(2)}) copy-start(bf16[1,16,8192]{2,1,0:T(8,128)(2,1)} %param.11) | copy-start | bytes 786436
  1.7 9.6 %copy-start.12 = (bf16[1,16,1024]{2,1,0:T(8,128)(2,1)S(1)}, bf16[1,16,1024]{2,1,0:T(8,128)(2,1)}, u32[]{:S(2)}) copy-start(bf16[1,16,1024]{2,1,0:T(8,128)(2,1)} %param.12) | copy-start | bytes 98308
  1.7 10.3 %copy-start.14 = (s32[3]{0:T(128)S(1)}, s32[3]{0:T(128)}, u32[]{:S(2)}) copy-start(s32[3]{0:T(128)} %param.13) | copy-start | bytes 40
  1.7 11.0 %collective-permute-start = (bf16[16,9216]{1,0:T(8,128)(2,1)S(1)}, bf16[16,9216]{1,0:T(8,128)(2,1)S(1)}, u32[]{:S(2)}, u32[]{:S(2)}) collective-permute-start(bf16[16,9216]{1,0:T(8,128)(2,1)S(1)} %get-tuple-element.28), channel_id=1, source_target_pairs={{0,8},{4,12},{8,0},{12,4},{16,24},{20,28},{24,16},{28,20},{1,9},{5... | collective-permute-start | bytes 884744 | tf_op jit(solution)/shard_map/ppermute | solution.py:92
  4.7 16.3 %collective-permute-start.1 = (bf16[16,9216]{1,0:T(8,128)(2,1)S(1)}, bf16[16,9216]{1,0:T(8,128)(2,1)S(1)}, u32[]{:S(2)}, u32[]{:S(2)}) collective-permute-start(bf16[16,9216]{1,0:T(8,128)(2,1)S(1)} %get-tuple-element.28), channel_id=1, source_target_pairs={{0,16},{4,20},{8,24},{12,28},{16,0},{20,4},{24,8},{28,12},{1,17},{... | collective-permute-start | bytes 884744 | tf_op jit(solution)/shard_map/ppermute | solution.py:92
  6.2 14.7 %collective-permute-start.2 = (bf16[16,9216]{1,0:T(8,128)(2,1)S(1)}, bf16[16,9216]{1,0:T(8,128)(2,1)S(1)}, u32[]{:S(2)}, u32[]{:S(2)}) collective-permute-start(bf16[16,9216]{1,0:T(8,128)(2,1)S(1)} %get-tuple-element.28), channel_id=1, source_target_pairs={{0,24},{4,28},{8,16},{12,20},{16,8},{20,12},{24,0},{28,4},{1,25},{... | collective-permute-start | bytes 884744 | tf_op jit(solution)/shard_map/ppermute | solution.py:92
  9.3 30.3 %collective-permute-start.6 = (bf16[512,1024]{1,0:T(8,128)(2,1)}, bf16[512,1024]{1,0:T(8,128)(2,1)}, u32[]{:S(2)}, u32[]{:S(2)}) collective-permute-start(bf16[512,1024]{1,0:T(8,128)(2,1)} %get-tuple-element.23), channel_id=1, source_target_pairs={{0,8},{1,17},{2,10},{3,19},{4,20},{5,13},{6,22},{7,15},{8,0},{9,25... | collective-permute-start | bytes 3145736 | tf_op jit(solution)/shard_map/ppermute | solution.py:52
  11.3 55.8 %collective-permute-start.4 = (bf16[512,1024]{1,0:T(8,128)(2,1)}, bf16[512,1024]{1,0:T(8,128)(2,1)}, u32[]{:S(2)}, u32[]{:S(2)}) collective-permute-start(bf16[512,1024]{1,0:T(8,128)(2,1)} %get-tuple-element.23), channel_id=1, source_target_pairs={{0,4},{4,0},{8,12},{12,8},{16,20},{20,16},{24,28},{28,24},{1,5},{5... | collective-permute-start | bytes 3145736 | tf_op jit(solution)/shard_map/ppermute | solution.py:49
  12.1 27.4 %copy-start.13 = (s32[3]{0:T(128)S(1)}, s32[3]{0:T(128)}, u32[]{:S(2)}) copy-start(s32[3]{0:T(128)} %param.14) | copy-start | bytes 40
  12.7 30.6 %collective-permute-start.5 = (bf16[512,1024]{1,0:T(8,128)(2,1)}, bf16[512,1024]{1,0:T(8,128)(2,1)}, u32[]{:S(2)}, u32[]{:S(2)}) collective-permute-start(bf16[512,1024]{1,0:T(8,128)(2,1)} %get-tuple-element.8), channel_id=1, source_target_pairs={{0,4},{4,0},{8,12},{12,8},{16,20},{20,16},{24,28},{28,24},{1,5},{5... | collective-permute-start | bytes 3145736 | tf_op jit(solution)/shard_map/ppermute | solution.py:49
  21.1 24.8 %collective-permute-start.3 = (bf16[4,16,9216]{2,1,0:T(8,128)(2,1)S(1)}, bf16[4,16,9216]{2,1,0:T(8,128)(2,1)S(1)}, u32[]{:S(2)}, u32[]{:S(2)}) collective-permute-start(bf16[4,16,9216]{2,1,0:T(8,128)(2,1)S(1)} %pad_maximum_fusion), channel_id=1, source_target_pairs={{0,4},{4,0},{8,12},{12,8},{16,20},{20,16},{24,28},{28,24},{1,5},{5... | collective-permute-start | bytes 3538952 | tf_op jit(solution)/shard_map/ppermute | solution.py:94
  39.6 38.2 %collective-permute-start.8 = (bf16[512,1024]{1,0:T(8,128)(2,1)}, bf16[512,1024]{1,0:T(8,128)(2,1)S(1)}, u32[]{:S(2)}, u32[]{:S(2)}) collective-permute-start(bf16[512,1024]{1,0:T(8,128)(2,1)} %get-tuple-element.8), channel_id=1, source_target_pairs={{0,8},{1,17},{2,10},{3,19},{4,20},{5,13},{6,22},{7,15},{8,0},{9,25... | collective-permute-start | bytes 3145736 | tf_op jit(solution)/shard_map/ppermute | solution.py:52
  39.6 37.6 %collective-permute-start.7 = (bf16[512,1024]{1,0:T(8,128)(2,1)}, bf16[512,1024]{1,0:T(8,128)(2,1)S(1)}, u32[]{:S(2)}, u32[]{:S(2)}) collective-permute-start(bf16[512,1024]{1,0:T(8,128)(2,1)} %collective-permute-done.6), channel_id=1, source_target_pairs={{0,4},{4,0},{8,12},{12,8},{16,20},{20,16},{24,28},{28,24},{1,5},{5... | collective-permute-start | bytes 3145736 | tf_op jit(solution)/shard_map/ppermute | solution.py:55
  43.2 3.8 %copy-start.11 = (bf16[8,16,9216]{2,1,0:T(8,128)(2,1)S(1)}, bf16[8,16,9216]{2,1,0:T(8,128)(2,1)}, u32[]{:S(2)}) copy-start(bf16[8,16,9216]{2,1,0:T(8,128)(2,1)} %constant_dynamic-update-slice_fusion.3) | copy-start | bytes 7077892
  43.3 35.5 %collective-permute-start.9 = (bf16[512,1024]{1,0:T(8,128)(2,1)}, bf16[512,1024]{1,0:T(8,128)(2,1)S(1)}, u32[]{:S(2)}, u32[]{:S(2)}) collective-permute-start(bf16[512,1024]{1,0:T(8,128)(2,1)} %collective-permute-done.6), channel_id=1, source_target_pairs={{0,16},{1,9},{2,18},{3,11},{4,12},{5,21},{6,14},{7,23},{8,24},{9,1... | collective-permute-start | bytes 3145736 | tf_op jit(solution)/shard_map/ppermute | solution.py:56
  43.8 7.5 %slice-start = ((s8[6291456]{0:T(1024)(128)(4,1)}), s8[4194304]{0:T(1024)(128)(4,1)S(1)}, s32[]{:S(2)}) async-start(s8[6291456]{0:T(1024)(128)(4,1)} %bitcast.107), calls=%async_computation | async-start | bytes 8388608
  45.9 33.4 %collective-permute-start.10 = (bf16[512,1024]{1,0:T(8,128)(2,1)}, bf16[512,1024]{1,0:T(8,128)(2,1)S(1)}, u32[]{:S(2)}, u32[]{:S(2)}) collective-permute-start(bf16[512,1024]{1,0:T(8,128)(2,1)} %collective-permute-done.6), channel_id=1, source_target_pairs={{0,1},{1,0},{2,3},{3,2},{4,5},{5,4},{6,7},{7,6},{8,9},{9,8},{10,11... | collective-permute-start | bytes 3145736 | tf_op jit(solution)/shard_map/ppermute | solution.py:57
  47.2 4.1 %slice-start.1 = ((s8[6291456]{0:T(1024)(128)(4,1)}), s8[2097152]{0:T(1024)(128)(4,1)S(1)}, s32[]{:S(2)}) async-start(s8[6291456]{0:T(1024)(128)(4,1)} %bitcast.107), calls=%async_computation.1 | async-start | bytes 4194304
  47.3 1.3 %copy-start.4 = (bf16[384,1024]{1,0:T(8,128)(2,1)S(1)}, bf16[384,1024]{1,0:T(8,128)(2,1)}, u32[]{:S(2)}) copy-start(bf16[384,1024]{1,0:T(8,128)(2,1)} %param.9) | copy-start | bytes 2359300
  60.1 1.6 %copy-start.2 = (bf16[1024,1024]{1,0:T(8,128)(2,1)S(1)}, bf16[1024,1024]{1,0:T(8,128)(2,1)}, u32[]{:S(2)}) copy-start(bf16[1024,1024]{1,0:T(8,128)(2,1)} %param.10) | copy-start | bytes 6291460
  63.6 1.8 %copy-start.10 = (f32[3,128,512]{2,1,0:T(8,128)S(1)}, f32[3,128,512]{2,1,0:T(8,128)}, u32[]{:S(2)}) copy-start(f32[3,128,512]{2,1,0:T(8,128)} %fusion.95) | copy-start | bytes 2359300
  66.6 1.1 copy-start.9
  67.1 17.5 %collective-permute-start.18 = (bf16[4,16,9216]{2,1,0:T(8,128)(2,1)S(1)}, bf16[4,16,9216]{2,1,0:T(8,128)(2,1)S(1)}, u32[]{:S(2)}, u32[]{:S(2)}) collective-permute-start(bf16[4,16,9216]{2,1,0:T(8,128)(2,1)S(1)} %pad_maximum_fusion.1), channel_id=1, source_target_pairs={{0,4},{4,0},{8,12},{12,8},{16,20},{20,16},{24,28},{28,24},{1,5},{5... | collective-permute-start | bytes 3538952 | tf_op jit(solution)/shard_map/ppermute | solution.py:137
  67.8 1.9 %copy-start.8 = (f32[3,128,512]{2,1,0:T(8,128)S(1)}, f32[3,128,512]{2,1,0:T(8,128)}, u32[]{:S(2)}) copy-start(f32[3,128,512]{2,1,0:T(8,128)} %fusion.91) | copy-start | bytes 2359300
  69.7 2.1 %copy-start.7 = (f32[3,128,512]{2,1,0:T(8,128)S(1)}, f32[3,128,512]{2,1,0:T(8,128)}, u32[]{:S(2)}) copy-start(f32[3,128,512]{2,1,0:T(8,128)} %fusion.89) | copy-start | bytes 2359300
  79.9 2.2 %copy-start.6 = (f32[3,128,512]{2,1,0:T(8,128)S(1)}, f32[3,128,512]{2,1,0:T(8,128)}, u32[]{:S(2)}) copy-start(f32[3,128,512]{2,1,0:T(8,128)} %fusion.87) | copy-start | bytes 2359300
  80.3 14.9 %collective-permute-start.14 = (bf16[512,1024]{1,0:T(8,128)(2,1)S(1)}, bf16[512,1024]{1,0:T(8,128)(2,1)S(1)}, u32[]{:S(2)}, u32[]{:S(2)}) collective-permute-start(bf16[512,1024]{1,0:T(8,128)(2,1)S(1)} %collective-permute-done.8), channel_id=1, source_target_pairs={{0,16},{1,9},{2,18},{3,11},{4,12},{5,21},{6,14},{7,23},{8,24},{9,1... | collective-permute-start | bytes 3145736 | tf_op jit(solution)/shard_map/ppermute | solution.py:56
  81.7 15.0 %collective-permute-start.11 = (bf16[512,1024]{1,0:T(8,128)(2,1)S(1)}, bf16[512,1024]{1,0:T(8,128)(2,1)S(1)}, u32[]{:S(2)}, u32[]{:S(2)}) collective-permute-start(bf16[512,1024]{1,0:T(8,128)(2,1)S(1)} %collective-permute-done.8), channel_id=1, source_target_pairs={{0,4},{4,0},{8,12},{12,8},{16,20},{20,16},{24,28},{28,24},{1,5},{5... | collective-permute-start | bytes 3145736 | tf_op jit(solution)/shard_map/ppermute | solution.py:55
  81.7 16.5 %collective-permute-start.12 = (bf16[512,1024]{1,0:T(8,128)(2,1)S(1)}, bf16[512,1024]{1,0:T(8,128)(2,1)S(1)}, u32[]{:S(2)}, u32[]{:S(2)}) collective-permute-start(bf16[512,1024]{1,0:T(8,128)(2,1)S(1)} %collective-permute-done.9), channel_id=1, source_target_pairs={{0,4},{4,0},{8,12},{12,8},{16,20},{20,16},{24,28},{28,24},{1,5},{5... | collective-permute-start | bytes 3145736 | tf_op jit(solution)/shard_map/ppermute | solution.py:61
  82.2 18.1 %collective-permute-start.13 = (bf16[512,1024]{1,0:T(8,128)(2,1)S(1)}, bf16[512,1024]{1,0:T(8,128)(2,1)S(1)}, u32[]{:S(2)}, u32[]{:S(2)}) collective-permute-start(bf16[512,1024]{1,0:T(8,128)(2,1)S(1)} %collective-permute-done.10), channel_id=1, source_target_pairs={{0,4},{4,0},{8,12},{12,8},{16,20},{20,16},{24,28},{28,24},{1,5},{5... | collective-permute-start | bytes 3145736 | tf_op jit(solution)/shard_map/ppermute | solution.py:63
  84.7 25.6 %collective-permute-start.15 = (bf16[512,1024]{1,0:T(8,128)(2,1)S(1)}, bf16[512,1024]{1,0:T(8,128)(2,1)S(1)}, u32[]{:S(2)}, u32[]{:S(2)}) collective-permute-start(bf16[512,1024]{1,0:T(8,128)(2,1)S(1)} %collective-permute-done.8), channel_id=1, source_target_pairs={{0,1},{1,0},{2,3},{3,2},{4,5},{5,4},{6,7},{7,6},{8,9},{9,8},{10,11... | collective-permute-start | bytes 3145736 | tf_op jit(solution)/shard_map/ppermute | solution.py:57
  95.2 20.0 %collective-permute-start.19 = (bf16[16,9216]{1,0:T(8,128)(2,1)S(1)}, bf16[16,9216]{1,0:T(8,128)(2,1)S(1)}, u32[]{:S(2)}, u32[]{:S(2)}) collective-permute-start(bf16[16,9216]{1,0:T(8,128)(2,1)S(1)} %get-tuple-element.9), channel_id=1, source_target_pairs={{0,8},{4,12},{8,0},{12,4},{16,24},{20,28},{24,16},{28,20},{1,9},{5... | collective-permute-start | bytes 884744 | tf_op jit(solution)/shard_map/ppermute | solution.py:150
  96.7 18.6 %collective-permute-start.20 = (bf16[16,9216]{1,0:T(8,128)(2,1)S(1)}, bf16[16,9216]{1,0:T(8,128)(2,1)S(1)}, u32[]{:S(2)}, u32[]{:S(2)}) collective-permute-start(bf16[16,9216]{1,0:T(8,128)(2,1)S(1)} %get-tuple-element.10), channel_id=1, source_target_pairs={{0,16},{4,20},{8,24},{12,28},{16,0},{20,4},{24,8},{28,12},{1,17},{... | collective-permute-start | bytes 884744 | tf_op jit(solution)/shard_map/ppermute | solution.py:150
  98.1 17.1 %collective-permute-start.21 = (bf16[16,9216]{1,0:T(8,128)(2,1)S(1)}, bf16[16,9216]{1,0:T(8,128)(2,1)S(1)}, u32[]{:S(2)}, u32[]{:S(2)}) collective-permute-start(bf16[16,9216]{1,0:T(8,128)(2,1)S(1)} %get-tuple-element.11), channel_id=1, source_target_pairs={{0,24},{4,28},{8,16},{12,20},{16,8},{20,12},{24,0},{28,4},{1,25},{... | collective-permute-start | bytes 884744 | tf_op jit(solution)/shard_map/ppermute | solution.py:150
  111.3 5.6 %collective-permute-start.16 = (bf16[512,1024]{1,0:T(8,128)(2,1)S(1)}, bf16[512,1024]{1,0:T(8,128)(2,1)S(1)}, u32[]{:S(2)}, u32[]{:S(2)}) collective-permute-start(bf16[512,1024]{1,0:T(8,128)(2,1)S(1)} %collective-permute-done.14), channel_id=1, source_target_pairs={{0,4},{4,0},{8,12},{12,8},{16,20},{20,16},{24,28},{28,24},{1,5},{5... | collective-permute-start | bytes 3145736 | tf_op jit(solution)/shard_map/ppermute | solution.py:61
  111.4 6.1 %collective-permute-start.17 = (bf16[512,1024]{1,0:T(8,128)(2,1)S(1)}, bf16[512,1024]{1,0:T(8,128)(2,1)S(1)}, u32[]{:S(2)}, u32[]{:S(2)}) collective-permute-start(bf16[512,1024]{1,0:T(8,128)(2,1)S(1)} %collective-permute-done.15), channel_id=1, source_target_pairs={{0,4},{4,0},{8,12},{12,8},{16,20},{20,16},{24,28},{28,24},{1,5},{5... | collective-permute-start | bytes 3145736 | tf_op jit(solution)/shard_map/ppermute | solution.py:63
  120.0 3.3 %copy-start.1 = (s32[32]{0:T(128)S(1)}, s32[32]{0:T(128)}, u32[]{:S(2)}) copy-start(s32[32]{0:T(128)} %param.15) | copy-start | bytes 388
  120.6 2.7 %copy-start.3 = (bf16[384,8192]{1,0:T(8,128)(2,1)}, bf16[384,8192]{1,0:T(8,128)(2,1)S(1)}, u32[]{:S(2)}) copy-start(bf16[384,8192]{1,0:T(8,128)(2,1)S(1)} %fusion.31) | copy-start | bytes 18874372

commit v14 on v9

--- a/solution.py
+++ b/solution.py
@@ -39,7 +39,7 @@
     sources = [me, me ^ (2 + 2 * role), me ^ 6, me ^ (4 - 2 * role)]
     sibling_sources = [sibling, sibling ^ (2 + 2 * sibling_role), sibling ^ 6,
                        sibling ^ (4 - 2 * sibling_role)]
-    bounds = [0, shard.shape[0] // 4, shard.shape[0]]
+    bounds = [0, 3 * shard.shape[0] // 4, shard.shape[0]]
     result = []
     previous = None
     for k in range(len(bounds) - 1):
@@ -56,9 +56,10 @@
         partner = lax.ppermute(first, ("fsdp", "dp"), partner_pairs)
         result.append((4.5 + 2 * k, sources[2], bounds[k], relayed))
         result.append((4.5 + 2 * k, sources[3], bounds[k], partner))
-        late = lax.ppermute(jnp.stack([relayed, partner]), "fsdp", xor_pairs(members, 1))
-        result.append((5.5 + 2 * k, sibling_sources[2], bounds[k], late[0]))
-        result.append((5.5 + 2 * k, sibling_sources[3], bounds[k], late[1]))
+        result.append((5.5 + 2 * k, sibling_sources[2], bounds[k],
+                       lax.ppermute(relayed, "fsdp", xor_pairs(members, 1))))
+        result.append((5.5 + 2 * k, sibling_sources[3], bounds[k],
+                       lax.ppermute(partner, "fsdp", xor_pairs(members, 1))))
     result.sort(key=lambda item: item[0])
     return [item[1:] for item in result]
 
@@ -140,7 +141,7 @@
     weight_pieces = relay_gather(frozen_value_weight, members, groups, me, dp_index)
     if weight_pieces and len(weight_pieces[0]) == 2:
         weight_pieces = [(source, 0, value) for source, value in weight_pieces]
-    last_pieces = tuple(value for _, _, value in weight_pieces[-4:])
+    last_pieces = (weight_pieces[-4][2],)
     grad_sum = pair_sums[0]
     for index, step in enumerate(even_steps):
         sent = pair_sums[index + 1].astype(jnp.bfloat16)

time: 161 us -> 164 us (1.019)
  local copies, waits for them, and re-layouts: 14.1 us -> 23.9 us
  matrix products: 52.4 us -> 45.7 us
  waiting for transfers between devices: 44.7 us -> 47.7 us
  other arithmetic: 11.6 us -> 8.91 us
    unnamed x50, local copies, waits for them, and re-layouts: 6.47 us -> 13.1 us
    dot_general x16, matrix products: 19.7 us -> 14 us  [on_device(): lax.dot_general(masked_cot, weight_piece, (((1,), (1,)), ((), ())), prefe...]
    dot_general x16, matrix products: 18.7 us -> 13.4 us  [on_device(): jnp.dot(token_piece, weight_piece, preferred_element_type=jnp.float32)]
    ppermute x2, waiting for transfers between devices: 11.5 us -> 16.3 us  [relay_gather(): relayed = lax.ppermute(first, ('fsdp', 'dp'), relay_pairs)]
    dot_general x16, matrix products: 10.4 us -> 14.7 us  [on_device(): jnp.einsum('uio,uof->uif', low_rank_gradient, down_piece, preferred_eleme...]
    ppermute x2, waiting for transfers between devices: 1.65 us -> 0.01 us  [relay_gather(): first = lax.ppermute(piece, ('fsdp', 'dp'), first_pairs)]
    add x10 -> x9, other arithmetic: 2.77 us -> 3.29 us  [on_device(): output_total + jnp.dot(token_piece, weight_piece, preferred_element_type=...]
  transfers between devices with their start and end apart: 20 -> 22, of which waited for: 6 -> 8; matrix products, arithmetic and copies ran while one was open for 45% -> 41% of each run, Pallas kernels for 0% -> 0%
where the time goes in v14:
time: 164 us; the launch traced here: 163 us
  waiting for transfers between devices  47.7 us (29%)
  matrix products  45.7 us (28%)
  local copies, waits for them, and re-layouts  23.9 us (15%)
  between operations  18.8 us (11%)
  starting transfers between devices  17.6 us (11%)
  other arithmetic  8.91 us (5%)
    ppermute x2, waiting for transfers between devices, relay_gather(): partner = lax.ppermute(first, ('fsdp', 'dp'), partner_pairs)  17.8 us
    ppermute x2, waiting for transfers between devices, relay_gather(): relayed = lax.ppermute(first, ('fsdp', 'dp'), relay_pairs)  16.3 us
    dot_general x16, matrix products, on_device(): jnp.einsum('uio,uof->uif', low_rank_gradient, down_piece, preferred_eleme...  14.7 us
    dot_general x16, matrix products, on_device(): lax.dot_general(masked_cot, weight_piece, (((1,), (1,)), ((), ())), prefe...  14 us
    dot_general x16, matrix products, on_device(): jnp.dot(token_piece, weight_piece, preferred_element_type=jnp.float32)  13.4 us
    unnamed x50, local copies, waits for them, and re-layouts  13.1 us
    ppermute x3, waiting for transfers between devices, on_device(): by_step[step] = lax.ppermute(own_adapter, 'fsdp', xor_pairs(members, step))  6.91 us
    ppermute x3, waiting for transfers between devices, on_device(): lax.ppermute(sent, 'fsdp', xor_pairs(members, step)).astype(jnp.float32)  6.63 us
  transfers between devices with their start and end apart: 22, of which 8 were waited for; matrix products, arithmetic and copies ran while one was open for 41% of the time, Pallas kernels for 0%

profile of v14, /device:TPU:0, one launch (start us, length us, event | category | flops | bytes accessed | tf_op | source)
XLA Modules:
  0.0 162.6 jit_solution(140209765901085026)
XLA Ops:
  0.6 1.0 fusion.137
  1.7 3.0 %collective-permute-start = (bf16[16,9216]{1,0:T(8,128)(2,1)S(1)}, bf16[16,9216]{1,0:T(8,128)(2,1)S(1)}, u32[]{:S(2)}, u32[]{:S(2)}) collective-permute-start(bf16[16,9216]{1,0:T(8,128)(2,1)S(1)} %get-tuple-element.26), channel_id=1, source_target_pairs={{0,8},{4,12},{8,0},{12,4},{16,24},{20,28},{24,16},{28,20},{1,9},{5... | collective-permute-start | bytes 884744 | tf_op jit(solution)/shard_map/ppermute | solution.py:91
  4.7 1.5 collective-permute-start.1
  6.2 2.7 %slice.49 = bf16[768,1024]{1,0:T(8,128)(2,1)} slice(bf16[1024,1024]{1,0:T(8,128)(2,1)} %param.10), slice={[0:768], [0:1024]} | slice | bytes 3145728 | tf_op jit(solution)/shard_map/slice | solution.py:46
  8.9 1.9 %collective-permute-start.6 = (bf16[768,1024]{1,0:T(8,128)(2,1)}, bf16[768,1024]{1,0:T(8,128)(2,1)}, u32[]{:S(2)}, u32[]{:S(2)}) collective-permute-start(bf16[768,1024]{1,0:T(8,128)(2,1)} %slice.49), channel_id=1, source_target_pairs={{0,8},{1,17},{2,10},{3,19},{4,20},{5,13},{6,22},{7,15},{8,0},{9,25... | collective-permute-start | bytes 4718600 | tf_op jit(solution)/shard_map/ppermute | solution.py:51
  11.6 1.9 %slice.50 = bf16[256,1024]{1,0:T(8,128)(2,1)} slice(bf16[1024,1024]{1,0:T(8,128)(2,1)} %param.10), slice={[768:1024], [0:1024]} | slice | bytes 1048576 | tf_op jit(solution)/shard_map/slice | solution.py:46
  14.0 6.9 %collective-permute-done.1 = bf16[16,9216]{1,0:T(8,128)(2,1)S(1)} collective-permute-done((bf16[16,9216]{1,0:T(8,128)(2,1)S(1)}, bf16[16,9216]{1,0:T(8,128)(2,1)S(1)}, u32[]{:S(2)}, u32[]{:S(2)}) %collective-permute-start.1) | collective-permute-done | bytes 294944 | tf_op jit(solution)/shard_map/ppermute | solution.py:91
  21.0 1.2 pad_maximum_fusion
  41.1 1.5 fusion.64
  42.6 1.7 %slice_dynamic-update-slice_fusion.3 = bf16[8,16,9216]{2,1,0:T(8,128)(2,1)} fusion(bf16[8,16,9216]{2,1,0:T(8,128)(2,1)} %constant_dynamic-update-slice_fusion.3, bf16[4,16,9216]{2,1,0:T(8,128)(2,1)} %collective-permute-done.3), kind=kLoop, calls=%fused_computation.106 | loop fusion | bytes 589824
  45.0 1.7 %slice_dynamic-update-slice_fusion.2 = bf16[8,16,9216]{2,1,0:T(8,128)(2,1)} fusion(bf16[8,16,9216]{2,1,0:T(8,128)(2,1)} %constant_dynamic-update-slice_fusion.2, bf16[4,16,9216]{2,1,0:T(8,128)(2,1)} %collective-permute-done.3), kind=kLoop, calls=%fused_computation.105 | loop fusion | bytes 589824
  47.5 1.8 %slice_dynamic-update-slice_fusion.1 = bf16[8,16,9216]{2,1,0:T(8,128)(2,1)} fusion(bf16[8,16,9216]{2,1,0:T(8,128)(2,1)} %constant_dynamic-update-slice_fusion.1, bf16[4,16,9216]{2,1,0:T(8,128)(2,1)} %collective-permute-done.3), kind=kLoop, calls=%fused_computation.104 | loop fusion | bytes 589824
  50.0 1.7 %slice_dynamic-update-slice_fusion = bf16[8,16,9216]{2,1,0:T(8,128)(2,1)} fusion(bf16[8,16,9216]{2,1,0:T(8,128)(2,1)} %constant_dynamic-update-slice_fusion, bf16[4,16,9216]{2,1,0:T(8,128)(2,1)} %collective-permute-done.3), kind=kLoop, calls=%fused_computation.103 | loop fusion | bytes 589824 | tf_op jit(solution)/shard_map/stack | solution.py:96
  51.7 1.2 constant_dynamic-slice_fusion.2
  53.1 1.7 %fusion.32 = bf16[3,16,128]{2,1,0:T(8,128)(2,1)S(1)} fusion(bf16[3,128,8192]{2,1,0:T(8,128)(2,1)S(1)} %bitcast.109, f32[3,128]{1,0:T(4,128)S(1)} %get-tuple-element.28, bf16[3,16,9216]{2,1,0:T(8,128)(2,1)S(1)} %pad_maximum_fusion.2), kind=kOutput, calls=%fused_computation.68 | convolution fusion | flops 100675584 | bytes 7092224 | tf_op jit(solution)/shard_map/cvj,coj->cvo/dot_general | solution.py:111
  55.8 0.9 fusion.143
  58.9 1.4 fusion.79
  60.7 1.4 fusion.75
  62.1 1.0 fusion.93
  63.1 1.4 fusion.73
  64.5 1.0 fusion.91
  65.5 1.0 fusion.89
  66.5 1.0 fusion.87
  67.5 1.0 fusion.85
  69.7 1.0 fusion.83
  70.7 1.4 fusion.71
  72.1 1.5 fusion.69
  76.1 2.2 %convolution_add_fusion.3 = f32[384,1024]{1,0:T(8,128)S(1)} fusion(f32[384,1024]{1,0:T(8,128)S(1)} %convolution_add_fusion.5, bf16[768,1024]{1,0:T(8,128)(2,1)} %collective-permute-done.4, bf16[384,8192]{1,0:T(8,128)(2,1)S(1)} %bitcast.108, s32[]{:T(128)S(6)} %select_n.292), kind=kOutput, calls=%fused_computation.12 | convolution fusion | flops 604372992 | bytes 5308420 | tf_op jit(solution)/shard_map/dot_general | solution.py:166
  78.6 2.4 %fusion.46 = f32[384,1024]{1,0:T(8,128)S(1)} fusion(bf16[768,1024]{1,0:T(8,128)(2,1)} %collective-permute-done.6, bf16[384,8192]{1,0:T(8,128)(2,1)S(1)} %bitcast.108, s32[]{:T(128)S(6)} %select_n.296), kind=kOutput, calls=%fused_computation.96 | convolution fusion | flops 603979776 | bytes 3735556 | tf_op jit(solution)/shard_map/dot_general | solution.py:166
  81.4 1.4 collective-permute-start.7
  82.8 2.2 %fusion.3 = bf16[384,8192]{1,0:T(8,128)(2,1)S(1)} fusion(bf16[384,8192]{1,0:T(8,128)(2,1)S(1)} %fusion.17, s32[]{:T(128)S(6)} %select_n.292, f32[384,768]{1,0:T(8,128)S(1)} %bitcast.122, bf16[768,1024]{1,0:T(8,128)(2,1)} %collective-permute-done.4, bf16[384,1024]{1,0:T(8,128)(2,1)S(1)} %copy-done.4, f32[384]{0:T(512)S(1)} %get-tuple-element.27), kind=kOutput, calls=%fused_computation.26 | convolution fusion | flops 605749248 | bytes 4130820 | tf_op jit(solution)/shard_map/dot_general | solution.py:170
  85.1 1.5 fusion.19
  86.6 1.3 collective-permute-start.14
  87.9 2.2 %fusion.5 = bf16[384,8192]{1,0:T(8,128)(2,1)S(1)} fusion(bf16[384,8192]{1,0:T(8,128)(2,1)S(1)} %fusion.19, s32[]{:T(128)S(6)} %select_n.296, f32[384,768]{1,0:T(8,128)S(1)} %bitcast.121, bf16[768,1024]{1,0:T(8,128)(2,1)} %collective-permute-done.6, bf16[384,1024]{1,0:T(8,128)(2,1)S(1)} %copy-done.4, f32[384]{0:T(512)S(1)} %get-tuple-element.27), kind=kOutput, calls=%fused_computation.28 | convolution fusion | flops 605749248 | bytes 4130820 | tf_op jit(solution)/shard_map/dot_general | solution.py:170
  90.2 1.3 collective-permute-start.15
  91.9 3.9 %collective-permute-done.14 = bf16[256,1024]{1,0:T(8,128)(2,1)S(1)} collective-permute-done((bf16[256,1024]{1,0:T(8,128)(2,1)S(1)}, bf16[256,1024]{1,0:T(8,128)(2,1)S(1)}, u32[]{:S(2)}, u32[]{:S(2)}) %collective-permute-start.14) | collective-permute-done | bytes 524320 | tf_op jit(solution)/shard_map/ppermute | solution.py:55
  96.6 1.5 collective-permute-start.19
  98.2 1.6 %collective-permute-start.20 = (bf16[16,9216]{1,0:T(8,128)(2,1)S(1)}, bf16[16,9216]{1,0:T(8,128)(2,1)S(1)}, u32[]{:S(2)}, u32[]{:S(2)}) collective-permute-start(bf16[16,9216]{1,0:T(8,128)(2,1)S(1)} %get-tuple-element.10), channel_id=1, source_target_pairs={{0,16},{4,20},{8,24},{12,28},{16,0},{20,4},{24,8},{28,12},{1,17},{... | collective-permute-start | bytes 884744 | tf_op jit(solution)/shard_map/ppermute | solution.py:149
  100.6 4.0 %collective-permute-done.15 = bf16[256,1024]{1,0:T(8,128)(2,1)S(1)} collective-permute-done((bf16[256,1024]{1,0:T(8,128)(2,1)S(1)}, bf16[256,1024]{1,0:T(8,128)(2,1)S(1)}, u32[]{:S(2)}, u32[]{:S(2)}) %collective-permute-start.15) | collective-permute-done | bytes 524320 | tf_op jit(solution)/shard_map/ppermute | solution.py:56
  104.5 1.0 collective-permute-start.9
  106.6 1.1 collective-permute-start.10
  107.7 2.6 %collective-permute-done.20 = bf16[16,9216]{1,0:T(8,128)(2,1)S(1)} collective-permute-done((bf16[16,9216]{1,0:T(8,128)(2,1)S(1)}, bf16[16,9216]{1,0:T(8,128)(2,1)S(1)}, u32[]{:S(2)}, u32[]{:S(2)}) %collective-permute-start.20) | collective-permute-done | bytes 294944 | tf_op jit(solution)/shard_map/ppermute | solution.py:149
  110.3 3.3 %collective-permute-done.21 = bf16[16,9216]{1,0:T(8,128)(2,1)S(1)} collective-permute-done((bf16[16,9216]{1,0:T(8,128)(2,1)S(1)}, bf16[16,9216]{1,0:T(8,128)(2,1)S(1)}, u32[]{:S(2)}, u32[]{:S(2)}) %collective-permute-start.21) | collective-permute-done | bytes 294944 | tf_op jit(solution)/shard_map/ppermute | solution.py:149
  116.4 12.4 %collective-permute-done.9 = bf16[768,1024]{1,0:T(8,128)(2,1)S(1)} collective-permute-done((bf16[768,1024]{1,0:T(8,128)(2,1)}, bf16[768,1024]{1,0:T(8,128)(2,1)S(1)}, u32[]{:S(2)}, u32[]{:S(2)}) %collective-permute-start.9) | collective-permute-done | bytes 1572896 | tf_op jit(solution)/shard_map/ppermute | solution.py:55
  128.9 13.8 %collective-permute-done.10 = bf16[768,1024]{1,0:T(8,128)(2,1)S(1)} collective-permute-done((bf16[768,1024]{1,0:T(8,128)(2,1)}, bf16[768,1024]{1,0:T(8,128)(2,1)S(1)}, u32[]{:S(2)}, u32[]{:S(2)}) %collective-permute-start.10) | collective-permute-done | bytes 1572896 | tf_op jit(solution)/shard_map/ppermute | solution.py:56
  146.6 0.9 copy-done.6
  154.1 1.0 multiply_convert_fusion.1
  159.9 2.7 %copy-done.3 = bf16[384,8192]{1,0:T(8,128)(2,1)} copy-done((bf16[384,8192]{1,0:T(8,128)(2,1)}, bf16[384,8192]{1,0:T(8,128)(2,1)S(1)}, u32[]{:S(2)}) %copy-start.3) | copy-done | bytes 6291480
  (135 shorter events, 33.6 us)
Async XLA Ops:
  0.6 21.5 %copy-start = (s32[32]{0:T(128)S(1)}, s32[32]{0:T(128)}, u32[]{:S(2)}) copy-start(s32[32]{0:T(128)} %param.15) | copy-start | bytes 388
  1.7 9.2 %copy-start.10 = (bf16[1,16,8192]{2,1,0:T(8,128)(2,1)S(1)}, bf16[1,16,8192]{2,1,0:T(8,128)(2,1)}, u32[]{:S(2)}) copy-start(bf16[1,16,8192]{2,1,0:T(8,128)(2,1)} %param.11) | copy-start | bytes 786436
  1.7 9.2 %copy-start.17 = (bf16[1,16,1024]{2,1,0:T(8,128)(2,1)S(1)}, bf16[1,16,1024]{2,1,0:T(8,128)(2,1)}, u32[]{:S(2)}) copy-start(bf16[1,16,1024]{2,1,0:T(8,128)(2,1)} %param.12) | copy-start | bytes 98308
  1.7 11.8 %collective-permute-start = (bf16[16,9216]{1,0:T(8,128)(2,1)S(1)}, bf16[16,9216]{1,0:T(8,128)(2,1)S(1)}, u32[]{:S(2)}, u32[]{:S(2)}) collective-permute-start(bf16[16,9216]{1,0:T(8,128)(2,1)S(1)} %get-tuple-element.26), channel_id=1, source_target_pairs={{0,8},{4,12},{8,0},{12,4},{16,24},{20,28},{24,16},{28,20},{1,9},{5... | collective-permute-start | bytes 884744 | tf_op jit(solution)/shard_map/ppermute | solution.py:91
  4.7 16.3 %collective-permute-start.1 = (bf16[16,9216]{1,0:T(8,128)(2,1)S(1)}, bf16[16,9216]{1,0:T(8,128)(2,1)S(1)}, u32[]{:S(2)}, u32[]{:S(2)}) collective-permute-start(bf16[16,9216]{1,0:T(8,128)(2,1)S(1)} %get-tuple-element.26), channel_id=1, source_target_pairs={{0,16},{4,20},{8,24},{12,28},{16,0},{20,4},{24,8},{28,12},{1,17},{... | collective-permute-start | bytes 884744 | tf_op jit(solution)/shard_map/ppermute | solution.py:91
  6.2 14.7 %collective-permute-start.2 = (bf16[16,9216]{1,0:T(8,128)(2,1)S(1)}, bf16[16,9216]{1,0:T(8,128)(2,1)S(1)}, u32[]{:S(2)}, u32[]{:S(2)}) collective-permute-start(bf16[16,9216]{1,0:T(8,128)(2,1)S(1)} %get-tuple-element.26), channel_id=1, source_target_pairs={{0,24},{4,28},{8,16},{12,20},{16,8},{20,12},{24,0},{28,4},{1,25},{... | collective-permute-start | bytes 884744 | tf_op jit(solution)/shard_map/ppermute | solution.py:91
  8.9 4.6 %copy-start.19 = (s32[3]{0:T(128)S(1)}, s32[3]{0:T(128)}, u32[]{:S(2)}) copy-start(s32[3]{0:T(128)} %param.13) | copy-start | bytes 40
  8.9 67.1 %collective-permute-start.6 = (bf16[768,1024]{1,0:T(8,128)(2,1)}, bf16[768,1024]{1,0:T(8,128)(2,1)}, u32[]{:S(2)}, u32[]{:S(2)}) collective-permute-start(bf16[768,1024]{1,0:T(8,128)(2,1)} %slice.49), channel_id=1, source_target_pairs={{0,8},{1,17},{2,10},{3,19},{4,20},{5,13},{6,22},{7,15},{8,0},{9,25... | collective-permute-start | bytes 4718600 | tf_op jit(solution)/shard_map/ppermute | solution.py:51
  10.8 65.2 %collective-permute-start.4 = (bf16[768,1024]{1,0:T(8,128)(2,1)}, bf16[768,1024]{1,0:T(8,128)(2,1)}, u32[]{:S(2)}, u32[]{:S(2)}) collective-permute-start(bf16[768,1024]{1,0:T(8,128)(2,1)} %slice.49), channel_id=1, source_target_pairs={{0,4},{4,0},{8,12},{12,8},{16,20},{20,16},{24,28},{28,24},{1,5},{5... | collective-permute-start | bytes 4718600 | tf_op jit(solution)/shard_map/ppermute | solution.py:48
  13.5 27.6 %collective-permute-start.5 = (bf16[256,1024]{1,0:T(8,128)(2,1)}, bf16[256,1024]{1,0:T(8,128)(2,1)}, u32[]{:S(2)}, u32[]{:S(2)}) collective-permute-start(bf16[256,1024]{1,0:T(8,128)(2,1)} %slice.50), channel_id=1, source_target_pairs={{0,4},{4,0},{8,12},{12,8},{16,20},{20,16},{24,28},{28,24},{1,5},{5... | collective-permute-start | bytes 1572872 | tf_op jit(solution)/shard_map/ppermute | solution.py:48
  20.9 19.9 %copy-start.18 = (s32[3]{0:T(128)S(1)}, s32[3]{0:T(128)}, u32[]{:S(2)}) copy-start(s32[3]{0:T(128)} %param.14) | copy-start | bytes 40
  21.0 32.2 %slice-start = ((s8[6291456]{0:T(1024)(128)(4,1)}), s8[2097152]{0:T(1024)(128)(4,1)S(1)}, s32[]{:S(2)}) async-start(s8[6291456]{0:T(1024)(128)(4,1)} %bitcast.107), calls=%async_computation | async-start | bytes 4194304
  22.1 20.4 %collective-permute-start.3 = (bf16[4,16,9216]{2,1,0:T(8,128)(2,1)}, bf16[4,16,9216]{2,1,0:T(8,128)(2,1)}, u32[]{:S(2)}, u32[]{:S(2)}) collective-permute-start(bf16[4,16,9216]{2,1,0:T(8,128)(2,1)} %pad_maximum_fusion), channel_id=1, source_target_pairs={{0,4},{4,0},{8,12},{12,8},{16,20},{20,16},{24,28},{28,24},{1,5},{5... | collective-permute-start | bytes 3538952 | tf_op jit(solution)/shard_map/ppermute | solution.py:93
  47.4 5.7 %slice-start.1 = ((s8[6291456]{0:T(1024)(128)(4,1)}), s8[4194304]{0:T(1024)(128)(4,1)S(1)}, s32[]{:S(2)}) async-start(s8[6291456]{0:T(1024)(128)(4,1)} %bitcast.107), calls=%async_computation.1 | async-start | bytes 8388608
  53.1 1.7 %copy-start.4 = (bf16[384,1024]{1,0:T(8,128)(2,1)S(1)}, bf16[384,1024]{1,0:T(8,128)(2,1)}, u32[]{:S(2)}) copy-start(bf16[384,1024]{1,0:T(8,128)(2,1)} %param.9) | copy-start | bytes 2359300
  57.5 38.7 %collective-permute-start.18 = (bf16[4,16,9216]{2,1,0:T(8,128)(2,1)S(1)}, bf16[4,16,9216]{2,1,0:T(8,128)(2,1)S(1)}, u32[]{:S(2)}, u32[]{:S(2)}) collective-permute-start(bf16[4,16,9216]{2,1,0:T(8,128)(2,1)S(1)} %pad_maximum_fusion.1), channel_id=1, source_target_pairs={{0,4},{4,0},{8,12},{12,8},{16,20},{20,16},{24,28},{28,24},{1,5},{5... | collective-permute-start | bytes 3538952 | tf_op jit(solution)/shard_map/ppermute | solution.py:136
  63.1 5.4 %copy-start.2 = (bf16[1024,1024]{1,0:T(8,128)(2,1)S(1)}, bf16[1024,1024]{1,0:T(8,128)(2,1)}, u32[]{:S(2)}) copy-start(bf16[1024,1024]{1,0:T(8,128)(2,1)} %param.10) | copy-start | bytes 6291460
  76.0 10.6 %collective-permute-start.8 = (bf16[256,1024]{1,0:T(8,128)(2,1)}, bf16[256,1024]{1,0:T(8,128)(2,1)S(1)}, u32[]{:S(2)}, u32[]{:S(2)}) collective-permute-start(bf16[256,1024]{1,0:T(8,128)(2,1)} %slice.50), channel_id=1, source_target_pairs={{0,8},{1,17},{2,10},{3,19},{4,20},{5,13},{6,22},{7,15},{8,0},{9,25... | collective-permute-start | bytes 1572872 | tf_op jit(solution)/shard_map/ppermute | solution.py:51
  81.0 1.8 %copy-start.9 = (f32[3,128,768]{2,1,0:T(8,128)S(1)}, f32[3,128,768]{2,1,0:T(8,128)}, u32[]{:S(2)}) copy-start(f32[3,128,768]{2,1,0:T(8,128)} %fusion.79) | copy-start | bytes 3538948
  81.4 33.9 %collective-permute-start.7 = (bf16[768,1024]{1,0:T(8,128)(2,1)}, bf16[768,1024]{1,0:T(8,128)(2,1)S(1)}, u32[]{:S(2)}, u32[]{:S(2)}) collective-permute-start(bf16[768,1024]{1,0:T(8,128)(2,1)} %collective-permute-done.6), channel_id=1, source_target_pairs={{0,4},{4,0},{8,12},{12,8},{16,20},{20,16},{24,28},{28,24},{1,5},{5... | collective-permute-start | bytes 4718600 | tf_op jit(solution)/shard_map/ppermute | solution.py:54
  86.6 9.2 %collective-permute-start.14 = (bf16[256,1024]{1,0:T(8,128)(2,1)S(1)}, bf16[256,1024]{1,0:T(8,128)(2,1)S(1)}, u32[]{:S(2)}, u32[]{:S(2)}) collective-permute-start(bf16[256,1024]{1,0:T(8,128)(2,1)S(1)} %collective-permute-done.8), channel_id=1, source_target_pairs={{0,16},{1,9},{2,18},{3,11},{4,12},{5,21},{6,14},{7,23},{8,24},{9,1... | collective-permute-start | bytes 1572872 | tf_op jit(solution)/shard_map/ppermute | solution.py:55
  90.1 9.7 %collective-permute-start.11 = (bf16[256,1024]{1,0:T(8,128)(2,1)S(1)}, bf16[256,1024]{1,0:T(8,128)(2,1)S(1)}, u32[]{:S(2)}, u32[]{:S(2)}) collective-permute-start(bf16[256,1024]{1,0:T(8,128)(2,1)S(1)} %collective-permute-done.8), channel_id=1, source_target_pairs={{0,4},{4,0},{8,12},{12,8},{16,20},{20,16},{24,28},{28,24},{1,5},{5... | collective-permute-start | bytes 1572872 | tf_op jit(solution)/shard_map/ppermute | solution.py:54
  90.2 14.3 %collective-permute-start.15 = (bf16[256,1024]{1,0:T(8,128)(2,1)S(1)}, bf16[256,1024]{1,0:T(8,128)(2,1)S(1)}, u32[]{:S(2)}, u32[]{:S(2)}) collective-permute-start(bf16[256,1024]{1,0:T(8,128)(2,1)S(1)} %collective-permute-done.8), channel_id=1, source_target_pairs={{0,1},{1,0},{2,3},{3,2},{4,5},{5,4},{6,7},{7,6},{8,9},{9,8},{10,11... | collective-permute-start | bytes 1572872 | tf_op jit(solution)/shard_map/ppermute | solution.py:56
  96.6 9.9 %collective-permute-start.19 = (bf16[16,9216]{1,0:T(8,128)(2,1)S(1)}, bf16[16,9216]{1,0:T(8,128)(2,1)S(1)}, u32[]{:S(2)}, u32[]{:S(2)}) collective-permute-start(bf16[16,9216]{1,0:T(8,128)(2,1)S(1)} %get-tuple-element.9), channel_id=1, source_target_pairs={{0,8},{4,12},{8,0},{12,4},{16,24},{20,28},{24,16},{28,20},{1,9},{5... | collective-permute-start | bytes 884744 | tf_op jit(solution)/shard_map/ppermute | solution.py:149
  98.2 12.1 %collective-permute-start.20 = (bf16[16,9216]{1,0:T(8,128)(2,1)S(1)}, bf16[16,9216]{1,0:T(8,128)(2,1)S(1)}, u32[]{:S(2)}, u32[]{:S(2)}) collective-permute-start(bf16[16,9216]{1,0:T(8,128)(2,1)S(1)} %get-tuple-element.10), channel_id=1, source_target_pairs={{0,16},{4,20},{8,24},{12,28},{16,0},{20,4},{24,8},{28,12},{1,17},{... | collective-permute-start | bytes 884744 | tf_op jit(solution)/shard_map/ppermute | solution.py:149
  99.8 13.8 %collective-permute-start.21 = (bf16[16,9216]{1,0:T(8,128)(2,1)S(1)}, bf16[16,9216]{1,0:T(8,128)(2,1)S(1)}, u32[]{:S(2)}, u32[]{:S(2)}) collective-permute-start(bf16[16,9216]{1,0:T(8,128)(2,1)S(1)} %get-tuple-element.11), channel_id=1, source_target_pairs={{0,24},{4,28},{8,16},{12,20},{16,8},{20,12},{24,0},{28,4},{1,25},{... | collective-permute-start | bytes 884744 | tf_op jit(solution)/shard_map/ppermute | solution.py:149
  104.5 24.3 %collective-permute-start.9 = (bf16[768,1024]{1,0:T(8,128)(2,1)}, bf16[768,1024]{1,0:T(8,128)(2,1)S(1)}, u32[]{:S(2)}, u32[]{:S(2)}) collective-permute-start(bf16[768,1024]{1,0:T(8,128)(2,1)} %collective-permute-done.6), channel_id=1, source_target_pairs={{0,16},{1,9},{2,18},{3,11},{4,12},{5,21},{6,14},{7,23},{8,24},{9,1... | collective-permute-start | bytes 4718600 | tf_op jit(solution)/shard_map/ppermute | solution.py:55
  106.6 36.2 %collective-permute-start.10 = (bf16[768,1024]{1,0:T(8,128)(2,1)}, bf16[768,1024]{1,0:T(8,128)(2,1)S(1)}, u32[]{:S(2)}, u32[]{:S(2)}) collective-permute-start(bf16[768,1024]{1,0:T(8,128)(2,1)} %collective-permute-done.6), channel_id=1, source_target_pairs={{0,1},{1,0},{2,3},{3,2},{4,5},{5,4},{6,7},{7,6},{8,9},{9,8},{10,11... | collective-permute-start | bytes 4718600 | tf_op jit(solution)/shard_map/ppermute | solution.py:56
  110.3 43.1 %collective-permute-start.16 = (bf16[256,1024]{1,0:T(8,128)(2,1)S(1)}, bf16[256,1024]{1,0:T(8,128)(2,1)S(1)}, u32[]{:S(2)}, u32[]{:S(2)}) collective-permute-start(bf16[256,1024]{1,0:T(8,128)(2,1)S(1)} %collective-permute-done.14), channel_id=1, source_target_pairs={{0,4},{4,0},{8,12},{12,8},{16,20},{20,16},{24,28},{28,24},{1,5},{5... | collective-permute-start | bytes 1572872 | tf_op jit(solution)/shard_map/ppermute | solution.py:60
  113.7 36.5 %collective-permute-start.17 = (bf16[256,1024]{1,0:T(8,128)(2,1)S(1)}, bf16[256,1024]{1,0:T(8,128)(2,1)S(1)}, u32[]{:S(2)}, u32[]{:S(2)}) collective-permute-start(bf16[256,1024]{1,0:T(8,128)(2,1)S(1)} %collective-permute-done.15), channel_id=1, source_target_pairs={{0,4},{4,0},{8,12},{12,8},{16,20},{20,16},{24,28},{28,24},{1,5},{5... | collective-permute-start | bytes 1572872 | tf_op jit(solution)/shard_map/ppermute | solution.py:62
  116.4 27.1 %copy-start.8 = (f32[3,128,768]{2,1,0:T(8,128)S(1)}, f32[3,128,768]{2,1,0:T(8,128)}, u32[]{:S(2)}) copy-start(f32[3,128,768]{2,1,0:T(8,128)} %fusion.75) | copy-start | bytes 3538948
  128.9 21.7 %collective-permute-start.12 = (bf16[768,1024]{1,0:T(8,128)(2,1)S(1)}, bf16[768,1024]{1,0:T(8,128)(2,1)S(1)}, u32[]{:S(2)}, u32[]{:S(2)}) collective-permute-start(bf16[768,1024]{1,0:T(8,128)(2,1)S(1)} %collective-permute-done.9), channel_id=1, source_target_pairs={{0,4},{4,0},{8,12},{12,8},{16,20},{20,16},{24,28},{28,24},{1,5},{5... | collective-permute-start | bytes 4718600 | tf_op jit(solution)/shard_map/ppermute | solution.py:60
  142.8 8.6 %collective-permute-start.13 = (bf16[768,1024]{1,0:T(8,128)(2,1)S(1)}, bf16[768,1024]{1,0:T(8,128)(2,1)S(1)}, u32[]{:S(2)}, u32[]{:S(2)}) collective-permute-start(bf16[768,1024]{1,0:T(8,128)(2,1)S(1)} %collective-permute-done.10), channel_id=1, source_target_pairs={{0,4},{4,0},{8,12},{12,8},{16,20},{20,16},{24,28},{28,24},{1,5},{5... | collective-permute-start | bytes 4718600 | tf_op jit(solution)/shard_map/ppermute | solution.py:62
  144.4 1.0 copy-start.16
  146.2 1.3 copy-start.6
  147.5 1.3 copy-start.7
  148.7 1.0 copy-start.15
  154.1 1.6 copy-start.5
  156.5 1.0 copy-start.14
  157.4 1.0 copy-start.13
  157.5 1.4 copy-start.12
  158.4 1.0 copy-start.11
  158.9 3.7 %copy-start.1 = (s32[32]{0:T(128)S(1)}, s32[32]{0:T(128)}, u32[]{:S(2)}) copy-start(s32[32]{0:T(128)} %param.15) | copy-start | bytes 388
  159.9 2.7 %copy-start.3 = (bf16[384,8192]{1,0:T(8,128)(2,1)}, bf16[384,8192]{1,0:T(8,128)(2,1)S(1)}, u32[]{:S(2)}) copy-start(bf16[384,8192]{1,0:T(8,128)(2,1)S(1)} %fusion.31) | copy-start | bytes 18874372

commit v15 on v13

--- a/solution.py
+++ b/solution.py
@@ -142,7 +142,7 @@
     weight_pieces = relay_gather(frozen_value_weight, members, groups, me, dp_index)
     if weight_pieces and len(weight_pieces[0]) == 2:
         weight_pieces = [(source, 0, value) for source, value in weight_pieces]
-    last_pieces = (weight_pieces[-4][2],)
+    last_pieces = (weight_pieces[-2][2],)
     grad_sum = pair_sums[0]
     for index, step in enumerate(even_steps):
         sent = pair_sums[index + 1].astype(jnp.bfloat16)

time: 124 us -> 136 us (1.097)
  waiting for transfers between devices: 24.9 us -> 39.7 us
  local copies, waits for them, and re-layouts: 11.4 us -> 8.73 us
    ppermute x3, waiting for transfers between devices: 0.01 us -> 8.85 us  [on_device(): lax.ppermute(sent, 'fsdp', xor_pairs(members, step)).astype(jnp.float32)]
    ppermute x2, waiting for transfers between devices: 8.15 us -> 15.2 us  [relay_gather(): partner = lax.ppermute(first, ('fsdp', 'dp'), partner_pairs)]
    unnamed x40, local copies, waits for them, and re-layouts: 4.9 us -> 2.21 us
  transfers between devices with their start and end apart: 22 -> 22, of which waited for: 3 -> 5; matrix products, arithmetic and copies ran while one was open for 43% -> 40% of each run, Pallas kernels for 0% -> 0%
where the time goes in v15:
time: 136 us; the launch traced here: 135 us
  matrix products  42.6 us (31%)
  waiting for transfers between devices  39.7 us (29%)
  between operations  19.1 us (14%)
  starting transfers between devices  17.1 us (13%)
  local copies, waits for them, and re-layouts  8.73 us (6%)
  other arithmetic  7.77 us (6%)
    dot_general x16, matrix products, on_device(): lax.dot_general(masked_cot, weight_piece, (((1,), (1,)), ((), ())), prefe...  15.3 us
    ppermute x2, waiting for transfers between devices, relay_gather(): partner = lax.ppermute(first, ('fsdp', 'dp'), partner_pairs)  15.2 us
    dot_general x16, matrix products, on_device(): jnp.dot(token_piece, weight_piece, preferred_element_type=jnp.float32)  13.3 us
    dot_general x16, matrix products, on_device(): jnp.einsum('uio,uof->uif', low_rank_gradient, down_piece, preferred_eleme...  10.3 us
    ppermute x3, waiting for transfers between devices, on_device(): lax.ppermute(sent, 'fsdp', xor_pairs(members, step)).astype(jnp.float32)  8.85 us
    ppermute x2, waiting for transfers between devices, relay_gather(): relayed = lax.ppermute(first, ('fsdp', 'dp'), relay_pairs)  8 us
    ppermute x3, waiting for transfers between devices, on_device(): by_step[step] = lax.ppermute(own_adapter, 'fsdp', xor_pairs(members, step))  7.71 us
    ppermute x3, starting transfers between devices, on_device(): by_step[step] = lax.ppermute(own_adapter, 'fsdp', xor_pairs(members, step))  4.54 us
  transfers between devices with their start and end apart: 22, of which 5 were waited for; matrix products, arithmetic and copies ran while one was open for 40% of the time, Pallas kernels for 0%

profile of v15, /device:TPU:0, one launch (start us, length us, event | category | flops | bytes accessed | tf_op | source)
XLA Modules:
  0.0 135.0 jit_solution(8626878243192176384)
XLA Ops:
  0.6 1.0 fusion.135
  1.7 3.0 %collective-permute-start = (bf16[16,9216]{1,0:T(8,128)(2,1)S(1)}, bf16[16,9216]{1,0:T(8,128)(2,1)S(1)}, u32[]{:S(2)}, u32[]{:S(2)}) collective-permute-start(bf16[16,9216]{1,0:T(8,128)(2,1)S(1)} %get-tuple-element.28), channel_id=1, source_target_pairs={{0,8},{4,12},{8,0},{12,4},{16,24},{20,28},{24,16},{28,20},{1,9},{5... | collective-permute-start | bytes 884744 | tf_op jit(solution)/shard_map/ppermute | solution.py:92
  4.7 1.5 %collective-permute-start.1 = (bf16[16,9216]{1,0:T(8,128)(2,1)S(1)}, bf16[16,9216]{1,0:T(8,128)(2,1)S(1)}, u32[]{:S(2)}, u32[]{:S(2)}) collective-permute-start(bf16[16,9216]{1,0:T(8,128)(2,1)S(1)} %get-tuple-element.28), channel_id=1, source_target_pairs={{0,16},{4,20},{8,24},{12,28},{16,0},{20,4},{24,8},{28,12},{1,17},{... | collective-permute-start | bytes 884744 | tf_op jit(solution)/shard_map/ppermute | solution.py:92
  6.2 3.1 %fusion.142 = (bf16[512,1024]{1,0:T(8,128)(2,1)}, bf16[512,1024]{1,0:T(8,128)(2,1)}) fusion(bf16[1024,1024]{1,0:T(8,128)(2,1)} %param.10), kind=kLoop, calls=%fused_computation.213 | loop fusion | bytes 4194304 | tf_op jit(solution)/shard_map/slice | solution.py:47
  9.3 1.9 %collective-permute-start.6 = (bf16[512,1024]{1,0:T(8,128)(2,1)}, bf16[512,1024]{1,0:T(8,128)(2,1)}, u32[]{:S(2)}, u32[]{:S(2)}) collective-permute-start(bf16[512,1024]{1,0:T(8,128)(2,1)} %get-tuple-element.23), channel_id=1, source_target_pairs={{0,8},{1,17},{2,10},{3,19},{4,20},{5,13},{6,22},{7,15},{8,0},{9,25... | collective-permute-start | bytes 3145736 | tf_op jit(solution)/shard_map/ppermute | solution.py:52
  11.3 0.7 constant_dynamic-update-slice_fusion.3
  12.1 0.6 gather_fusion
  13.2 7.7 %collective-permute-done.1 = bf16[16,9216]{1,0:T(8,128)(2,1)S(1)} collective-permute-done((bf16[16,9216]{1,0:T(8,128)(2,1)S(1)}, bf16[16,9216]{1,0:T(8,128)(2,1)S(1)}, u32[]{:S(2)}, u32[]{:S(2)}) %collective-permute-start.1) | collective-permute-done | bytes 294944 | tf_op jit(solution)/shard_map/ppermute | solution.py:92
  39.6 1.7 %collective-permute-start.7 = (bf16[512,1024]{1,0:T(8,128)(2,1)}, bf16[512,1024]{1,0:T(8,128)(2,1)S(1)}, u32[]{:S(2)}, u32[]{:S(2)}) collective-permute-start(bf16[512,1024]{1,0:T(8,128)(2,1)} %collective-permute-done.6), channel_id=1, source_target_pairs={{0,4},{4,0},{8,12},{12,8},{16,20},{20,16},{24,28},{28,24},{1,5},{5... | collective-permute-start | bytes 3145736 | tf_op jit(solution)/shard_map/ppermute | solution.py:55
  41.3 1.9 %fusion.57 = f32[384,1024]{1,0:T(8,128)S(1)} fusion(bf16[512,1024]{1,0:T(8,128)(2,1)} %collective-permute-done.6, bf16[384,8192]{1,0:T(8,128)(2,1)} %param.8, s32[]{:T(128)S(6)} %select_n.296), kind=kOutput, calls=%fused_computation.107 | convolution fusion | flops 402653184 | bytes 3014660 | tf_op jit(solution)/shard_map/dot_general | solution.py:167
  43.8 2.1 %fusion.59 = f32[384,1024]{1,0:T(8,128)S(1)} fusion(bf16[512,1024]{1,0:T(8,128)(2,1)} %collective-permute-done.5, bf16[384,8192]{1,0:T(8,128)(2,1)} %param.8, s32[]{:T(128)S(6)} %select_n.293), kind=kOutput, calls=%fused_computation.109 | convolution fusion | flops 402653184 | bytes 3014660 | tf_op jit(solution)/shard_map/dot_general | solution.py:167
  45.9 1.1 collective-permute-start.10
  47.5 1.1 copy-done.4
  48.9 1.2 fusion.91
  50.1 1.2 fusion.89
  51.4 0.9 fusion.144
  52.3 1.7 %fusion.32 = bf16[3,16,128]{2,1,0:T(8,128)(2,1)S(1)} fusion(bf16[3,128,8192]{2,1,0:T(8,128)(2,1)S(1)} %bitcast.110, f32[3,128]{1,0:T(4,128)S(1)} %get-tuple-element.30, bf16[3,16,9216]{2,1,0:T(8,128)(2,1)S(1)} %pad_maximum_fusion.2), kind=kOutput, calls=%fused_computation.68 | convolution fusion | flops 100675584 | bytes 7092224 | tf_op jit(solution)/shard_map/cvj,coj->cvo/dot_general | solution.py:112
  54.7 1.2 fusion.97
  55.9 1.2 fusion.95
  57.0 1.2 fusion.93
  58.3 1.2 fusion.87
  62.9 0.7 broadcast_in_dim.44
  63.6 1.8 %fusion.1 = bf16[384,8192]{1,0:T(8,128)(2,1)S(1)} fusion(bf16[384,8192]{1,0:T(8,128)(2,1)S(1)} %broadcast_in_dim.44, s32[]{:T(128)S(6)} %select_n.290, f32[384,512]{1,0:T(8,128)} %bitcast.133, bf16[1024,1024]{1,0:T(8,128)(2,1)S(1)} %copy-done.2, bf16[384,1024]{1,0:T(8,128)(2,1)S(1)} %copy-done.4, f32[384]{0:T(512)S(1)} %get-tuple-element.29), kind=kOutput, calls=%fused_computation.32 | convolution fusion | flops 404226048 | bytes 3016708 | tf_op jit(solution)/shard_map/dot_general | solution.py:171
  65.5 0.6 fusion.3
  67.8 1.9 %fusion.5 = bf16[384,8192]{1,0:T(8,128)(2,1)S(1)} fusion(bf16[384,8192]{1,0:T(8,128)(2,1)S(1)} %fusion.3, s32[]{:T(128)S(6)} %select_n.292, f32[384,512]{1,0:T(8,128)S(1)} %bitcast.131, bf16[512,1024]{1,0:T(8,128)(2,1)} %collective-permute-done.4, bf16[384,1024]{1,0:T(8,128)(2,1)S(1)} %copy-done.4, f32[384]{0:T(512)S(1)} %get-tuple-element.29), kind=kOutput, calls=%fused_computation.36 | convolution fusion | flops 404226048 | bytes 3016708 | tf_op jit(solution)/shard_map/dot_general | solution.py:171
  69.7 2.1 %fusion.7 = bf16[384,8192]{1,0:T(8,128)(2,1)S(1)} fusion(bf16[384,8192]{1,0:T(8,128)(2,1)S(1)} %fusion.5, s32[]{:T(128)S(6)} %select_n.293, f32[384,512]{1,0:T(8,128)S(1)} %bitcast.130, bf16[512,1024]{1,0:T(8,128)(2,1)} %collective-permute-done.5, bf16[384,1024]{1,0:T(8,128)(2,1)S(1)} %copy-done.4, f32[384]{0:T(512)S(1)} %get-tuple-element.29), kind=kOutput, calls=%fused_computation.38 | convolution fusion | flops 404226048 | bytes 3016708 | tf_op jit(solution)/shard_map/dot_general | solution.py:171
  71.9 1.8 %fusion.9 = bf16[384,8192]{1,0:T(8,128)(2,1)S(1)} fusion(bf16[384,8192]{1,0:T(8,128)(2,1)S(1)} %fusion.7, s32[]{:T(128)S(6)} %select_n.296, f32[384,512]{1,0:T(8,128)S(1)} %bitcast.129, bf16[512,1024]{1,0:T(8,128)(2,1)} %collective-permute-done.6, bf16[384,1024]{1,0:T(8,128)(2,1)S(1)} %copy-done.4, f32[384]{0:T(512)S(1)} %get-tuple-element.29), kind=kOutput, calls=%fused_computation.40 | convolution fusion | flops 404226048 | bytes 3016708 | tf_op jit(solution)/shard_map/dot_general | solution.py:171
  73.7 1.8 %convolution_add_fusion.4 = f32[384,1024]{1,0:T(8,128)S(1)} fusion(f32[384,1024]{1,0:T(8,128)S(1)} %convolution_add_fusion.5, bf16[512,1024]{1,0:T(8,128)(2,1)} %collective-permute-done.4, bf16[384,8192]{1,0:T(8,128)(2,1)S(1)} %bitcast.108, s32[]{:T(128)S(6)} %select_n.292), kind=kOutput, calls=%fused_computation.12 | convolution fusion | flops 403046400 | bytes 4587524 | tf_op jit(solution)/shard_map/dot_general | solution.py:167
  80.3 1.3 collective-permute-start.14
  82.8 0.6 fusion.13
  83.4 0.6 fusion.15
  84.0 0.6 fusion.17
  84.7 1.1 collective-permute-start.15
  87.2 8.0 %collective-permute-done.14 = bf16[512,1024]{1,0:T(8,128)(2,1)S(1)} collective-permute-done((bf16[512,1024]{1,0:T(8,128)(2,1)S(1)}, bf16[512,1024]{1,0:T(8,128)(2,1)S(1)}, u32[]{:S(2)}, u32[]{:S(2)}) %collective-permute-start.14) | collective-permute-done | bytes 1048608 | tf_op jit(solution)/shard_map/ppermute | solution.py:56
  95.2 15.1 %collective-permute-done.15 = bf16[512,1024]{1,0:T(8,128)(2,1)S(1)} collective-permute-done((bf16[512,1024]{1,0:T(8,128)(2,1)S(1)}, bf16[512,1024]{1,0:T(8,128)(2,1)S(1)}, u32[]{:S(2)}, u32[]{:S(2)}) %collective-permute-start.15) | collective-permute-done | bytes 1048608 | tf_op jit(solution)/shard_map/ppermute | solution.py:57
  110.9 0.6 fusion.19
  112.1 0.6 fusion.21
  112.8 0.6 fusion.23
  115.6 0.8 fusion.25
  116.5 0.6 fusion.27
  117.1 0.8 collective-permute-start.19
  117.9 1.5 %collective-permute-start.20 = (bf16[16,9216]{1,0:T(8,128)(2,1)S(1)}, bf16[16,9216]{1,0:T(8,128)(2,1)S(1)}, u32[]{:S(2)}, u32[]{:S(2)}) collective-permute-start(bf16[16,9216]{1,0:T(8,128)(2,1)S(1)} %get-tuple-element.10), channel_id=1, source_target_pairs={{0,16},{4,20},{8,24},{12,28},{16,0},{20,4},{24,8},{28,12},{1,17},{... | collective-permute-start | bytes 884744 | tf_op jit(solution)/shard_map/ppermute | solution.py:150
  119.4 1.3 collective-permute-start.21
  122.2 1.0 multiply_convert_fusion.1
  124.5 2.5 %collective-permute-done.19 = bf16[16,9216]{1,0:T(8,128)(2,1)S(1)} collective-permute-done((bf16[16,9216]{1,0:T(8,128)(2,1)S(1)}, bf16[16,9216]{1,0:T(8,128)(2,1)S(1)}, u32[]{:S(2)}, u32[]{:S(2)}) %collective-permute-start.19) | collective-permute-done | bytes 294944 | tf_op jit(solution)/shard_map/ppermute | solution.py:150
  127.0 6.4 %collective-permute-done.20 = bf16[16,9216]{1,0:T(8,128)(2,1)S(1)} collective-permute-done((bf16[16,9216]{1,0:T(8,128)(2,1)S(1)}, bf16[16,9216]{1,0:T(8,128)(2,1)S(1)}, u32[]{:S(2)}, u32[]{:S(2)}) %collective-permute-start.20) | collective-permute-done | bytes 294944 | tf_op jit(solution)/shard_map/ppermute | solution.py:150
  133.7 0.7 slice_bitcast_fusion
  134.4 0.6 slice_bitcast_fusion.1
  (124 shorter events, 22.1 us)
Async XLA Ops:
  0.6 11.4 %copy-start = (s32[32]{0:T(128)S(1)}, s32[32]{0:T(128)}, u32[]{:S(2)}) copy-start(s32[32]{0:T(128)} %param.15) | copy-start | bytes 388
  1.7 9.6 %copy-start.5 = (bf16[1,16,8192]{2,1,0:T(8,128)(2,1)S(1)}, bf16[1,16,8192]{2,1,0:T(8,128)(2,1)}, u32[]{:S(2)}) copy-start(bf16[1,16,8192]{2,1,0:T(8,128)(2,1)} %param.11) | copy-start | bytes 786436
  1.7 9.6 %copy-start.12 = (bf16[1,16,1024]{2,1,0:T(8,128)(2,1)S(1)}, bf16[1,16,1024]{2,1,0:T(8,128)(2,1)}, u32[]{:S(2)}) copy-start(bf16[1,16,1024]{2,1,0:T(8,128)(2,1)} %param.12) | copy-start | bytes 98308
  1.7 10.3 %copy-start.14 = (s32[3]{0:T(128)S(1)}, s32[3]{0:T(128)}, u32[]{:S(2)}) copy-start(s32[3]{0:T(128)} %param.13) | copy-start | bytes 40
  1.7 11.0 %collective-permute-start = (bf16[16,9216]{1,0:T(8,128)(2,1)S(1)}, bf16[16,9216]{1,0:T(8,128)(2,1)S(1)}, u32[]{:S(2)}, u32[]{:S(2)}) collective-permute-start(bf16[16,9216]{1,0:T(8,128)(2,1)S(1)} %get-tuple-element.28), channel_id=1, source_target_pairs={{0,8},{4,12},{8,0},{12,4},{16,24},{20,28},{24,16},{28,20},{1,9},{5... | collective-permute-start | bytes 884744 | tf_op jit(solution)/shard_map/ppermute | solution.py:92
  4.7 16.3 %collective-permute-start.1 = (bf16[16,9216]{1,0:T(8,128)(2,1)S(1)}, bf16[16,9216]{1,0:T(8,128)(2,1)S(1)}, u32[]{:S(2)}, u32[]{:S(2)}) collective-permute-start(bf16[16,9216]{1,0:T(8,128)(2,1)S(1)} %get-tuple-element.28), channel_id=1, source_target_pairs={{0,16},{4,20},{8,24},{12,28},{16,0},{20,4},{24,8},{28,12},{1,17},{... | collective-permute-start | bytes 884744 | tf_op jit(solution)/shard_map/ppermute | solution.py:92
  6.2 14.7 %collective-permute-start.2 = (bf16[16,9216]{1,0:T(8,128)(2,1)S(1)}, bf16[16,9216]{1,0:T(8,128)(2,1)S(1)}, u32[]{:S(2)}, u32[]{:S(2)}) collective-permute-start(bf16[16,9216]{1,0:T(8,128)(2,1)S(1)} %get-tuple-element.28), channel_id=1, source_target_pairs={{0,24},{4,28},{8,16},{12,20},{16,8},{20,12},{24,0},{28,4},{1,25},{... | collective-permute-start | bytes 884744 | tf_op jit(solution)/shard_map/ppermute | solution.py:92
  9.3 30.3 %collective-permute-start.6 = (bf16[512,1024]{1,0:T(8,128)(2,1)}, bf16[512,1024]{1,0:T(8,128)(2,1)}, u32[]{:S(2)}, u32[]{:S(2)}) collective-permute-start(bf16[512,1024]{1,0:T(8,128)(2,1)} %get-tuple-element.23), channel_id=1, source_target_pairs={{0,8},{1,17},{2,10},{3,19},{4,20},{5,13},{6,22},{7,15},{8,0},{9,25... | collective-permute-start | bytes 3145736 | tf_op jit(solution)/shard_map/ppermute | solution.py:52
  11.3 55.8 %collective-permute-start.4 = (bf16[512,1024]{1,0:T(8,128)(2,1)}, bf16[512,1024]{1,0:T(8,128)(2,1)}, u32[]{:S(2)}, u32[]{:S(2)}) collective-permute-start(bf16[512,1024]{1,0:T(8,128)(2,1)} %get-tuple-element.23), channel_id=1, source_target_pairs={{0,4},{4,0},{8,12},{12,8},{16,20},{20,16},{24,28},{28,24},{1,5},{5... | collective-permute-start | bytes 3145736 | tf_op jit(solution)/shard_map/ppermute | solution.py:49
  12.1 27.4 %copy-start.13 = (s32[3]{0:T(128)S(1)}, s32[3]{0:T(128)}, u32[]{:S(2)}) copy-start(s32[3]{0:T(128)} %param.14) | copy-start | bytes 40
  12.7 30.6 %collective-permute-start.5 = (bf16[512,1024]{1,0:T(8,128)(2,1)}, bf16[512,1024]{1,0:T(8,128)(2,1)}, u32[]{:S(2)}, u32[]{:S(2)}) collective-permute-start(bf16[512,1024]{1,0:T(8,128)(2,1)} %get-tuple-element.8), channel_id=1, source_target_pairs={{0,4},{4,0},{8,12},{12,8},{16,20},{20,16},{24,28},{28,24},{1,5},{5... | collective-permute-start | bytes 3145736 | tf_op jit(solution)/shard_map/ppermute | solution.py:49
  21.1 24.8 %collective-permute-start.3 = (bf16[4,16,9216]{2,1,0:T(8,128)(2,1)S(1)}, bf16[4,16,9216]{2,1,0:T(8,128)(2,1)S(1)}, u32[]{:S(2)}, u32[]{:S(2)}) collective-permute-start(bf16[4,16,9216]{2,1,0:T(8,128)(2,1)S(1)} %pad_maximum_fusion), channel_id=1, source_target_pairs={{0,4},{4,0},{8,12},{12,8},{16,20},{20,16},{24,28},{28,24},{1,5},{5... | collective-permute-start | bytes 3538952 | tf_op jit(solution)/shard_map/ppermute | solution.py:94
  39.6 38.2 %collective-permute-start.8 = (bf16[512,1024]{1,0:T(8,128)(2,1)}, bf16[512,1024]{1,0:T(8,128)(2,1)S(1)}, u32[]{:S(2)}, u32[]{:S(2)}) collective-permute-start(bf16[512,1024]{1,0:T(8,128)(2,1)} %get-tuple-element.8), channel_id=1, source_target_pairs={{0,8},{1,17},{2,10},{3,19},{4,20},{5,13},{6,22},{7,15},{8,0},{9,25... | collective-permute-start | bytes 3145736 | tf_op jit(solution)/shard_map/ppermute | solution.py:52
  39.6 37.6 %collective-permute-start.7 = (bf16[512,1024]{1,0:T(8,128)(2,1)}, bf16[512,1024]{1,0:T(8,128)(2,1)S(1)}, u32[]{:S(2)}, u32[]{:S(2)}) collective-permute-start(bf16[512,1024]{1,0:T(8,128)(2,1)} %collective-permute-done.6), channel_id=1, source_target_pairs={{0,4},{4,0},{8,12},{12,8},{16,20},{20,16},{24,28},{28,24},{1,5},{5... | collective-permute-start | bytes 3145736 | tf_op jit(solution)/shard_map/ppermute | solution.py:55
  43.2 3.8 %copy-start.11 = (bf16[8,16,9216]{2,1,0:T(8,128)(2,1)S(1)}, bf16[8,16,9216]{2,1,0:T(8,128)(2,1)}, u32[]{:S(2)}) copy-start(bf16[8,16,9216]{2,1,0:T(8,128)(2,1)} %constant_dynamic-update-slice_fusion.3) | copy-start | bytes 7077892
  43.3 35.5 %collective-permute-start.9 = (bf16[512,1024]{1,0:T(8,128)(2,1)}, bf16[512,1024]{1,0:T(8,128)(2,1)S(1)}, u32[]{:S(2)}, u32[]{:S(2)}) collective-permute-start(bf16[512,1024]{1,0:T(8,128)(2,1)} %collective-permute-done.6), channel_id=1, source_target_pairs={{0,16},{1,9},{2,18},{3,11},{4,12},{5,21},{6,14},{7,23},{8,24},{9,1... | collective-permute-start | bytes 3145736 | tf_op jit(solution)/shard_map/ppermute | solution.py:56
  43.8 7.5 %slice-start = ((s8[6291456]{0:T(1024)(128)(4,1)}), s8[4194304]{0:T(1024)(128)(4,1)S(1)}, s32[]{:S(2)}) async-start(s8[6291456]{0:T(1024)(128)(4,1)} %bitcast.107), calls=%async_computation | async-start | bytes 8388608
  45.9 33.4 %collective-permute-start.10 = (bf16[512,1024]{1,0:T(8,128)(2,1)}, bf16[512,1024]{1,0:T(8,128)(2,1)S(1)}, u32[]{:S(2)}, u32[]{:S(2)}) collective-permute-start(bf16[512,1024]{1,0:T(8,128)(2,1)} %collective-permute-done.6), channel_id=1, source_target_pairs={{0,1},{1,0},{2,3},{3,2},{4,5},{5,4},{6,7},{7,6},{8,9},{9,8},{10,11... | collective-permute-start | bytes 3145736 | tf_op jit(solution)/shard_map/ppermute | solution.py:57
  47.2 4.1 %slice-start.1 = ((s8[6291456]{0:T(1024)(128)(4,1)}), s8[2097152]{0:T(1024)(128)(4,1)S(1)}, s32[]{:S(2)}) async-start(s8[6291456]{0:T(1024)(128)(4,1)} %bitcast.107), calls=%async_computation.1 | async-start | bytes 4194304
  47.3 1.3 copy-start.4
  60.1 1.6 %copy-start.2 = (bf16[1024,1024]{1,0:T(8,128)(2,1)S(1)}, bf16[1024,1024]{1,0:T(8,128)(2,1)}, u32[]{:S(2)}) copy-start(bf16[1024,1024]{1,0:T(8,128)(2,1)} %param.10) | copy-start | bytes 6291460
  63.6 1.8 %copy-start.10 = (f32[3,128,512]{2,1,0:T(8,128)S(1)}, f32[3,128,512]{2,1,0:T(8,128)}, u32[]{:S(2)}) copy-start(f32[3,128,512]{2,1,0:T(8,128)} %fusion.95) | copy-start | bytes 2359300
  66.6 1.1 copy-start.9
  67.1 17.5 %collective-permute-start.18 = (bf16[4,16,9216]{2,1,0:T(8,128)(2,1)S(1)}, bf16[4,16,9216]{2,1,0:T(8,128)(2,1)S(1)}, u32[]{:S(2)}, u32[]{:S(2)}) collective-permute-start(bf16[4,16,9216]{2,1,0:T(8,128)(2,1)S(1)} %pad_maximum_fusion.1), channel_id=1, source_target_pairs={{0,4},{4,0},{8,12},{12,8},{16,20},{20,16},{24,28},{28,24},{1,5},{5... | collective-permute-start | bytes 3538952 | tf_op jit(solution)/shard_map/ppermute | solution.py:137
  67.8 1.9 %copy-start.8 = (f32[3,128,512]{2,1,0:T(8,128)S(1)}, f32[3,128,512]{2,1,0:T(8,128)}, u32[]{:S(2)}) copy-start(f32[3,128,512]{2,1,0:T(8,128)} %fusion.91) | copy-start | bytes 2359300
  69.7 2.1 %copy-start.7 = (f32[3,128,512]{2,1,0:T(8,128)S(1)}, f32[3,128,512]{2,1,0:T(8,128)}, u32[]{:S(2)}) copy-start(f32[3,128,512]{2,1,0:T(8,128)} %fusion.89) | copy-start | bytes 2359300
  79.9 2.2 %copy-start.6 = (f32[3,128,512]{2,1,0:T(8,128)S(1)}, f32[3,128,512]{2,1,0:T(8,128)}, u32[]{:S(2)}) copy-start(f32[3,128,512]{2,1,0:T(8,128)} %fusion.87) | copy-start | bytes 2359300
  80.3 14.9 %collective-permute-start.14 = (bf16[512,1024]{1,0:T(8,128)(2,1)S(1)}, bf16[512,1024]{1,0:T(8,128)(2,1)S(1)}, u32[]{:S(2)}, u32[]{:S(2)}) collective-permute-start(bf16[512,1024]{1,0:T(8,128)(2,1)S(1)} %collective-permute-done.8), channel_id=1, source_target_pairs={{0,16},{1,9},{2,18},{3,11},{4,12},{5,21},{6,14},{7,23},{8,24},{9,1... | collective-permute-start | bytes 3145736 | tf_op jit(solution)/shard_map/ppermute | solution.py:56
  81.7 4.6 %collective-permute-start.11 = (bf16[512,1024]{1,0:T(8,128)(2,1)S(1)}, bf16[512,1024]{1,0:T(8,128)(2,1)S(1)}, u32[]{:S(2)}, u32[]{:S(2)}) collective-permute-start(bf16[512,1024]{1,0:T(8,128)(2,1)S(1)} %collective-permute-done.8), channel_id=1, source_target_pairs={{0,4},{4,0},{8,12},{12,8},{16,20},{20,16},{24,28},{28,24},{1,5},{5... | collective-permute-start | bytes 3145736 | tf_op jit(solution)/shard_map/ppermute | solution.py:55
  81.7 29.9 %collective-permute-start.12 = (bf16[512,1024]{1,0:T(8,128)(2,1)S(1)}, bf16[512,1024]{1,0:T(8,128)(2,1)S(1)}, u32[]{:S(2)}, u32[]{:S(2)}) collective-permute-start(bf16[512,1024]{1,0:T(8,128)(2,1)S(1)} %collective-permute-done.9), channel_id=1, source_target_pairs={{0,4},{4,0},{8,12},{12,8},{16,20},{20,16},{24,28},{28,24},{1,5},{5... | collective-permute-start | bytes 3145736 | tf_op jit(solution)/shard_map/ppermute | solution.py:61
  82.2 28.2 %collective-permute-start.13 = (bf16[512,1024]{1,0:T(8,128)(2,1)S(1)}, bf16[512,1024]{1,0:T(8,128)(2,1)S(1)}, u32[]{:S(2)}, u32[]{:S(2)}) collective-permute-start(bf16[512,1024]{1,0:T(8,128)(2,1)S(1)} %collective-permute-done.10), channel_id=1, source_target_pairs={{0,4},{4,0},{8,12},{12,8},{16,20},{20,16},{24,28},{28,24},{1,5},{5... | collective-permute-start | bytes 3145736 | tf_op jit(solution)/shard_map/ppermute | solution.py:63
  84.7 25.6 %collective-permute-start.15 = (bf16[512,1024]{1,0:T(8,128)(2,1)S(1)}, bf16[512,1024]{1,0:T(8,128)(2,1)S(1)}, u32[]{:S(2)}, u32[]{:S(2)}) collective-permute-start(bf16[512,1024]{1,0:T(8,128)(2,1)S(1)} %collective-permute-done.8), channel_id=1, source_target_pairs={{0,1},{1,0},{2,3},{3,2},{4,5},{5,4},{6,7},{7,6},{8,9},{9,8},{10,11... | collective-permute-start | bytes 3145736 | tf_op jit(solution)/shard_map/ppermute | solution.py:57
  95.2 21.9 %collective-permute-start.16 = (bf16[512,1024]{1,0:T(8,128)(2,1)S(1)}, bf16[512,1024]{1,0:T(8,128)(2,1)S(1)}, u32[]{:S(2)}, u32[]{:S(2)}) collective-permute-start(bf16[512,1024]{1,0:T(8,128)(2,1)S(1)} %collective-permute-done.14), channel_id=1, source_target_pairs={{0,4},{4,0},{8,12},{12,8},{16,20},{20,16},{24,28},{28,24},{1,5},{5... | collective-permute-start | bytes 3145736 | tf_op jit(solution)/shard_map/ppermute | solution.py:61
  110.3 11.0 %collective-permute-start.17 = (bf16[512,1024]{1,0:T(8,128)(2,1)S(1)}, bf16[512,1024]{1,0:T(8,128)(2,1)S(1)}, u32[]{:S(2)}, u32[]{:S(2)}) collective-permute-start(bf16[512,1024]{1,0:T(8,128)(2,1)S(1)} %collective-permute-done.15), channel_id=1, source_target_pairs={{0,4},{4,0},{8,12},{12,8},{16,20},{20,16},{24,28},{28,24},{1,5},{5... | collective-permute-start | bytes 3145736 | tf_op jit(solution)/shard_map/ppermute | solution.py:63
  117.1 9.9 %collective-permute-start.19 = (bf16[16,9216]{1,0:T(8,128)(2,1)S(1)}, bf16[16,9216]{1,0:T(8,128)(2,1)S(1)}, u32[]{:S(2)}, u32[]{:S(2)}) collective-permute-start(bf16[16,9216]{1,0:T(8,128)(2,1)S(1)} %get-tuple-element.9), channel_id=1, source_target_pairs={{0,8},{4,12},{8,0},{12,4},{16,24},{20,28},{24,16},{28,20},{1,9},{5... | collective-permute-start | bytes 884744 | tf_op jit(solution)/shard_map/ppermute | solution.py:150
  117.9 15.5 %collective-permute-start.20 = (bf16[16,9216]{1,0:T(8,128)(2,1)S(1)}, bf16[16,9216]{1,0:T(8,128)(2,1)S(1)}, u32[]{:S(2)}, u32[]{:S(2)}) collective-permute-start(bf16[16,9216]{1,0:T(8,128)(2,1)S(1)} %get-tuple-element.10), channel_id=1, source_target_pairs={{0,16},{4,20},{8,24},{12,28},{16,0},{20,4},{24,8},{28,12},{1,17},{... | collective-permute-start | bytes 884744 | tf_op jit(solution)/shard_map/ppermute | solution.py:150
  119.4 14.0 %collective-permute-start.21 = (bf16[16,9216]{1,0:T(8,128)(2,1)S(1)}, bf16[16,9216]{1,0:T(8,128)(2,1)S(1)}, u32[]{:S(2)}, u32[]{:S(2)}) collective-permute-start(bf16[16,9216]{1,0:T(8,128)(2,1)S(1)} %get-tuple-element.11), channel_id=1, source_target_pairs={{0,24},{4,28},{8,16},{12,20},{16,8},{20,12},{24,0},{28,4},{1,25},{... | collective-permute-start | bytes 884744 | tf_op jit(solution)/shard_map/ppermute | solution.py:150
  123.9 11.1 %copy-start.1 = (s32[32]{0:T(128)S(1)}, s32[32]{0:T(128)}, u32[]{:S(2)}) copy-start(s32[32]{0:T(128)} %param.15) | copy-start | bytes 388
  124.5 10.5 %copy-start.3 = (bf16[384,8192]{1,0:T(8,128)(2,1)}, bf16[384,8192]{1,0:T(8,128)(2,1)S(1)}, u32[]{:S(2)}) copy-start(bf16[384,8192]{1,0:T(8,128)(2,1)S(1)} %fusion.31) | copy-start | bytes 18874372

commit v16 on v13

--- a/solution.py
+++ b/solution.py
@@ -43,10 +43,11 @@
     rows = shard.shape[0] // WEIGHT_CHUNKS
     result = []
     previous = None
+    sibling_shard = lax.ppermute(shard, "fsdp", xor_pairs(members, 1))
     for k in range(WEIGHT_CHUNKS):
         piece = shard[k * rows:(k + 1) * rows]
         result.append((0.0, sources[0], k, piece))
-        result.append((1.0, sibling_sources[0], k, lax.ppermute(piece, "fsdp", xor_pairs(members, 1))))
+        result.append((1.0, sibling_sources[0], k, sibling_shard[k * rows:(k + 1) * rows]))
         if previous is not None:
             piece, _ = lax.optimization_barrier((piece, previous))
         first = lax.ppermute(piece, ("fsdp", "dp"), first_pairs)

time: 124 us -> 118 us (0.952)
  waiting for transfers between devices: 24.9 us -> 17.7 us
  local copies, waits for them, and re-layouts: 11.4 us -> 14.9 us
  matrix products: 42.6 us -> 39.8 us
    ppermute x3, waiting for transfers between devices: 7.71 us -> 0.01 us  [on_device(): by_step[step] = lax.ppermute(own_adapter, 'fsdp', xor_pairs(members, step))]
    ppermute x2, waiting for transfers between devices: 8.15 us -> 14.1 us  [relay_gather(): partner = lax.ppermute(first, ('fsdp', 'dp'), partner_pairs)]
    ppermute x2, waiting for transfers between devices: 8.97 us -> 3.58 us  [relay_gather(): relayed = lax.ppermute(first, ('fsdp', 'dp'), relay_pairs)]
    dot_general x16, matrix products: 15.3 us -> 11.5 us  [on_device(): lax.dot_general(masked_cot, weight_piece, (((1,), (1,)), ((), ())), prefe...]
    unnamed x40 -> x50, local copies, waits for them, and re-layouts: 4.9 us -> 8.44 us
    dot_general x16, matrix products: 10.3 us -> 13.8 us  [on_device(): jnp.einsum('uio,uof->uif', low_rank_gradient, down_piece, preferred_eleme...]
    dot_general x16, matrix products: 13.3 us -> 10.8 us  [on_device(): jnp.dot(token_piece, weight_piece, preferred_element_type=jnp.float32)]
    ppermute x2, starting transfers between devices: 1.72 us -> 0.01 us  [relay_gather(): lax.ppermute(first, 'fsdp', xor_pairs(members, 1))]
  transfers between devices with their start and end apart: 22 -> 21, of which waited for: 3 -> 2; matrix products, arithmetic and copies ran while one was open for 43% -> 43% of each run, Pallas kernels for 0% -> 0%
where the time goes in v16:
time: 118 us; the launch traced here: 117 us
  matrix products  39.8 us (34%)
  between operations  18.9 us (16%)
  waiting for transfers between devices  17.7 us (15%)
  starting transfers between devices  17.2 us (15%)
  local copies, waits for them, and re-layouts  14.9 us (13%)
  other arithmetic  8.27 us (7%)
    ppermute x2, waiting for transfers between devices, relay_gather(): partner = lax.ppermute(first, ('fsdp', 'dp'), partner_pairs)  14.1 us
    dot_general x16, matrix products, on_device(): jnp.einsum('uio,uof->uif', low_rank_gradient, down_piece, preferred_eleme...  13.8 us
    dot_general x16, matrix products, on_device(): lax.dot_general(masked_cot, weight_piece, (((1,), (1,)), ((), ())), prefe...  11.5 us
    dot_general x16, matrix products, on_device(): jnp.dot(token_piece, weight_piece, preferred_element_type=jnp.float32)  10.8 us
    unnamed x50, local copies, waits for them, and re-layouts  8.44 us
    ppermute x3, starting transfers between devices, on_device(): by_step[step] = lax.ppermute(own_adapter, 'fsdp', xor_pairs(members, step))  4.47 us
    ppermute x2, waiting for transfers between devices, relay_gather(): relayed = lax.ppermute(first, ('fsdp', 'dp'), relay_pairs)  3.58 us
    ppermute x3, starting transfers between devices, on_device(): lax.ppermute(sent, 'fsdp', xor_pairs(members, step)).astype(jnp.float32)  3.55 us
  transfers between devices with their start and end apart: 21, of which 2 were waited for; matrix products, arithmetic and copies ran while one was open for 43% of the time, Pallas kernels for 0%

profile of v16, /device:TPU:0, one launch (start us, length us, event | category | flops | bytes accessed | tf_op | source)
XLA Modules:
  0.0 116.8 jit_solution(149111689023950886)
XLA Ops:
  0.6 1.7 %fusion.139 = (bf16[1,16,9216]{2,1,0:T(8,128)(2,1)S(1)}, bf16[16,9216]{1,0:T(8,128)(2,1)}) fusion(bf16[16,1024]{1,0:T(8,128)(2,1)} %bitcast.130, bf16[16,8192]{1,0:T(8,128)(2,1)} %bitcast.112), kind=kLoop, calls=%fused_computation.212 | loop fusion | flops 589824 | bytes 884736 | tf_op jit(solution)/shard_map/stack | solution.py:98
  2.4 2.9 %collective-permute-start = (bf16[16,9216]{1,0:T(8,128)(2,1)}, bf16[16,9216]{1,0:T(8,128)(2,1)S(1)}, u32[]{:S(2)}, u32[]{:S(2)}) collective-permute-start(bf16[16,9216]{1,0:T(8,128)(2,1)} %get-tuple-element.28), channel_id=1, source_target_pairs={{0,8},{4,12},{8,0},{12,4},{16,24},{20,28},{24,16},{28,20},{1,9},{5... | collective-permute-start | bytes 884744 | tf_op jit(solution)/shard_map/ppermute | solution.py:93
  5.3 1.5 %collective-permute-start.1 = (bf16[16,9216]{1,0:T(8,128)(2,1)}, bf16[16,9216]{1,0:T(8,128)(2,1)S(1)}, u32[]{:S(2)}, u32[]{:S(2)}) collective-permute-start(bf16[16,9216]{1,0:T(8,128)(2,1)} %get-tuple-element.28), channel_id=1, source_target_pairs={{0,16},{4,20},{8,24},{12,28},{16,0},{20,4},{24,8},{28,12},{1,17},{... | collective-permute-start | bytes 884744 | tf_op jit(solution)/shard_map/ppermute | solution.py:93
  6.9 3.0 %fusion.146 = (bf16[512,1024]{1,0:T(8,128)(2,1)}, bf16[512,1024]{1,0:T(8,128)(2,1)}) fusion(bf16[1024,1024]{1,0:T(8,128)(2,1)} %param.10), kind=kLoop, calls=%fused_computation.217 | loop fusion | bytes 4194304 | tf_op jit(solution)/shard_map/slice | solution.py:48
  9.9 2.0 %collective-permute-start.5 = (bf16[512,1024]{1,0:T(8,128)(2,1)}, bf16[512,1024]{1,0:T(8,128)(2,1)}, u32[]{:S(2)}, u32[]{:S(2)}) collective-permute-start(bf16[512,1024]{1,0:T(8,128)(2,1)} %get-tuple-element.23), channel_id=1, source_target_pairs={{0,8},{1,17},{2,10},{3,19},{4,20},{5,13},{6,22},{7,15},{8,0},{9,25... | collective-permute-start | bytes 3145736 | tf_op jit(solution)/shard_map/ppermute | solution.py:53
  11.9 0.6 gather_fusion
  12.5 0.7 and_select_fusion
  13.3 0.6 fusion.147
  32.6 1.0 collective-permute-start.7
  33.6 1.1 collective-permute-start.8
  34.7 1.9 %fusion.62 = f32[384,1024]{1,0:T(8,128)S(1)} fusion(bf16[512,1024]{1,0:T(8,128)(2,1)} %collective-permute-done.5, bf16[384,8192]{1,0:T(8,128)(2,1)} %param.8, s32[]{:T(128)S(6)} %select_n.296), kind=kOutput, calls=%fused_computation.112 | convolution fusion | flops 402653184 | bytes 3014660 | tf_op jit(solution)/shard_map/dot_general | solution.py:168
  36.6 1.6 %collective-permute-start.9 = (bf16[512,1024]{1,0:T(8,128)(2,1)}, bf16[512,1024]{1,0:T(8,128)(2,1)S(1)}, u32[]{:S(2)}, u32[]{:S(2)}) collective-permute-start(bf16[512,1024]{1,0:T(8,128)(2,1)} %collective-permute-done.5), channel_id=1, source_target_pairs={{0,1},{1,0},{2,3},{3,2},{4,5},{5,4},{6,7},{7,6},{8,9},{9,8},{10,11... | collective-permute-start | bytes 3145736 | tf_op jit(solution)/shard_map/ppermute | solution.py:58
  38.7 1.2 %slice-done.1 = s8[2097152]{0:T(1024)(128)(4,1)S(1)} async-done(((s8[6291456]{0:T(1024)(128)(4,1)}), s8[2097152]{0:T(1024)(128)(4,1)S(1)}, s32[]{:S(2)}) %slice-start.1) | async-done | bytes 2097176
  39.9 1.7 %fusion.32 = bf16[3,16,128]{2,1,0:T(8,128)(2,1)S(1)} fusion(bf16[3,128,8192]{2,1,0:T(8,128)(2,1)S(1)} %bitcast.105, f32[3,128]{1,0:T(4,128)S(1)} %get-tuple-element.30, bf16[3,16,9216]{2,1,0:T(8,128)(2,1)S(1)} %pad_maximum_fusion.2), kind=kOutput, calls=%fused_computation.68 | convolution fusion | flops 100675584 | bytes 7092224 | tf_op jit(solution)/shard_map/cvj,coj->cvo/dot_general | solution.py:113
  42.6 0.9 fusion.148
  43.6 1.2 %fusion.93 = f32[3,128,512]{2,1,0:T(8,128)} fusion(bf16[3,16,128]{2,1,0:T(8,128)(2,1)S(1)} %fusion.33, bf16[3,16,8192]{2,1,0:T(8,128)(2,1)S(1)} %slice.139, s32[]{:T(128)S(6)} %select_n.296), kind=kOutput, calls=%fused_computation.150 | convolution fusion | flops 6291456 | bytes 847876 | tf_op jit(solution)/shard_map/uio,uof->uif/dot_general | solution.py:174
  45.4 1.2 %fusion.97 = f32[3,128,512]{2,1,0:T(8,128)} fusion(bf16[3,16,128]{2,1,0:T(8,128)(2,1)S(1)} %fusion.33, bf16[3,16,8192]{2,1,0:T(8,128)(2,1)S(1)} %slice.139, s32[]{:T(128)S(6)} %select_n.292), kind=kOutput, calls=%fused_computation.154 | convolution fusion | flops 6291456 | bytes 847876 | tf_op jit(solution)/shard_map/uio,uof->uif/dot_general | solution.py:174
  46.6 1.2 %fusion.95 = f32[3,128,512]{2,1,0:T(8,128)} fusion(bf16[3,16,128]{2,1,0:T(8,128)(2,1)S(1)} %fusion.33, bf16[3,16,8192]{2,1,0:T(8,128)(2,1)S(1)} %slice.139, s32[]{:T(128)S(6)} %select_n.293), kind=kOutput, calls=%fused_computation.152 | convolution fusion | flops 6291456 | bytes 847876 | tf_op jit(solution)/shard_map/uio,uof->uif/dot_general | solution.py:174
  47.8 1.2 %fusion.91 = f32[3,128,512]{2,1,0:T(8,128)} fusion(bf16[3,16,128]{2,1,0:T(8,128)(2,1)S(1)} %fusion.33, bf16[3,16,8192]{2,1,0:T(8,128)(2,1)S(1)} %slice.139, s32[]{:T(128)S(6)} %select_n.297), kind=kOutput, calls=%fused_computation.148 | convolution fusion | flops 6291456 | bytes 847876 | tf_op jit(solution)/shard_map/uio,uof->uif/dot_general | solution.py:174
  49.0 1.2 %fusion.89 = f32[3,128,512]{2,1,0:T(8,128)} fusion(bf16[3,16,128]{2,1,0:T(8,128)(2,1)S(1)} %fusion.33, bf16[3,16,8192]{2,1,0:T(8,128)(2,1)S(1)} %slice.139, s32[]{:T(128)S(6)} %select_n.298), kind=kOutput, calls=%fused_computation.146 | convolution fusion | flops 6291456 | bytes 847876 | tf_op jit(solution)/shard_map/uio,uof->uif/dot_general | solution.py:174
  50.2 1.2 %fusion.87 = f32[3,128,512]{2,1,0:T(8,128)} fusion(bf16[3,16,128]{2,1,0:T(8,128)(2,1)S(1)} %fusion.33, bf16[3,16,8192]{2,1,0:T(8,128)(2,1)S(1)} %slice.139, s32[]{:T(128)S(6)} %select_n.299), kind=kOutput, calls=%fused_computation.144 | convolution fusion | flops 6291456 | bytes 847876 | tf_op jit(solution)/shard_map/uio,uof->uif/dot_general | solution.py:174
  51.4 1.2 %fusion.85 = f32[3,128,512]{2,1,0:T(8,128)} fusion(bf16[3,16,128]{2,1,0:T(8,128)(2,1)S(1)} %fusion.33, bf16[3,16,8192]{2,1,0:T(8,128)(2,1)S(1)} %slice.139, s32[]{:T(128)S(6)} %select_n.300), kind=kOutput, calls=%fused_computation.142 | convolution fusion | flops 6291456 | bytes 847876 | tf_op jit(solution)/shard_map/uio,uof->uif/dot_general | solution.py:174
  52.6 1.2 %fusion.83 = f32[3,128,512]{2,1,0:T(8,128)} fusion(bf16[3,16,128]{2,1,0:T(8,128)(2,1)S(1)} %fusion.33, bf16[3,16,8192]{2,1,0:T(8,128)(2,1)S(1)} %slice.139, s32[]{:T(128)S(6)} %select_n.301), kind=kOutput, calls=%fused_computation.140 | convolution fusion | flops 6291456 | bytes 847876 | tf_op jit(solution)/shard_map/uio,uof->uif/dot_general | solution.py:174
  53.8 1.2 %fusion.81 = f32[3,128,512]{2,1,0:T(8,128)} fusion(bf16[3,16,128]{2,1,0:T(8,128)(2,1)S(1)} %fusion.33, bf16[3,16,8192]{2,1,0:T(8,128)(2,1)S(1)} %slice.139, s32[]{:T(128)S(6)} %select_n.302), kind=kOutput, calls=%fused_computation.138 | convolution fusion | flops 6291456 | bytes 847876 | tf_op jit(solution)/shard_map/uio,uof->uif/dot_general | solution.py:174
  55.0 1.2 %fusion.79 = f32[3,128,512]{2,1,0:T(8,128)} fusion(bf16[3,16,128]{2,1,0:T(8,128)(2,1)S(1)} %fusion.33, bf16[3,16,8192]{2,1,0:T(8,128)(2,1)S(1)} %slice.139, s32[]{:T(128)S(6)} %select_n.303), kind=kOutput, calls=%fused_computation.136 | convolution fusion | flops 6291456 | bytes 847876 | tf_op jit(solution)/shard_map/uio,uof->uif/dot_general | solution.py:174
  57.1 0.7 broadcast_in_dim.44
  57.9 0.6 fusion.1
  58.5 0.6 fusion.3
  62.0 0.8 fusion.35
  66.6 1.6 %collective-permute-start.13 = (bf16[512,1024]{1,0:T(8,128)(2,1)S(1)}, bf16[512,1024]{1,0:T(8,128)(2,1)S(1)}, u32[]{:S(2)}, u32[]{:S(2)}) collective-permute-start(bf16[512,1024]{1,0:T(8,128)(2,1)S(1)} %collective-permute-done.7), channel_id=1, source_target_pairs={{0,16},{1,9},{2,18},{3,11},{4,12},{5,21},{6,14},{7,23},{8,24},{9,1... | collective-permute-start | bytes 3145736 | tf_op jit(solution)/shard_map/ppermute | solution.py:57
  71.0 1.9 %fusion.9 = bf16[384,8192]{1,0:T(8,128)(2,1)S(1)} fusion(bf16[384,8192]{1,0:T(8,128)(2,1)S(1)} %fusion.7, s32[]{:T(128)S(6)} %select_n.296, f32[384,512]{1,0:T(8,128)S(1)} %bitcast.124, bf16[512,1024]{1,0:T(8,128)(2,1)} %collective-permute-done.5, bf16[384,1024]{1,0:T(8,128)(2,1)S(1)} %copy-done.4, f32[384]{0:T(512)S(1)} %get-tuple-element.29), kind=kOutput, calls=%fused_computation.40 | convolution fusion | flops 404226048 | bytes 3016708 | tf_op jit(solution)/shard_map/dot_general | solution.py:172
  72.9 0.6 fusion.11
  74.0 0.6 fusion.13
  75.2 0.6 fusion.15
  76.3 0.6 fusion.17
  77.9 3.6 %collective-permute-done.13 = bf16[512,1024]{1,0:T(8,128)(2,1)S(1)} collective-permute-done((bf16[512,1024]{1,0:T(8,128)(2,1)S(1)}, bf16[512,1024]{1,0:T(8,128)(2,1)S(1)}, u32[]{:S(2)}, u32[]{:S(2)}) %collective-permute-start.13) | collective-permute-done | bytes 1048608 | tf_op jit(solution)/shard_map/ppermute | solution.py:57
  81.5 1.4 %collective-permute-start.18 = (bf16[16,9216]{1,0:T(8,128)(2,1)S(1)}, bf16[16,9216]{1,0:T(8,128)(2,1)S(1)}, u32[]{:S(2)}, u32[]{:S(2)}) collective-permute-start(bf16[16,9216]{1,0:T(8,128)(2,1)S(1)} %get-tuple-element.9), channel_id=1, source_target_pairs={{0,8},{4,12},{8,0},{12,4},{16,24},{20,28},{24,16},{28,20},{1,9},{5... | collective-permute-start | bytes 884744 | tf_op jit(solution)/shard_map/ppermute | solution.py:151
  84.4 1.5 %collective-permute-start.20 = (bf16[16,9216]{1,0:T(8,128)(2,1)S(1)}, bf16[16,9216]{1,0:T(8,128)(2,1)S(1)}, u32[]{:S(2)}, u32[]{:S(2)}) collective-permute-start(bf16[16,9216]{1,0:T(8,128)(2,1)S(1)} %get-tuple-element.11), channel_id=1, source_target_pairs={{0,24},{4,28},{8,16},{12,20},{16,8},{20,12},{24,0},{28,4},{1,25},{... | collective-permute-start | bytes 884744 | tf_op jit(solution)/shard_map/ppermute | solution.py:151
  88.5 14.1 %collective-permute-done.14 = bf16[512,1024]{1,0:T(8,128)(2,1)S(1)} collective-permute-done((bf16[512,1024]{1,0:T(8,128)(2,1)S(1)}, bf16[512,1024]{1,0:T(8,128)(2,1)S(1)}, u32[]{:S(2)}, u32[]{:S(2)}) %collective-permute-start.14) | collective-permute-done | bytes 1048608 | tf_op jit(solution)/shard_map/ppermute | solution.py:58
  106.6 0.8 fusion.23
  107.4 0.6 fusion.25
  108.0 0.6 fusion.27
  109.0 0.7 slice_bitcast_fusion
  109.7 0.6 slice_bitcast_fusion.1
  111.8 1.0 multiply_convert_fusion.1
  112.8 0.6 fusion.29
  113.5 0.6 fusion.31
  114.1 2.7 %copy-done.3 = bf16[384,8192]{1,0:T(8,128)(2,1)} copy-done((bf16[384,8192]{1,0:T(8,128)(2,1)}, bf16[384,8192]{1,0:T(8,128)(2,1)S(1)}, u32[]{:S(2)}) %copy-start.3) | copy-done | bytes 6291480
  (132 shorter events, 25.6 us)
Async XLA Ops:
  0.6 11.2 %copy-start = (s32[32]{0:T(128)S(1)}, s32[32]{0:T(128)}, u32[]{:S(2)}) copy-start(s32[32]{0:T(128)} %param.15) | copy-start | bytes 388
  2.4 9.5 %copy-start.19 = (s32[3]{0:T(128)S(1)}, s32[3]{0:T(128)}, u32[]{:S(2)}) copy-start(s32[3]{0:T(128)} %param.13) | copy-start | bytes 40
  2.4 10.8 %copy-start.18 = (s32[3]{0:T(128)S(1)}, s32[3]{0:T(128)}, u32[]{:S(2)}) copy-start(s32[3]{0:T(128)} %param.14) | copy-start | bytes 40
  2.4 29.1 %collective-permute-start = (bf16[16,9216]{1,0:T(8,128)(2,1)}, bf16[16,9216]{1,0:T(8,128)(2,1)S(1)}, u32[]{:S(2)}, u32[]{:S(2)}) collective-permute-start(bf16[16,9216]{1,0:T(8,128)(2,1)} %get-tuple-element.28), channel_id=1, source_target_pairs={{0,8},{4,12},{8,0},{12,4},{16,24},{20,28},{24,16},{28,20},{1,9},{5... | collective-permute-start | bytes 884744 | tf_op jit(solution)/shard_map/ppermute | solution.py:93
  5.3 26.2 %collective-permute-start.1 = (bf16[16,9216]{1,0:T(8,128)(2,1)}, bf16[16,9216]{1,0:T(8,128)(2,1)S(1)}, u32[]{:S(2)}, u32[]{:S(2)}) collective-permute-start(bf16[16,9216]{1,0:T(8,128)(2,1)} %get-tuple-element.28), channel_id=1, source_target_pairs={{0,16},{4,20},{8,24},{12,28},{16,0},{20,4},{24,8},{28,12},{1,17},{... | collective-permute-start | bytes 884744 | tf_op jit(solution)/shard_map/ppermute | solution.py:93
  6.8 24.7 %collective-permute-start.2 = (bf16[16,9216]{1,0:T(8,128)(2,1)}, bf16[16,9216]{1,0:T(8,128)(2,1)S(1)}, u32[]{:S(2)}, u32[]{:S(2)}) collective-permute-start(bf16[16,9216]{1,0:T(8,128)(2,1)} %get-tuple-element.28), channel_id=1, source_target_pairs={{0,24},{4,28},{8,16},{12,20},{16,8},{20,12},{24,0},{28,4},{1,25},{... | collective-permute-start | bytes 884744 | tf_op jit(solution)/shard_map/ppermute | solution.py:93
  6.9 54.5 %collective-permute-start.4 = (bf16[1024,1024]{1,0:T(8,128)(2,1)}, bf16[1024,1024]{1,0:T(8,128)(2,1)S(1)}, u32[]{:S(2)}, u32[]{:S(2)}) collective-permute-start(bf16[1024,1024]{1,0:T(8,128)(2,1)} %param.10), channel_id=1, source_target_pairs={{0,4},{4,0},{8,12},{12,8},{16,20},{20,16},{24,28},{28,24},{1,5},{5... | collective-permute-start | bytes 6291464 | tf_op jit(solution)/shard_map/ppermute | solution.py:46
  9.9 22.3 %collective-permute-start.5 = (bf16[512,1024]{1,0:T(8,128)(2,1)}, bf16[512,1024]{1,0:T(8,128)(2,1)}, u32[]{:S(2)}, u32[]{:S(2)}) collective-permute-start(bf16[512,1024]{1,0:T(8,128)(2,1)} %get-tuple-element.23), channel_id=1, source_target_pairs={{0,8},{1,17},{2,10},{3,19},{4,20},{5,13},{6,22},{7,15},{8,0},{9,25... | collective-permute-start | bytes 3145736 | tf_op jit(solution)/shard_map/ppermute | solution.py:53
  11.9 20.1 %copy-start.5 = (bf16[1,16,8192]{2,1,0:T(8,128)(2,1)S(1)}, bf16[1,16,8192]{2,1,0:T(8,128)(2,1)}, u32[]{:S(2)}) copy-start(bf16[1,16,8192]{2,1,0:T(8,128)(2,1)} %param.11) | copy-start | bytes 786436
  31.4 0.8 copy-start.17
  31.4 1.2 %copy-start.6 = (bf16[512,1024]{1,0:T(8,128)(2,1)S(1)}, bf16[512,1024]{1,0:T(8,128)(2,1)}, u32[]{:S(2)}) copy-start(bf16[512,1024]{1,0:T(8,128)(2,1)} %get-tuple-element.8) | copy-start | bytes 3145732
  31.5 7.2 %slice-start = ((s8[6291456]{0:T(1024)(128)(4,1)}), s8[4194304]{0:T(1024)(128)(4,1)S(1)}, s32[]{:S(2)}) async-start(s8[6291456]{0:T(1024)(128)(4,1)} %bitcast.103), calls=%async_computation | async-start | bytes 8388608
  31.7 5.0 %collective-permute-start.3 = (bf16[4,16,9216]{2,1,0:T(8,128)(2,1)S(1)}, bf16[4,16,9216]{2,1,0:T(8,128)(2,1)S(1)}, u32[]{:S(2)}, u32[]{:S(2)}) collective-permute-start(bf16[4,16,9216]{2,1,0:T(8,128)(2,1)S(1)} %pad_maximum_fusion), channel_id=1, source_target_pairs={{0,4},{4,0},{8,12},{12,8},{16,20},{20,16},{24,28},{28,24},{1,5},{5... | collective-permute-start | bytes 3538952 | tf_op jit(solution)/shard_map/ppermute | solution.py:95
  32.6 31.4 %collective-permute-start.7 = (bf16[512,1024]{1,0:T(8,128)(2,1)S(1)}, bf16[512,1024]{1,0:T(8,128)(2,1)S(1)}, u32[]{:S(2)}, u32[]{:S(2)}) collective-permute-start(bf16[512,1024]{1,0:T(8,128)(2,1)S(1)} %copy-done.6), channel_id=1, source_target_pairs={{0,8},{1,17},{2,10},{3,19},{4,20},{5,13},{6,22},{7,15},{8,0},{9,25... | collective-permute-start | bytes 3145736 | tf_op jit(solution)/shard_map/ppermute | solution.py:53
  33.6 29.9 %collective-permute-start.6 = (bf16[512,1024]{1,0:T(8,128)(2,1)}, bf16[512,1024]{1,0:T(8,128)(2,1)S(1)}, u32[]{:S(2)}, u32[]{:S(2)}) collective-permute-start(bf16[512,1024]{1,0:T(8,128)(2,1)} %collective-permute-done.5), channel_id=1, source_target_pairs={{0,4},{4,0},{8,12},{12,8},{16,20},{20,16},{24,28},{28,24},{1,5},{5... | collective-permute-start | bytes 3145736 | tf_op jit(solution)/shard_map/ppermute | solution.py:56
  33.6 31.4 %collective-permute-start.8 = (bf16[512,1024]{1,0:T(8,128)(2,1)}, bf16[512,1024]{1,0:T(8,128)(2,1)S(1)}, u32[]{:S(2)}, u32[]{:S(2)}) collective-permute-start(bf16[512,1024]{1,0:T(8,128)(2,1)} %collective-permute-done.5), channel_id=1, source_target_pairs={{0,16},{1,9},{2,18},{3,11},{4,12},{5,21},{6,14},{7,23},{8,24},{9,1... | collective-permute-start | bytes 3145736 | tf_op jit(solution)/shard_map/ppermute | solution.py:57
  36.6 29.0 %collective-permute-start.9 = (bf16[512,1024]{1,0:T(8,128)(2,1)}, bf16[512,1024]{1,0:T(8,128)(2,1)S(1)}, u32[]{:S(2)}, u32[]{:S(2)}) collective-permute-start(bf16[512,1024]{1,0:T(8,128)(2,1)} %collective-permute-done.5), channel_id=1, source_target_pairs={{0,1},{1,0},{2,3},{3,2},{4,5},{5,4},{6,7},{7,6},{8,9},{9,8},{10,11... | collective-permute-start | bytes 3145736 | tf_op jit(solution)/shard_map/ppermute | solution.py:58
  38.3 1.6 %slice-start.1 = ((s8[6291456]{0:T(1024)(128)(4,1)}), s8[2097152]{0:T(1024)(128)(4,1)S(1)}, s32[]{:S(2)}) async-start(s8[6291456]{0:T(1024)(128)(4,1)} %bitcast.103), calls=%async_computation.1 | async-start | bytes 4194304
  39.9 1.7 %copy-start.4 = (bf16[384,1024]{1,0:T(8,128)(2,1)S(1)}, bf16[384,1024]{1,0:T(8,128)(2,1)}, u32[]{:S(2)}) copy-start(bf16[384,1024]{1,0:T(8,128)(2,1)} %param.9) | copy-start | bytes 2359300
  52.6 3.9 %copy-start.2 = (bf16[1024,1024]{1,0:T(8,128)(2,1)S(1)}, bf16[1024,1024]{1,0:T(8,128)(2,1)}, u32[]{:S(2)}) copy-start(bf16[1024,1024]{1,0:T(8,128)(2,1)} %param.10) | copy-start | bytes 6291460
  61.4 15.6 %collective-permute-start.17 = (bf16[4,16,9216]{2,1,0:T(8,128)(2,1)S(1)}, bf16[4,16,9216]{2,1,0:T(8,128)(2,1)S(1)}, u32[]{:S(2)}, u32[]{:S(2)}) collective-permute-start(bf16[4,16,9216]{2,1,0:T(8,128)(2,1)S(1)} %pad_maximum_fusion.1), channel_id=1, source_target_pairs={{0,4},{4,0},{8,12},{12,8},{16,20},{20,16},{24,28},{28,24},{1,5},{5... | collective-permute-start | bytes 3538952 | tf_op jit(solution)/shard_map/ppermute | solution.py:138
  66.2 2.5 %copy-start.16 = (f32[3,128,512]{2,1,0:T(8,128)S(1)}, f32[3,128,512]{2,1,0:T(8,128)}, u32[]{:S(2)}) copy-start(f32[3,128,512]{2,1,0:T(8,128)} %fusion.97) | copy-start | bytes 2359300
  66.6 14.9 %collective-permute-start.13 = (bf16[512,1024]{1,0:T(8,128)(2,1)S(1)}, bf16[512,1024]{1,0:T(8,128)(2,1)S(1)}, u32[]{:S(2)}, u32[]{:S(2)}) collective-permute-start(bf16[512,1024]{1,0:T(8,128)(2,1)S(1)} %collective-permute-done.7), channel_id=1, source_target_pairs={{0,16},{1,9},{2,18},{3,11},{4,12},{5,21},{6,14},{7,23},{8,24},{9,1... | collective-permute-start | bytes 3145736 | tf_op jit(solution)/shard_map/ppermute | solution.py:57
  68.2 14.7 %collective-permute-start.10 = (bf16[512,1024]{1,0:T(8,128)(2,1)S(1)}, bf16[512,1024]{1,0:T(8,128)(2,1)S(1)}, u32[]{:S(2)}, u32[]{:S(2)}) collective-permute-start(bf16[512,1024]{1,0:T(8,128)(2,1)S(1)} %collective-permute-done.7), channel_id=1, source_target_pairs={{0,4},{4,0},{8,12},{12,8},{16,20},{20,16},{24,28},{28,24},{1,5},{5... | collective-permute-start | bytes 3145736 | tf_op jit(solution)/shard_map/ppermute | solution.py:56
  68.2 16.3 %collective-permute-start.11 = (bf16[512,1024]{1,0:T(8,128)(2,1)S(1)}, bf16[512,1024]{1,0:T(8,128)(2,1)S(1)}, u32[]{:S(2)}, u32[]{:S(2)}) collective-permute-start(bf16[512,1024]{1,0:T(8,128)(2,1)S(1)} %collective-permute-done.8), channel_id=1, source_target_pairs={{0,4},{4,0},{8,12},{12,8},{16,20},{20,16},{24,28},{28,24},{1,5},{5... | collective-permute-start | bytes 3145736 | tf_op jit(solution)/shard_map/ppermute | solution.py:62
  68.7 17.9 %collective-permute-start.12 = (bf16[512,1024]{1,0:T(8,128)(2,1)S(1)}, bf16[512,1024]{1,0:T(8,128)(2,1)S(1)}, u32[]{:S(2)}, u32[]{:S(2)}) collective-permute-start(bf16[512,1024]{1,0:T(8,128)(2,1)S(1)} %collective-permute-done.9), channel_id=1, source_target_pairs={{0,4},{4,0},{8,12},{12,8},{16,20},{20,16},{24,28},{28,24},{1,5},{5... | collective-permute-start | bytes 3145736 | tf_op jit(solution)/shard_map/ppermute | solution.py:64
  68.7 1.1 copy-start.15
  69.8 1.1 copy-start.13
  71.0 1.9 %copy-start.14 = (f32[3,128,512]{2,1,0:T(8,128)S(1)}, f32[3,128,512]{2,1,0:T(8,128)}, u32[]{:S(2)}) copy-start(f32[3,128,512]{2,1,0:T(8,128)} %fusion.91) | copy-start | bytes 2359300
  72.9 1.1 copy-start.12
  74.0 1.1 copy-start.11
  75.2 1.1 copy-start.10
  76.9 25.6 %collective-permute-start.14 = (bf16[512,1024]{1,0:T(8,128)(2,1)S(1)}, bf16[512,1024]{1,0:T(8,128)(2,1)S(1)}, u32[]{:S(2)}, u32[]{:S(2)}) collective-permute-start(bf16[512,1024]{1,0:T(8,128)(2,1)S(1)} %collective-permute-done.7), channel_id=1, source_target_pairs={{0,1},{1,0},{2,3},{3,2},{4,5},{5,4},{6,7},{7,6},{8,9},{9,8},{10,11... | collective-permute-start | bytes 3145736 | tf_op jit(solution)/shard_map/ppermute | solution.py:58
  81.5 27.2 %collective-permute-start.18 = (bf16[16,9216]{1,0:T(8,128)(2,1)S(1)}, bf16[16,9216]{1,0:T(8,128)(2,1)S(1)}, u32[]{:S(2)}, u32[]{:S(2)}) collective-permute-start(bf16[16,9216]{1,0:T(8,128)(2,1)S(1)} %get-tuple-element.9), channel_id=1, source_target_pairs={{0,8},{4,12},{8,0},{12,4},{16,24},{20,28},{24,16},{28,20},{1,9},{5... | collective-permute-start | bytes 884744 | tf_op jit(solution)/shard_map/ppermute | solution.py:151
  82.9 25.8 %collective-permute-start.19 = (bf16[16,9216]{1,0:T(8,128)(2,1)S(1)}, bf16[16,9216]{1,0:T(8,128)(2,1)S(1)}, u32[]{:S(2)}, u32[]{:S(2)}) collective-permute-start(bf16[16,9216]{1,0:T(8,128)(2,1)S(1)} %get-tuple-element.10), channel_id=1, source_target_pairs={{0,16},{4,20},{8,24},{12,28},{16,0},{20,4},{24,8},{28,12},{1,17},{... | collective-permute-start | bytes 884744 | tf_op jit(solution)/shard_map/ppermute | solution.py:151
  84.4 24.3 %collective-permute-start.20 = (bf16[16,9216]{1,0:T(8,128)(2,1)S(1)}, bf16[16,9216]{1,0:T(8,128)(2,1)S(1)}, u32[]{:S(2)}, u32[]{:S(2)}) collective-permute-start(bf16[16,9216]{1,0:T(8,128)(2,1)S(1)} %get-tuple-element.11), channel_id=1, source_target_pairs={{0,24},{4,28},{8,16},{12,20},{16,8},{20,12},{24,0},{28,4},{1,25},{... | collective-permute-start | bytes 884744 | tf_op jit(solution)/shard_map/ppermute | solution.py:151
  103.2 1.1 copy-start.9
  103.5 6.8 %collective-permute-start.15 = (bf16[512,1024]{1,0:T(8,128)(2,1)S(1)}, bf16[512,1024]{1,0:T(8,128)(2,1)S(1)}, u32[]{:S(2)}, u32[]{:S(2)}) collective-permute-start(bf16[512,1024]{1,0:T(8,128)(2,1)S(1)} %collective-permute-done.13), channel_id=1, source_target_pairs={{0,4},{4,0},{8,12},{12,8},{16,20},{20,16},{24,28},{28,24},{1,5},{5... | collective-permute-start | bytes 3145736 | tf_op jit(solution)/shard_map/ppermute | solution.py:62
  103.6 7.3 %collective-permute-start.16 = (bf16[512,1024]{1,0:T(8,128)(2,1)S(1)}, bf16[512,1024]{1,0:T(8,128)(2,1)S(1)}, u32[]{:S(2)}, u32[]{:S(2)}) collective-permute-start(bf16[512,1024]{1,0:T(8,128)(2,1)S(1)} %collective-permute-done.14), channel_id=1, source_target_pairs={{0,4},{4,0},{8,12},{12,8},{16,20},{20,16},{24,28},{28,24},{1,5},{5... | collective-permute-start | bytes 3145736 | tf_op jit(solution)/shard_map/ppermute | solution.py:64
  104.3 1.1 copy-start.8
  105.4 1.1 copy-start.7
  113.5 3.4 %copy-start.1 = (s32[32]{0:T(128)S(1)}, s32[32]{0:T(128)}, u32[]{:S(2)}) copy-start(s32[32]{0:T(128)} %param.15) | copy-start | bytes 388
  114.1 2.7 %copy-start.3 = (bf16[384,8192]{1,0:T(8,128)(2,1)}, bf16[384,8192]{1,0:T(8,128)(2,1)S(1)}, u32[]{:S(2)}) copy-start(bf16[384,8192]{1,0:T(8,128)(2,1)S(1)} %fusion.31) | copy-start | bytes 18874372

commit v17 on v16

--- a/solution.py
+++ b/solution.py
@@ -58,10 +58,14 @@
         partner = lax.ppermute(first, ("fsdp", "dp"), partner_pairs)
         result.append((4.5 + 2 * k, sources[2], k, relayed))
         result.append((4.5 + 2 * k, sources[3], k, partner))
-        result.append((5.5 + 2 * k, sibling_sources[2], k,
-                       lax.ppermute(relayed, "fsdp", xor_pairs(members, 1))))
-        result.append((5.5 + 2 * k, sibling_sources[3], k,
-                       lax.ppermute(partner, "fsdp", xor_pairs(members, 1))))
+        if k + 1 < WEIGHT_CHUNKS:
+            late = lax.ppermute(jnp.stack([relayed, partner]), "fsdp", xor_pairs(members, 1))
+            late_pieces = (late[0], late[1])
+        else:
+            late_pieces = (lax.ppermute(relayed, "fsdp", xor_pairs(members, 1)),
+                           lax.ppermute(partner, "fsdp", xor_pairs(members, 1)))
+        result.append((5.5 + 2 * k, sibling_sources[2], k, late_pieces[0]))
+        result.append((5.5 + 2 * k, sibling_sources[3], k, late_pieces[1]))
     result.sort(key=lambda item: item[0])
     return [item[1:] for item in result]
 

time: 118 us -> 115 us (0.975)
  matrix products: 39.8 us -> 43.9 us
  waiting for transfers between devices: 17.7 us -> 13.6 us
  local copies, waits for them, and re-layouts: 14.9 us -> 12 us
    ppermute x2, waiting for transfers between devices: 14.1 us -> 8.89 us  [relay_gather(): partner = lax.ppermute(first, ('fsdp', 'dp'), partner_pairs)]
    unnamed x50 -> x46, local copies, waits for them, and re-layouts: 8.44 us -> 5.47 us
    dot_general x16, matrix products: 10.8 us -> 13.5 us  [on_device(): jnp.dot(token_piece, weight_piece, preferred_element_type=jnp.float32)]
    ppermute x3, waiting for transfers between devices: 0.01 us -> 2.47 us  [on_device(): lax.ppermute(sent, 'fsdp', xor_pairs(members, step)).astype(jnp.float32)]
    dot_general x16, matrix products: 11.5 us -> 13.8 us  [on_device(): lax.dot_general(masked_cot, weight_piece, (((1,), (1,)), ((), ())), prefe...]
    ppermute x2, waiting for transfers between devices: 3.58 us -> 2.17 us  [relay_gather(): relayed = lax.ppermute(first, ('fsdp', 'dp'), relay_pairs)]
  transfers between devices with their start and end apart: 21 -> 20, of which waited for: 2 -> 5; matrix products, arithmetic and copies ran while one was open for 43% -> 45% of each run, Pallas kernels for 0% -> 0%
where the time goes in v17:
time: 115 us; the launch traced here: 114 us
  matrix products  43.9 us (38%)
  between operations  18.8 us (16%)
  starting transfers between devices  17.9 us (16%)
  waiting for transfers between devices  13.6 us (12%)
  local copies, waits for them, and re-layouts  12 us (10%)
  other arithmetic  8.15 us (7%)
    dot_general x16, matrix products, on_device(): lax.dot_general(masked_cot, weight_piece, (((1,), (1,)), ((), ())), prefe...  13.8 us
    dot_general x16, matrix products, on_device(): jnp.dot(token_piece, weight_piece, preferred_element_type=jnp.float32)  13.5 us
    dot_general x16, matrix products, on_device(): jnp.einsum('uio,uof->uif', low_rank_gradient, down_piece, preferred_eleme...  13 us
    ppermute x2, waiting for transfers between devices, relay_gather(): partner = lax.ppermute(first, ('fsdp', 'dp'), partner_pairs)  8.89 us
    unnamed x46, local copies, waits for them, and re-layouts  5.47 us
    ppermute x3, starting transfers between devices, on_device(): by_step[step] = lax.ppermute(own_adapter, 'fsdp', xor_pairs(members, step))  4.47 us
    ppermute x3, starting transfers between devices, on_device(): lax.ppermute(sent, 'fsdp', xor_pairs(members, step)).astype(jnp.float32)  3.49 us
    ppermute x2, starting transfers between devices, relay_gather(): first = lax.ppermute(piece, ('fsdp', 'dp'), first_pairs)  3.35 us
  transfers between devices with their start and end apart: 20, of which 5 were waited for; matrix products, arithmetic and copies ran while one was open for 45% of the time, Pallas kernels for 0%

profile of v17, /device:TPU:0, one launch (start us, length us, event | category | flops | bytes accessed | tf_op | source)
XLA Modules:
  0.0 114.3 jit_solution(674240766540123857)
XLA Ops:
  0.6 1.7 %fusion.139 = (bf16[1,16,9216]{2,1,0:T(8,128)(2,1)S(1)}, bf16[16,9216]{1,0:T(8,128)(2,1)}) fusion(bf16[16,1024]{1,0:T(8,128)(2,1)} %bitcast.138, bf16[16,8192]{1,0:T(8,128)(2,1)} %bitcast.120), kind=kLoop, calls=%fused_computation.215 | loop fusion | flops 589824 | bytes 884736 | tf_op jit(solution)/shard_map/stack | solution.py:102
  2.4 2.9 %collective-permute-start = (bf16[16,9216]{1,0:T(8,128)(2,1)}, bf16[16,9216]{1,0:T(8,128)(2,1)S(1)}, u32[]{:S(2)}, u32[]{:S(2)}) collective-permute-start(bf16[16,9216]{1,0:T(8,128)(2,1)} %get-tuple-element.28), channel_id=1, source_target_pairs={{0,8},{4,12},{8,0},{12,4},{16,24},{20,28},{24,16},{28,20},{1,9},{5... | collective-permute-start | bytes 884744 | tf_op jit(solution)/shard_map/ppermute | solution.py:97
  5.3 1.5 %collective-permute-start.1 = (bf16[16,9216]{1,0:T(8,128)(2,1)}, bf16[16,9216]{1,0:T(8,128)(2,1)S(1)}, u32[]{:S(2)}, u32[]{:S(2)}) collective-permute-start(bf16[16,9216]{1,0:T(8,128)(2,1)} %get-tuple-element.28), channel_id=1, source_target_pairs={{0,16},{4,20},{8,24},{12,28},{16,0},{20,4},{24,8},{28,12},{1,17},{... | collective-permute-start | bytes 884744 | tf_op jit(solution)/shard_map/ppermute | solution.py:97
  6.9 3.1 %fusion.146 = (bf16[512,1024]{1,0:T(8,128)(2,1)}, bf16[512,1024]{1,0:T(8,128)(2,1)}) fusion(bf16[1024,1024]{1,0:T(8,128)(2,1)} %param.10), kind=kLoop, calls=%fused_computation.220 | loop fusion | bytes 4194304 | tf_op jit(solution)/shard_map/slice | solution.py:48
  9.9 2.0 %collective-permute-start.5 = (bf16[512,1024]{1,0:T(8,128)(2,1)}, bf16[512,1024]{1,0:T(8,128)(2,1)}, u32[]{:S(2)}, u32[]{:S(2)}) collective-permute-start(bf16[512,1024]{1,0:T(8,128)(2,1)} %get-tuple-element.23), channel_id=1, source_target_pairs={{0,8},{1,17},{2,10},{3,19},{4,20},{5,13},{6,22},{7,15},{8,0},{9,25... | collective-permute-start | bytes 3145736 | tf_op jit(solution)/shard_map/ppermute | solution.py:53
  11.9 0.6 gather_fusion
  12.5 0.7 and_select_fusion
  13.3 0.6 fusion.147
  32.1 1.4 %collective-permute-start.7 = (bf16[512,1024]{1,0:T(8,128)(2,1)}, bf16[512,1024]{1,0:T(8,128)(2,1)}, u32[]{:S(2)}, u32[]{:S(2)}) collective-permute-start(bf16[512,1024]{1,0:T(8,128)(2,1)} %get-tuple-element.8), channel_id=1, source_target_pairs={{0,8},{1,17},{2,10},{3,19},{4,20},{5,13},{6,22},{7,15},{8,0},{9,25... | collective-permute-start | bytes 3145736 | tf_op jit(solution)/shard_map/ppermute | solution.py:53
  33.5 0.7 collective-permute-start.8
  34.2 1.9 %fusion.62 = f32[384,1024]{1,0:T(8,128)S(1)} fusion(bf16[512,1024]{1,0:T(8,128)(2,1)} %collective-permute-done.5, bf16[384,8192]{1,0:T(8,128)(2,1)} %param.8, s32[]{:T(128)S(6)} %select_n.296), kind=kOutput, calls=%fused_computation.115 | convolution fusion | flops 402653184 | bytes 3014660 | tf_op jit(solution)/shard_map/dot_general | solution.py:172
  36.2 1.6 %collective-permute-start.9 = (bf16[512,1024]{1,0:T(8,128)(2,1)}, bf16[512,1024]{1,0:T(8,128)(2,1)S(1)}, u32[]{:S(2)}, u32[]{:S(2)}) collective-permute-start(bf16[512,1024]{1,0:T(8,128)(2,1)} %collective-permute-done.5), channel_id=1, source_target_pairs={{0,1},{1,0},{2,3},{3,2},{4,5},{5,4},{6,7},{7,6},{8,9},{9,8},{10,11... | collective-permute-start | bytes 3145736 | tf_op jit(solution)/shard_map/ppermute | solution.py:58
  38.3 1.2 %slice-done.1 = s8[2097152]{0:T(1024)(128)(4,1)S(1)} async-done(((s8[6291456]{0:T(1024)(128)(4,1)}), s8[2097152]{0:T(1024)(128)(4,1)S(1)}, s32[]{:S(2)}) %slice-start.1) | async-done | bytes 2097176
  39.5 1.7 %fusion.32 = bf16[3,16,128]{2,1,0:T(8,128)(2,1)S(1)} fusion(bf16[3,128,8192]{2,1,0:T(8,128)(2,1)S(1)} %bitcast.111, f32[3,128]{1,0:T(4,128)S(1)} %get-tuple-element.30, bf16[3,16,9216]{2,1,0:T(8,128)(2,1)S(1)} %pad_maximum_fusion.3), kind=kOutput, calls=%fused_computation.69 | convolution fusion | flops 100675584 | bytes 7092224 | tf_op jit(solution)/shard_map/cvj,coj->cvo/dot_general | solution.py:117
  42.2 0.9 fusion.148
  43.1 1.3 %fusion.93 = f32[3,128,512]{2,1,0:T(8,128)} fusion(bf16[3,16,128]{2,1,0:T(8,128)(2,1)S(1)} %fusion.33, bf16[3,16,8192]{2,1,0:T(8,128)(2,1)S(1)} %slice.147, s32[]{:T(128)S(6)} %select_n.296), kind=kOutput, calls=%fused_computation.153 | convolution fusion | flops 6291456 | bytes 847876 | tf_op jit(solution)/shard_map/uio,uof->uif/dot_general | solution.py:178
  45.0 1.2 %fusion.97 = f32[3,128,512]{2,1,0:T(8,128)} fusion(bf16[3,16,128]{2,1,0:T(8,128)(2,1)S(1)} %fusion.33, bf16[3,16,8192]{2,1,0:T(8,128)(2,1)S(1)} %slice.147, s32[]{:T(128)S(6)} %select_n.292), kind=kOutput, calls=%fused_computation.157 | convolution fusion | flops 6291456 | bytes 847876 | tf_op jit(solution)/shard_map/uio,uof->uif/dot_general | solution.py:178
  46.2 1.2 %fusion.95 = f32[3,128,512]{2,1,0:T(8,128)} fusion(bf16[3,16,128]{2,1,0:T(8,128)(2,1)S(1)} %fusion.33, bf16[3,16,8192]{2,1,0:T(8,128)(2,1)S(1)} %slice.147, s32[]{:T(128)S(6)} %select_n.293), kind=kOutput, calls=%fused_computation.155 | convolution fusion | flops 6291456 | bytes 847876 | tf_op jit(solution)/shard_map/uio,uof->uif/dot_general | solution.py:178
  47.4 1.3 %fusion.91 = f32[3,128,512]{2,1,0:T(8,128)} fusion(bf16[3,16,128]{2,1,0:T(8,128)(2,1)S(1)} %fusion.33, bf16[3,16,8192]{2,1,0:T(8,128)(2,1)S(1)} %slice.147, s32[]{:T(128)S(6)} %select_n.297), kind=kOutput, calls=%fused_computation.151 | convolution fusion | flops 6291456 | bytes 847876 | tf_op jit(solution)/shard_map/uio,uof->uif/dot_general | solution.py:178
  48.6 1.2 %fusion.89 = f32[3,128,512]{2,1,0:T(8,128)} fusion(bf16[3,16,128]{2,1,0:T(8,128)(2,1)S(1)} %fusion.33, bf16[3,16,8192]{2,1,0:T(8,128)(2,1)S(1)} %slice.147, s32[]{:T(128)S(6)} %select_n.298), kind=kOutput, calls=%fused_computation.149 | convolution fusion | flops 6291456 | bytes 847876 | tf_op jit(solution)/shard_map/uio,uof->uif/dot_general | solution.py:178
  49.8 1.2 %fusion.87 = f32[3,128,512]{2,1,0:T(8,128)} fusion(bf16[3,16,128]{2,1,0:T(8,128)(2,1)S(1)} %fusion.33, bf16[3,16,8192]{2,1,0:T(8,128)(2,1)S(1)} %slice.147, s32[]{:T(128)S(6)} %select_n.299), kind=kOutput, calls=%fused_computation.147 | convolution fusion | flops 6291456 | bytes 847876 | tf_op jit(solution)/shard_map/uio,uof->uif/dot_general | solution.py:178
  51.1 1.2 %fusion.85 = f32[3,128,512]{2,1,0:T(8,128)} fusion(bf16[3,16,128]{2,1,0:T(8,128)(2,1)S(1)} %fusion.33, bf16[3,16,8192]{2,1,0:T(8,128)(2,1)S(1)} %slice.147, s32[]{:T(128)S(6)} %select_n.300), kind=kOutput, calls=%fused_computation.145 | convolution fusion | flops 6291456 | bytes 847876 | tf_op jit(solution)/shard_map/uio,uof->uif/dot_general | solution.py:178
  52.3 1.2 %fusion.83 = f32[3,128,512]{2,1,0:T(8,128)} fusion(bf16[3,16,128]{2,1,0:T(8,128)(2,1)S(1)} %fusion.33, bf16[3,16,8192]{2,1,0:T(8,128)(2,1)S(1)} %slice.147, s32[]{:T(128)S(6)} %select_n.301), kind=kOutput, calls=%fused_computation.143 | convolution fusion | flops 6291456 | bytes 847876 | tf_op jit(solution)/shard_map/uio,uof->uif/dot_general | solution.py:178
  53.4 1.2 %fusion.81 = f32[3,128,512]{2,1,0:T(8,128)} fusion(bf16[3,16,128]{2,1,0:T(8,128)(2,1)S(1)} %fusion.33, bf16[3,16,8192]{2,1,0:T(8,128)(2,1)S(1)} %slice.147, s32[]{:T(128)S(6)} %select_n.302), kind=kOutput, calls=%fused_computation.141 | convolution fusion | flops 6291456 | bytes 847876 | tf_op jit(solution)/shard_map/uio,uof->uif/dot_general | solution.py:178
  55.8 0.7 broadcast_in_dim.44
  60.2 1.5 %collective-permute-done.9 = bf16[512,1024]{1,0:T(8,128)(2,1)S(1)} collective-permute-done((bf16[512,1024]{1,0:T(8,128)(2,1)}, bf16[512,1024]{1,0:T(8,128)(2,1)S(1)}, u32[]{:S(2)}, u32[]{:S(2)}) %collective-permute-start.9) | collective-permute-done | bytes 1048608 | tf_op jit(solution)/shard_map/ppermute | solution.py:58
  62.6 0.8 fusion.37
  64.0 1.8 %convolution_add_fusion.3 = f32[384,1024]{1,0:T(8,128)S(1)} fusion(f32[384,1024]{1,0:T(8,128)S(1)} %add.347, bf16[512,1024]{1,0:T(8,128)(2,1)} %collective-permute-done.6, bf16[384,8192]{1,0:T(8,128)(2,1)S(1)} %bitcast.110, s32[]{:T(128)S(6)} %select_n.297), kind=kOutput, calls=%fused_computation.12 | convolution fusion | flops 403046400 | bytes 4587524 | tf_op jit(solution)/shard_map/dot_general | solution.py:172
  65.8 1.8 %fusion.59 = f32[384,1024]{1,0:T(8,128)S(1)} fusion(bf16[512,1024]{1,0:T(8,128)(2,1)} %collective-permute-done.7, bf16[384,8192]{1,0:T(8,128)(2,1)S(1)} %bitcast.110, s32[]{:T(128)S(6)} %select_n.298), kind=kOutput, calls=%fused_computation.112 | convolution fusion | flops 402653184 | bytes 3014660 | tf_op jit(solution)/shard_map/dot_general | solution.py:172
  69.4 1.6 %collective-permute-start.12 = (bf16[512,1024]{1,0:T(8,128)(2,1)}, bf16[512,1024]{1,0:T(8,128)(2,1)S(1)}, u32[]{:S(2)}, u32[]{:S(2)}) collective-permute-start(bf16[512,1024]{1,0:T(8,128)(2,1)} %collective-permute-done.7), channel_id=1, source_target_pairs={{0,16},{1,9},{2,18},{3,11},{4,12},{5,21},{6,14},{7,23},{8,24},{9,1... | collective-permute-start | bytes 3145736 | tf_op jit(solution)/shard_map/ppermute | solution.py:57
  71.0 1.6 %collective-permute-start.13 = (bf16[512,1024]{1,0:T(8,128)(2,1)}, bf16[512,1024]{1,0:T(8,128)(2,1)S(1)}, u32[]{:S(2)}, u32[]{:S(2)}) collective-permute-start(bf16[512,1024]{1,0:T(8,128)(2,1)} %collective-permute-done.7), channel_id=1, source_target_pairs={{0,1},{1,0},{2,3},{3,2},{4,5},{5,4},{6,7},{7,6},{8,9},{9,8},{10,11... | collective-permute-start | bytes 3145736 | tf_op jit(solution)/shard_map/ppermute | solution.py:58
  74.3 1.8 %fusion.9 = bf16[384,8192]{1,0:T(8,128)(2,1)S(1)} fusion(bf16[384,8192]{1,0:T(8,128)(2,1)S(1)} %fusion.7, s32[]{:T(128)S(6)} %select_n.296, f32[384,512]{1,0:T(8,128)S(1)} %bitcast.132, bf16[512,1024]{1,0:T(8,128)(2,1)} %collective-permute-done.5, bf16[384,1024]{1,0:T(8,128)(2,1)S(1)} %copy-done.4, f32[384]{0:T(512)S(1)} %get-tuple-element.29), kind=kOutput, calls=%fused_computation.41 | convolution fusion | flops 404226048 | bytes 3016708 | tf_op jit(solution)/shard_map/dot_general | solution.py:176
  76.2 1.9 %fusion.11 = bf16[384,8192]{1,0:T(8,128)(2,1)S(1)} fusion(bf16[384,8192]{1,0:T(8,128)(2,1)S(1)} %fusion.9, s32[]{:T(128)S(6)} %select_n.297, f32[384,512]{1,0:T(8,128)S(1)} %bitcast.133, bf16[512,1024]{1,0:T(8,128)(2,1)} %collective-permute-done.6, bf16[384,1024]{1,0:T(8,128)(2,1)S(1)} %copy-done.4, f32[384]{0:T(512)S(1)} %get-tuple-element.29), kind=kOutput, calls=%fused_computation.43 | convolution fusion | flops 404226048 | bytes 3016708 | tf_op jit(solution)/shard_map/dot_general | solution.py:176
  78.1 1.9 %fusion.13 = bf16[384,8192]{1,0:T(8,128)(2,1)S(1)} fusion(bf16[384,8192]{1,0:T(8,128)(2,1)S(1)} %fusion.11, s32[]{:T(128)S(6)} %select_n.298, f32[384,512]{1,0:T(8,128)S(1)} %bitcast.131, bf16[512,1024]{1,0:T(8,128)(2,1)} %collective-permute-done.7, bf16[384,1024]{1,0:T(8,128)(2,1)S(1)} %copy-done.4, f32[384]{0:T(512)S(1)} %get-tuple-element.29), kind=kOutput, calls=%fused_computation.45 | convolution fusion | flops 404226048 | bytes 3016708 | tf_op jit(solution)/shard_map/dot_general | solution.py:176
  80.0 0.6 fusion.15
  82.3 2.2 %collective-permute-done.12 = bf16[512,1024]{1,0:T(8,128)(2,1)S(1)} collective-permute-done((bf16[512,1024]{1,0:T(8,128)(2,1)}, bf16[512,1024]{1,0:T(8,128)(2,1)S(1)}, u32[]{:S(2)}, u32[]{:S(2)}) %collective-permute-start.12) | collective-permute-done | bytes 1048608 | tf_op jit(solution)/shard_map/ppermute | solution.py:57
  84.4 1.4 %collective-permute-start.17 = (bf16[16,9216]{1,0:T(8,128)(2,1)S(1)}, bf16[16,9216]{1,0:T(8,128)(2,1)S(1)}, u32[]{:S(2)}, u32[]{:S(2)}) collective-permute-start(bf16[16,9216]{1,0:T(8,128)(2,1)S(1)} %get-tuple-element.9), channel_id=1, source_target_pairs={{0,8},{4,12},{8,0},{12,4},{16,24},{20,28},{24,16},{28,20},{1,9},{5... | collective-permute-start | bytes 884744 | tf_op jit(solution)/shard_map/ppermute | solution.py:155
  85.8 0.7 collective-permute-start.18
  86.5 1.4 %collective-permute-start.19 = (bf16[16,9216]{1,0:T(8,128)(2,1)S(1)}, bf16[16,9216]{1,0:T(8,128)(2,1)S(1)}, u32[]{:S(2)}, u32[]{:S(2)}) collective-permute-start(bf16[16,9216]{1,0:T(8,128)(2,1)S(1)} %get-tuple-element.11), channel_id=1, source_target_pairs={{0,24},{4,28},{8,16},{12,20},{16,8},{20,12},{24,0},{28,4},{1,25},{... | collective-permute-start | bytes 884744 | tf_op jit(solution)/shard_map/ppermute | solution.py:155
  89.4 7.4 %collective-permute-done.13 = bf16[512,1024]{1,0:T(8,128)(2,1)S(1)} collective-permute-done((bf16[512,1024]{1,0:T(8,128)(2,1)}, bf16[512,1024]{1,0:T(8,128)(2,1)S(1)}, u32[]{:S(2)}, u32[]{:S(2)}) %collective-permute-start.13) | collective-permute-done | bytes 1048608 | tf_op jit(solution)/shard_map/ppermute | solution.py:58
  97.9 0.7 collective-permute-done.18
  98.6 1.7 %collective-permute-done.19 = bf16[16,9216]{1,0:T(8,128)(2,1)S(1)} collective-permute-done((bf16[16,9216]{1,0:T(8,128)(2,1)S(1)}, bf16[16,9216]{1,0:T(8,128)(2,1)S(1)}, u32[]{:S(2)}, u32[]{:S(2)}) %collective-permute-start.19) | collective-permute-done | bytes 294944 | tf_op jit(solution)/shard_map/ppermute | solution.py:155
  100.6 0.7 slice_bitcast_fusion.6
  104.7 0.8 convolution_add_fusion
  106.6 1.0 multiply_convert_fusion.1
  108.5 0.6 fusion.23
  109.1 0.6 fusion.25
  111.6 2.7 %copy-done.3 = bf16[384,8192]{1,0:T(8,128)(2,1)} copy-done((bf16[384,8192]{1,0:T(8,128)(2,1)}, bf16[384,8192]{1,0:T(8,128)(2,1)S(1)}, u32[]{:S(2)}) %copy-start.3) | copy-done | bytes 6291480
  (127 shorter events, 23.8 us)
Async XLA Ops:
  0.6 11.3 %copy-start = (s32[32]{0:T(128)S(1)}, s32[32]{0:T(128)}, u32[]{:S(2)}) copy-start(s32[32]{0:T(128)} %param.15) | copy-start | bytes 388
  2.4 9.5 %copy-start.17 = (s32[3]{0:T(128)S(1)}, s32[3]{0:T(128)}, u32[]{:S(2)}) copy-start(s32[3]{0:T(128)} %param.13) | copy-start | bytes 40
  2.4 10.8 %copy-start.16 = (s32[3]{0:T(128)S(1)}, s32[3]{0:T(128)}, u32[]{:S(2)}) copy-start(s32[3]{0:T(128)} %param.14) | copy-start | bytes 40
  2.4 29.0 %collective-permute-start = (bf16[16,9216]{1,0:T(8,128)(2,1)}, bf16[16,9216]{1,0:T(8,128)(2,1)S(1)}, u32[]{:S(2)}, u32[]{:S(2)}) collective-permute-start(bf16[16,9216]{1,0:T(8,128)(2,1)} %get-tuple-element.28), channel_id=1, source_target_pairs={{0,8},{4,12},{8,0},{12,4},{16,24},{20,28},{24,16},{28,20},{1,9},{5... | collective-permute-start | bytes 884744 | tf_op jit(solution)/shard_map/ppermute | solution.py:97
  5.3 26.1 %collective-permute-start.1 = (bf16[16,9216]{1,0:T(8,128)(2,1)}, bf16[16,9216]{1,0:T(8,128)(2,1)S(1)}, u32[]{:S(2)}, u32[]{:S(2)}) collective-permute-start(bf16[16,9216]{1,0:T(8,128)(2,1)} %get-tuple-element.28), channel_id=1, source_target_pairs={{0,16},{4,20},{8,24},{12,28},{16,0},{20,4},{24,8},{28,12},{1,17},{... | collective-permute-start | bytes 884744 | tf_op jit(solution)/shard_map/ppermute | solution.py:97
  6.8 24.6 %collective-permute-start.2 = (bf16[16,9216]{1,0:T(8,128)(2,1)}, bf16[16,9216]{1,0:T(8,128)(2,1)S(1)}, u32[]{:S(2)}, u32[]{:S(2)}) collective-permute-start(bf16[16,9216]{1,0:T(8,128)(2,1)} %get-tuple-element.28), channel_id=1, source_target_pairs={{0,24},{4,28},{8,16},{12,20},{16,8},{20,12},{24,0},{28,4},{1,25},{... | collective-permute-start | bytes 884744 | tf_op jit(solution)/shard_map/ppermute | solution.py:97
  6.9 55.1 %collective-permute-start.4 = (bf16[1024,1024]{1,0:T(8,128)(2,1)}, bf16[1024,1024]{1,0:T(8,128)(2,1)S(1)}, u32[]{:S(2)}, u32[]{:S(2)}) collective-permute-start(bf16[1024,1024]{1,0:T(8,128)(2,1)} %param.10), channel_id=1, source_target_pairs={{0,4},{4,0},{8,12},{12,8},{16,20},{20,16},{24,28},{28,24},{1,5},{5... | collective-permute-start | bytes 6291464 | tf_op jit(solution)/shard_map/ppermute | solution.py:46
  9.9 22.0 %copy-start.5 = (bf16[1,16,8192]{2,1,0:T(8,128)(2,1)S(1)}, bf16[1,16,8192]{2,1,0:T(8,128)(2,1)}, u32[]{:S(2)}) copy-start(bf16[1,16,8192]{2,1,0:T(8,128)(2,1)} %param.11) | copy-start | bytes 786436
  9.9 22.2 %collective-permute-start.5 = (bf16[512,1024]{1,0:T(8,128)(2,1)}, bf16[512,1024]{1,0:T(8,128)(2,1)}, u32[]{:S(2)}, u32[]{:S(2)}) collective-permute-start(bf16[512,1024]{1,0:T(8,128)(2,1)} %get-tuple-element.23), channel_id=1, source_target_pairs={{0,8},{1,17},{2,10},{3,19},{4,20},{5,13},{6,22},{7,15},{8,0},{9,25... | collective-permute-start | bytes 3145736 | tf_op jit(solution)/shard_map/ppermute | solution.py:53
  31.3 0.8 copy-start.15
  31.4 6.9 %slice-start = ((s8[6291456]{0:T(1024)(128)(4,1)}), s8[4194304]{0:T(1024)(128)(4,1)S(1)}, s32[]{:S(2)}) async-start(s8[6291456]{0:T(1024)(128)(4,1)} %bitcast.109), calls=%async_computation | async-start | bytes 8388608
  31.6 4.6 %collective-permute-start.3 = (bf16[4,16,9216]{2,1,0:T(8,128)(2,1)S(1)}, bf16[4,16,9216]{2,1,0:T(8,128)(2,1)S(1)}, u32[]{:S(2)}, u32[]{:S(2)}) collective-permute-start(bf16[4,16,9216]{2,1,0:T(8,128)(2,1)S(1)} %pad_maximum_fusion.1), channel_id=1, source_target_pairs={{0,4},{4,0},{8,12},{12,8},{16,20},{20,16},{24,28},{28,24},{1,5},{5... | collective-permute-start | bytes 3538952 | tf_op jit(solution)/shard_map/ppermute | solution.py:99
  32.1 33.7 %collective-permute-start.7 = (bf16[512,1024]{1,0:T(8,128)(2,1)}, bf16[512,1024]{1,0:T(8,128)(2,1)}, u32[]{:S(2)}, u32[]{:S(2)}) collective-permute-start(bf16[512,1024]{1,0:T(8,128)(2,1)} %get-tuple-element.8), channel_id=1, source_target_pairs={{0,8},{1,17},{2,10},{3,19},{4,20},{5,13},{6,22},{7,15},{8,0},{9,25... | collective-permute-start | bytes 3145736 | tf_op jit(solution)/shard_map/ppermute | solution.py:53
  33.5 30.5 %collective-permute-start.6 = (bf16[512,1024]{1,0:T(8,128)(2,1)}, bf16[512,1024]{1,0:T(8,128)(2,1)}, u32[]{:S(2)}, u32[]{:S(2)}) collective-permute-start(bf16[512,1024]{1,0:T(8,128)(2,1)} %collective-permute-done.5), channel_id=1, source_target_pairs={{0,4},{4,0},{8,12},{12,8},{16,20},{20,16},{24,28},{28,24},{1,5},{5... | collective-permute-start | bytes 3145736 | tf_op jit(solution)/shard_map/ppermute | solution.py:56
  33.5 26.6 %collective-permute-start.8 = (bf16[512,1024]{1,0:T(8,128)(2,1)}, bf16[512,1024]{1,0:T(8,128)(2,1)S(1)}, u32[]{:S(2)}, u32[]{:S(2)}) collective-permute-start(bf16[512,1024]{1,0:T(8,128)(2,1)} %collective-permute-done.5), channel_id=1, source_target_pairs={{0,16},{1,9},{2,18},{3,11},{4,12},{5,21},{6,14},{7,23},{8,24},{9,1... | collective-permute-start | bytes 3145736 | tf_op jit(solution)/shard_map/ppermute | solution.py:57
  36.2 25.5 %collective-permute-start.9 = (bf16[512,1024]{1,0:T(8,128)(2,1)}, bf16[512,1024]{1,0:T(8,128)(2,1)S(1)}, u32[]{:S(2)}, u32[]{:S(2)}) collective-permute-start(bf16[512,1024]{1,0:T(8,128)(2,1)} %collective-permute-done.5), channel_id=1, source_target_pairs={{0,1},{1,0},{2,3},{3,2},{4,5},{5,4},{6,7},{7,6},{8,9},{9,8},{10,11... | collective-permute-start | bytes 3145736 | tf_op jit(solution)/shard_map/ppermute | solution.py:58
  37.9 1.6 %slice-start.1 = ((s8[6291456]{0:T(1024)(128)(4,1)}), s8[2097152]{0:T(1024)(128)(4,1)S(1)}, s32[]{:S(2)}) async-start(s8[6291456]{0:T(1024)(128)(4,1)} %bitcast.109), calls=%async_computation.1 | async-start | bytes 4194304
  39.5 1.7 %copy-start.4 = (bf16[384,1024]{1,0:T(8,128)(2,1)S(1)}, bf16[384,1024]{1,0:T(8,128)(2,1)}, u32[]{:S(2)}) copy-start(bf16[384,1024]{1,0:T(8,128)(2,1)} %param.9) | copy-start | bytes 2359300
  51.1 4.2 %copy-start.2 = (bf16[1024,1024]{1,0:T(8,128)(2,1)S(1)}, bf16[1024,1024]{1,0:T(8,128)(2,1)}, u32[]{:S(2)}) copy-start(bf16[1024,1024]{1,0:T(8,128)(2,1)} %param.10) | copy-start | bytes 6291460
  60.1 21.7 %collective-permute-start.16 = (bf16[4,16,9216]{2,1,0:T(8,128)(2,1)S(1)}, bf16[4,16,9216]{2,1,0:T(8,128)(2,1)S(1)}, u32[]{:S(2)}, u32[]{:S(2)}) collective-permute-start(bf16[4,16,9216]{2,1,0:T(8,128)(2,1)S(1)} %pad_maximum_fusion.2), channel_id=1, source_target_pairs={{0,4},{4,0},{8,12},{12,8},{16,20},{20,16},{24,28},{28,24},{1,5},{5... | collective-permute-start | bytes 3538952 | tf_op jit(solution)/shard_map/ppermute | solution.py:142
  61.9 40.1 %collective-permute-start.11 = (bf16[2,512,1024]{2,1,0:T(8,128)(2,1)S(1)}, bf16[2,512,1024]{2,1,0:T(8,128)(2,1)S(1)}, u32[]{:S(2)}, u32[]{:S(2)}) collective-permute-start(bf16[2,512,1024]{2,1,0:T(8,128)(2,1)S(1)} %pad_maximum_fusion), channel_id=1, source_target_pairs={{0,4},{4,0},{8,12},{12,8},{16,20},{20,16},{24,28},{28,24},{1,5},{5... | collective-permute-start | bytes 6291464 | tf_op jit(solution)/shard_map/ppermute | solution.py:62
  69.1 3.5 %copy-start.14 = (f32[3,128,512]{2,1,0:T(8,128)S(1)}, f32[3,128,512]{2,1,0:T(8,128)}, u32[]{:S(2)}) copy-start(f32[3,128,512]{2,1,0:T(8,128)} %fusion.97) | copy-start | bytes 2359300
  69.3 3.8 %copy-start.13 = (f32[3,128,512]{2,1,0:T(8,128)S(1)}, f32[3,128,512]{2,1,0:T(8,128)}, u32[]{:S(2)}) copy-start(f32[3,128,512]{2,1,0:T(8,128)} %fusion.95) | copy-start | bytes 2359300
  69.4 15.1 %collective-permute-start.12 = (bf16[512,1024]{1,0:T(8,128)(2,1)}, bf16[512,1024]{1,0:T(8,128)(2,1)S(1)}, u32[]{:S(2)}, u32[]{:S(2)}) collective-permute-start(bf16[512,1024]{1,0:T(8,128)(2,1)} %collective-permute-done.7), channel_id=1, source_target_pairs={{0,16},{1,9},{2,18},{3,11},{4,12},{5,21},{6,14},{7,23},{8,24},{9,1... | collective-permute-start | bytes 3145736 | tf_op jit(solution)/shard_map/ppermute | solution.py:57
  71.0 15.5 %collective-permute-start.10 = (bf16[512,1024]{1,0:T(8,128)(2,1)}, bf16[512,1024]{1,0:T(8,128)(2,1)S(1)}, u32[]{:S(2)}, u32[]{:S(2)}) collective-permute-start(bf16[512,1024]{1,0:T(8,128)(2,1)} %collective-permute-done.7), channel_id=1, source_target_pairs={{0,4},{4,0},{8,12},{12,8},{16,20},{20,16},{24,28},{28,24},{1,5},{5... | collective-permute-start | bytes 3145736 | tf_op jit(solution)/shard_map/ppermute | solution.py:56
  71.0 25.8 %collective-permute-start.13 = (bf16[512,1024]{1,0:T(8,128)(2,1)}, bf16[512,1024]{1,0:T(8,128)(2,1)S(1)}, u32[]{:S(2)}, u32[]{:S(2)}) collective-permute-start(bf16[512,1024]{1,0:T(8,128)(2,1)} %collective-permute-done.7), channel_id=1, source_target_pairs={{0,1},{1,0},{2,3},{3,2},{4,5},{5,4},{6,7},{7,6},{8,9},{9,8},{10,11... | collective-permute-start | bytes 3145736 | tf_op jit(solution)/shard_map/ppermute | solution.py:58
  73.2 1.1 copy-start.11
  73.8 2.3 %copy-start.12 = (f32[3,128,512]{2,1,0:T(8,128)S(1)}, f32[3,128,512]{2,1,0:T(8,128)}, u32[]{:S(2)}) copy-start(f32[3,128,512]{2,1,0:T(8,128)} %fusion.91) | copy-start | bytes 2359300
  76.1 2.0 %copy-start.10 = (f32[3,128,512]{2,1,0:T(8,128)S(1)}, f32[3,128,512]{2,1,0:T(8,128)}, u32[]{:S(2)}) copy-start(f32[3,128,512]{2,1,0:T(8,128)} %fusion.89) | copy-start | bytes 2359300
  78.1 2.0 %copy-start.9 = (f32[3,128,512]{2,1,0:T(8,128)S(1)}, f32[3,128,512]{2,1,0:T(8,128)}, u32[]{:S(2)}) copy-start(f32[3,128,512]{2,1,0:T(8,128)} %fusion.87) | copy-start | bytes 2359300
  80.0 1.1 copy-start.8
  81.8 6.1 %copy-start.7 = (f32[3,128,512]{2,1,0:T(8,128)S(1)}, f32[3,128,512]{2,1,0:T(8,128)}, u32[]{:S(2)}) copy-start(f32[3,128,512]{2,1,0:T(8,128)} %fusion.83) | copy-start | bytes 2359300
  84.4 12.9 %collective-permute-start.17 = (bf16[16,9216]{1,0:T(8,128)(2,1)S(1)}, bf16[16,9216]{1,0:T(8,128)(2,1)S(1)}, u32[]{:S(2)}, u32[]{:S(2)}) collective-permute-start(bf16[16,9216]{1,0:T(8,128)(2,1)S(1)} %get-tuple-element.9), channel_id=1, source_target_pairs={{0,8},{4,12},{8,0},{12,4},{16,24},{20,28},{24,16},{28,20},{1,9},{5... | collective-permute-start | bytes 884744 | tf_op jit(solution)/shard_map/ppermute | solution.py:155
  85.8 12.8 %collective-permute-start.18 = (bf16[16,9216]{1,0:T(8,128)(2,1)S(1)}, bf16[16,9216]{1,0:T(8,128)(2,1)S(1)}, u32[]{:S(2)}, u32[]{:S(2)}) collective-permute-start(bf16[16,9216]{1,0:T(8,128)(2,1)S(1)} %get-tuple-element.10), channel_id=1, source_target_pairs={{0,16},{4,20},{8,24},{12,28},{16,0},{20,4},{24,8},{28,12},{1,17},{... | collective-permute-start | bytes 884744 | tf_op jit(solution)/shard_map/ppermute | solution.py:155
  86.5 13.9 %collective-permute-start.19 = (bf16[16,9216]{1,0:T(8,128)(2,1)S(1)}, bf16[16,9216]{1,0:T(8,128)(2,1)S(1)}, u32[]{:S(2)}, u32[]{:S(2)}) collective-permute-start(bf16[16,9216]{1,0:T(8,128)(2,1)S(1)} %get-tuple-element.11), channel_id=1, source_target_pairs={{0,24},{4,28},{8,16},{12,20},{16,8},{20,12},{24,0},{28,4},{1,25},{... | collective-permute-start | bytes 884744 | tf_op jit(solution)/shard_map/ppermute | solution.py:155
  96.7 8.0 %collective-permute-start.14 = (bf16[512,1024]{1,0:T(8,128)(2,1)S(1)}, bf16[512,1024]{1,0:T(8,128)(2,1)S(1)}, u32[]{:S(2)}, u32[]{:S(2)}) collective-permute-start(bf16[512,1024]{1,0:T(8,128)(2,1)S(1)} %collective-permute-done.12), channel_id=1, source_target_pairs={{0,4},{4,0},{8,12},{12,8},{16,20},{20,16},{24,28},{28,24},{1,5},{5... | collective-permute-start | bytes 3145736 | tf_op jit(solution)/shard_map/ppermute | solution.py:65
  97.3 8.3 %collective-permute-start.15 = (bf16[512,1024]{1,0:T(8,128)(2,1)S(1)}, bf16[512,1024]{1,0:T(8,128)(2,1)S(1)}, u32[]{:S(2)}, u32[]{:S(2)}) collective-permute-start(bf16[512,1024]{1,0:T(8,128)(2,1)S(1)} %collective-permute-done.13), channel_id=1, source_target_pairs={{0,4},{4,0},{8,12},{12,8},{16,20},{20,16},{24,28},{28,24},{1,5},{5... | collective-permute-start | bytes 3145736 | tf_op jit(solution)/shard_map/ppermute | solution.py:66
  106.5 1.3 %copy-start.6 = (f32[3,128,512]{2,1,0:T(8,128)S(1)}, f32[3,128,512]{2,1,0:T(8,128)}, u32[]{:S(2)}) copy-start(f32[3,128,512]{2,1,0:T(8,128)} %fusion.81) | copy-start | bytes 2359300
  110.4 4.0 %copy-start.1 = (s32[32]{0:T(128)S(1)}, s32[32]{0:T(128)}, u32[]{:S(2)}) copy-start(s32[32]{0:T(128)} %param.15) | copy-start | bytes 388
  111.6 2.7 %copy-start.3 = (bf16[384,8192]{1,0:T(8,128)(2,1)}, bf16[384,8192]{1,0:T(8,128)(2,1)S(1)}, u32[]{:S(2)}) copy-start(bf16[384,8192]{1,0:T(8,128)(2,1)S(1)} %fusion.31) | copy-start | bytes 18874372

commit v18 on v17

--- a/solution.py
+++ b/solution.py
@@ -53,14 +53,17 @@
         first = lax.ppermute(piece, ("fsdp", "dp"), first_pairs)
         previous = first
         result.append((2.0 + 2 * k, sources[1], k, first))
-        result.append((3.0 + 2 * k, sibling_sources[1], k, lax.ppermute(first, "fsdp", xor_pairs(members, 1))))
+        if k + 1 == WEIGHT_CHUNKS:
+            result.append((3.0 + 2 * k, sibling_sources[1], k,
+                           lax.ppermute(first, "fsdp", xor_pairs(members, 1))))
         relayed = lax.ppermute(first, ("fsdp", "dp"), relay_pairs)
         partner = lax.ppermute(first, ("fsdp", "dp"), partner_pairs)
         result.append((4.5 + 2 * k, sources[2], k, relayed))
         result.append((4.5 + 2 * k, sources[3], k, partner))
         if k + 1 < WEIGHT_CHUNKS:
-            late = lax.ppermute(jnp.stack([relayed, partner]), "fsdp", xor_pairs(members, 1))
+            late = lax.ppermute(jnp.stack([relayed, partner, first]), "fsdp", xor_pairs(members, 1))
             late_pieces = (late[0], late[1])
+            result.append((5.5 + 2 * k, sibling_sources[1], k, late[2]))
         else:
             late_pieces = (lax.ppermute(relayed, "fsdp", xor_pairs(members, 1)),
                            lax.ppermute(partner, "fsdp", xor_pairs(members, 1)))

time: 115 us -> 121 us (1.052)
  matrix products: 43.9 us -> 48 us
  other arithmetic: 8.15 us -> 9.45 us
    dot_general x16, matrix products: 13 us -> 16.6 us  [on_device(): jnp.einsum('uio,uof->uif', low_rank_gradient, down_piece, preferred_eleme...]
    ppermute x2, waiting for transfers between devices: 2.17 us -> 4.02 us  [relay_gather(): relayed = lax.ppermute(first, ('fsdp', 'dp'), relay_pairs)]
    ppermute x2, waiting for transfers between devices: 8.89 us -> 7.3 us  [relay_gather(): partner = lax.ppermute(first, ('fsdp', 'dp'), partner_pairs)]
    unnamed x46 -> x54, local copies, waits for them, and re-layouts: 5.47 us -> 6.92 us
    add x9 -> x10, other arithmetic: 2.71 us -> 2.86 us  [on_device(): output_total + jnp.dot(token_piece, weight_piece, preferred_element_type=...]
  transfers between devices with their start and end apart: 20 -> 19, of which waited for: 5 -> 4; matrix products, arithmetic and copies ran while one was open for 45% -> 47% of each run, Pallas kernels for 0% -> 0%
where the time goes in v18:
time: 121 us; the launch traced here: 120 us
  matrix products  48 us (40%)
  between operations  19 us (16%)
  starting transfers between devices  17.1 us (14%)
  waiting for transfers between devices  13.4 us (11%)
  local copies, waits for them, and re-layouts  13 us (11%)
  other arithmetic  9.45 us (8%)
    dot_general x16, matrix products, on_device(): jnp.einsum('uio,uof->uif', low_rank_gradient, down_piece, preferred_eleme...  16.6 us
    dot_general x16, matrix products, on_device(): jnp.dot(token_piece, weight_piece, preferred_element_type=jnp.float32)  14.1 us
    dot_general x16, matrix products, on_device(): lax.dot_general(masked_cot, weight_piece, (((1,), (1,)), ((), ())), prefe...  13.6 us
    ppermute x2, waiting for transfers between devices, relay_gather(): partner = lax.ppermute(first, ('fsdp', 'dp'), partner_pairs)  7.3 us
    unnamed x54, local copies, waits for them, and re-layouts  6.92 us
    ppermute x3, starting transfers between devices, on_device(): by_step[step] = lax.ppermute(own_adapter, 'fsdp', xor_pairs(members, step))  4.47 us
    ppermute x2, waiting for transfers between devices, relay_gather(): relayed = lax.ppermute(first, ('fsdp', 'dp'), relay_pairs)  4.02 us
    ppermute x3, starting transfers between devices, on_device(): lax.ppermute(sent, 'fsdp', xor_pairs(members, step)).astype(jnp.float32)  3.49 us
  transfers between devices with their start and end apart: 19, of which 4 were waited for; matrix products, arithmetic and copies ran while one was open for 47% of the time, Pallas kernels for 0%

profile of v18, /device:TPU:0, one launch (start us, length us, event | category | flops | bytes accessed | tf_op | source)
XLA Modules:
  0.0 120.0 jit_solution(15024874427897837057)
XLA Ops:
  0.6 1.7 %fusion.140 = (bf16[1,16,9216]{2,1,0:T(8,128)(2,1)S(1)}, bf16[16,9216]{1,0:T(8,128)(2,1)}) fusion(bf16[16,1024]{1,0:T(8,128)(2,1)} %bitcast.142, bf16[16,8192]{1,0:T(8,128)(2,1)} %bitcast.124), kind=kLoop, calls=%fused_computation.216 | loop fusion | flops 589824 | bytes 884736 | tf_op jit(solution)/shard_map/stack | solution.py:105
  2.4 2.9 %collective-permute-start = (bf16[16,9216]{1,0:T(8,128)(2,1)}, bf16[16,9216]{1,0:T(8,128)(2,1)S(1)}, u32[]{:S(2)}, u32[]{:S(2)}) collective-permute-start(bf16[16,9216]{1,0:T(8,128)(2,1)} %get-tuple-element.28), channel_id=1, source_target_pairs={{0,8},{4,12},{8,0},{12,4},{16,24},{20,28},{24,16},{28,20},{1,9},{5... | collective-permute-start | bytes 884744 | tf_op jit(solution)/shard_map/ppermute | solution.py:100
  5.3 1.5 %collective-permute-start.1 = (bf16[16,9216]{1,0:T(8,128)(2,1)}, bf16[16,9216]{1,0:T(8,128)(2,1)S(1)}, u32[]{:S(2)}, u32[]{:S(2)}) collective-permute-start(bf16[16,9216]{1,0:T(8,128)(2,1)} %get-tuple-element.28), channel_id=1, source_target_pairs={{0,16},{4,20},{8,24},{12,28},{16,0},{20,4},{24,8},{28,12},{1,17},{... | collective-permute-start | bytes 884744 | tf_op jit(solution)/shard_map/ppermute | solution.py:100
  6.9 2.7 %fusion.147 = (bf16[512,1024]{1,0:T(8,128)(2,1)}, bf16[512,1024]{1,0:T(8,128)(2,1)S(1)}) fusion(bf16[1024,1024]{1,0:T(8,128)(2,1)} %param.10), kind=kLoop, calls=%fused_computation.221 | loop fusion | bytes 4194304 | tf_op jit(solution)/shard_map/slice | solution.py:48
  9.5 2.0 %collective-permute-start.5 = (bf16[512,1024]{1,0:T(8,128)(2,1)S(1)}, bf16[512,1024]{1,0:T(8,128)(2,1)S(1)}, u32[]{:S(2)}, u32[]{:S(2)}) collective-permute-start(bf16[512,1024]{1,0:T(8,128)(2,1)S(1)} %get-tuple-element.23), channel_id=1, source_target_pairs={{0,8},{1,17},{2,10},{3,19},{4,20},{5,13},{6,22},{7,15},{8,0},{9,25... | collective-permute-start | bytes 3145736 | tf_op jit(solution)/shard_map/ppermute | solution.py:53
  11.5 0.6 gather_fusion
  12.2 0.7 and_select_fusion
  31.9 1.4 %collective-permute-start.6 = (bf16[512,1024]{1,0:T(8,128)(2,1)}, bf16[512,1024]{1,0:T(8,128)(2,1)}, u32[]{:S(2)}, u32[]{:S(2)}) collective-permute-start(bf16[512,1024]{1,0:T(8,128)(2,1)} %get-tuple-element.8), channel_id=1, source_target_pairs={{0,8},{1,17},{2,10},{3,19},{4,20},{5,13},{6,22},{7,15},{8,0},{9,25... | collective-permute-start | bytes 3145736 | tf_op jit(solution)/shard_map/ppermute | solution.py:53
  33.3 0.7 collective-permute-start.7
  34.0 1.5 %collective-permute-start.8 = (bf16[512,1024]{1,0:T(8,128)(2,1)S(1)}, bf16[512,1024]{1,0:T(8,128)(2,1)S(1)}, u32[]{:S(2)}, u32[]{:S(2)}) collective-permute-start(bf16[512,1024]{1,0:T(8,128)(2,1)S(1)} %collective-permute-done.5), channel_id=1, source_target_pairs={{0,1},{1,0},{2,3},{3,2},{4,5},{5,4},{6,7},{7,6},{8,9},{9,8},{10,11... | collective-permute-start | bytes 3145736 | tf_op jit(solution)/shard_map/ppermute | solution.py:60
  35.6 1.6 %fusion.63 = f32[384,1024]{1,0:T(8,128)S(1)} fusion(bf16[512,1024]{1,0:T(8,128)(2,1)S(1)} %collective-permute-done.5, bf16[384,8192]{1,0:T(8,128)(2,1)} %param.8, s32[]{:T(128)S(6)} %select_n.296), kind=kOutput, calls=%fused_computation.116 | convolution fusion | flops 402653184 | bytes 3014660 | tf_op jit(solution)/shard_map/dot_general | solution.py:175
  37.7 1.2 slice-done.1
  38.9 1.7 %fusion.32 = bf16[3,16,128]{2,1,0:T(8,128)(2,1)S(1)} fusion(bf16[3,128,8192]{2,1,0:T(8,128)(2,1)S(1)} %bitcast.114, f32[3,128]{1,0:T(4,128)S(1)} %get-tuple-element.30, bf16[3,16,9216]{2,1,0:T(8,128)(2,1)S(1)} %pad_maximum_fusion.3), kind=kOutput, calls=%fused_computation.68 | convolution fusion | flops 100675584 | bytes 7092224 | tf_op jit(solution)/shard_map/cvj,coj->cvo/dot_general | solution.py:120
  41.6 0.9 fusion.149
  43.1 1.2 pad_maximum_fusion.2
  44.2 1.2 %fusion.94 = f32[3,128,512]{2,1,0:T(8,128)} fusion(bf16[3,16,128]{2,1,0:T(8,128)(2,1)S(1)} %fusion.33, bf16[3,16,8192]{2,1,0:T(8,128)(2,1)S(1)} %slice.151, s32[]{:T(128)S(6)} %select_n.296), kind=kOutput, calls=%fused_computation.154 | convolution fusion | flops 6291456 | bytes 847876 | tf_op jit(solution)/shard_map/uio,uof->uif/dot_general | solution.py:181
  46.0 1.2 fusion.98
  47.2 1.2 %fusion.96 = f32[3,128,512]{2,1,0:T(8,128)} fusion(bf16[3,16,128]{2,1,0:T(8,128)(2,1)S(1)} %fusion.33, bf16[3,16,8192]{2,1,0:T(8,128)(2,1)S(1)} %slice.151, s32[]{:T(128)S(6)} %select_n.293), kind=kOutput, calls=%fused_computation.156 | convolution fusion | flops 6291456 | bytes 847876 | tf_op jit(solution)/shard_map/uio,uof->uif/dot_general | solution.py:181
  48.4 1.2 fusion.92
  49.6 1.2 fusion.90
  50.8 1.2 fusion.88
  52.0 1.3 %fusion.86 = f32[3,128,512]{2,1,0:T(8,128)} fusion(bf16[3,16,128]{2,1,0:T(8,128)(2,1)S(1)} %fusion.33, bf16[3,16,8192]{2,1,0:T(8,128)(2,1)S(1)} %slice.151, s32[]{:T(128)S(6)} %select_n.300), kind=kOutput, calls=%fused_computation.146 | convolution fusion | flops 6291456 | bytes 847876 | tf_op jit(solution)/shard_map/uio,uof->uif/dot_general | solution.py:181
  53.3 1.2 %fusion.84 = f32[3,128,512]{2,1,0:T(8,128)} fusion(bf16[3,16,128]{2,1,0:T(8,128)(2,1)S(1)} %fusion.33, bf16[3,16,8192]{2,1,0:T(8,128)(2,1)S(1)} %slice.151, s32[]{:T(128)S(6)} %select_n.301), kind=kOutput, calls=%fused_computation.144 | convolution fusion | flops 6291456 | bytes 847876 | tf_op jit(solution)/shard_map/uio,uof->uif/dot_general | solution.py:181
  55.6 1.2 %fusion.82 = f32[3,128,512]{2,1,0:T(8,128)} fusion(bf16[3,16,128]{2,1,0:T(8,128)(2,1)S(1)} %fusion.33, bf16[3,16,8192]{2,1,0:T(8,128)(2,1)S(1)} %slice.151, s32[]{:T(128)S(6)} %select_n.302), kind=kOutput, calls=%fused_computation.142 | convolution fusion | flops 6291456 | bytes 847876 | tf_op jit(solution)/shard_map/uio,uof->uif/dot_general | solution.py:181
  56.9 1.2 %fusion.80 = f32[3,128,512]{2,1,0:T(8,128)} fusion(bf16[3,16,128]{2,1,0:T(8,128)(2,1)S(1)} %fusion.33, bf16[3,16,8192]{2,1,0:T(8,128)(2,1)S(1)} %slice.151, s32[]{:T(128)S(6)} %select_n.303), kind=kOutput, calls=%fused_computation.140 | convolution fusion | flops 6291456 | bytes 847876 | tf_op jit(solution)/shard_map/uio,uof->uif/dot_general | solution.py:181
  58.1 1.3 %fusion.78 = f32[3,128,512]{2,1,0:T(8,128)} fusion(bf16[3,16,128]{2,1,0:T(8,128)(2,1)S(1)} %fusion.33, bf16[3,16,8192]{2,1,0:T(8,128)(2,1)S(1)} %slice.151, s32[]{:T(128)S(6)} %select_n.304), kind=kOutput, calls=%fused_computation.138 | convolution fusion | flops 6291456 | bytes 847876 | tf_op jit(solution)/shard_map/uio,uof->uif/dot_general | solution.py:181
  59.3 1.2 %fusion.76 = f32[3,128,512]{2,1,0:T(8,128)} fusion(bf16[3,16,128]{2,1,0:T(8,128)(2,1)S(1)} %fusion.33, bf16[3,16,8192]{2,1,0:T(8,128)(2,1)S(1)} %slice.151, s32[]{:T(128)S(6)} %select_n.305), kind=kOutput, calls=%fused_computation.136 | convolution fusion | flops 6291456 | bytes 847876 | tf_op jit(solution)/shard_map/uio,uof->uif/dot_general | solution.py:181
  60.6 1.2 fusion.74
  61.8 0.7 broadcast_in_dim.44
  62.5 0.6 fusion.1
  63.1 0.6 fusion.3
  65.0 2.0 %convolution_add_fusion.3 = f32[384,1024]{1,0:T(8,128)S(1)} fusion(f32[384,1024]{1,0:T(8,128)S(1)} %convolution_add_fusion.4, bf16[1024,1024]{1,0:T(8,128)(2,1)} %collective-permute-done.4, bf16[384,8192]{1,0:T(8,128)(2,1)S(1)} %bitcast.113, s32[]{:T(128)S(6)} %select_n.292), kind=kOutput, calls=%fused_computation.12 | convolution fusion | flops 403046400 | bytes 4587524 | tf_op jit(solution)/shard_map/dot_general | solution.py:175
  67.0 1.8 %fusion.38 = f32[384,1024]{1,0:T(8,128)S(1)} fusion(bf16[1024,1024]{1,0:T(8,128)(2,1)} %collective-permute-done.4, bf16[384,8192]{1,0:T(8,128)(2,1)S(1)} %bitcast.113, s32[]{:T(128)S(6)} %select_n.293), kind=kOutput, calls=%fused_computation.77 | convolution fusion | flops 402653184 | bytes 3014660 | tf_op jit(solution)/shard_map/dot_general | solution.py:175
  69.4 1.8 %fusion.61 = f32[384,1024]{1,0:T(8,128)S(1)} fusion(bf16[512,1024]{1,0:T(8,128)(2,1)} %collective-permute-done.6, bf16[384,8192]{1,0:T(8,128)(2,1)S(1)} %bitcast.113, s32[]{:T(128)S(6)} %select_n.297), kind=kOutput, calls=%fused_computation.114 | convolution fusion | flops 402653184 | bytes 3014660 | tf_op jit(solution)/shard_map/dot_general | solution.py:175
  73.0 1.6 %collective-permute-start.11 = (bf16[512,1024]{1,0:T(8,128)(2,1)}, bf16[512,1024]{1,0:T(8,128)(2,1)S(1)}, u32[]{:S(2)}, u32[]{:S(2)}) collective-permute-start(bf16[512,1024]{1,0:T(8,128)(2,1)} %collective-permute-done.6), channel_id=1, source_target_pairs={{0,16},{1,9},{2,18},{3,11},{4,12},{5,21},{6,14},{7,23},{8,24},{9,1... | collective-permute-start | bytes 3145736 | tf_op jit(solution)/shard_map/ppermute | solution.py:59
  75.0 1.8 %fusion.5 = bf16[384,8192]{1,0:T(8,128)(2,1)S(1)} fusion(bf16[384,8192]{1,0:T(8,128)(2,1)S(1)} %fusion.3, s32[]{:T(128)S(6)} %select_n.292, f32[384,512]{1,0:T(8,128)S(1)} %bitcast.139, bf16[1024,1024]{1,0:T(8,128)(2,1)} %collective-permute-done.4, bf16[384,1024]{1,0:T(8,128)(2,1)S(1)} %copy-done.4, f32[384]{0:T(512)S(1)} %get-tuple-element.29), kind=kOutput, calls=%fused_computation.36 | convolution fusion | flops 404226048 | bytes 3016708 | tf_op jit(solution)/shard_map/dot_general | solution.py:179
  76.9 1.9 %fusion.7 = bf16[384,8192]{1,0:T(8,128)(2,1)S(1)} fusion(bf16[384,8192]{1,0:T(8,128)(2,1)S(1)} %fusion.5, s32[]{:T(128)S(6)} %select_n.293, f32[384,512]{1,0:T(8,128)S(1)} %bitcast.138, bf16[1024,1024]{1,0:T(8,128)(2,1)} %collective-permute-done.4, bf16[384,1024]{1,0:T(8,128)(2,1)S(1)} %copy-done.4, f32[384]{0:T(512)S(1)} %get-tuple-element.29), kind=kOutput, calls=%fused_computation.38 | convolution fusion | flops 404226048 | bytes 3016708 | tf_op jit(solution)/shard_map/dot_general | solution.py:179
  79.9 1.8 %fusion.11 = bf16[384,8192]{1,0:T(8,128)(2,1)S(1)} fusion(bf16[384,8192]{1,0:T(8,128)(2,1)S(1)} %fusion.9, s32[]{:T(128)S(6)} %select_n.297, f32[384,512]{1,0:T(8,128)S(1)} %bitcast.137, bf16[512,1024]{1,0:T(8,128)(2,1)} %collective-permute-done.6, bf16[384,1024]{1,0:T(8,128)(2,1)S(1)} %copy-done.4, f32[384]{0:T(512)S(1)} %get-tuple-element.29), kind=kOutput, calls=%fused_computation.42 | convolution fusion | flops 404226048 | bytes 3016708 | tf_op jit(solution)/shard_map/dot_general | solution.py:179
  84.0 4.0 %collective-permute-done.11 = bf16[512,1024]{1,0:T(8,128)(2,1)S(1)} collective-permute-done((bf16[512,1024]{1,0:T(8,128)(2,1)}, bf16[512,1024]{1,0:T(8,128)(2,1)S(1)}, u32[]{:S(2)}, u32[]{:S(2)}) %collective-permute-start.11) | collective-permute-done | bytes 1048608 | tf_op jit(solution)/shard_map/ppermute | solution.py:59
  88.0 1.3 %collective-permute-start.16 = (bf16[16,9216]{1,0:T(8,128)(2,1)S(1)}, bf16[16,9216]{1,0:T(8,128)(2,1)S(1)}, u32[]{:S(2)}, u32[]{:S(2)}) collective-permute-start(bf16[16,9216]{1,0:T(8,128)(2,1)S(1)} %get-tuple-element.9), channel_id=1, source_target_pairs={{0,8},{4,12},{8,0},{12,4},{16,24},{20,28},{24,16},{28,20},{1,9},{5... | collective-permute-start | bytes 884744 | tf_op jit(solution)/shard_map/ppermute | solution.py:158
  89.4 0.7 collective-permute-start.17
  90.1 1.4 %collective-permute-start.18 = (bf16[16,9216]{1,0:T(8,128)(2,1)S(1)}, bf16[16,9216]{1,0:T(8,128)(2,1)S(1)}, u32[]{:S(2)}, u32[]{:S(2)}) collective-permute-start(bf16[16,9216]{1,0:T(8,128)(2,1)S(1)} %get-tuple-element.11), channel_id=1, source_target_pairs={{0,24},{4,28},{8,16},{12,20},{16,8},{20,12},{24,0},{28,4},{1,25},{... | collective-permute-start | bytes 884744 | tf_op jit(solution)/shard_map/ppermute | solution.py:158
  93.0 7.3 %collective-permute-done.12 = bf16[512,1024]{1,0:T(8,128)(2,1)S(1)} collective-permute-done((bf16[512,1024]{1,0:T(8,128)(2,1)}, bf16[512,1024]{1,0:T(8,128)(2,1)S(1)}, u32[]{:S(2)}, u32[]{:S(2)}) %collective-permute-start.12) | collective-permute-done | bytes 1048608 | tf_op jit(solution)/shard_map/ppermute | solution.py:60
  101.8 1.7 %collective-permute-done.18 = bf16[16,9216]{1,0:T(8,128)(2,1)S(1)} collective-permute-done((bf16[16,9216]{1,0:T(8,128)(2,1)S(1)}, bf16[16,9216]{1,0:T(8,128)(2,1)S(1)}, u32[]{:S(2)}, u32[]{:S(2)}) %collective-permute-start.18) | collective-permute-done | bytes 294944 | tf_op jit(solution)/shard_map/ppermute | solution.py:158
  104.4 0.7 slice_bitcast_fusion.9
  110.2 1.0 multiply_convert_fusion.1
  116.7 0.6 fusion.31
  117.3 2.7 %copy-done.3 = bf16[384,8192]{1,0:T(8,128)(2,1)} copy-done((bf16[384,8192]{1,0:T(8,128)(2,1)}, bf16[384,8192]{1,0:T(8,128)(2,1)S(1)}, u32[]{:S(2)}) %copy-start.3) | copy-done | bytes 6291480
  (134 shorter events, 26.5 us)
Async XLA Ops:
  0.6 10.9 %copy-start = (s32[32]{0:T(128)S(1)}, s32[32]{0:T(128)}, u32[]{:S(2)}) copy-start(s32[32]{0:T(128)} %param.15) | copy-start | bytes 388
  2.4 9.1 %copy-start.21 = (s32[3]{0:T(128)S(1)}, s32[3]{0:T(128)}, u32[]{:S(2)}) copy-start(s32[3]{0:T(128)} %param.13) | copy-start | bytes 40
  2.4 10.5 %copy-start.20 = (s32[3]{0:T(128)S(1)}, s32[3]{0:T(128)}, u32[]{:S(2)}) copy-start(s32[3]{0:T(128)} %param.14) | copy-start | bytes 40
  2.4 28.8 %collective-permute-start = (bf16[16,9216]{1,0:T(8,128)(2,1)}, bf16[16,9216]{1,0:T(8,128)(2,1)S(1)}, u32[]{:S(2)}, u32[]{:S(2)}) collective-permute-start(bf16[16,9216]{1,0:T(8,128)(2,1)} %get-tuple-element.28), channel_id=1, source_target_pairs={{0,8},{4,12},{8,0},{12,4},{16,24},{20,28},{24,16},{28,20},{1,9},{5... | collective-permute-start | bytes 884744 | tf_op jit(solution)/shard_map/ppermute | solution.py:100
  5.3 25.9 %collective-permute-start.1 = (bf16[16,9216]{1,0:T(8,128)(2,1)}, bf16[16,9216]{1,0:T(8,128)(2,1)S(1)}, u32[]{:S(2)}, u32[]{:S(2)}) collective-permute-start(bf16[16,9216]{1,0:T(8,128)(2,1)} %get-tuple-element.28), channel_id=1, source_target_pairs={{0,16},{4,20},{8,24},{12,28},{16,0},{20,4},{24,8},{28,12},{1,17},{... | collective-permute-start | bytes 884744 | tf_op jit(solution)/shard_map/ppermute | solution.py:100
  6.8 24.4 %collective-permute-start.2 = (bf16[16,9216]{1,0:T(8,128)(2,1)}, bf16[16,9216]{1,0:T(8,128)(2,1)S(1)}, u32[]{:S(2)}, u32[]{:S(2)}) collective-permute-start(bf16[16,9216]{1,0:T(8,128)(2,1)} %get-tuple-element.28), channel_id=1, source_target_pairs={{0,24},{4,28},{8,16},{12,20},{16,8},{20,12},{24,0},{28,4},{1,25},{... | collective-permute-start | bytes 884744 | tf_op jit(solution)/shard_map/ppermute | solution.py:100
  6.9 58.2 %collective-permute-start.4 = (bf16[1024,1024]{1,0:T(8,128)(2,1)}, bf16[1024,1024]{1,0:T(8,128)(2,1)}, u32[]{:S(2)}, u32[]{:S(2)}) collective-permute-start(bf16[1024,1024]{1,0:T(8,128)(2,1)} %param.10), channel_id=1, source_target_pairs={{0,4},{4,0},{8,12},{12,8},{16,20},{20,16},{24,28},{28,24},{1,5},{5... | collective-permute-start | bytes 6291464 | tf_op jit(solution)/shard_map/ppermute | solution.py:46
  9.5 22.2 %copy-start.5 = (bf16[1,16,8192]{2,1,0:T(8,128)(2,1)S(1)}, bf16[1,16,8192]{2,1,0:T(8,128)(2,1)}, u32[]{:S(2)}) copy-start(bf16[1,16,8192]{2,1,0:T(8,128)(2,1)} %param.11) | copy-start | bytes 786436
  9.5 22.4 %collective-permute-start.5 = (bf16[512,1024]{1,0:T(8,128)(2,1)S(1)}, bf16[512,1024]{1,0:T(8,128)(2,1)S(1)}, u32[]{:S(2)}, u32[]{:S(2)}) collective-permute-start(bf16[512,1024]{1,0:T(8,128)(2,1)S(1)} %get-tuple-element.23), channel_id=1, source_target_pairs={{0,8},{1,17},{2,10},{3,19},{4,20},{5,13},{6,22},{7,15},{8,0},{9,25... | collective-permute-start | bytes 3145736 | tf_op jit(solution)/shard_map/ppermute | solution.py:53
  31.1 0.8 copy-start.19
  31.2 6.4 %slice-start = ((s8[6291456]{0:T(1024)(128)(4,1)}), s8[4194304]{0:T(1024)(128)(4,1)S(1)}, s32[]{:S(2)}) async-start(s8[6291456]{0:T(1024)(128)(4,1)} %bitcast.112), calls=%async_computation | async-start | bytes 8388608
  31.4 5.8 %collective-permute-start.3 = (bf16[4,16,9216]{2,1,0:T(8,128)(2,1)S(1)}, bf16[4,16,9216]{2,1,0:T(8,128)(2,1)S(1)}, u32[]{:S(2)}, u32[]{:S(2)}) collective-permute-start(bf16[4,16,9216]{2,1,0:T(8,128)(2,1)S(1)} %pad_maximum_fusion.1), channel_id=1, source_target_pairs={{0,4},{4,0},{8,12},{12,8},{16,20},{20,16},{24,28},{28,24},{1,5},{5... | collective-permute-start | bytes 3538952 | tf_op jit(solution)/shard_map/ppermute | solution.py:102
  31.9 37.5 %collective-permute-start.6 = (bf16[512,1024]{1,0:T(8,128)(2,1)}, bf16[512,1024]{1,0:T(8,128)(2,1)}, u32[]{:S(2)}, u32[]{:S(2)}) collective-permute-start(bf16[512,1024]{1,0:T(8,128)(2,1)} %get-tuple-element.8), channel_id=1, source_target_pairs={{0,8},{1,17},{2,10},{3,19},{4,20},{5,13},{6,22},{7,15},{8,0},{9,25... | collective-permute-start | bytes 3145736 | tf_op jit(solution)/shard_map/ppermute | solution.py:53
  33.3 30.8 %collective-permute-start.7 = (bf16[512,1024]{1,0:T(8,128)(2,1)S(1)}, bf16[512,1024]{1,0:T(8,128)(2,1)S(1)}, u32[]{:S(2)}, u32[]{:S(2)}) collective-permute-start(bf16[512,1024]{1,0:T(8,128)(2,1)S(1)} %collective-permute-done.5), channel_id=1, source_target_pairs={{0,16},{1,9},{2,18},{3,11},{4,12},{5,21},{6,14},{7,23},{8,24},{9,1... | collective-permute-start | bytes 3145736 | tf_op jit(solution)/shard_map/ppermute | solution.py:59
  34.0 30.1 %collective-permute-start.8 = (bf16[512,1024]{1,0:T(8,128)(2,1)S(1)}, bf16[512,1024]{1,0:T(8,128)(2,1)S(1)}, u32[]{:S(2)}, u32[]{:S(2)}) collective-permute-start(bf16[512,1024]{1,0:T(8,128)(2,1)S(1)} %collective-permute-done.5), channel_id=1, source_target_pairs={{0,1},{1,0},{2,3},{3,2},{4,5},{5,4},{6,7},{7,6},{8,9},{9,8},{10,11... | collective-permute-start | bytes 3145736 | tf_op jit(solution)/shard_map/ppermute | solution.py:60
  37.3 1.6 %slice-start.1 = ((s8[6291456]{0:T(1024)(128)(4,1)}), s8[2097152]{0:T(1024)(128)(4,1)S(1)}, s32[]{:S(2)}) async-start(s8[6291456]{0:T(1024)(128)(4,1)} %bitcast.112), calls=%async_computation.1 | async-start | bytes 4194304
  38.9 1.7 %copy-start.4 = (bf16[384,1024]{1,0:T(8,128)(2,1)S(1)}, bf16[384,1024]{1,0:T(8,128)(2,1)}, u32[]{:S(2)}) copy-start(bf16[384,1024]{1,0:T(8,128)(2,1)} %param.9) | copy-start | bytes 2359300
  44.2 39.3 %collective-permute-start.15 = (bf16[4,16,9216]{2,1,0:T(8,128)(2,1)}, bf16[4,16,9216]{2,1,0:T(8,128)(2,1)S(1)}, u32[]{:S(2)}, u32[]{:S(2)}) collective-permute-start(bf16[4,16,9216]{2,1,0:T(8,128)(2,1)} %pad_maximum_fusion.2), channel_id=1, source_target_pairs={{0,4},{4,0},{8,12},{12,8},{16,20},{20,16},{24,28},{28,24},{1,5},{5... | collective-permute-start | bytes 3538952 | tf_op jit(solution)/shard_map/ppermute | solution.py:145
  48.4 6.0 %copy-start.2 = (bf16[1024,1024]{1,0:T(8,128)(2,1)S(1)}, bf16[1024,1024]{1,0:T(8,128)(2,1)}, u32[]{:S(2)}) copy-start(bf16[1024,1024]{1,0:T(8,128)(2,1)} %param.10) | copy-start | bytes 6291460
  64.5 41.2 %collective-permute-start.10 = (bf16[3,512,1024]{2,1,0:T(8,128)(2,1)S(1)}, bf16[3,512,1024]{2,1,0:T(8,128)(2,1)S(1)}, u32[]{:S(2)}, u32[]{:S(2)}) collective-permute-start(bf16[3,512,1024]{2,1,0:T(8,128)(2,1)S(1)} %pad_maximum_fusion), channel_id=1, source_target_pairs={{0,4},{4,0},{8,12},{12,8},{16,20},{20,16},{24,28},{28,24},{1,5},{5... | collective-permute-start | bytes 9437192 | tf_op jit(solution)/shard_map/ppermute | solution.py:64
  72.6 2.4 %copy-start.18 = (f32[3,128,512]{2,1,0:T(8,128)S(1)}, f32[3,128,512]{2,1,0:T(8,128)}, u32[]{:S(2)}) copy-start(f32[3,128,512]{2,1,0:T(8,128)} %fusion.98) | copy-start | bytes 2359300
  72.9 3.9 %copy-start.17 = (f32[3,128,512]{2,1,0:T(8,128)S(1)}, f32[3,128,512]{2,1,0:T(8,128)}, u32[]{:S(2)}) copy-start(f32[3,128,512]{2,1,0:T(8,128)} %fusion.96) | copy-start | bytes 2359300
  73.0 15.1 %collective-permute-start.11 = (bf16[512,1024]{1,0:T(8,128)(2,1)}, bf16[512,1024]{1,0:T(8,128)(2,1)S(1)}, u32[]{:S(2)}, u32[]{:S(2)}) collective-permute-start(bf16[512,1024]{1,0:T(8,128)(2,1)} %collective-permute-done.6), channel_id=1, source_target_pairs={{0,16},{1,9},{2,18},{3,11},{4,12},{5,21},{6,14},{7,23},{8,24},{9,1... | collective-permute-start | bytes 3145736 | tf_op jit(solution)/shard_map/ppermute | solution.py:59
  74.5 15.6 %collective-permute-start.9 = (bf16[512,1024]{1,0:T(8,128)(2,1)}, bf16[512,1024]{1,0:T(8,128)(2,1)S(1)}, u32[]{:S(2)}, u32[]{:S(2)}) collective-permute-start(bf16[512,1024]{1,0:T(8,128)(2,1)} %collective-permute-done.6), channel_id=1, source_target_pairs={{0,4},{4,0},{8,12},{12,8},{16,20},{20,16},{24,28},{28,24},{1,5},{5... | collective-permute-start | bytes 3145736 | tf_op jit(solution)/shard_map/ppermute | solution.py:58
  74.5 25.8 %collective-permute-start.12 = (bf16[512,1024]{1,0:T(8,128)(2,1)}, bf16[512,1024]{1,0:T(8,128)(2,1)S(1)}, u32[]{:S(2)}, u32[]{:S(2)}) collective-permute-start(bf16[512,1024]{1,0:T(8,128)(2,1)} %collective-permute-done.6), channel_id=1, source_target_pairs={{0,1},{1,0},{2,3},{3,2},{4,5},{5,4},{6,7},{7,6},{8,9},{9,8},{10,11... | collective-permute-start | bytes 3145736 | tf_op jit(solution)/shard_map/ppermute | solution.py:60
  76.8 2.0 %copy-start.15 = (f32[3,128,512]{2,1,0:T(8,128)S(1)}, f32[3,128,512]{2,1,0:T(8,128)}, u32[]{:S(2)}) copy-start(f32[3,128,512]{2,1,0:T(8,128)} %fusion.94) | copy-start | bytes 2359300
  78.8 1.1 copy-start.16
  79.4 2.4 %copy-start.14 = (f32[3,128,512]{2,1,0:T(8,128)S(1)}, f32[3,128,512]{2,1,0:T(8,128)}, u32[]{:S(2)}) copy-start(f32[3,128,512]{2,1,0:T(8,128)} %fusion.90) | copy-start | bytes 2359300
  81.8 1.1 copy-start.13
  83.5 8.0 %copy-start.12 = (f32[3,128,512]{2,1,0:T(8,128)S(1)}, f32[3,128,512]{2,1,0:T(8,128)}, u32[]{:S(2)}) copy-start(f32[3,128,512]{2,1,0:T(8,128)} %fusion.86) | copy-start | bytes 2359300
  88.0 12.9 %collective-permute-start.16 = (bf16[16,9216]{1,0:T(8,128)(2,1)S(1)}, bf16[16,9216]{1,0:T(8,128)(2,1)S(1)}, u32[]{:S(2)}, u32[]{:S(2)}) collective-permute-start(bf16[16,9216]{1,0:T(8,128)(2,1)S(1)} %get-tuple-element.9), channel_id=1, source_target_pairs={{0,8},{4,12},{8,0},{12,4},{16,24},{20,28},{24,16},{28,20},{1,9},{5... | collective-permute-start | bytes 884744 | tf_op jit(solution)/shard_map/ppermute | solution.py:158
  89.4 12.4 %collective-permute-start.17 = (bf16[16,9216]{1,0:T(8,128)(2,1)S(1)}, bf16[16,9216]{1,0:T(8,128)(2,1)S(1)}, u32[]{:S(2)}, u32[]{:S(2)}) collective-permute-start(bf16[16,9216]{1,0:T(8,128)(2,1)S(1)} %get-tuple-element.10), channel_id=1, source_target_pairs={{0,16},{4,20},{8,24},{12,28},{16,0},{20,4},{24,8},{28,12},{1,17},{... | collective-permute-start | bytes 884744 | tf_op jit(solution)/shard_map/ppermute | solution.py:158
  90.1 13.4 %collective-permute-start.18 = (bf16[16,9216]{1,0:T(8,128)(2,1)S(1)}, bf16[16,9216]{1,0:T(8,128)(2,1)S(1)}, u32[]{:S(2)}, u32[]{:S(2)}) collective-permute-start(bf16[16,9216]{1,0:T(8,128)(2,1)S(1)} %get-tuple-element.11), channel_id=1, source_target_pairs={{0,24},{4,28},{8,16},{12,20},{16,8},{20,12},{24,0},{28,4},{1,25},{... | collective-permute-start | bytes 884744 | tf_op jit(solution)/shard_map/ppermute | solution.py:158
  100.3 9.0 %collective-permute-start.13 = (bf16[512,1024]{1,0:T(8,128)(2,1)S(1)}, bf16[512,1024]{1,0:T(8,128)(2,1)S(1)}, u32[]{:S(2)}, u32[]{:S(2)}) collective-permute-start(bf16[512,1024]{1,0:T(8,128)(2,1)S(1)} %collective-permute-done.11), channel_id=1, source_target_pairs={{0,4},{4,0},{8,12},{12,8},{16,20},{20,16},{24,28},{28,24},{1,5},{5... | collective-permute-start | bytes 3145736 | tf_op jit(solution)/shard_map/ppermute | solution.py:68
  100.9 4.2 %collective-permute-start.14 = (bf16[512,1024]{1,0:T(8,128)(2,1)S(1)}, bf16[512,1024]{1,0:T(8,128)(2,1)S(1)}, u32[]{:S(2)}, u32[]{:S(2)}) collective-permute-start(bf16[512,1024]{1,0:T(8,128)(2,1)S(1)} %collective-permute-done.12), channel_id=1, source_target_pairs={{0,4},{4,0},{8,12},{12,8},{16,20},{20,16},{24,28},{28,24},{1,5},{5... | collective-permute-start | bytes 3145736 | tf_op jit(solution)/shard_map/ppermute | solution.py:69
  110.2 1.3 %copy-start.10 = (f32[3,128,512]{2,1,0:T(8,128)S(1)}, f32[3,128,512]{2,1,0:T(8,128)}, u32[]{:S(2)}) copy-start(f32[3,128,512]{2,1,0:T(8,128)} %fusion.84) | copy-start | bytes 2359300
  111.2 1.2 copy-start.11
  112.1 1.2 copy-start.9
  113.0 1.2 copy-start.8
  113.9 1.2 copy-start.7
  114.9 1.2 copy-start.6
  116.1 4.0 %copy-start.1 = (s32[32]{0:T(128)S(1)}, s32[32]{0:T(128)}, u32[]{:S(2)}) copy-start(s32[32]{0:T(128)} %param.15) | copy-start | bytes 388
  117.3 2.7 %copy-start.3 = (bf16[384,8192]{1,0:T(8,128)(2,1)}, bf16[384,8192]{1,0:T(8,128)(2,1)S(1)}, u32[]{:S(2)}) copy-start(bf16[384,8192]{1,0:T(8,128)(2,1)S(1)} %fusion.31) | copy-start | bytes 18874372

commit v19 on v17

--- a/solution.py
+++ b/solution.py
@@ -43,14 +43,17 @@
     rows = shard.shape[0] // WEIGHT_CHUNKS
     result = []
     previous = None
-    sibling_shard = lax.ppermute(shard, "fsdp", xor_pairs(members, 1))
     for k in range(WEIGHT_CHUNKS):
         piece = shard[k * rows:(k + 1) * rows]
         result.append((0.0, sources[0], k, piece))
-        result.append((1.0, sibling_sources[0], k, sibling_shard[k * rows:(k + 1) * rows]))
         if previous is not None:
             piece, _ = lax.optimization_barrier((piece, previous))
         first = lax.ppermute(piece, ("fsdp", "dp"), first_pairs)
+        if previous is None:
+            held, _ = lax.optimization_barrier((shard, first))
+            sibling_shard = lax.ppermute(held, "fsdp", xor_pairs(members, 1))
+            for j in range(WEIGHT_CHUNKS):
+                result.append((2.5, sibling_sources[0], j, sibling_shard[j * rows:(j + 1) * rows]))
         previous = first
         result.append((2.0 + 2 * k, sources[1], k, first))
         result.append((3.0 + 2 * k, sibling_sources[1], k, lax.ppermute(first, "fsdp", xor_pairs(members, 1))))

time: 115 us -> 133 us (1.16)
  waiting for transfers between devices: 13.6 us -> 26.9 us
  local copies, waits for them, and re-layouts: 12 us -> 16.8 us
  matrix products: 43.9 us -> 41 us
  other arithmetic: 8.15 us -> 11 us
    ppermute x2, waiting for transfers between devices: 2.17 us -> 10.4 us  [relay_gather(): relayed = lax.ppermute(first, ('fsdp', 'dp'), relay_pairs)]
    ppermute x3, waiting for transfers between devices: 0.01 us -> 7.79 us  [on_device(): by_step[step] = lax.ppermute(own_adapter, 'fsdp', xor_pairs(members, step))]
    unnamed x46, local copies, waits for them, and re-layouts: 5.47 us -> 8.67 us
    ppermute x3, waiting for transfers between devices: 2.47 us -> 0.01 us  [on_device(): lax.ppermute(sent, 'fsdp', xor_pairs(members, step)).astype(jnp.float32)]
    ppermute x1, starting transfers between devices: 0.01 us -> 1.73 us  [relay_gather(): sibling_shard = lax.ppermute(held, 'fsdp', xor_pairs(members, 1))]
    dot_general x16, matrix products: 13.8 us -> 12.3 us  [on_device(): lax.dot_general(masked_cot, weight_piece, (((1,), (1,)), ((), ())), prefe...]
    dot_general x16, matrix products: 13.5 us -> 12.1 us  [on_device(): jnp.dot(token_piece, weight_piece, preferred_element_type=jnp.float32)]
  transfers between devices with their start and end apart: 20 -> 20, of which waited for: 5 -> 3; matrix products, arithmetic and copies ran while one was open for 45% -> 42% of each run, Pallas kernels for 0% -> 0%
where the time goes in v19:
time: 133 us; the launch traced here: 132 us
  matrix products  41 us (31%)
  waiting for transfers between devices  26.9 us (20%)
  between operations  19 us (14%)
  starting transfers between devices  17.6 us (13%)
  local copies, waits for them, and re-layouts  16.8 us (13%)
  other arithmetic  11 us (8%)
    dot_general x16, matrix products, on_device(): jnp.einsum('uio,uof->uif', low_rank_gradient, down_piece, preferred_eleme...  13 us
    dot_general x16, matrix products, on_device(): lax.dot_general(masked_cot, weight_piece, (((1,), (1,)), ((), ())), prefe...  12.3 us
    dot_general x16, matrix products, on_device(): jnp.dot(token_piece, weight_piece, preferred_element_type=jnp.float32)  12.1 us
    ppermute x2, waiting for transfers between devices, relay_gather(): relayed = lax.ppermute(first, ('fsdp', 'dp'), relay_pairs)  10.4 us
    unnamed x46, local copies, waits for them, and re-layouts  8.67 us
    ppermute x2, waiting for transfers between devices, relay_gather(): partner = lax.ppermute(first, ('fsdp', 'dp'), partner_pairs)  8.59 us
    ppermute x3, waiting for transfers between devices, on_device(): by_step[step] = lax.ppermute(own_adapter, 'fsdp', xor_pairs(members, step))  7.79 us
    ppermute x3, starting transfers between devices, on_device(): by_step[step] = lax.ppermute(own_adapter, 'fsdp', xor_pairs(members, step))  4.47 us
  transfers between devices with their start and end apart: 20, of which 3 were waited for; matrix products, arithmetic and copies ran while one was open for 42% of the time, Pallas kernels for 0%

profile of v19, /device:TPU:0, one launch (start us, length us, event | category | flops | bytes accessed | tf_op | source)
XLA Modules:
  0.0 132.3 jit_solution(1321587066430103890)
XLA Ops:
  0.6 1.7 %fusion.139 = (bf16[1,16,9216]{2,1,0:T(8,128)(2,1)S(1)}, bf16[16,9216]{1,0:T(8,128)(2,1)}) fusion(bf16[16,1024]{1,0:T(8,128)(2,1)} %bitcast.138, bf16[16,8192]{1,0:T(8,128)(2,1)} %bitcast.120), kind=kLoop, calls=%fused_computation.215 | loop fusion | flops 589824 | bytes 884736 | tf_op jit(solution)/shard_map/stack | solution.py:105
  2.4 2.9 %collective-permute-start = (bf16[16,9216]{1,0:T(8,128)(2,1)}, bf16[16,9216]{1,0:T(8,128)(2,1)S(1)}, u32[]{:S(2)}, u32[]{:S(2)}) collective-permute-start(bf16[16,9216]{1,0:T(8,128)(2,1)} %get-tuple-element.30), channel_id=1, source_target_pairs={{0,8},{4,12},{8,0},{12,4},{16,24},{20,28},{24,16},{28,20},{1,9},{5... | collective-permute-start | bytes 884744 | tf_op jit(solution)/shard_map/ppermute | solution.py:100
  5.3 1.5 %collective-permute-start.1 = (bf16[16,9216]{1,0:T(8,128)(2,1)}, bf16[16,9216]{1,0:T(8,128)(2,1)S(1)}, u32[]{:S(2)}, u32[]{:S(2)}) collective-permute-start(bf16[16,9216]{1,0:T(8,128)(2,1)} %get-tuple-element.30), channel_id=1, source_target_pairs={{0,16},{4,20},{8,24},{12,28},{16,0},{20,4},{24,8},{28,12},{1,17},{... | collective-permute-start | bytes 884744 | tf_op jit(solution)/shard_map/ppermute | solution.py:100
  6.9 3.2 %fusion.146 = (bf16[512,1024]{1,0:T(8,128)(2,1)}, bf16[512,1024]{1,0:T(8,128)(2,1)}) fusion(bf16[1024,1024]{1,0:T(8,128)(2,1)} %param.10), kind=kLoop, calls=%fused_computation.220 | loop fusion | bytes 4194304 | tf_op jit(solution)/shard_map/slice | solution.py:47
  10.1 2.0 %collective-permute-start.4 = (bf16[512,1024]{1,0:T(8,128)(2,1)}, bf16[512,1024]{1,0:T(8,128)(2,1)}, u32[]{:S(2)}, u32[]{:S(2)}) collective-permute-start(bf16[512,1024]{1,0:T(8,128)(2,1)} %get-tuple-element.25), channel_id=1, source_target_pairs={{0,8},{1,17},{2,10},{3,19},{4,20},{5,13},{6,22},{7,15},{8,0},{9,25... | collective-permute-start | bytes 3145736 | tf_op jit(solution)/shard_map/ppermute | solution.py:51
  12.1 1.1 gather_fusion
  13.3 0.7 fusion.137
  14.0 7.8 %collective-permute-done.1 = bf16[16,9216]{1,0:T(8,128)(2,1)S(1)} collective-permute-done((bf16[16,9216]{1,0:T(8,128)(2,1)}, bf16[16,9216]{1,0:T(8,128)(2,1)S(1)}, u32[]{:S(2)}, u32[]{:S(2)}) %collective-permute-start.1) | collective-permute-done | bytes 294944 | tf_op jit(solution)/shard_map/ppermute | solution.py:100
  21.8 1.2 pad_maximum_fusion.1
  23.0 0.7 and_select_fusion
  41.8 0.8 constant_dynamic-update-slice_fusion.3
  42.7 1.7 %collective-permute-start.5 = (bf16[1024,1024]{1,0:T(8,128)(2,1)}, bf16[1024,1024]{1,0:T(8,128)(2,1)S(1)}, u32[]{:S(2)}, u32[]{:S(2)}) collective-permute-start(bf16[1024,1024]{1,0:T(8,128)(2,1)} %param.10), channel_id=1, source_target_pairs={{0,4},{4,0},{8,12},{12,8},{16,20},{20,16},{24,28},{28,24},{1,5},{5... | collective-permute-start | bytes 6291464 | tf_op jit(solution)/shard_map/ppermute | solution.py:54
  45.0 1.0 collective-permute-start.9
  46.0 1.0 slice_dynamic-update-slice_fusion.3
  47.0 1.1 slice_dynamic-update-slice_fusion.2
  48.2 1.1 slice_dynamic-update-slice_fusion.1
  49.4 1.0 slice_dynamic-update-slice_fusion
  50.6 1.7 %fusion.32 = bf16[3,16,128]{2,1,0:T(8,128)(2,1)S(1)} fusion(bf16[3,128,8192]{2,1,0:T(8,128)(2,1)S(1)} %bitcast.111, f32[3,128]{1,0:T(4,128)S(1)} %get-tuple-element.32, bf16[3,16,9216]{2,1,0:T(8,128)(2,1)S(1)} %pad_maximum_fusion.3), kind=kOutput, calls=%fused_computation.69 | convolution fusion | flops 100675584 | bytes 7092224 | tf_op jit(solution)/shard_map/cvj,coj->cvo/dot_general | solution.py:120
  53.3 0.9 fusion.148
  55.4 1.2 fusion.99
  56.6 1.2 fusion.97
  59.0 1.2 fusion.87
  60.2 1.3 fusion.85
  61.4 1.3 fusion.83
  62.7 1.2 fusion.81
  63.9 1.2 fusion.79
  65.1 1.2 fusion.77
  66.3 1.2 fusion.75
  68.7 0.7 broadcast_in_dim.44
  69.4 0.6 fusion.1
  70.1 1.9 %convolution_add_fusion.4 = f32[384,1024]{1,0:T(8,128)S(1)} fusion(f32[384,1024]{1,0:T(8,128)S(1)} %convolution_add_fusion.5, bf16[512,1024]{1,0:T(8,128)(2,1)} %collective-permute-done.4, bf16[384,8192]{1,0:T(8,128)(2,1)S(1)} %bitcast.110, s32[]{:T(128)S(6)} %select_n.294), kind=kOutput, calls=%fused_computation.13 | convolution fusion | flops 403046400 | bytes 4587524 | tf_op jit(solution)/shard_map/dot_general | solution.py:175
  73.5 1.8 %fusion.5 = bf16[384,8192]{1,0:T(8,128)(2,1)S(1)} fusion(bf16[384,8192]{1,0:T(8,128)(2,1)S(1)} %fusion.3, s32[]{:T(128)S(6)} %select_n.294, f32[384,512]{1,0:T(8,128)S(1)} %bitcast.135, bf16[512,1024]{1,0:T(8,128)(2,1)} %collective-permute-done.4, bf16[384,1024]{1,0:T(8,128)(2,1)S(1)} %copy-done.4, f32[384]{0:T(512)S(1)} %get-tuple-element.31), kind=kOutput, calls=%fused_computation.37 | convolution fusion | flops 404226048 | bytes 3016708 | tf_op jit(solution)/shard_map/dot_general | solution.py:179
  76.4 1.3 collective-permute-start.12
  77.7 1.8 %fusion.60 = f32[384,1024]{1,0:T(8,128)S(1)} fusion(bf16[512,1024]{1,0:T(8,128)(2,1)} %collective-permute-done.7, bf16[384,8192]{1,0:T(8,128)(2,1)S(1)} %bitcast.110, s32[]{:T(128)S(6)} %select_n.298), kind=kOutput, calls=%fused_computation.113 | convolution fusion | flops 402653184 | bytes 3014660 | tf_op jit(solution)/shard_map/dot_general | solution.py:175
  81.0 10.4 %collective-permute-done.12 = bf16[512,1024]{1,0:T(8,128)(2,1)S(1)} collective-permute-done((bf16[512,1024]{1,0:T(8,128)(2,1)}, bf16[512,1024]{1,0:T(8,128)(2,1)S(1)}, u32[]{:S(2)}, u32[]{:S(2)}) %collective-permute-start.12) | collective-permute-done | bytes 1048608 | tf_op jit(solution)/shard_map/ppermute | solution.py:60
  91.4 1.0 collective-permute-start.13
  92.4 1.3 collective-permute-start.17
  94.3 0.6 fusion.7
  94.9 0.6 fusion.9
  96.7 1.9 %fusion.13 = bf16[384,8192]{1,0:T(8,128)(2,1)S(1)} fusion(bf16[384,8192]{1,0:T(8,128)(2,1)S(1)} %fusion.11, s32[]{:T(128)S(6)} %select_n.298, f32[384,512]{1,0:T(8,128)S(1)} %bitcast.131, bf16[512,1024]{1,0:T(8,128)(2,1)} %collective-permute-done.7, bf16[384,1024]{1,0:T(8,128)(2,1)S(1)} %copy-done.4, f32[384]{0:T(512)S(1)} %get-tuple-element.31), kind=kOutput, calls=%fused_computation.45 | convolution fusion | flops 404226048 | bytes 3016708 | tf_op jit(solution)/shard_map/dot_general | solution.py:179
  99.9 0.8 copy-done.12
  103.4 1.7 %collective-permute-start.19 = (bf16[16,9216]{1,0:T(8,128)(2,1)S(1)}, bf16[16,9216]{1,0:T(8,128)(2,1)S(1)}, u32[]{:S(2)}, u32[]{:S(2)}) collective-permute-start(bf16[16,9216]{1,0:T(8,128)(2,1)S(1)} %get-tuple-element.13), channel_id=1, source_target_pairs={{0,24},{4,28},{8,16},{12,20},{16,8},{20,12},{24,0},{28,4},{1,25},{... | collective-permute-start | bytes 884744 | tf_op jit(solution)/shard_map/ppermute | solution.py:158
  107.7 8.6 %collective-permute-done.13 = bf16[512,1024]{1,0:T(8,128)(2,1)S(1)} collective-permute-done((bf16[512,1024]{1,0:T(8,128)(2,1)}, bf16[512,1024]{1,0:T(8,128)(2,1)S(1)}, u32[]{:S(2)}, u32[]{:S(2)}) %collective-permute-start.13) | collective-permute-done | bytes 1048608 | tf_op jit(solution)/shard_map/ppermute | solution.py:61
  117.7 0.7 slice_bitcast_fusion.6
  118.5 0.6 slice_bitcast_fusion.7
  121.9 0.8 convolution_add_fusion
  123.7 1.0 multiply_convert_fusion.1
  129.6 2.7 %copy-done.3 = bf16[384,8192]{1,0:T(8,128)(2,1)} copy-done((bf16[384,8192]{1,0:T(8,128)(2,1)}, bf16[384,8192]{1,0:T(8,128)(2,1)S(1)}, u32[]{:S(2)}) %copy-start.3) | copy-done | bytes 6291480
  (127 shorter events, 28.1 us)
Async XLA Ops:
  0.6 11.5 %copy-start = (s32[32]{0:T(128)S(1)}, s32[32]{0:T(128)}, u32[]{:S(2)}) copy-start(s32[32]{0:T(128)} %param.15) | copy-start | bytes 388
  2.4 9.6 %copy-start.17 = (s32[3]{0:T(128)S(1)}, s32[3]{0:T(128)}, u32[]{:S(2)}) copy-start(s32[3]{0:T(128)} %param.13) | copy-start | bytes 40
  2.4 9.6 %copy-start.15 = (s32[3]{0:T(128)S(1)}, s32[3]{0:T(128)}, u32[]{:S(2)}) copy-start(s32[3]{0:T(128)} %param.14) | copy-start | bytes 40
  2.4 11.6 %collective-permute-start = (bf16[16,9216]{1,0:T(8,128)(2,1)}, bf16[16,9216]{1,0:T(8,128)(2,1)S(1)}, u32[]{:S(2)}, u32[]{:S(2)}) collective-permute-start(bf16[16,9216]{1,0:T(8,128)(2,1)} %get-tuple-element.30), channel_id=1, source_target_pairs={{0,8},{4,12},{8,0},{12,4},{16,24},{20,28},{24,16},{28,20},{1,9},{5... | collective-permute-start | bytes 884744 | tf_op jit(solution)/shard_map/ppermute | solution.py:100
  5.3 16.5 %collective-permute-start.1 = (bf16[16,9216]{1,0:T(8,128)(2,1)}, bf16[16,9216]{1,0:T(8,128)(2,1)S(1)}, u32[]{:S(2)}, u32[]{:S(2)}) collective-permute-start(bf16[16,9216]{1,0:T(8,128)(2,1)} %get-tuple-element.30), channel_id=1, source_target_pairs={{0,16},{4,20},{8,24},{12,28},{16,0},{20,4},{24,8},{28,12},{1,17},{... | collective-permute-start | bytes 884744 | tf_op jit(solution)/shard_map/ppermute | solution.py:100
  6.8 14.9 %collective-permute-start.2 = (bf16[16,9216]{1,0:T(8,128)(2,1)}, bf16[16,9216]{1,0:T(8,128)(2,1)S(1)}, u32[]{:S(2)}, u32[]{:S(2)}) collective-permute-start(bf16[16,9216]{1,0:T(8,128)(2,1)} %get-tuple-element.30), channel_id=1, source_target_pairs={{0,24},{4,28},{8,16},{12,20},{16,8},{20,12},{24,0},{28,4},{1,25},{... | collective-permute-start | bytes 884744 | tf_op jit(solution)/shard_map/ppermute | solution.py:100
  6.9 43.8 %slice-start = ((s8[6291456]{0:T(1024)(128)(4,1)}), s8[2097152]{0:T(1024)(128)(4,1)S(1)}, s32[]{:S(2)}) async-start(s8[6291456]{0:T(1024)(128)(4,1)} %bitcast.109), calls=%async_computation | async-start | bytes 4194304
  10.1 31.8 %copy-start.5 = (bf16[1,16,8192]{2,1,0:T(8,128)(2,1)S(1)}, bf16[1,16,8192]{2,1,0:T(8,128)(2,1)}, u32[]{:S(2)}) copy-start(bf16[1,16,8192]{2,1,0:T(8,128)(2,1)} %param.11) | copy-start | bytes 786436
  10.1 32.6 %collective-permute-start.4 = (bf16[512,1024]{1,0:T(8,128)(2,1)}, bf16[512,1024]{1,0:T(8,128)(2,1)}, u32[]{:S(2)}, u32[]{:S(2)}) collective-permute-start(bf16[512,1024]{1,0:T(8,128)(2,1)} %get-tuple-element.25), channel_id=1, source_target_pairs={{0,8},{1,17},{2,10},{3,19},{4,20},{5,13},{6,22},{7,15},{8,0},{9,25... | collective-permute-start | bytes 3145736 | tf_op jit(solution)/shard_map/ppermute | solution.py:51
  13.3 9.7 %copy-start.16 = (s32[3]{0:T(128)S(1)}, s32[3]{0:T(128)}, u32[]{:S(2)}) copy-start(s32[3]{0:T(128)} %gather_fusion) | copy-start | bytes 40
  22.9 23.1 %collective-permute-start.3 = (bf16[4,16,9216]{2,1,0:T(8,128)(2,1)}, bf16[4,16,9216]{2,1,0:T(8,128)(2,1)}, u32[]{:S(2)}, u32[]{:S(2)}) collective-permute-start(bf16[4,16,9216]{2,1,0:T(8,128)(2,1)} %pad_maximum_fusion.1), channel_id=1, source_target_pairs={{0,4},{4,0},{8,12},{12,8},{16,20},{20,16},{24,28},{28,24},{1,5},{5... | collective-permute-start | bytes 3538952 | tf_op jit(solution)/shard_map/ppermute | solution.py:102
  42.6 33.7 %collective-permute-start.7 = (bf16[512,1024]{1,0:T(8,128)(2,1)}, bf16[512,1024]{1,0:T(8,128)(2,1)}, u32[]{:S(2)}, u32[]{:S(2)}) collective-permute-start(bf16[512,1024]{1,0:T(8,128)(2,1)} %get-tuple-element.10), channel_id=1, source_target_pairs={{0,8},{1,17},{2,10},{3,19},{4,20},{5,13},{6,22},{7,15},{8,0},{9,25... | collective-permute-start | bytes 3145736 | tf_op jit(solution)/shard_map/ppermute | solution.py:51
  42.7 49.7 %collective-permute-start.5 = (bf16[1024,1024]{1,0:T(8,128)(2,1)}, bf16[1024,1024]{1,0:T(8,128)(2,1)S(1)}, u32[]{:S(2)}, u32[]{:S(2)}) collective-permute-start(bf16[1024,1024]{1,0:T(8,128)(2,1)} %param.10), channel_id=1, source_target_pairs={{0,4},{4,0},{8,12},{12,8},{16,20},{20,16},{24,28},{28,24},{1,5},{5... | collective-permute-start | bytes 6291464 | tf_op jit(solution)/shard_map/ppermute | solution.py:54
  44.4 30.9 %collective-permute-start.8 = (bf16[512,1024]{1,0:T(8,128)(2,1)}, bf16[512,1024]{1,0:T(8,128)(2,1)S(1)}, u32[]{:S(2)}, u32[]{:S(2)}) collective-permute-start(bf16[512,1024]{1,0:T(8,128)(2,1)} %collective-permute-done.4), channel_id=1, source_target_pairs={{0,16},{1,9},{2,18},{3,11},{4,12},{5,21},{6,14},{7,23},{8,24},{9,1... | collective-permute-start | bytes 3145736 | tf_op jit(solution)/shard_map/ppermute | solution.py:60
  45.0 30.9 %collective-permute-start.9 = (bf16[512,1024]{1,0:T(8,128)(2,1)}, bf16[512,1024]{1,0:T(8,128)(2,1)S(1)}, u32[]{:S(2)}, u32[]{:S(2)}) collective-permute-start(bf16[512,1024]{1,0:T(8,128)(2,1)} %collective-permute-done.4), channel_id=1, source_target_pairs={{0,1},{1,0},{2,3},{3,2},{4,5},{5,4},{6,7},{7,6},{8,9},{9,8},{10,11... | collective-permute-start | bytes 3145736 | tf_op jit(solution)/shard_map/ppermute | solution.py:61
  47.0 3.6 %slice-start.1 = ((s8[6291456]{0:T(1024)(128)(4,1)}), s8[4194304]{0:T(1024)(128)(4,1)S(1)}, s32[]{:S(2)}) async-start(s8[6291456]{0:T(1024)(128)(4,1)} %bitcast.109), calls=%async_computation.1 | async-start | bytes 8388608
  50.6 1.7 %copy-start.4 = (bf16[384,1024]{1,0:T(8,128)(2,1)S(1)}, bf16[384,1024]{1,0:T(8,128)(2,1)}, u32[]{:S(2)}) copy-start(bf16[384,1024]{1,0:T(8,128)(2,1)} %param.9) | copy-start | bytes 2359300
  55.0 25.1 %collective-permute-start.16 = (bf16[4,16,9216]{2,1,0:T(8,128)(2,1)S(1)}, bf16[4,16,9216]{2,1,0:T(8,128)(2,1)S(1)}, u32[]{:S(2)}, u32[]{:S(2)}) collective-permute-start(bf16[4,16,9216]{2,1,0:T(8,128)(2,1)S(1)} %pad_maximum_fusion.2), channel_id=1, source_target_pairs={{0,4},{4,0},{8,12},{12,8},{16,20},{20,16},{24,28},{28,24},{1,5},{5... | collective-permute-start | bytes 3538952 | tf_op jit(solution)/shard_map/ppermute | solution.py:145
  61.4 6.1 %copy-start.2 = (bf16[1024,1024]{1,0:T(8,128)(2,1)S(1)}, bf16[1024,1024]{1,0:T(8,128)(2,1)}, u32[]{:S(2)}) copy-start(bf16[1024,1024]{1,0:T(8,128)(2,1)} %param.10) | copy-start | bytes 6291460
  70.1 2.2 %copy-start.14 = (f32[3,128,512]{2,1,0:T(8,128)S(1)}, f32[3,128,512]{2,1,0:T(8,128)}, u32[]{:S(2)}) copy-start(f32[3,128,512]{2,1,0:T(8,128)} %fusion.99) | copy-start | bytes 2359300
  72.3 1.1 copy-start.13
  75.3 20.2 %collective-permute-start.6 = (bf16[512,1024]{1,0:T(8,128)(2,1)}, bf16[512,1024]{1,0:T(8,128)(2,1)S(1)}, u32[]{:S(2)}, u32[]{:S(2)}) collective-permute-start(bf16[512,1024]{1,0:T(8,128)(2,1)} %collective-permute-done.4), channel_id=1, source_target_pairs={{0,4},{4,0},{8,12},{12,8},{16,20},{20,16},{24,28},{28,24},{1,5},{5... | collective-permute-start | bytes 3145736 | tf_op jit(solution)/shard_map/ppermute | solution.py:59
  76.1 43.0 %collective-permute-start.11 = (bf16[2,512,1024]{2,1,0:T(8,128)(2,1)S(1)}, bf16[2,512,1024]{2,1,0:T(8,128)(2,1)S(1)}, u32[]{:S(2)}, u32[]{:S(2)}) collective-permute-start(bf16[2,512,1024]{2,1,0:T(8,128)(2,1)S(1)} %pad_maximum_fusion), channel_id=1, source_target_pairs={{0,4},{4,0},{8,12},{12,8},{16,20},{20,16},{24,28},{28,24},{1,5},{5... | collective-permute-start | bytes 6291464 | tf_op jit(solution)/shard_map/ppermute | solution.py:65
  76.4 15.1 %collective-permute-start.12 = (bf16[512,1024]{1,0:T(8,128)(2,1)}, bf16[512,1024]{1,0:T(8,128)(2,1)S(1)}, u32[]{:S(2)}, u32[]{:S(2)}) collective-permute-start(bf16[512,1024]{1,0:T(8,128)(2,1)} %collective-permute-done.7), channel_id=1, source_target_pairs={{0,16},{1,9},{2,18},{3,11},{4,12},{5,21},{6,14},{7,23},{8,24},{9,1... | collective-permute-start | bytes 3145736 | tf_op jit(solution)/shard_map/ppermute | solution.py:60
  80.1 23.3 %collective-permute-start.10 = (bf16[512,1024]{1,0:T(8,128)(2,1)}, bf16[512,1024]{1,0:T(8,128)(2,1)S(1)}, u32[]{:S(2)}, u32[]{:S(2)}) collective-permute-start(bf16[512,1024]{1,0:T(8,128)(2,1)} %collective-permute-done.7), channel_id=1, source_target_pairs={{0,4},{4,0},{8,12},{12,8},{16,20},{20,16},{24,28},{28,24},{1,5},{5... | collective-permute-start | bytes 3145736 | tf_op jit(solution)/shard_map/ppermute | solution.py:59
  91.4 24.8 %collective-permute-start.13 = (bf16[512,1024]{1,0:T(8,128)(2,1)}, bf16[512,1024]{1,0:T(8,128)(2,1)S(1)}, u32[]{:S(2)}, u32[]{:S(2)}) collective-permute-start(bf16[512,1024]{1,0:T(8,128)(2,1)} %collective-permute-done.7), channel_id=1, source_target_pairs={{0,1},{1,0},{2,3},{3,2},{4,5},{5,4},{6,7},{7,6},{8,9},{9,8},{10,11... | collective-permute-start | bytes 3145736 | tf_op jit(solution)/shard_map/ppermute | solution.py:61
  92.4 24.5 %collective-permute-start.17 = (bf16[16,9216]{1,0:T(8,128)(2,1)S(1)}, bf16[16,9216]{1,0:T(8,128)(2,1)S(1)}, u32[]{:S(2)}, u32[]{:S(2)}) collective-permute-start(bf16[16,9216]{1,0:T(8,128)(2,1)S(1)} %get-tuple-element.11), channel_id=1, source_target_pairs={{0,8},{4,12},{8,0},{12,4},{16,24},{20,28},{24,16},{28,20},{1,9},{5... | collective-permute-start | bytes 884744 | tf_op jit(solution)/shard_map/ppermute | solution.py:158
  95.5 21.9 %collective-permute-start.18 = (bf16[16,9216]{1,0:T(8,128)(2,1)S(1)}, bf16[16,9216]{1,0:T(8,128)(2,1)S(1)}, u32[]{:S(2)}, u32[]{:S(2)}) collective-permute-start(bf16[16,9216]{1,0:T(8,128)(2,1)S(1)} %get-tuple-element.12), channel_id=1, source_target_pairs={{0,16},{4,20},{8,24},{12,28},{16,0},{20,4},{24,8},{28,12},{1,17},{... | collective-permute-start | bytes 884744 | tf_op jit(solution)/shard_map/ppermute | solution.py:158
  99.5 1.1 copy-start.12
  101.3 1.1 copy-start.11
  103.0 2.1 %copy-start.10 = (f32[3,128,512]{2,1,0:T(8,128)S(1)}, f32[3,128,512]{2,1,0:T(8,128)}, u32[]{:S(2)}) copy-start(f32[3,128,512]{2,1,0:T(8,128)} %fusion.83) | copy-start | bytes 2359300
  103.4 14.0 %collective-permute-start.19 = (bf16[16,9216]{1,0:T(8,128)(2,1)S(1)}, bf16[16,9216]{1,0:T(8,128)(2,1)S(1)}, u32[]{:S(2)}, u32[]{:S(2)}) collective-permute-start(bf16[16,9216]{1,0:T(8,128)(2,1)S(1)} %get-tuple-element.13), channel_id=1, source_target_pairs={{0,24},{4,28},{8,16},{12,20},{16,8},{20,12},{24,0},{28,4},{1,25},{... | collective-permute-start | bytes 884744 | tf_op jit(solution)/shard_map/ppermute | solution.py:158
  116.3 5.7 %collective-permute-start.14 = (bf16[512,1024]{1,0:T(8,128)(2,1)S(1)}, bf16[512,1024]{1,0:T(8,128)(2,1)S(1)}, u32[]{:S(2)}, u32[]{:S(2)}) collective-permute-start(bf16[512,1024]{1,0:T(8,128)(2,1)S(1)} %collective-permute-done.12), channel_id=1, source_target_pairs={{0,4},{4,0},{8,12},{12,8},{16,20},{20,16},{24,28},{28,24},{1,5},{5... | collective-permute-start | bytes 3145736 | tf_op jit(solution)/shard_map/ppermute | solution.py:68
  116.9 5.9 %collective-permute-start.15 = (bf16[512,1024]{1,0:T(8,128)(2,1)S(1)}, bf16[512,1024]{1,0:T(8,128)(2,1)S(1)}, u32[]{:S(2)}, u32[]{:S(2)}) collective-permute-start(bf16[512,1024]{1,0:T(8,128)(2,1)S(1)} %collective-permute-done.13), channel_id=1, source_target_pairs={{0,4},{4,0},{8,12},{12,8},{16,20},{20,16},{24,28},{28,24},{1,5},{5... | collective-permute-start | bytes 3145736 | tf_op jit(solution)/shard_map/ppermute | solution.py:69
  123.6 1.3 copy-start.9
  124.7 1.2 copy-start.8
  125.5 1.2 copy-start.7
  126.5 1.2 copy-start.6
  128.3 4.0 %copy-start.1 = (s32[32]{0:T(128)S(1)}, s32[32]{0:T(128)}, u32[]{:S(2)}) copy-start(s32[32]{0:T(128)} %param.15) | copy-start | bytes 388
  129.6 2.7 %copy-start.3 = (bf16[384,8192]{1,0:T(8,128)(2,1)}, bf16[384,8192]{1,0:T(8,128)(2,1)S(1)}, u32[]{:S(2)}) copy-start(bf16[384,8192]{1,0:T(8,128)(2,1)S(1)} %fusion.31) | copy-start | bytes 18874372
